TPU v7x, 32 devices: a whole 2x2x4 slice. The times are simulated.
32 devices in a mesh: ev: 8 (over z, y), col: 4 (over x, core).
Axes of the slice: x: 2, y: 2, z: 4, core: 2. Of those that a mesh axis runs over, the one named last changes fastest.
Arguments:
- panel: bfloat16 [256, 131072], P('col', 'ev'), may hold values from -12 to 12
- signs: int32 [131072], P('ev'), may hold values from -1 to 1, as said below
- offsets: int32 [2048], replicated, may hold values from 0 to 63
Outputs:
- gram: float32 [256, 256], P('col')
Inputs may be any that keep to these rules, and one draw needn't show every extreme that they name: `signs`: every entry is -1 or +1.
All inputs are finite; a program needn't handle non-finite values.
Results may differ from a plain program's by a relative error of at most 0.0003.
Values sent between devices are 32-bit elements; how exact they have to be, the bound alone decides.
No kernel may reach another device: no remote copies, remote signals or barrier semaphores. Data moves between devices by JAX's collectives and lax.ppermute only.
A program may use at most 64 MiB of HBM per device.

v0:
```python
import math

import jax
import jax.numpy as jnp
from jax import lax
from jax.sharding import PartitionSpec as P

STRIDE = 64


def swapped(value, axis, stride):
    mask = 2**stride
    pairs = [(source, source ^ mask) for source in range(lax.axis_size(axis))]
    return lax.ppermute(value, axis, pairs)


def hadamard(order):
    index = jnp.arange(order, dtype=jnp.int32)
    both = index[:, None] & index[None, :]
    parity = jnp.zeros((order, order), jnp.int32)
    for level in range(order.bit_length() - 1):
        parity = parity + (both >> level & 1)
    return (1 - 2 * (parity % 2)).astype(jnp.float32)


def pick_local(values, offsets, my_index, strata):
    columns = values.shape[0]
    chosen = lax.dynamic_slice_in_dim(offsets, my_index * strata, strata)
    grouped = values.reshape(columns, strata, STRIDE)
    return jnp.take_along_axis(grouped, chosen[None, :, None], axis=2)[:, :, 0]


def per_device(panel, signs, offsets):
    columns, length = panel.shape
    groups = lax.axis_size("ev")
    my_index = lax.axis_index("ev")
    inner_len = length // 128
    strata = length // STRIDE
    high = lax.Precision.HIGHEST
    signed = panel * signs.astype(jnp.bfloat16)[None, :]
    blocks = signed.reshape(columns, 128, inner_len)
    first = jnp.einsum(
        "xa,cab->cxb",
        hadamard(128).astype(jnp.bfloat16),
        blocks,
        preferred_element_type=jnp.float32,
    )
    local = jnp.einsum("yb,cxb->cxy", hadamard(inner_len), first, precision=high).reshape(
        columns, length
    )
    total_events = length * groups
    scale = 1.0 / math.sqrt(total_events * (total_events // STRIDE))
    values = local
    for level in range(groups.bit_length() - 1):
        partner = swapped(values, "ev", level)
        upper_half = my_index >> level & 1 == 1
        values = jnp.where(upper_half, partner - values, values + partner)
    picked = pick_local(values, offsets, my_index, strata)
    sketch = picked * scale
    partial_gram = jnp.dot(
        sketch,
        lax.all_gather(sketch, "col", axis=0, tiled=True).T,
        precision=high,
        preferred_element_type=jnp.float32,
    )
    return lax.psum(partial_gram, "ev")


def solution(mesh):
    return jax.shard_map(
        per_device,
        mesh=mesh,
        in_specs=(P("col", "ev"), P("ev"), P()),
        out_specs=P("col", None),
        check_vma=False,
    )
```

profile of v0, /device:TPU:0, one launch (start us, length us, event | category | flops | bytes accessed | tf_op | source)
XLA Modules:
  0.0 503.6 jit_solution(14643924601332694307)
XLA Ops:
  6.5 0.8 convert_element_type.12
  7.4 1.9 multiply_bitcast_fusion
  9.2 0.6 copy.12
  9.8 0.8 fusion.12
  10.6 6.7 %fusion = f32[64,128,128]{2,1,0:T(8,128)S(1)} fusion(f32[64,128,128]{2,1,0:T(8,128)S(1)} %fusion.12), kind=kOutput, calls=%fused_computation.2 | convolution fusion | flops 1611186176 | bytes 8388608 | tf_op jit(solution)/shard_map/yb,cxb->cxy/dot_general | solution.py:48
  17.3 4.3 copy.17
  21.6 3.0 collective-permute-start
  24.6 90.9 %collective-permute-done = f32[64,16384]{1,0:T(8,128)} collective-permute-done((f32[64,16384]{1,0:T(8,128)}, f32[64,16384]{1,0:T(8,128)}, u32[]{:S(2)}, u32[]{:S(2)}) %collective-permute-start) | collective-permute-done | bytes 4194336 | tf_op jit(solution)/shard_map/ppermute | solution.py:14
  115.5 8.4 %add_select_fusion.2 = f32[64,16384]{1,0:T(8,128)} fusion(f32[64,16384]{1,0:T(8,128)} %collective-permute-done, pred[]{:T(512)S(6)} %eq.14, f32[8,8,128,128]{3,2,1,0:T(8,128)} %bitcast.28), kind=kLoop, calls=%fused_computation.6 | loop fusion | flops 3145728 | bytes 12582913 | tf_op jit(solution)/shard_map/jit(_where)/select_n | solution.py:57
  123.9 1.8 collective-permute-start.1
  125.7 90.3 %collective-permute-done.1 = f32[64,16384]{1,0:T(8,128)} collective-permute-done((f32[64,16384]{1,0:T(8,128)}, f32[64,16384]{1,0:T(8,128)}, u32[]{:S(2)}, u32[]{:S(2)}) %collective-permute-start.1) | collective-permute-done | bytes 4194336 | tf_op jit(solution)/shard_map/ppermute | solution.py:14
  216.0 5.9 %add_select_fusion.1 = f32[64,16384]{1,0:T(8,128)} fusion(f32[64,16384]{1,0:T(8,128)} %add_select_fusion.2, f32[64,16384]{1,0:T(8,128)} %collective-permute-done.1, pred[]{:T(512)S(6)} %eq.13), kind=kLoop, calls=%fused_computation.5 | loop fusion | flops 3145728 | bytes 12582913 | tf_op jit(solution)/shard_map/jit(_where)/select_n | solution.py:57
  221.8 2.5 collective-permute-start.2
  224.3 0.8 compare_and_fusion
  225.1 178.6 %collective-permute-done.2 = f32[64,16384]{1,0:T(8,128)} collective-permute-done((f32[64,16384]{1,0:T(8,128)}, f32[64,16384]{1,0:T(8,128)}, u32[]{:S(2)}, u32[]{:S(2)}) %collective-permute-start.2) | collective-permute-done | bytes 4194336 | tf_op jit(solution)/shard_map/ppermute | solution.py:14
  403.8 5.9 %add_select_fusion = f32[64,16384]{1,0:T(8,128)} fusion(f32[64,16384]{1,0:T(8,128)} %add_select_fusion.1, f32[64,16384]{1,0:T(8,128)} %collective-permute-done.2, pred[]{:T(512)S(6)} %eq.12), kind=kLoop, calls=%fused_computation.4 | loop fusion | flops 3145728 | bytes 12582913 | tf_op jit(solution)/shard_map/jit(_where)/select_n | solution.py:57
  409.6 6.9 %copy.8 = f32[64,16384]{0,1:T(8,128)} copy(f32[64,16384]{1,0:T(8,128)} %add_select_fusion) | data formatting | bytes 8388608 | tf_op jit(solution)/shard_map/jit(_where)/select_n | solution.py:57
  416.5 2.3 gather_fusion
  418.8 0.1 fusion.3
  419.0 0.1 copy.9
  419.0 5.8 %all_gather.3 = f32[256,256]{1,0:T(8,128)S(1)} all-gather(f32[64,256]{1,0:T(8,128)S(1)} %copy.9), channel_id=1, replica_groups=mesh['ev'=8,'col'=4] {'col'}, dimensions={0}, use_global_device_ids=true | all-gather | bytes 327680 | tf_op jit(solution)/shard_map/all_gather | solution.py:62
  424.8 1.1 fusion.2
  425.9 69.4 %all-reduce.2.cloned.1.call-done = f32[64,256]{1,0:T(8,128)} async-done(((f32[64,256]{1,0:T(8,128)}), f32[64,256]{1,0:T(8,128)}) %all-reduce.2.cloned.1.call-update) | async-done | bytes 65552 | tf_op jit(solution)/shard_map/psum | solution.py:66
  495.3 1.5 copy.19
  (7 shorter events, 0.0 us)
Async XLA Ops:
  6.5 488.8 %all-reduce.2.cloned.1.call-start = ((), (), s32[]{:S(2)}) async-start(), calls=%async_computation | async-start | bytes 131072 | tf_op jit(solution)/shard_map/psum | solution.py:66
  17.3 4.3 copy-start
  21.6 93.9 %collective-permute-start = (f32[64,16384]{1,0:T(8,128)}, f32[64,16384]{1,0:T(8,128)}, u32[]{:S(2)}, u32[]{:S(2)}) collective-permute-start(f32[64,16384]{1,0:T(8,128)} %bitcast.26), channel_id=1, source_target_pairs={{0,4},{4,0},{8,12},{12,8},{16,20},{20,16},{24,28},{28,24},{1,5},{5... | collective-permute-start | bytes 12582920 | tf_op jit(solution)/shard_map/ppermute | solution.py:14
  123.9 92.1 %collective-permute-start.1 = (f32[64,16384]{1,0:T(8,128)}, f32[64,16384]{1,0:T(8,128)}, u32[]{:S(2)}, u32[]{:S(2)}) collective-permute-start(f32[64,16384]{1,0:T(8,128)} %add_select_fusion.2), channel_id=1, source_target_pairs={{0,8},{4,12},{8,0},{12,4},{16,24},{20,28},{24,16},{28,20},{1,9},{5... | collective-permute-start | bytes 12582920 | tf_op jit(solution)/shard_map/ppermute | solution.py:14
  221.8 181.9 %collective-permute-start.2 = (f32[64,16384]{1,0:T(8,128)}, f32[64,16384]{1,0:T(8,128)}, u32[]{:S(2)}, u32[]{:S(2)}) collective-permute-start(f32[64,16384]{1,0:T(8,128)} %add_select_fusion.1), channel_id=1, source_target_pairs={{0,16},{4,20},{8,24},{12,28},{16,0},{20,4},{24,8},{28,12},{1,17},{... | collective-permute-start | bytes 12582920 | tf_op jit(solution)/shard_map/ppermute | solution.py:14
Sparse Core Ops, SparseCore 0:
  426.1 69.2 all-reduce.1
where the time goes:
time: 504 us
  waiting for transfers between devices  429 us (85%)
  other arithmetic  23.7 us (5%)
  local copies, waits for them, and re-layouts  15.7 us (3%)
  between operations  13.4 us (3%)
  matrix products  8.53 us (2%)
  starting transfers between devices  7.27 us (1%)
  blocking collectives  5.79 us (1%)
    ppermute x3, waiting for transfers between devices, swapped(): return lax.ppermute(value, axis, pairs)  360 us
    psum x1, waiting for transfers between devices, per_device(): return lax.psum(partial_gram, 'ev')  69.4 us
    select_n x3, other arithmetic, per_device(): values = jnp.where(upper_half, partner - values, values + partner)  20.1 us
  transfers between devices with their start and end apart: 4, of which 4 were waited for; matrix products, arithmetic and copies ran while one was open for 0% of the time, Pallas kernels for 0%

commit v1 on v0

v1 whole, which is shorter than its diff:
```python
import math

import jax
import jax.numpy as jnp
from jax import lax
from jax.sharding import PartitionSpec as P

STRIDE = 64
OUTER = 128


def hadamard(order):
    index = jnp.arange(order, dtype=jnp.int32)
    both = index[:, None] & index[None, :]
    parity = jnp.zeros((order, order), jnp.int32)
    for level in range(order.bit_length() - 1):
        parity = parity + (both >> level & 1)
    return (1 - 2 * (parity % 2)).astype(jnp.float32)


def exchange(value, axis, bit):
    mask = 1 << bit
    pairs = [(source, source ^ mask) for source in range(lax.axis_size(axis))]
    return lax.ppermute(value, axis, pairs)


def split3(value):
    hi = lax.reduce_precision(value, exponent_bits=8, mantissa_bits=7)
    rest = value - hi
    mid = lax.reduce_precision(rest, exponent_bits=8, mantissa_bits=7)
    low = rest - mid
    return tuple(piece.astype(jnp.bfloat16) for piece in (hi, mid, low))


def selection(offsets, my_index, groups, inner):
    per_row = inner // STRIDE
    off = offsets.reshape(groups, OUTER, per_row)
    rows = jnp.arange(per_row, dtype=jnp.int32)[None, None, :] * STRIDE + off
    rows = rows.transpose(1, 0, 2)
    lanes = jnp.arange(inner, dtype=jnp.int32)
    parity = lax.population_count(rows[:, None, :, :] & lanes[None, :, None, None]) & 1
    group_parity = lax.population_count(jnp.arange(groups, dtype=jnp.int32) & my_index) & 1
    parity = parity ^ group_parity[None, None, :, None]
    return (1 - 2 * parity).astype(jnp.bfloat16).reshape(OUTER, inner, groups * per_row)


def per_device(panel, signs, offsets):
    columns, length = panel.shape
    groups = lax.axis_size("ev")
    levels = groups.bit_length() - 1
    my_index = lax.axis_index("ev")
    inner = length // OUTER
    per_row = inner // STRIDE
    high = lax.Precision.HIGHEST

    signed = panel * signs.astype(jnp.bfloat16)[None, :]
    blocks = signed.reshape(columns, OUTER, inner)
    first = jnp.einsum(
        "xa,cab->xcb",
        hadamard(OUTER).astype(jnp.bfloat16),
        blocks,
        preferred_element_type=jnp.float32,
    )
    pick = selection(offsets, my_index, groups, inner)
    pieces = jnp.concatenate(split3(first), axis=1)
    sampled = jnp.einsum("xcb,xbj->xcj", pieces, pick, preferred_element_type=jnp.float32)
    sampled = sampled[:, :columns] + sampled[:, columns : 2 * columns] + sampled[:, 2 * columns :]
    chunks = sampled.reshape(OUTER, columns, groups, per_row).transpose(2, 1, 0, 3)
    chunks = chunks.reshape([2] * levels + [columns, OUTER * per_row])
    chunks = chunks.transpose(list(range(levels))[::-1] + [levels, levels + 1])
    for level in range(levels):
        bit = my_index >> level & 1
        keep = lax.dynamic_index_in_dim(chunks, bit, axis=0, keepdims=False)
        send = lax.dynamic_index_in_dim(chunks, 1 - bit, axis=0, keepdims=False)
        chunks = keep + exchange(send, "ev", level)

    total_events = length * groups
    scale = 1.0 / math.sqrt(total_events * (total_events // STRIDE))
    sketch = chunks * scale
    partial_gram = jnp.dot(
        sketch,
        lax.all_gather(sketch, "col", axis=0, tiled=True).T,
        precision=high,
        preferred_element_type=jnp.float32,
    )
    for level in range(levels):
        partial_gram = partial_gram + exchange(partial_gram, "ev", level)
    return partial_gram


def solution(mesh):
    return jax.shard_map(
        per_device,
        mesh=mesh,
        in_specs=(P("col", "ev"), P("ev"), P()),
        out_specs=P("col", None),
        check_vma=False,
    )
```

time: 504 us -> 66.9 us (0.13)
  waiting for transfers between devices: 429 us -> 28.5 us
  other arithmetic: 23.7 us -> 7.06 us
  local copies, waits for them, and re-layouts: 15.7 us -> 2.12 us
  between operations: 13.4 us -> 0.14 us
  starting transfers between devices: 7.27 us -> 13.2 us
    ppermute x3 -> x6, waiting for transfers between devices: 360 us -> 28.5 us  [exchange(): return lax.ppermute(value, axis, pairs)]
    psum x1 -> x0, waiting for transfers between devices: 69.4 us -> none  [per_device(): return lax.psum(partial_gram, 'ev')]
    select_n x3 -> x0, other arithmetic: 20.1 us -> none  [per_device(): values = jnp.where(upper_half, partner - values, values + partner)]
    select_n x1 -> x0, local copies, waits for them, and re-layouts: 6.9 us -> none  [per_device(): values = jnp.where(upper_half, partner - values, values + partner)]
    ppermute x3 -> x6, starting transfers between devices: 7.27 us -> 13.2 us  [exchange(): return lax.ppermute(value, axis, pairs)]
    unnamed x6 -> x3, local copies, waits for them, and re-layouts: 6.38 us -> 0.58 us
  transfers between devices with their start and end apart: 4 -> 6, of which waited for: 4 -> 6; matrix products, arithmetic and copies ran while one was open for 0% -> 0% of each run, Pallas kernels for 0% -> 0%
where the time goes in v1:
time: 66.9 us; the launch traced here: 66.6 us
  waiting for transfers between devices  28.5 us (43%)
  starting transfers between devices  13.2 us (20%)
  matrix products  9.92 us (15%)
  other arithmetic  7.06 us (11%)
  blocking collectives  5.79 us (9%)
  local copies, waits for them, and re-layouts  2.12 us (3%)
    ppermute x6, waiting for transfers between devices, exchange(): return lax.ppermute(value, axis, pairs)  28.5 us
    ppermute x6, starting transfers between devices, exchange(): return lax.ppermute(value, axis, pairs)  13.2 us
    dot_general x1, matrix products, per_device(): jnp.einsum('xcb,xbj->xcj', pieces, pick, preferred_element_type=jnp.float32)  5.97 us
    all_gather x1, blocking collectives, per_device(): lax.all_gather(sketch, 'col', axis=0, tiled=True)  5.79 us
    dot_general x1, matrix products, per_device(): jnp.einsum('xa,cab->xcb', hadamard(OUTER).astype(jnp.bfloat16), blocks, p...  3.58 us
    concatenate x1, other arithmetic, per_device(): pieces = jnp.concatenate(split3(first), axis=1)  3.21 us
    unnamed x1, other arithmetic  1.85 us
  transfers between devices with their start and end apart: 6, of which 6 were waited for; matrix products, arithmetic and copies ran while one was open for 0% of the time, Pallas kernels for 0%

profile of v1, /device:TPU:0, one launch (start us, length us, event | category | flops | bytes accessed | tf_op | source)
XLA Modules:
  0.0 66.6 jit_solution(10068642665675930995)
XLA Ops:
  0.0 0.8 %convert_element_type.24 = bf16[16384]{0:T(1024)(128)(2,1)S(1)} convert(s32[16384]{0:T(1024)} %param.4) | non-fusion elementwise | flops 16384 | bytes 98304 | tf_op jit(solution)/shard_map/convert_element_type | solution.py:56
  0.8 1.9 %multiply_bitcast_fusion = bf16[8,8,128,128]{3,1,2,0:T(8,128)(2,1)S(1)} fusion(bf16[64,16384]{1,0:T(8,128)(2,1)} %param.3, bf16[16384]{0:T(1024)(128)(2,1)S(1)} %convert_element_type.24), kind=kLoop, calls=%fused_computation.8 | loop fusion | flops 1048576 | bytes 4227072
  2.7 0.6 copy.19
  3.3 3.6 %reduce-precision_convert_fusion.1 = (bf16[128,64,128]{2,0,1:T(8,128)(2,1)S(1)}, bf16[128,64,128]{2,0,1:T(8,128)(2,1)}, bf16[128,64,128]{2,0,1:T(8,128)(2,1)}) fusion(bf16[64,128,128]{2,1,0:T(8,128)(2,1)S(1)} %bitcast.37), kind=kOutput, calls=%fused_computation.6 | convolution fusion | flops 276365312 | bytes 8388608 | tf_op jit(solution)/shard_map/xa,cab->xcb/dot_general | solution.py:58
  7.0 0.5 reshape.30
  7.9 3.2 %pad_maximum_fusion = bf16[128,192,128]{2,0,1:T(8,128)(2,1)S(1)} fusion(bf16[128,64,128]{2,0,1:T(8,128)(2,1)} %get-tuple-element.6, bf16[128,64,128]{2,0,1:T(8,128)(2,1)} %get-tuple-element.7, bf16[128,64,128]{2,0,1:T(8,128)(2,1)S(1)} %get-tuple-element.5), kind=kLoop, calls=%fused_computation | loop fusion | flops 6291456 | bytes 12582912 | tf_op jit(solution)/shard_map/concatenate | solution.py:65
  11.1 6.0 %fusion = f32[128,192,16]{1,2,0:T(8,128)S(1)} fusion(bf16[128,192,128]{2,0,1:T(8,128)(2,1)S(1)} %pad_maximum_fusion, s32[16]{0:T(128)S(1)} %xor.14, s32[128,16]{1,0:T(8,128)S(1)} %copy.12), kind=kOutput, calls=%fused_computation.1 | convolution fusion | flops 102498304 | bytes 7872576 | tf_op jit(solution)/shard_map/xcb,xbj->xcj/dot_general | solution.py:66
  17.1 0.3 slice_add_fusion
  17.4 0.4 copy.14
  17.8 3.0 %collective-permute-start = (f32[2,2,64,256]{2,3,0,1:T(8,128)S(1)}, f32[2,2,64,256]{2,3,0,1:T(8,128)S(1)}, u32[]{:S(2)}, u32[]{:S(2)}) collective-permute-start(f32[2,2,64,256]{2,3,0,1:T(8,128)S(1)} %dynamic-slice_bitcast_fusion), channel_id=1, source_target_pairs={{0,4},{4,0},{8,12},{12,8},{16,20},{20,16},{24,28},{28,24},{1,5},{5... | collective-permute-start | bytes 786440 | tf_op jit(solution)/shard_map/ppermute | solution.py:24
  20.9 11.9 %collective-permute-done = f32[2,2,64,256]{2,3,0,1:T(8,128)S(1)} collective-permute-done((f32[2,2,64,256]{2,3,0,1:T(8,128)S(1)}, f32[2,2,64,256]{2,3,0,1:T(8,128)S(1)}, u32[]{:S(2)}, u32[]{:S(2)}) %collective-permute-start) | collective-permute-done | bytes 262176 | tf_op jit(solution)/shard_map/ppermute | solution.py:24
  32.9 1.9 %collective-permute-start.1 = (f32[2,64,256]{1,2,0:T(8,128)S(1)}, f32[2,64,256]{1,2,0:T(8,128)S(1)}, u32[]{:S(2)}, u32[]{:S(2)}) collective-permute-start(f32[2,64,256]{1,2,0:T(8,128)S(1)} %dynamic-slice_bitcast_fusion.1), channel_id=1, source_target_pairs={{0,8},{4,12},{8,0},{12,4},{16,24},{20,28},{24,16},{28,20},{1,9},{5... | collective-permute-start | bytes 393224 | tf_op jit(solution)/shard_map/ppermute | solution.py:24
  34.8 5.7 %collective-permute-done.1 = f32[2,64,256]{1,2,0:T(8,128)S(1)} collective-permute-done((f32[2,64,256]{1,2,0:T(8,128)S(1)}, f32[2,64,256]{1,2,0:T(8,128)S(1)}, u32[]{:S(2)}, u32[]{:S(2)}) %collective-permute-start.1) | collective-permute-done | bytes 131104 | tf_op jit(solution)/shard_map/ppermute | solution.py:24
  40.6 2.5 %collective-permute-start.2 = (f32[64,256]{1,0:T(8,128)S(1)}, f32[64,256]{1,0:T(8,128)S(1)}, u32[]{:S(2)}, u32[]{:S(2)}) collective-permute-start(f32[64,256]{1,0:T(8,128)S(1)} %bitcast.41), channel_id=1, source_target_pairs={{0,16},{4,20},{8,24},{12,28},{16,0},{20,4},{24,8},{28,12},{1,17},{... | collective-permute-start | bytes 196616 | tf_op jit(solution)/shard_map/ppermute | solution.py:24
  43.2 2.6 %collective-permute-done.2 = f32[64,256]{1,0:T(8,128)S(1)} collective-permute-done((f32[64,256]{1,0:T(8,128)S(1)}, f32[64,256]{1,0:T(8,128)S(1)}, u32[]{:S(2)}, u32[]{:S(2)}) %collective-permute-start.2) | collective-permute-done | bytes 65568 | tf_op jit(solution)/shard_map/ppermute | solution.py:24
  45.9 5.8 %all_gather.3 = f32[256,256]{1,0:T(8,128)S(1)} all-gather(f32[64,256]{1,0:T(8,128)S(1)} %fusion.12), channel_id=1, replica_groups=mesh['ev'=8,'col'=4] {'col'}, dimensions={0}, use_global_device_ids=true | all-gather | bytes 327680 | tf_op jit(solution)/shard_map/all_gather | solution.py:82
  51.6 0.4 fusion.32
  52.0 1.5 %collective-permute-start.3 = (f32[64,256]{1,0:T(8,128)S(1)}, f32[64,256]{1,0:T(8,128)S(1)}, u32[]{:S(2)}, u32[]{:S(2)}) collective-permute-start(f32[64,256]{1,0:T(8,128)S(1)} %fusion.32), channel_id=1, source_target_pairs={{0,4},{4,0},{8,12},{12,8},{16,20},{20,16},{24,28},{28,24},{1,5},{5... | collective-permute-start | bytes 196616 | tf_op jit(solution)/shard_map/ppermute | solution.py:24
  53.5 2.9 %collective-permute-done.3 = f32[64,256]{1,0:T(8,128)S(1)} collective-permute-done((f32[64,256]{1,0:T(8,128)S(1)}, f32[64,256]{1,0:T(8,128)S(1)}, u32[]{:S(2)}, u32[]{:S(2)}) %collective-permute-start.3) | collective-permute-done | bytes 65568 | tf_op jit(solution)/shard_map/ppermute | solution.py:24
  56.4 1.5 %collective-permute-start.4 = (f32[64,256]{1,0:T(8,128)S(1)}, f32[64,256]{1,0:T(8,128)S(1)}, u32[]{:S(2)}, u32[]{:S(2)}) collective-permute-start(f32[64,256]{1,0:T(8,128)S(1)} %add.100), channel_id=1, source_target_pairs={{0,8},{4,12},{8,0},{12,4},{16,24},{20,28},{24,16},{28,20},{1,9},{5... | collective-permute-start | bytes 196616 | tf_op jit(solution)/shard_map/ppermute | solution.py:24
  58.0 2.8 %collective-permute-done.4 = f32[64,256]{1,0:T(8,128)S(1)} collective-permute-done((f32[64,256]{1,0:T(8,128)S(1)}, f32[64,256]{1,0:T(8,128)S(1)}, u32[]{:S(2)}, u32[]{:S(2)}) %collective-permute-start.4) | collective-permute-done | bytes 65568 | tf_op jit(solution)/shard_map/ppermute | solution.py:24
  60.8 2.7 %collective-permute-start.5 = (f32[64,256]{1,0:T(8,128)S(1)}, f32[64,256]{1,0:T(8,128)S(1)}, u32[]{:S(2)}, u32[]{:S(2)}) collective-permute-start(f32[64,256]{1,0:T(8,128)S(1)} %add.101), channel_id=1, source_target_pairs={{0,16},{4,20},{8,24},{12,28},{16,0},{20,4},{24,8},{28,12},{1,17},{... | collective-permute-start | bytes 196616 | tf_op jit(solution)/shard_map/ppermute | solution.py:24
  63.5 2.5 %collective-permute-done.5 = f32[64,256]{1,0:T(8,128)S(1)} collective-permute-done((f32[64,256]{1,0:T(8,128)S(1)}, f32[64,256]{1,0:T(8,128)S(1)}, u32[]{:S(2)}, u32[]{:S(2)}) %collective-permute-start.5) | collective-permute-done | bytes 65568 | tf_op jit(solution)/shard_map/ppermute | solution.py:24
  66.0 0.6 add.102
  (19 shorter events, 0.9 us)
Async XLA Ops:
  3.3 3.8 %copy-start = (s32[2048]{0:T(1024)S(1)}, s32[2048]{0:T(1024)}, u32[]{:S(2)}) copy-start(s32[2048]{0:T(1024)} %param.5) | copy-start | bytes 24580
  17.8 15.0 %collective-permute-start = (f32[2,2,64,256]{2,3,0,1:T(8,128)S(1)}, f32[2,2,64,256]{2,3,0,1:T(8,128)S(1)}, u32[]{:S(2)}, u32[]{:S(2)}) collective-permute-start(f32[2,2,64,256]{2,3,0,1:T(8,128)S(1)} %dynamic-slice_bitcast_fusion), channel_id=1, source_target_pairs={{0,4},{4,0},{8,12},{12,8},{16,20},{20,16},{24,28},{28,24},{1,5},{5... | collective-permute-start | bytes 786440 | tf_op jit(solution)/shard_map/ppermute | solution.py:24
  32.9 7.6 %collective-permute-start.1 = (f32[2,64,256]{1,2,0:T(8,128)S(1)}, f32[2,64,256]{1,2,0:T(8,128)S(1)}, u32[]{:S(2)}, u32[]{:S(2)}) collective-permute-start(f32[2,64,256]{1,2,0:T(8,128)S(1)} %dynamic-slice_bitcast_fusion.1), channel_id=1, source_target_pairs={{0,8},{4,12},{8,0},{12,4},{16,24},{20,28},{24,16},{28,20},{1,9},{5... | collective-permute-start | bytes 393224 | tf_op jit(solution)/shard_map/ppermute | solution.py:24
  40.6 5.2 %collective-permute-start.2 = (f32[64,256]{1,0:T(8,128)S(1)}, f32[64,256]{1,0:T(8,128)S(1)}, u32[]{:S(2)}, u32[]{:S(2)}) collective-permute-start(f32[64,256]{1,0:T(8,128)S(1)} %bitcast.41), channel_id=1, source_target_pairs={{0,16},{4,20},{8,24},{12,28},{16,0},{20,4},{24,8},{28,12},{1,17},{... | collective-permute-start | bytes 196616 | tf_op jit(solution)/shard_map/ppermute | solution.py:24
  52.0 4.4 %collective-permute-start.3 = (f32[64,256]{1,0:T(8,128)S(1)}, f32[64,256]{1,0:T(8,128)S(1)}, u32[]{:S(2)}, u32[]{:S(2)}) collective-permute-start(f32[64,256]{1,0:T(8,128)S(1)} %fusion.32), channel_id=1, source_target_pairs={{0,4},{4,0},{8,12},{12,8},{16,20},{20,16},{24,28},{28,24},{1,5},{5... | collective-permute-start | bytes 196616 | tf_op jit(solution)/shard_map/ppermute | solution.py:24
  56.4 4.3 %collective-permute-start.4 = (f32[64,256]{1,0:T(8,128)S(1)}, f32[64,256]{1,0:T(8,128)S(1)}, u32[]{:S(2)}, u32[]{:S(2)}) collective-permute-start(f32[64,256]{1,0:T(8,128)S(1)} %add.100), channel_id=1, source_target_pairs={{0,8},{4,12},{8,0},{12,4},{16,24},{20,28},{24,16},{28,20},{1,9},{5... | collective-permute-start | bytes 196616 | tf_op jit(solution)/shard_map/ppermute | solution.py:24
  60.8 5.2 %collective-permute-start.5 = (f32[64,256]{1,0:T(8,128)S(1)}, f32[64,256]{1,0:T(8,128)S(1)}, u32[]{:S(2)}, u32[]{:S(2)}) collective-permute-start(f32[64,256]{1,0:T(8,128)S(1)} %add.101), channel_id=1, source_target_pairs={{0,16},{4,20},{8,24},{12,28},{16,0},{20,4},{24,8},{28,12},{1,17},{... | collective-permute-start | bytes 196616 | tf_op jit(solution)/shard_map/ppermute | solution.py:24

commit v2 on v1

--- a/solution.py
+++ b/solution.py
@@ -66,13 +66,8 @@
     sampled = jnp.einsum("xcb,xbj->xcj", pieces, pick, preferred_element_type=jnp.float32)
     sampled = sampled[:, :columns] + sampled[:, columns : 2 * columns] + sampled[:, 2 * columns :]
     chunks = sampled.reshape(OUTER, columns, groups, per_row).transpose(2, 1, 0, 3)
-    chunks = chunks.reshape([2] * levels + [columns, OUTER * per_row])
-    chunks = chunks.transpose(list(range(levels))[::-1] + [levels, levels + 1])
-    for level in range(levels):
-        bit = my_index >> level & 1
-        keep = lax.dynamic_index_in_dim(chunks, bit, axis=0, keepdims=False)
-        send = lax.dynamic_index_in_dim(chunks, 1 - bit, axis=0, keepdims=False)
-        chunks = keep + exchange(send, "ev", level)
+    chunks = chunks.reshape(groups, columns, OUTER * per_row)
+    chunks = lax.all_to_all(chunks, "ev", 0, 0, tiled=True).sum(axis=0)
 
     total_events = length * groups
     scale = 1.0 / math.sqrt(total_events * (total_events // STRIDE))
@@ -83,9 +78,7 @@
         precision=high,
         preferred_element_type=jnp.float32,
     )
-    for level in range(levels):
-        partial_gram = partial_gram + exchange(partial_gram, "ev", level)
-    return partial_gram
+    return lax.all_gather(partial_gram, "ev").sum(axis=0)
 
 
 def solution(mesh):

time: 66.9 us -> 78.3 us (1.17)
  blocking collectives: 5.79 us -> 58.9 us
  waiting for transfers between devices: 28.5 us -> 0 us
  starting transfers between devices: 13.2 us -> 0 us
    all_gather x0 -> x1, blocking collectives: none -> 31.5 us  [per_device(): return lax.all_gather(partial_gram, 'ev').sum(axis=0)]
    ppermute x6 -> x0, waiting for transfers between devices: 28.5 us -> none  [exchange(): return lax.ppermute(value, axis, pairs)]
    all_to_all x0 -> x1, blocking collectives: none -> 21.6 us  [per_device(): chunks = lax.all_to_all(chunks, 'ev', 0, 0, tiled=True).sum(axis=0)]
    ppermute x6 -> x0, starting transfers between devices: 13.2 us -> none  [exchange(): return lax.ppermute(value, axis, pairs)]
  transfers between devices with their start and end apart: 6 -> 0, of which waited for: 6 -> 0; matrix products, arithmetic and copies ran while one was open for 0% -> 0% of each run, Pallas kernels for 0% -> 0%
where the time goes in v2:
time: 78.3 us; the launch traced here: 78 us
  blocking collectives  58.9 us (75%)
  matrix products  9.94 us (13%)
  other arithmetic  7.01 us (9%)
  local copies, waits for them, and re-layouts  2.09 us (3%)
    all_gather x1, blocking collectives, per_device(): return lax.all_gather(partial_gram, 'ev').sum(axis=0)  31.5 us
    all_to_all x1, blocking collectives, per_device(): chunks = lax.all_to_all(chunks, 'ev', 0, 0, tiled=True).sum(axis=0)  21.6 us
    dot_general x1, matrix products, per_device(): jnp.einsum('xcb,xbj->xcj', pieces, pick, preferred_element_type=jnp.float32)  5.97 us
    all_gather x1, blocking collectives, per_device(): lax.all_gather(sketch, 'col', axis=0, tiled=True)  5.79 us
    dot_general x1, matrix products, per_device(): jnp.einsum('xa,cab->xcb', hadamard(OUTER).astype(jnp.bfloat16), blocks, p...  3.59 us
    concatenate x1, other arithmetic, per_device(): pieces = jnp.concatenate(split3(first), axis=1)  3.21 us
    unnamed x1, other arithmetic  1.85 us

profile of v2, /device:TPU:0, one launch (start us, length us, event | category | flops | bytes accessed | tf_op | source)
XLA Modules:
  0.0 78.0 jit_solution(12383569468095717709)
XLA Ops:
  0.0 0.8 %convert_element_type.24 = bf16[16384]{0:T(1024)(128)(2,1)S(1)} convert(s32[16384]{0:T(1024)} %param.4) | non-fusion elementwise | flops 16384 | bytes 98304 | tf_op jit(solution)/shard_map/convert_element_type | solution.py:56
  0.8 1.9 %multiply_bitcast_fusion = bf16[8,8,128,128]{3,1,2,0:T(8,128)(2,1)S(1)} fusion(bf16[64,16384]{1,0:T(8,128)(2,1)} %param.3, bf16[16384]{0:T(1024)(128)(2,1)S(1)} %convert_element_type.24), kind=kLoop, calls=%fused_computation.8 | loop fusion | flops 1048576 | bytes 4227072
  2.7 0.6 copy.23
  3.3 0.0 copy-start
  3.3 3.6 %reduce-precision_convert_fusion.1 = (bf16[128,64,128]{2,0,1:T(8,128)(2,1)S(1)}, bf16[128,64,128]{2,0,1:T(8,128)(2,1)}, bf16[128,64,128]{2,0,1:T(8,128)(2,1)}) fusion(bf16[64,128,128]{2,1,0:T(8,128)(2,1)S(1)} %bitcast.18), kind=kOutput, calls=%fused_computation.6 | convolution fusion | flops 276365312 | bytes 8388608 | tf_op jit(solution)/shard_map/xa,cab->xcb/dot_general | solution.py:58
  6.9 0.0 copy-done
  6.9 0.5 reshape.30
  7.4 0.2 copy.15
  7.6 0.1 copy.16
  7.7 0.1 xor.13
  7.8 0.1 xor.14
  7.9 3.2 %pad_maximum_fusion = bf16[128,192,128]{2,0,1:T(8,128)(2,1)S(1)} fusion(bf16[128,64,128]{2,0,1:T(8,128)(2,1)} %get-tuple-element.6, bf16[128,64,128]{2,0,1:T(8,128)(2,1)} %get-tuple-element.7, bf16[128,64,128]{2,0,1:T(8,128)(2,1)S(1)} %get-tuple-element.5), kind=kLoop, calls=%fused_computation | loop fusion | flops 6291456 | bytes 12582912 | tf_op jit(solution)/shard_map/concatenate | solution.py:65
  11.1 6.0 %fusion = f32[128,192,16]{1,2,0:T(8,128)S(1)} fusion(bf16[128,192,128]{2,0,1:T(8,128)(2,1)S(1)} %pad_maximum_fusion, s32[16]{0:T(128)S(1)} %xor.14, s32[128,16]{1,0:T(8,128)S(1)} %copy.16), kind=kOutput, calls=%fused_computation.1 | convolution fusion | flops 102498304 | bytes 7872576 | tf_op jit(solution)/shard_map/xcb,xbj->xcj/dot_general | solution.py:66
  17.1 0.3 slice_add_fusion
  17.4 0.1 copy.18
  17.5 0.4 copy.19
  17.9 21.6 %all_to_all.5 = f32[8,64,256]{2,1,0:T(8,128)S(1)} all-to-all(f32[8,64,256]{2,1,0:T(8,128)S(1)} %copy.19), channel_id=1, replica_groups=mesh['ev'=8,'col'=4] {'ev'}, dimensions={0} | all-to-all | bytes 1048576 | tf_op jit(solution)/shard_map/all_to_all | solution.py:70
  39.5 0.1 copy.22
  39.6 0.1 copy.21
  39.7 5.8 %all_gather.9 = f32[256,256]{1,0:T(8,128)S(1)} all-gather(f32[64,256]{1,0:T(8,128)S(1)} %copy.21), channel_id=1, replica_groups=mesh['ev'=8,'col'=4] {'col'}, dimensions={0}, use_global_device_ids=true | all-gather | bytes 327680 | tf_op jit(solution)/shard_map/all_gather | solution.py:77
  45.5 0.4 fusion.31
  45.9 31.5 %all-gather = f32[512,256]{1,0:T(8,128)S(1)} all-gather(f32[64,256]{1,0:T(8,128)S(1)} %fusion.31), channel_id=2, replica_groups=mesh['ev'=8,'col'=4] {'ev'}, dimensions={0}, use_global_device_ids=true | all-gather | bytes 589824 | tf_op jit(solution)/shard_map/all_gather | solution.py:81
  77.4 0.7 reduce_sum.19
  (5 shorter events, 0.1 us)
Async XLA Ops:
  3.3 3.6 %copy-start = (s32[2048]{0:T(1024)S(1)}, s32[2048]{0:T(1024)}, u32[]{:S(2)}) copy-start(s32[2048]{0:T(1024)} %param.5) | copy-start | bytes 24580

commit v3 on v2

--- a/solution.py
+++ b/solution.py
@@ -78,7 +78,9 @@
         precision=high,
         preferred_element_type=jnp.float32,
     )
-    return lax.all_gather(partial_gram, "ev").sum(axis=0)
+    for level in range(levels):
+        partial_gram = partial_gram + exchange(partial_gram, "ev", level)
+    return partial_gram
 
 
 def solution(mesh):

time: 78.3 us -> 61.5 us (0.79)
  blocking collectives: 58.9 us -> 27.4 us
  waiting for transfers between devices: 0 us -> 10.8 us
  starting transfers between devices: 0 us -> 3.84 us
    all_gather x1 -> x0, blocking collectives: 31.5 us -> none  [per_device(): return lax.all_gather(partial_gram, 'ev').sum(axis=0)]
    ppermute x0 -> x3, waiting for transfers between devices: none -> 10.8 us  [exchange(): return lax.ppermute(value, axis, pairs)]
    ppermute x0 -> x3, starting transfers between devices: none -> 3.84 us  [exchange(): return lax.ppermute(value, axis, pairs)]
  transfers between devices with their start and end apart: 0 -> 3, of which waited for: 0 -> 3; matrix products, arithmetic and copies ran while one was open for 0% -> 0% of each run, Pallas kernels for 0% -> 0%
where the time goes in v3:
time: 61.5 us; the launch traced here: 61.2 us
  blocking collectives  27.4 us (45%)
  waiting for transfers between devices  10.8 us (18%)
  matrix products  9.92 us (16%)
  other arithmetic  7 us (11%)
  starting transfers between devices  3.84 us (6%)
  local copies, waits for them, and re-layouts  2.09 us (3%)
    all_to_all x1, blocking collectives, per_device(): chunks = lax.all_to_all(chunks, 'ev', 0, 0, tiled=True).sum(axis=0)  21.6 us
    ppermute x3, waiting for transfers between devices, exchange(): return lax.ppermute(value, axis, pairs)  10.8 us
    dot_general x1, matrix products, per_device(): jnp.einsum('xcb,xbj->xcj', pieces, pick, preferred_element_type=jnp.float32)  5.97 us
    all_gather x1, blocking collectives, per_device(): lax.all_gather(sketch, 'col', axis=0, tiled=True)  5.79 us
    ppermute x3, starting transfers between devices, exchange(): return lax.ppermute(value, axis, pairs)  3.84 us
    dot_general x1, matrix products, per_device(): jnp.einsum('xa,cab->xcb', hadamard(OUTER).astype(jnp.bfloat16), blocks, p...  3.58 us
    concatenate x1, other arithmetic, per_device(): pieces = jnp.concatenate(split3(first), axis=1)  3.21 us
    unnamed x1, other arithmetic  1.85 us
  transfers between devices with their start and end apart: 3, of which 3 were waited for; matrix products, arithmetic and copies ran while one was open for 0% of the time, Pallas kernels for 0%

profile of v3, /device:TPU:0, one launch (start us, length us, event | category | flops | bytes accessed | tf_op | source)
XLA Modules:
  0.0 61.2 jit_solution(16897973568686185095)
XLA Ops:
  0.0 0.8 %convert_element_type.24 = bf16[16384]{0:T(1024)(128)(2,1)S(1)} convert(s32[16384]{0:T(1024)} %param.4) | non-fusion elementwise | flops 16384 | bytes 98304 | tf_op jit(solution)/shard_map/convert_element_type | solution.py:56
  0.8 1.9 %multiply_bitcast_fusion = bf16[8,8,128,128]{3,1,2,0:T(8,128)(2,1)S(1)} fusion(bf16[64,16384]{1,0:T(8,128)(2,1)} %param.3, bf16[16384]{0:T(1024)(128)(2,1)S(1)} %convert_element_type.24), kind=kLoop, calls=%fused_computation.8 | loop fusion | flops 1048576 | bytes 4227072
  2.7 0.6 copy.23
  3.3 3.6 %reduce-precision_convert_fusion.1 = (bf16[128,64,128]{2,0,1:T(8,128)(2,1)S(1)}, bf16[128,64,128]{2,0,1:T(8,128)(2,1)}, bf16[128,64,128]{2,0,1:T(8,128)(2,1)}) fusion(bf16[64,128,128]{2,1,0:T(8,128)(2,1)S(1)} %bitcast.17), kind=kOutput, calls=%fused_computation.6 | convolution fusion | flops 276365312 | bytes 8388608 | tf_op jit(solution)/shard_map/xa,cab->xcb/dot_general | solution.py:58
  6.9 0.5 reshape.30
  7.4 0.2 copy.15
  7.6 0.1 copy.16
  7.8 0.1 xor.14
  7.9 3.2 %pad_maximum_fusion = bf16[128,192,128]{2,0,1:T(8,128)(2,1)S(1)} fusion(bf16[128,64,128]{2,0,1:T(8,128)(2,1)} %get-tuple-element.6, bf16[128,64,128]{2,0,1:T(8,128)(2,1)} %get-tuple-element.7, bf16[128,64,128]{2,0,1:T(8,128)(2,1)S(1)} %get-tuple-element.5), kind=kLoop, calls=%fused_computation | loop fusion | flops 6291456 | bytes 12582912 | tf_op jit(solution)/shard_map/concatenate | solution.py:65
  11.1 6.0 %fusion = f32[128,192,16]{1,2,0:T(8,128)S(1)} fusion(bf16[128,192,128]{2,0,1:T(8,128)(2,1)S(1)} %pad_maximum_fusion, s32[16]{0:T(128)S(1)} %xor.14, s32[128,16]{1,0:T(8,128)S(1)} %copy.16), kind=kOutput, calls=%fused_computation.1 | convolution fusion | flops 102498304 | bytes 7872576 | tf_op jit(solution)/shard_map/xcb,xbj->xcj/dot_general | solution.py:66
  17.0 0.3 slice_add_fusion
  17.5 0.4 copy.19
  17.9 21.6 %all_to_all.5 = f32[8,64,256]{2,1,0:T(8,128)S(1)} all-to-all(f32[8,64,256]{2,1,0:T(8,128)S(1)} %copy.19), channel_id=1, replica_groups=mesh['ev'=8,'col'=4] {'ev'}, dimensions={0} | all-to-all | bytes 1048576 | tf_op jit(solution)/shard_map/all_to_all | solution.py:70
  39.5 0.1 copy.22
  39.6 0.1 copy.21
  39.7 5.8 %all_gather.3 = f32[256,256]{1,0:T(8,128)S(1)} all-gather(f32[64,256]{1,0:T(8,128)S(1)} %copy.21), channel_id=1, replica_groups=mesh['ev'=8,'col'=4] {'col'}, dimensions={0}, use_global_device_ids=true | all-gather | bytes 327680 | tf_op jit(solution)/shard_map/all_gather | solution.py:77
  45.5 0.4 fusion.31
  45.9 1.5 %collective-permute-start = (f32[64,256]{1,0:T(8,128)S(1)}, f32[64,256]{1,0:T(8,128)S(1)}, u32[]{:S(2)}, u32[]{:S(2)}) collective-permute-start(f32[64,256]{1,0:T(8,128)S(1)} %fusion.31), channel_id=1, source_target_pairs={{0,4},{4,0},{8,12},{12,8},{16,20},{20,16},{24,28},{28,24},{1,5},{5... | collective-permute-start | bytes 196616 | tf_op jit(solution)/shard_map/ppermute | solution.py:24
  47.4 2.9 %collective-permute-done = f32[64,256]{1,0:T(8,128)S(1)} collective-permute-done((f32[64,256]{1,0:T(8,128)S(1)}, f32[64,256]{1,0:T(8,128)S(1)}, u32[]{:S(2)}, u32[]{:S(2)}) %collective-permute-start) | collective-permute-done | bytes 65568 | tf_op jit(solution)/shard_map/ppermute | solution.py:24
  50.3 1.2 %collective-permute-start.1 = (f32[64,256]{1,0:T(8,128)S(1)}, f32[64,256]{1,0:T(8,128)S(1)}, u32[]{:S(2)}, u32[]{:S(2)}) collective-permute-start(f32[64,256]{1,0:T(8,128)S(1)} %add.58), channel_id=1, source_target_pairs={{0,8},{4,12},{8,0},{12,4},{16,24},{20,28},{24,16},{28,20},{1,9},{5... | collective-permute-start | bytes 196616 | tf_op jit(solution)/shard_map/ppermute | solution.py:24
  51.5 3.2 %collective-permute-done.1 = f32[64,256]{1,0:T(8,128)S(1)} collective-permute-done((f32[64,256]{1,0:T(8,128)S(1)}, f32[64,256]{1,0:T(8,128)S(1)}, u32[]{:S(2)}, u32[]{:S(2)}) %collective-permute-start.1) | collective-permute-done | bytes 65568 | tf_op jit(solution)/shard_map/ppermute | solution.py:24
  54.6 1.1 %collective-permute-start.2 = (f32[64,256]{1,0:T(8,128)S(1)}, f32[64,256]{1,0:T(8,128)S(1)}, u32[]{:S(2)}, u32[]{:S(2)}) collective-permute-start(f32[64,256]{1,0:T(8,128)S(1)} %add.59), channel_id=1, source_target_pairs={{0,16},{4,20},{8,24},{12,28},{16,0},{20,4},{24,8},{28,12},{1,17},{... | collective-permute-start | bytes 196616 | tf_op jit(solution)/shard_map/ppermute | solution.py:24
  55.8 4.8 %collective-permute-done.2 = f32[64,256]{1,0:T(8,128)S(1)} collective-permute-done((f32[64,256]{1,0:T(8,128)S(1)}, f32[64,256]{1,0:T(8,128)S(1)}, u32[]{:S(2)}, u32[]{:S(2)}) %collective-permute-start.2) | collective-permute-done | bytes 65568 | tf_op jit(solution)/shard_map/ppermute | solution.py:24
  60.6 0.6 %add.60 = f32[64,256]{1,0:T(8,128)} add(f32[64,256]{1,0:T(8,128)S(1)} %add.59, f32[64,256]{1,0:T(8,128)S(1)} %collective-permute-done.2) | non-fusion elementwise | flops 16384 | bytes 196608 | tf_op jit(solution)/shard_map/add | solution.py:82
  (11 shorter events, 0.3 us)
Async XLA Ops:
  3.3 3.6 %copy-start = (s32[2048]{0:T(1024)S(1)}, s32[2048]{0:T(1024)}, u32[]{:S(2)}) copy-start(s32[2048]{0:T(1024)} %param.5) | copy-start | bytes 24580
  45.9 4.4 %collective-permute-start = (f32[64,256]{1,0:T(8,128)S(1)}, f32[64,256]{1,0:T(8,128)S(1)}, u32[]{:S(2)}, u32[]{:S(2)}) collective-permute-start(f32[64,256]{1,0:T(8,128)S(1)} %fusion.31), channel_id=1, source_target_pairs={{0,4},{4,0},{8,12},{12,8},{16,20},{20,16},{24,28},{28,24},{1,5},{5... | collective-permute-start | bytes 196616 | tf_op jit(solution)/shard_map/ppermute | solution.py:24
  50.3 4.3 %collective-permute-start.1 = (f32[64,256]{1,0:T(8,128)S(1)}, f32[64,256]{1,0:T(8,128)S(1)}, u32[]{:S(2)}, u32[]{:S(2)}) collective-permute-start(f32[64,256]{1,0:T(8,128)S(1)} %add.58), channel_id=1, source_target_pairs={{0,8},{4,12},{8,0},{12,4},{16,24},{20,28},{24,16},{28,20},{1,9},{5... | collective-permute-start | bytes 196616 | tf_op jit(solution)/shard_map/ppermute | solution.py:24
  54.6 5.9 %collective-permute-start.2 = (f32[64,256]{1,0:T(8,128)S(1)}, f32[64,256]{1,0:T(8,128)S(1)}, u32[]{:S(2)}, u32[]{:S(2)}) collective-permute-start(f32[64,256]{1,0:T(8,128)S(1)} %add.59), channel_id=1, source_target_pairs={{0,16},{4,20},{8,24},{12,28},{16,0},{20,4},{24,8},{28,12},{1,17},{... | collective-permute-start | bytes 196616 | tf_op jit(solution)/shard_map/ppermute | solution.py:24

commit v4 on v3

--- a/solution.py
+++ b/solution.py
@@ -62,9 +62,13 @@
         preferred_element_type=jnp.float32,
     )
     pick = selection(offsets, my_index, groups, inner)
-    pieces = jnp.concatenate(split3(first), axis=1)
-    sampled = jnp.einsum("xcb,xbj->xcj", pieces, pick, preferred_element_type=jnp.float32)
-    sampled = sampled[:, :columns] + sampled[:, columns : 2 * columns] + sampled[:, 2 * columns :]
+    sampled = jnp.einsum(
+        "xcb,xbj->xcj",
+        first,
+        pick.astype(jnp.float32),
+        precision=lax.Precision.HIGH,
+        preferred_element_type=jnp.float32,
+    )
     chunks = sampled.reshape(OUTER, columns, groups, per_row).transpose(2, 1, 0, 3)
     chunks = chunks.reshape(groups, columns, OUTER * per_row)
     chunks = lax.all_to_all(chunks, "ev", 0, 0, tiled=True).sum(axis=0)

time: 61.5 us -> 57.4 us (0.933)
  other arithmetic: 7 us -> 3.45 us
    concatenate x1 -> x0, other arithmetic: 3.21 us -> none  [per_device(): pieces = jnp.concatenate(split3(first), axis=1)]
    dot_general x1, matrix products: 3.58 us -> 2.67 us  [per_device(): jnp.einsum('xa,cab->xcb', hadamard(OUTER).astype(jnp.bfloat16), blocks, p...]
where the time goes in v4:
time: 57.4 us; the launch traced here: 57.1 us
  blocking collectives  27.4 us (48%)
  waiting for transfers between devices  10.8 us (19%)
  matrix products  9.39 us (16%)
  starting transfers between devices  3.83 us (7%)
  other arithmetic  3.45 us (6%)
  local copies, waits for them, and re-layouts  2.09 us (4%)
    all_to_all x1, blocking collectives, per_device(): chunks = lax.all_to_all(chunks, 'ev', 0, 0, tiled=True).sum(axis=0)  21.6 us
    ppermute x3, waiting for transfers between devices, exchange(): return lax.ppermute(value, axis, pairs)  10.8 us
    dot_general x1, matrix products, per_device(): jnp.einsum('xcb,xbj->xcj', first, pick.astype(jnp.float32), precision=lax...  6.33 us
    all_gather x1, blocking collectives, per_device(): lax.all_gather(sketch, 'col', axis=0, tiled=True)  5.79 us
    ppermute x3, starting transfers between devices, exchange(): return lax.ppermute(value, axis, pairs)  3.83 us
    dot_general x1, matrix products, per_device(): jnp.einsum('xa,cab->xcb', hadamard(OUTER).astype(jnp.bfloat16), blocks, p...  2.67 us
    unnamed x1, other arithmetic  1.85 us
  transfers between devices with their start and end apart: 3, of which 3 were waited for; matrix products, arithmetic and copies ran while one was open for 0% of the time, Pallas kernels for 0%

profile of v4, /device:TPU:0, one launch (start us, length us, event | category | flops | bytes accessed | tf_op | source)
XLA Modules:
  0.0 57.1 jit_solution(2866121797305346877)
XLA Ops:
  0.0 0.8 %convert_element_type.16 = bf16[16384]{0:T(1024)(128)(2,1)S(1)} convert(s32[16384]{0:T(1024)} %param.4) | non-fusion elementwise | flops 16384 | bytes 98304 | tf_op jit(solution)/shard_map/convert_element_type | solution.py:56
  0.8 1.9 %multiply_bitcast_fusion = bf16[8,8,128,128]{3,1,2,0:T(8,128)(2,1)S(1)} fusion(bf16[64,16384]{1,0:T(8,128)(2,1)} %param.3, bf16[16384]{0:T(1024)(128)(2,1)S(1)} %convert_element_type.16), kind=kLoop, calls=%fused_computation.2 | loop fusion | flops 1048576 | bytes 4227072
  2.7 0.6 %copy.21 = bf16[8,8,128,128]{3,2,1,0:T(8,128)(2,1)S(1)} copy(bf16[8,8,128,128]{3,1,2,0:T(8,128)(2,1)S(1)} %multiply_bitcast_fusion) | data formatting | bytes 4194304
  3.3 2.7 %fusion.12 = f32[128,64,128]{2,0,1:T(8,128)} fusion(bf16[64,128,128]{2,1,0:T(8,128)(2,1)S(1)} %bitcast.15), kind=kOutput, calls=%fused_computation.19 | convolution fusion | flops 269025280 | bytes 6291456 | tf_op jit(solution)/shard_map/xa,cab->xcb/dot_general | solution.py:58
  6.0 0.5 reshape.30
  6.5 0.2 copy.13
  6.7 0.1 copy.14
  6.8 0.1 xor.13
  6.9 0.1 xor.14
  7.0 6.3 %fusion = f32[128,64,16]{1,2,0:T(8,128)S(1)} fusion(f32[128,64,128]{2,0,1:T(8,128)} %fusion.12, s32[16]{0:T(128)S(1)} %xor.14, s32[128,16]{1,0:T(8,128)S(1)} %copy.14), kind=kOutput, calls=%fused_computation | convolution fusion | flops 102498304 | bytes 4726848 | tf_op jit(solution)/shard_map/xcb,xbj->xcj/dot_general | solution.py:65
  13.3 0.1 copy.16
  13.4 0.4 copy.17
  13.8 21.6 %all_to_all.5 = f32[8,64,256]{2,1,0:T(8,128)S(1)} all-to-all(f32[8,64,256]{2,1,0:T(8,128)S(1)} %copy.17), channel_id=1, replica_groups=mesh['ev'=8,'col'=4] {'ev'}, dimensions={0} | all-to-all | bytes 1048576 | tf_op jit(solution)/shard_map/all_to_all | solution.py:74
  35.4 0.1 copy.20
  35.5 0.1 copy.19
  35.6 5.8 %all_gather.3 = f32[256,256]{1,0:T(8,128)S(1)} all-gather(f32[64,256]{1,0:T(8,128)S(1)} %copy.19), channel_id=1, replica_groups=mesh['ev'=8,'col'=4] {'col'}, dimensions={0}, use_global_device_ids=true | all-gather | bytes 327680 | tf_op jit(solution)/shard_map/all_gather | solution.py:81
  41.4 0.4 fusion.30
  41.8 1.5 %collective-permute-start = (f32[64,256]{1,0:T(8,128)S(1)}, f32[64,256]{1,0:T(8,128)S(1)}, u32[]{:S(2)}, u32[]{:S(2)}) collective-permute-start(f32[64,256]{1,0:T(8,128)S(1)} %fusion.30), channel_id=1, source_target_pairs={{0,4},{4,0},{8,12},{12,8},{16,20},{20,16},{24,28},{28,24},{1,5},{5... | collective-permute-start | bytes 196616 | tf_op jit(solution)/shard_map/ppermute | solution.py:24
  43.3 2.9 %collective-permute-done = f32[64,256]{1,0:T(8,128)S(1)} collective-permute-done((f32[64,256]{1,0:T(8,128)S(1)}, f32[64,256]{1,0:T(8,128)S(1)}, u32[]{:S(2)}, u32[]{:S(2)}) %collective-permute-start) | collective-permute-done | bytes 65568 | tf_op jit(solution)/shard_map/ppermute | solution.py:24
  46.2 1.2 %collective-permute-start.1 = (f32[64,256]{1,0:T(8,128)S(1)}, f32[64,256]{1,0:T(8,128)S(1)}, u32[]{:S(2)}, u32[]{:S(2)}) collective-permute-start(f32[64,256]{1,0:T(8,128)S(1)} %add.50), channel_id=1, source_target_pairs={{0,8},{4,12},{8,0},{12,4},{16,24},{20,28},{24,16},{28,20},{1,9},{5... | collective-permute-start | bytes 196616 | tf_op jit(solution)/shard_map/ppermute | solution.py:24
  47.4 3.2 %collective-permute-done.1 = f32[64,256]{1,0:T(8,128)S(1)} collective-permute-done((f32[64,256]{1,0:T(8,128)S(1)}, f32[64,256]{1,0:T(8,128)S(1)}, u32[]{:S(2)}, u32[]{:S(2)}) %collective-permute-start.1) | collective-permute-done | bytes 65568 | tf_op jit(solution)/shard_map/ppermute | solution.py:24
  50.5 1.1 %collective-permute-start.2 = (f32[64,256]{1,0:T(8,128)S(1)}, f32[64,256]{1,0:T(8,128)S(1)}, u32[]{:S(2)}, u32[]{:S(2)}) collective-permute-start(f32[64,256]{1,0:T(8,128)S(1)} %add.51), channel_id=1, source_target_pairs={{0,16},{4,20},{8,24},{12,28},{16,0},{20,4},{24,8},{28,12},{1,17},{... | collective-permute-start | bytes 196616 | tf_op jit(solution)/shard_map/ppermute | solution.py:24
  51.7 4.8 %collective-permute-done.2 = f32[64,256]{1,0:T(8,128)S(1)} collective-permute-done((f32[64,256]{1,0:T(8,128)S(1)}, f32[64,256]{1,0:T(8,128)S(1)}, u32[]{:S(2)}, u32[]{:S(2)}) %collective-permute-start.2) | collective-permute-done | bytes 65568 | tf_op jit(solution)/shard_map/ppermute | solution.py:24
  56.5 0.6 %add.52 = f32[64,256]{1,0:T(8,128)} add(f32[64,256]{1,0:T(8,128)S(1)} %add.51, f32[64,256]{1,0:T(8,128)S(1)} %collective-permute-done.2) | non-fusion elementwise | flops 16384 | bytes 196608 | tf_op jit(solution)/shard_map/add | solution.py:86
  (9 shorter events, 0.1 us)
Async XLA Ops:
  3.3 2.7 %copy-start = (s32[2048]{0:T(1024)S(1)}, s32[2048]{0:T(1024)}, u32[]{:S(2)}) copy-start(s32[2048]{0:T(1024)} %param.5) | copy-start | bytes 24580
  41.8 4.4 %collective-permute-start = (f32[64,256]{1,0:T(8,128)S(1)}, f32[64,256]{1,0:T(8,128)S(1)}, u32[]{:S(2)}, u32[]{:S(2)}) collective-permute-start(f32[64,256]{1,0:T(8,128)S(1)} %fusion.30), channel_id=1, source_target_pairs={{0,4},{4,0},{8,12},{12,8},{16,20},{20,16},{24,28},{28,24},{1,5},{5... | collective-permute-start | bytes 196616 | tf_op jit(solution)/shard_map/ppermute | solution.py:24
  46.2 4.3 %collective-permute-start.1 = (f32[64,256]{1,0:T(8,128)S(1)}, f32[64,256]{1,0:T(8,128)S(1)}, u32[]{:S(2)}, u32[]{:S(2)}) collective-permute-start(f32[64,256]{1,0:T(8,128)S(1)} %add.50), channel_id=1, source_target_pairs={{0,8},{4,12},{8,0},{12,4},{16,24},{20,28},{24,16},{28,20},{1,9},{5... | collective-permute-start | bytes 196616 | tf_op jit(solution)/shard_map/ppermute | solution.py:24
  50.5 5.9 %collective-permute-start.2 = (f32[64,256]{1,0:T(8,128)S(1)}, f32[64,256]{1,0:T(8,128)S(1)}, u32[]{:S(2)}, u32[]{:S(2)}) collective-permute-start(f32[64,256]{1,0:T(8,128)S(1)} %add.51), channel_id=1, source_target_pairs={{0,16},{4,20},{8,24},{12,28},{16,0},{20,4},{24,8},{28,12},{1,17},{... | collective-permute-start | bytes 196616 | tf_op jit(solution)/shard_map/ppermute | solution.py:24

commit v5 on v4

--- a/solution.py
+++ b/solution.py
@@ -71,7 +71,16 @@
     )
     chunks = sampled.reshape(OUTER, columns, groups, per_row).transpose(2, 1, 0, 3)
     chunks = chunks.reshape(groups, columns, OUTER * per_row)
-    chunks = lax.all_to_all(chunks, "ev", 0, 0, tiled=True).sum(axis=0)
+    own = lax.dynamic_index_in_dim(chunks, my_index, axis=0, keepdims=False)
+    arrived = []
+    for distance in range(1, groups):
+        target = my_index ^ distance
+        block = lax.dynamic_index_in_dim(chunks, target, axis=0, keepdims=False)
+        pairs = [(source, source ^ distance) for source in range(groups)]
+        arrived.append(lax.ppermute(block, "ev", pairs))
+    chunks = own
+    for block in arrived:
+        chunks = chunks + block
 
     total_events = length * groups
     scale = 1.0 / math.sqrt(total_events * (total_events // STRIDE))

time: 57.4 us -> 54.1 us (0.943)
  blocking collectives: 27.4 us -> 5.79 us
  starting transfers between devices: 3.83 us -> 17.8 us
  waiting for transfers between devices: 10.8 us -> 14.4 us
  local copies, waits for them, and re-layouts: 2.09 us -> 2.91 us
    all_to_all x1 -> x0, blocking collectives: 21.6 us -> none  [per_device(): chunks = lax.all_to_all(chunks, 'ev', 0, 0, tiled=True).sum(axis=0)]
    ppermute x0 -> x7, starting transfers between devices: none -> 12.9 us  [per_device(): arrived.append(lax.ppermute(block, 'ev', pairs))]
    ppermute x0 -> x7, waiting for transfers between devices: none -> 4.64 us  [per_device(): arrived.append(lax.ppermute(block, 'ev', pairs))]
    dynamic_slice x0 -> x9, local copies, waits for them, and re-layouts: none -> 1.36 us  [the longest x2 0.82 us: per_device(): own = lax.dynamic_index_in_dim(chunks, my_index, axis=0, keepdims=False)]
    ppermute x3, waiting for transfers between devices: 10.8 us -> 9.73 us  [exchange(): return lax.ppermute(value, axis, pairs)]
    ppermute x3, starting transfers between devices: 3.83 us -> 4.94 us  [exchange(): return lax.ppermute(value, axis, pairs)]
  transfers between devices with their start and end apart: 3 -> 10, of which waited for: 3 -> 6; matrix products, arithmetic and copies ran while one was open for 0% -> 1% of each run, Pallas kernels for 0% -> 0%
where the time goes in v5:
time: 54.1 us; the launch traced here: 53.9 us
  starting transfers between devices  17.8 us (33%)
  waiting for transfers between devices  14.4 us (27%)
  matrix products  9.41 us (17%)
  blocking collectives  5.79 us (11%)
  other arithmetic  3.44 us (6%)
  local copies, waits for them, and re-layouts  2.91 us (5%)
    ppermute x7, starting transfers between devices, per_device(): arrived.append(lax.ppermute(block, 'ev', pairs))  12.9 us
    ppermute x3, waiting for transfers between devices, exchange(): return lax.ppermute(value, axis, pairs)  9.73 us
    dot_general x1, matrix products, per_device(): jnp.einsum('xcb,xbj->xcj', first, pick.astype(jnp.float32), precision=lax...  6.35 us
    all_gather x1, blocking collectives, per_device(): lax.all_gather(sketch, 'col', axis=0, tiled=True)  5.79 us
    ppermute x3, starting transfers between devices, exchange(): return lax.ppermute(value, axis, pairs)  4.94 us
    ppermute x7, waiting for transfers between devices, per_device(): arrived.append(lax.ppermute(block, 'ev', pairs))  4.64 us
    dot_general x1, matrix products, per_device(): jnp.einsum('xa,cab->xcb', hadamard(OUTER).astype(jnp.bfloat16), blocks, p...  2.69 us
    unnamed x1, other arithmetic  1.85 us
  transfers between devices with their start and end apart: 10, of which 6 were waited for; matrix products, arithmetic and copies ran while one was open for 1% of the time, Pallas kernels for 0%

profile of v5, /device:TPU:0, one launch (start us, length us, event | category | flops | bytes accessed | tf_op | source)
XLA Modules:
  0.0 53.9 jit_solution(14712138390333899366)
XLA Ops:
  0.0 0.8 %convert_element_type.16 = bf16[16384]{0:T(1024)(128)(2,1)S(1)} convert(s32[16384]{0:T(1024)} %param.4) | non-fusion elementwise | flops 16384 | bytes 98304 | tf_op jit(solution)/shard_map/convert_element_type | solution.py:56
  0.9 1.9 %multiply_bitcast_fusion = bf16[8,8,128,128]{3,1,2,0:T(8,128)(2,1)S(1)} fusion(bf16[64,16384]{1,0:T(8,128)(2,1)} %param.3, bf16[16384]{0:T(1024)(128)(2,1)S(1)} %convert_element_type.16), kind=kLoop, calls=%fused_computation.2 | loop fusion | flops 1048576 | bytes 4227072
  2.7 0.6 %copy.23 = bf16[8,8,128,128]{3,2,1,0:T(8,128)(2,1)S(1)} copy(bf16[8,8,128,128]{3,1,2,0:T(8,128)(2,1)S(1)} %multiply_bitcast_fusion) | data formatting | bytes 4194304
  3.3 2.7 %fusion.19 = f32[128,64,128]{2,0,1:T(8,128)} fusion(bf16[64,128,128]{2,1,0:T(8,128)(2,1)S(1)} %bitcast.39), kind=kOutput, calls=%fused_computation.26 | convolution fusion | flops 269025280 | bytes 6291456 | tf_op jit(solution)/shard_map/xa,cab->xcb/dot_general | solution.py:58
  6.2 0.5 reshape.30
  7.0 6.3 %fusion = f32[128,64,16]{1,2,0:T(8,128)S(1)} fusion(f32[128,64,128]{2,0,1:T(8,128)} %fusion.19, s32[16]{0:T(128)S(1)} %xor.35, s32[128,16]{1,0:T(8,128)S(1)} %copy.12), kind=kOutput, calls=%fused_computation | convolution fusion | flops 102498304 | bytes 4726848 | tf_op jit(solution)/shard_map/xcb,xbj->xcj/dot_general | solution.py:65
  13.4 0.7 %constant_dynamic-slice_fusion.7 = (f32[1,64,256]{1,0,2:T(1,128)S(1)}, f32[1,64,256]{1,0,2:T(1,128)S(1)}, f32[1,64,256]{1,0,2:T(1,128)S(1)}, f32[1,64,256]{1,0,2...) fusion(f32[8,64,256]{1,0,2:T(8,128)S(1)} %bitcast.40, ...), kind=kLoop, calls=%fused_computation.41 | loop fusion | bytes 1048608 | tf_op jit(solution)/shard_map/jit(dynamic_index_in_dim)/dynamic_slice | solution.py:74
  14.3 6.1 %collective-permute-start.6 = (f32[64,256]{1,0:T(8,128)S(1)}, f32[64,256]{1,0:T(8,128)S(1)}, u32[]{:S(2)}, u32[]{:S(2)}) collective-permute-start(f32[64,256]{1,0:T(8,128)S(1)} %bitcast.48), channel_id=1, source_target_pairs={{0,28},{4,24},{8,20},{12,16},{16,12},{20,8},{24,4},{28,0},{1,29},{... | collective-permute-start | bytes 196616 | tf_op jit(solution)/shard_map/ppermute | solution.py:80
  20.8 0.8 %collective-permute-start.4 = (f32[64,256]{1,0:T(8,128)S(1)}, f32[64,256]{1,0:T(8,128)S(1)}, u32[]{:S(2)}, u32[]{:S(2)}) collective-permute-start(f32[64,256]{1,0:T(8,128)S(1)} %bitcast.42), channel_id=1, source_target_pairs={{0,20},{4,16},{8,28},{12,24},{16,4},{20,0},{24,12},{28,8},{1,21},{... | collective-permute-start | bytes 196616 | tf_op jit(solution)/shard_map/ppermute | solution.py:80
  21.7 2.0 %collective-permute-start.3 = (f32[64,256]{1,0:T(8,128)S(1)}, f32[64,256]{1,0:T(8,128)S(1)}, u32[]{:S(2)}, u32[]{:S(2)}) collective-permute-start(f32[64,256]{1,0:T(8,128)S(1)} %bitcast.43), channel_id=1, source_target_pairs={{0,16},{4,20},{8,24},{12,28},{16,0},{20,4},{24,8},{28,12},{1,17},{... | collective-permute-start | bytes 196616 | tf_op jit(solution)/shard_map/ppermute | solution.py:80
  23.9 2.4 %collective-permute-start.2 = (f32[64,256]{1,0:T(8,128)S(1)}, f32[64,256]{1,0:T(8,128)S(1)}, u32[]{:S(2)}, u32[]{:S(2)}) collective-permute-start(f32[64,256]{1,0:T(8,128)S(1)} %bitcast.44), channel_id=1, source_target_pairs={{0,12},{4,8},{8,4},{12,0},{16,28},{20,24},{24,20},{28,16},{1,13},{... | collective-permute-start | bytes 196616 | tf_op jit(solution)/shard_map/ppermute | solution.py:80
  26.5 0.8 %collective-permute-start.1 = (f32[64,256]{1,0:T(8,128)S(1)}, f32[64,256]{1,0:T(8,128)S(1)}, u32[]{:S(2)}, u32[]{:S(2)}) collective-permute-start(f32[64,256]{1,0:T(8,128)S(1)} %bitcast.47), channel_id=1, source_target_pairs={{0,8},{4,12},{8,0},{12,4},{16,24},{20,28},{24,16},{28,20},{1,9},{5... | collective-permute-start | bytes 196616 | tf_op jit(solution)/shard_map/ppermute | solution.py:80
  27.7 1.9 %collective-permute-done.4 = f32[64,256]{1,0:T(8,128)S(1)} collective-permute-done((f32[64,256]{1,0:T(8,128)S(1)}, f32[64,256]{1,0:T(8,128)S(1)}, u32[]{:S(2)}, u32[]{:S(2)}) %collective-permute-start.4) | collective-permute-done | bytes 65568 | tf_op jit(solution)/shard_map/ppermute | solution.py:80
  29.6 2.0 %collective-permute-done.3 = f32[64,256]{1,0:T(8,128)S(1)} collective-permute-done((f32[64,256]{1,0:T(8,128)S(1)}, f32[64,256]{1,0:T(8,128)S(1)}, u32[]{:S(2)}, u32[]{:S(2)}) %collective-permute-start.3) | collective-permute-done | bytes 65568 | tf_op jit(solution)/shard_map/ppermute | solution.py:80
  31.6 0.7 %collective-permute-done.1 = f32[64,256]{1,0:T(8,128)S(1)} collective-permute-done((f32[64,256]{1,0:T(8,128)S(1)}, f32[64,256]{1,0:T(8,128)S(1)}, u32[]{:S(2)}, u32[]{:S(2)}) %collective-permute-start.1) | collective-permute-done | bytes 65568 | tf_op jit(solution)/shard_map/ppermute | solution.py:80
  32.4 5.8 %all_gather.3 = f32[256,256]{1,0:T(8,128)S(1)} all-gather(f32[64,256]{1,0:T(8,128)S(1)} %fusion.17), channel_id=1, replica_groups=mesh['ev'=8,'col'=4] {'col'}, dimensions={0}, use_global_device_ids=true | all-gather | bytes 327680 | tf_op jit(solution)/shard_map/all_gather | solution.py:90
  38.2 0.4 fusion.37
  38.6 0.8 %collective-permute-start.7 = (f32[64,256]{1,0:T(8,128)S(1)}, f32[64,256]{1,0:T(8,128)S(1)}, u32[]{:S(2)}, u32[]{:S(2)}) collective-permute-start(f32[64,256]{1,0:T(8,128)S(1)} %fusion.37), channel_id=1, source_target_pairs={{0,4},{4,0},{8,12},{12,8},{16,20},{20,16},{24,28},{28,24},{1,5},{5... | collective-permute-start | bytes 196616 | tf_op jit(solution)/shard_map/ppermute | solution.py:24
  39.4 3.6 %collective-permute-done.7 = f32[64,256]{1,0:T(8,128)S(1)} collective-permute-done((f32[64,256]{1,0:T(8,128)S(1)}, f32[64,256]{1,0:T(8,128)S(1)}, u32[]{:S(2)}, u32[]{:S(2)}) %collective-permute-start.7) | collective-permute-done | bytes 65568 | tf_op jit(solution)/shard_map/ppermute | solution.py:24
  43.0 1.2 %collective-permute-start.8 = (f32[64,256]{1,0:T(8,128)S(1)}, f32[64,256]{1,0:T(8,128)S(1)}, u32[]{:S(2)}, u32[]{:S(2)}) collective-permute-start(f32[64,256]{1,0:T(8,128)S(1)} %add.111), channel_id=1, source_target_pairs={{0,8},{4,12},{8,0},{12,4},{16,24},{20,28},{24,16},{28,20},{1,9},{5... | collective-permute-start | bytes 196616 | tf_op jit(solution)/shard_map/ppermute | solution.py:24
  44.2 3.1 %collective-permute-done.8 = f32[64,256]{1,0:T(8,128)S(1)} collective-permute-done((f32[64,256]{1,0:T(8,128)S(1)}, f32[64,256]{1,0:T(8,128)S(1)}, u32[]{:S(2)}, u32[]{:S(2)}) %collective-permute-start.8) | collective-permute-done | bytes 65568 | tf_op jit(solution)/shard_map/ppermute | solution.py:24
  47.3 2.9 %collective-permute-start.9 = (f32[64,256]{1,0:T(8,128)S(1)}, f32[64,256]{1,0:T(8,128)S(1)}, u32[]{:S(2)}, u32[]{:S(2)}) collective-permute-start(f32[64,256]{1,0:T(8,128)S(1)} %add.112), channel_id=1, source_target_pairs={{0,16},{4,20},{8,24},{12,28},{16,0},{20,4},{24,8},{28,12},{1,17},{... | collective-permute-start | bytes 196616 | tf_op jit(solution)/shard_map/ppermute | solution.py:24
  50.2 3.0 %collective-permute-done.9 = f32[64,256]{1,0:T(8,128)S(1)} collective-permute-done((f32[64,256]{1,0:T(8,128)S(1)}, f32[64,256]{1,0:T(8,128)S(1)}, u32[]{:S(2)}, u32[]{:S(2)}) %collective-permute-start.9) | collective-permute-done | bytes 65568 | tf_op jit(solution)/shard_map/ppermute | solution.py:24
  53.3 0.6 %add.113 = f32[64,256]{1,0:T(8,128)} add(f32[64,256]{1,0:T(8,128)S(1)} %add.112, f32[64,256]{1,0:T(8,128)S(1)} %collective-permute-done.9) | non-fusion elementwise | flops 16384 | bytes 196608 | tf_op jit(solution)/shard_map/add | solution.py:95
  (27 shorter events, 1.9 us)
Async XLA Ops:
  3.3 2.9 %copy-start = (s32[2048]{0:T(1024)S(1)}, s32[2048]{0:T(1024)}, u32[]{:S(2)}) copy-start(s32[2048]{0:T(1024)} %param.5) | copy-start | bytes 24580
  14.3 12.2 %collective-permute-start.6 = (f32[64,256]{1,0:T(8,128)S(1)}, f32[64,256]{1,0:T(8,128)S(1)}, u32[]{:S(2)}, u32[]{:S(2)}) collective-permute-start(f32[64,256]{1,0:T(8,128)S(1)} %bitcast.48), channel_id=1, source_target_pairs={{0,28},{4,24},{8,20},{12,16},{16,12},{20,8},{24,4},{28,0},{1,29},{... | collective-permute-start | bytes 196616 | tf_op jit(solution)/shard_map/ppermute | solution.py:80
  20.5 6.8 %collective-permute-start.5 = (f32[64,256]{1,0:T(8,128)S(1)}, f32[64,256]{1,0:T(8,128)S(1)}, u32[]{:S(2)}, u32[]{:S(2)}) collective-permute-start(f32[64,256]{1,0:T(8,128)S(1)} %bitcast.46), channel_id=1, source_target_pairs={{0,24},{4,28},{8,16},{12,20},{16,8},{20,12},{24,0},{28,4},{1,25},{... | collective-permute-start | bytes 196616 | tf_op jit(solution)/shard_map/ppermute | solution.py:80
  20.8 8.8 %collective-permute-start.4 = (f32[64,256]{1,0:T(8,128)S(1)}, f32[64,256]{1,0:T(8,128)S(1)}, u32[]{:S(2)}, u32[]{:S(2)}) collective-permute-start(f32[64,256]{1,0:T(8,128)S(1)} %bitcast.42), channel_id=1, source_target_pairs={{0,20},{4,16},{8,28},{12,24},{16,4},{20,0},{24,12},{28,8},{1,21},{... | collective-permute-start | bytes 196616 | tf_op jit(solution)/shard_map/ppermute | solution.py:80
  21.7 9.9 %collective-permute-start.3 = (f32[64,256]{1,0:T(8,128)S(1)}, f32[64,256]{1,0:T(8,128)S(1)}, u32[]{:S(2)}, u32[]{:S(2)}) collective-permute-start(f32[64,256]{1,0:T(8,128)S(1)} %bitcast.43), channel_id=1, source_target_pairs={{0,16},{4,20},{8,24},{12,28},{16,0},{20,4},{24,8},{28,12},{1,17},{... | collective-permute-start | bytes 196616 | tf_op jit(solution)/shard_map/ppermute | solution.py:80
  23.9 7.8 %collective-permute-start.2 = (f32[64,256]{1,0:T(8,128)S(1)}, f32[64,256]{1,0:T(8,128)S(1)}, u32[]{:S(2)}, u32[]{:S(2)}) collective-permute-start(f32[64,256]{1,0:T(8,128)S(1)} %bitcast.44), channel_id=1, source_target_pairs={{0,12},{4,8},{8,4},{12,0},{16,28},{20,24},{24,20},{28,16},{1,13},{... | collective-permute-start | bytes 196616 | tf_op jit(solution)/shard_map/ppermute | solution.py:80
  26.5 5.9 %collective-permute-start.1 = (f32[64,256]{1,0:T(8,128)S(1)}, f32[64,256]{1,0:T(8,128)S(1)}, u32[]{:S(2)}, u32[]{:S(2)}) collective-permute-start(f32[64,256]{1,0:T(8,128)S(1)} %bitcast.47), channel_id=1, source_target_pairs={{0,8},{4,12},{8,0},{12,4},{16,24},{20,28},{24,16},{28,20},{1,9},{5... | collective-permute-start | bytes 196616 | tf_op jit(solution)/shard_map/ppermute | solution.py:80
  27.3 5.1 %collective-permute-start = (f32[64,256]{1,0:T(8,128)S(1)}, f32[64,256]{1,0:T(8,128)S(1)}, u32[]{:S(2)}, u32[]{:S(2)}) collective-permute-start(f32[64,256]{1,0:T(8,128)S(1)} %bitcast.45), channel_id=1, source_target_pairs={{0,4},{4,0},{8,12},{12,8},{16,20},{20,16},{24,28},{28,24},{1,5},{5... | collective-permute-start | bytes 196616 | tf_op jit(solution)/shard_map/ppermute | solution.py:80
  38.6 4.4 %collective-permute-start.7 = (f32[64,256]{1,0:T(8,128)S(1)}, f32[64,256]{1,0:T(8,128)S(1)}, u32[]{:S(2)}, u32[]{:S(2)}) collective-permute-start(f32[64,256]{1,0:T(8,128)S(1)} %fusion.37), channel_id=1, source_target_pairs={{0,4},{4,0},{8,12},{12,8},{16,20},{20,16},{24,28},{28,24},{1,5},{5... | collective-permute-start | bytes 196616 | tf_op jit(solution)/shard_map/ppermute | solution.py:24
  43.0 4.3 %collective-permute-start.8 = (f32[64,256]{1,0:T(8,128)S(1)}, f32[64,256]{1,0:T(8,128)S(1)}, u32[]{:S(2)}, u32[]{:S(2)}) collective-permute-start(f32[64,256]{1,0:T(8,128)S(1)} %add.111), channel_id=1, source_target_pairs={{0,8},{4,12},{8,0},{12,4},{16,24},{20,28},{24,16},{28,20},{1,9},{5... | collective-permute-start | bytes 196616 | tf_op jit(solution)/shard_map/ppermute | solution.py:24
  47.3 5.9 %collective-permute-start.9 = (f32[64,256]{1,0:T(8,128)S(1)}, f32[64,256]{1,0:T(8,128)S(1)}, u32[]{:S(2)}, u32[]{:S(2)}) collective-permute-start(f32[64,256]{1,0:T(8,128)S(1)} %add.112), channel_id=1, source_target_pairs={{0,16},{4,20},{8,24},{12,28},{16,0},{20,4},{24,8},{28,12},{1,17},{... | collective-permute-start | bytes 196616 | tf_op jit(solution)/shard_map/ppermute | solution.py:24

commit v6 on v5

--- a/solution.py
+++ b/solution.py
@@ -62,13 +62,20 @@
         preferred_element_type=jnp.float32,
     )
     pick = selection(offsets, my_index, groups, inner)
-    sampled = jnp.einsum(
-        "xcb,xbj->xcj",
-        first,
-        pick.astype(jnp.float32),
+    width = groups * per_row
+    group = max(1, OUTER // width)
+    count = OUTER // group
+    lhs = first.reshape(count, group * columns, inner)
+    rhs = pick.reshape(count, group, inner, width).transpose(0, 2, 1, 3).reshape(count, inner, group * width)
+    wide = jnp.einsum(
+        "gmb,gbn->gmn",
+        lhs,
+        rhs.astype(jnp.float32),
         precision=lax.Precision.HIGH,
         preferred_element_type=jnp.float32,
-    )
+    ).reshape(count, group, columns, group, width)
+    eye = (jnp.arange(group)[:, None] == jnp.arange(group)[None, :]).astype(jnp.float32)
+    sampled = (wide * eye[None, :, None, :, None]).sum(axis=3).reshape(OUTER, columns, width)
     chunks = sampled.reshape(OUTER, columns, groups, per_row).transpose(2, 1, 0, 3)
     chunks = chunks.reshape(groups, columns, OUTER * per_row)
     own = lax.dynamic_index_in_dim(chunks, my_index, axis=0, keepdims=False)

time: 54.1 us -> 68.7 us (1.27)
  local copies, waits for them, and re-layouts: 2.91 us -> 15.4 us
  other arithmetic: 3.44 us -> 8.08 us
  matrix products: 9.41 us -> 6.71 us
    reshape x1, local copies, waits for them, and re-layouts: 0.07 us -> 7.05 us  [per_device(): wide = jnp.einsum('gmb,gbn->gmn', lhs, rhs.astype(jnp.float32), precision...]
    reduce_sum x0 -> x1, other arithmetic: none -> 4.63 us  [per_device(): (wide * eye[None, :, None, :, None]).sum(axis=3)]
    dot_general x0 -> x1, local copies, waits for them, and re-layouts: none -> 4.38 us  [per_device(): jnp.einsum('xa,cab->xcb', hadamard(OUTER).astype(jnp.bfloat16), blocks, p...]
    dot_general x1, matrix products: 2.69 us -> 0.74 us  [per_device(): jnp.einsum('xa,cab->xcb', hadamard(OUTER).astype(jnp.bfloat16), blocks, p...]
    dot_general x1, matrix products: 6.35 us -> 5.6 us  [per_device(): jnp.einsum('gmb,gbn->gmn', lhs, rhs.astype(jnp.float32), precision=lax.Pr...]
where the time goes in v6:
time: 68.7 us; the launch traced here: 68.3 us
  starting transfers between devices  17.8 us (26%)
  local copies, waits for them, and re-layouts  15.4 us (22%)
  waiting for transfers between devices  14.4 us (21%)
  other arithmetic  8.08 us (12%)
  matrix products  6.71 us (10%)
  blocking collectives  5.79 us (8%)
    ppermute x7, starting transfers between devices, per_device(): arrived.append(lax.ppermute(block, 'ev', pairs))  12.8 us
    ppermute x3, waiting for transfers between devices, exchange(): return lax.ppermute(value, axis, pairs)  9.74 us
    reshape x1, local copies, waits for them, and re-layouts, per_device(): wide = jnp.einsum('gmb,gbn->gmn', lhs, rhs.astype(jnp.float32), precision...  7.05 us
    all_gather x1, blocking collectives, per_device(): lax.all_gather(sketch, 'col', axis=0, tiled=True)  5.79 us
    dot_general x1, matrix products, per_device(): jnp.einsum('gmb,gbn->gmn', lhs, rhs.astype(jnp.float32), precision=lax.Pr...  5.6 us
    ppermute x3, starting transfers between devices, exchange(): return lax.ppermute(value, axis, pairs)  4.93 us
    ppermute x7, waiting for transfers between devices, per_device(): arrived.append(lax.ppermute(block, 'ev', pairs))  4.65 us
    reduce_sum x1, other arithmetic, per_device(): (wide * eye[None, :, None, :, None]).sum(axis=3)  4.63 us
  transfers between devices with their start and end apart: 10, of which 6 were waited for; matrix products, arithmetic and copies ran while one was open for 1% of the time, Pallas kernels for 0%

profile of v6, /device:TPU:0, one launch (start us, length us, event | category | flops | bytes accessed | tf_op | source)
XLA Modules:
  0.0 68.3 jit_solution(17091724824036391942)
XLA Ops:
  0.0 0.8 %convert_element_type.25 = bf16[16384]{0:T(1024)(128)(2,1)S(1)} convert(s32[16384]{0:T(1024)} %param.4) | non-fusion elementwise | flops 16384 | bytes 98304 | tf_op jit(solution)/shard_map/convert_element_type | solution.py:56
  0.9 1.9 %multiply_bitcast_fusion = bf16[8,8,128,128]{3,1,2,0:T(8,128)(2,1)S(1)} fusion(bf16[64,16384]{1,0:T(8,128)(2,1)} %param.3, bf16[16384]{0:T(1024)(128)(2,1)S(1)} %convert_element_type.25), kind=kLoop, calls=%fused_computation.1 | loop fusion | flops 1048576 | bytes 4227072
  3.3 0.7 %fusion.18 = f32[128,64,128]{2,0,1:T(8,128)S(1)} fusion(bf16[64,128,128]{2,1,0:T(8,128)(2,1)S(1)} %bitcast.43), kind=kOutput, calls=%fused_computation.26 | convolution fusion | flops 269025280 | bytes 6291456 | tf_op jit(solution)/shard_map/xa,cab->xcb/dot_general | solution.py:58
  4.1 4.4 %copy.13 = f32[128,64,128]{2,1,0:T(8,128)} copy(f32[128,64,128]{2,0,1:T(8,128)S(1)} %fusion.18) | data formatting | bytes 8388608 | tf_op jit(solution)/shard_map/xa,cab->xcb/dot_general | solution.py:58
  9.8 5.6 %fusion = f32[16,512,128]{1,2,0:T(8,128)} fusion(f32[16,512,128]{2,1,0:T(8,128)} %bitcast.42, s32[128]{0:T(128)S(1)} %xor.43, s32[16,128]{1,0:T(8,128)S(1)} %and.92), kind=kOutput, calls=%fused_computation.3 | convolution fusion | flops 807141376 | bytes 8397312 | tf_op jit(solution)/shard_map/gmb,gbn->gmn/dot_general | solution.py:70
  15.4 7.1 %reshape.53 = f32[16,8,64,8,16]{2,1,4,3,0:T(8,128)} reshape(f32[16,512,128]{1,2,0:T(8,128)} %fusion) | data formatting | bytes 8388608 | tf_op jit(solution)/shard_map/reshape | solution.py:76
  22.5 4.6 %multiply_reduce_fusion = f32[16,8,64,16]{2,1,3,0:T(8,128)S(1)} fusion(f32[16,8,64,8,16]{2,1,4,3,0:T(8,128)} %reshape.53, f32[8,8]{0,1:T(8,128)S(1)} %fusion.27), kind=kLoop, calls=%fused_computation | loop fusion | flops 1966080 | bytes 4718848 | tf_op jit(solution)/shard_map/reduce_sum | solution.py:78
  27.9 0.7 %constant_dynamic-slice_fusion.7 = (f32[1,64,256]{1,0,2:T(1,128)S(1)}, f32[1,64,256]{1,0,2:T(1,128)S(1)}, f32[1,64,256]{1,0,2:T(1,128)S(1)}, f32[1,64,256]{1,0,2...) fusion(f32[8,64,256]{1,0,2:T(8,128)S(1)} %bitcast.44, ...), kind=kLoop, calls=%fused_computation.43 | loop fusion | bytes 1048608 | tf_op jit(solution)/shard_map/jit(dynamic_index_in_dim)/dynamic_slice | solution.py:81
  28.7 6.1 %collective-permute-start.6 = (f32[64,256]{1,0:T(8,128)S(1)}, f32[64,256]{1,0:T(8,128)S(1)}, u32[]{:S(2)}, u32[]{:S(2)}) collective-permute-start(f32[64,256]{1,0:T(8,128)S(1)} %bitcast.52), channel_id=1, source_target_pairs={{0,28},{4,24},{8,20},{12,16},{16,12},{20,8},{24,4},{28,0},{1,29},{... | collective-permute-start | bytes 196616 | tf_op jit(solution)/shard_map/ppermute | solution.py:87
  35.2 0.8 %collective-permute-start.4 = (f32[64,256]{1,0:T(8,128)S(1)}, f32[64,256]{1,0:T(8,128)S(1)}, u32[]{:S(2)}, u32[]{:S(2)}) collective-permute-start(f32[64,256]{1,0:T(8,128)S(1)} %bitcast.46), channel_id=1, source_target_pairs={{0,20},{4,16},{8,28},{12,24},{16,4},{20,0},{24,12},{28,8},{1,21},{... | collective-permute-start | bytes 196616 | tf_op jit(solution)/shard_map/ppermute | solution.py:87
  36.1 2.0 %collective-permute-start.3 = (f32[64,256]{1,0:T(8,128)S(1)}, f32[64,256]{1,0:T(8,128)S(1)}, u32[]{:S(2)}, u32[]{:S(2)}) collective-permute-start(f32[64,256]{1,0:T(8,128)S(1)} %bitcast.47), channel_id=1, source_target_pairs={{0,16},{4,20},{8,24},{12,28},{16,0},{20,4},{24,8},{28,12},{1,17},{... | collective-permute-start | bytes 196616 | tf_op jit(solution)/shard_map/ppermute | solution.py:87
  38.3 2.4 %collective-permute-start.2 = (f32[64,256]{1,0:T(8,128)S(1)}, f32[64,256]{1,0:T(8,128)S(1)}, u32[]{:S(2)}, u32[]{:S(2)}) collective-permute-start(f32[64,256]{1,0:T(8,128)S(1)} %bitcast.48), channel_id=1, source_target_pairs={{0,12},{4,8},{8,4},{12,0},{16,28},{20,24},{24,20},{28,16},{1,13},{... | collective-permute-start | bytes 196616 | tf_op jit(solution)/shard_map/ppermute | solution.py:87
  40.9 0.8 %collective-permute-start.1 = (f32[64,256]{1,0:T(8,128)S(1)}, f32[64,256]{1,0:T(8,128)S(1)}, u32[]{:S(2)}, u32[]{:S(2)}) collective-permute-start(f32[64,256]{1,0:T(8,128)S(1)} %bitcast.51), channel_id=1, source_target_pairs={{0,8},{4,12},{8,0},{12,4},{16,24},{20,28},{24,16},{28,20},{1,9},{5... | collective-permute-start | bytes 196616 | tf_op jit(solution)/shard_map/ppermute | solution.py:87
  42.1 1.9 %collective-permute-done.4 = f32[64,256]{1,0:T(8,128)S(1)} collective-permute-done((f32[64,256]{1,0:T(8,128)S(1)}, f32[64,256]{1,0:T(8,128)S(1)}, u32[]{:S(2)}, u32[]{:S(2)}) %collective-permute-start.4) | collective-permute-done | bytes 65568 | tf_op jit(solution)/shard_map/ppermute | solution.py:87
  44.0 2.0 %collective-permute-done.3 = f32[64,256]{1,0:T(8,128)S(1)} collective-permute-done((f32[64,256]{1,0:T(8,128)S(1)}, f32[64,256]{1,0:T(8,128)S(1)}, u32[]{:S(2)}, u32[]{:S(2)}) %collective-permute-start.3) | collective-permute-done | bytes 65568 | tf_op jit(solution)/shard_map/ppermute | solution.py:87
  46.0 0.7 %collective-permute-done.1 = f32[64,256]{1,0:T(8,128)S(1)} collective-permute-done((f32[64,256]{1,0:T(8,128)S(1)}, f32[64,256]{1,0:T(8,128)S(1)}, u32[]{:S(2)}, u32[]{:S(2)}) %collective-permute-start.1) | collective-permute-done | bytes 65568 | tf_op jit(solution)/shard_map/ppermute | solution.py:87
  46.8 5.8 %all_gather.3 = f32[256,256]{1,0:T(8,128)S(1)} all-gather(f32[64,256]{1,0:T(8,128)S(1)} %fusion.16), channel_id=1, replica_groups=mesh['ev'=8,'col'=4] {'col'}, dimensions={0}, use_global_device_ids=true | all-gather | bytes 327680 | tf_op jit(solution)/shard_map/all_gather | solution.py:97
  53.0 0.8 %collective-permute-start.7 = (f32[64,256]{1,0:T(8,128)S(1)}, f32[64,256]{1,0:T(8,128)S(1)}, u32[]{:S(2)}, u32[]{:S(2)}) collective-permute-start(f32[64,256]{1,0:T(8,128)S(1)} %fusion.37), channel_id=1, source_target_pairs={{0,4},{4,0},{8,12},{12,8},{16,20},{20,16},{24,28},{28,24},{1,5},{5... | collective-permute-start | bytes 196616 | tf_op jit(solution)/shard_map/ppermute | solution.py:24
  53.8 3.6 %collective-permute-done.7 = f32[64,256]{1,0:T(8,128)S(1)} collective-permute-done((f32[64,256]{1,0:T(8,128)S(1)}, f32[64,256]{1,0:T(8,128)S(1)}, u32[]{:S(2)}, u32[]{:S(2)}) %collective-permute-start.7) | collective-permute-done | bytes 65568 | tf_op jit(solution)/shard_map/ppermute | solution.py:24
  57.4 1.2 %collective-permute-start.8 = (f32[64,256]{1,0:T(8,128)S(1)}, f32[64,256]{1,0:T(8,128)S(1)}, u32[]{:S(2)}, u32[]{:S(2)}) collective-permute-start(f32[64,256]{1,0:T(8,128)S(1)} %add.111), channel_id=1, source_target_pairs={{0,8},{4,12},{8,0},{12,4},{16,24},{20,28},{24,16},{28,20},{1,9},{5... | collective-permute-start | bytes 196616 | tf_op jit(solution)/shard_map/ppermute | solution.py:24
  58.6 3.1 %collective-permute-done.8 = f32[64,256]{1,0:T(8,128)S(1)} collective-permute-done((f32[64,256]{1,0:T(8,128)S(1)}, f32[64,256]{1,0:T(8,128)S(1)}, u32[]{:S(2)}, u32[]{:S(2)}) %collective-permute-start.8) | collective-permute-done | bytes 65568 | tf_op jit(solution)/shard_map/ppermute | solution.py:24
  61.7 2.9 %collective-permute-start.9 = (f32[64,256]{1,0:T(8,128)S(1)}, f32[64,256]{1,0:T(8,128)S(1)}, u32[]{:S(2)}, u32[]{:S(2)}) collective-permute-start(f32[64,256]{1,0:T(8,128)S(1)} %add.112), channel_id=1, source_target_pairs={{0,16},{4,20},{8,24},{12,28},{16,0},{20,4},{24,8},{28,12},{1,17},{... | collective-permute-start | bytes 196616 | tf_op jit(solution)/shard_map/ppermute | solution.py:24
  64.6 3.0 %collective-permute-done.9 = f32[64,256]{1,0:T(8,128)S(1)} collective-permute-done((f32[64,256]{1,0:T(8,128)S(1)}, f32[64,256]{1,0:T(8,128)S(1)}, u32[]{:S(2)}, u32[]{:S(2)}) %collective-permute-start.9) | collective-permute-done | bytes 65568 | tf_op jit(solution)/shard_map/ppermute | solution.py:24
  67.7 0.6 add.113
  (34 shorter events, 4.3 us)
Async XLA Ops:
  4.1 4.6 %copy-start = (s32[2048]{0:T(1024)S(1)}, s32[2048]{0:T(1024)}, u32[]{:S(2)}) copy-start(s32[2048]{0:T(1024)} %param.5) | copy-start | bytes 24580
  28.7 12.2 %collective-permute-start.6 = (f32[64,256]{1,0:T(8,128)S(1)}, f32[64,256]{1,0:T(8,128)S(1)}, u32[]{:S(2)}, u32[]{:S(2)}) collective-permute-start(f32[64,256]{1,0:T(8,128)S(1)} %bitcast.52), channel_id=1, source_target_pairs={{0,28},{4,24},{8,20},{12,16},{16,12},{20,8},{24,4},{28,0},{1,29},{... | collective-permute-start | bytes 196616 | tf_op jit(solution)/shard_map/ppermute | solution.py:87
  34.9 6.8 %collective-permute-start.5 = (f32[64,256]{1,0:T(8,128)S(1)}, f32[64,256]{1,0:T(8,128)S(1)}, u32[]{:S(2)}, u32[]{:S(2)}) collective-permute-start(f32[64,256]{1,0:T(8,128)S(1)} %bitcast.50), channel_id=1, source_target_pairs={{0,24},{4,28},{8,16},{12,20},{16,8},{20,12},{24,0},{28,4},{1,25},{... | collective-permute-start | bytes 196616 | tf_op jit(solution)/shard_map/ppermute | solution.py:87
  35.2 8.8 %collective-permute-start.4 = (f32[64,256]{1,0:T(8,128)S(1)}, f32[64,256]{1,0:T(8,128)S(1)}, u32[]{:S(2)}, u32[]{:S(2)}) collective-permute-start(f32[64,256]{1,0:T(8,128)S(1)} %bitcast.46), channel_id=1, source_target_pairs={{0,20},{4,16},{8,28},{12,24},{16,4},{20,0},{24,12},{28,8},{1,21},{... | collective-permute-start | bytes 196616 | tf_op jit(solution)/shard_map/ppermute | solution.py:87
  36.1 9.9 %collective-permute-start.3 = (f32[64,256]{1,0:T(8,128)S(1)}, f32[64,256]{1,0:T(8,128)S(1)}, u32[]{:S(2)}, u32[]{:S(2)}) collective-permute-start(f32[64,256]{1,0:T(8,128)S(1)} %bitcast.47), channel_id=1, source_target_pairs={{0,16},{4,20},{8,24},{12,28},{16,0},{20,4},{24,8},{28,12},{1,17},{... | collective-permute-start | bytes 196616 | tf_op jit(solution)/shard_map/ppermute | solution.py:87
  38.3 7.8 %collective-permute-start.2 = (f32[64,256]{1,0:T(8,128)S(1)}, f32[64,256]{1,0:T(8,128)S(1)}, u32[]{:S(2)}, u32[]{:S(2)}) collective-permute-start(f32[64,256]{1,0:T(8,128)S(1)} %bitcast.48), channel_id=1, source_target_pairs={{0,12},{4,8},{8,4},{12,0},{16,28},{20,24},{24,20},{28,16},{1,13},{... | collective-permute-start | bytes 196616 | tf_op jit(solution)/shard_map/ppermute | solution.py:87
  40.9 5.9 %collective-permute-start.1 = (f32[64,256]{1,0:T(8,128)S(1)}, f32[64,256]{1,0:T(8,128)S(1)}, u32[]{:S(2)}, u32[]{:S(2)}) collective-permute-start(f32[64,256]{1,0:T(8,128)S(1)} %bitcast.51), channel_id=1, source_target_pairs={{0,8},{4,12},{8,0},{12,4},{16,24},{20,28},{24,16},{28,20},{1,9},{5... | collective-permute-start | bytes 196616 | tf_op jit(solution)/shard_map/ppermute | solution.py:87
  41.7 5.1 %collective-permute-start = (f32[64,256]{1,0:T(8,128)S(1)}, f32[64,256]{1,0:T(8,128)S(1)}, u32[]{:S(2)}, u32[]{:S(2)}) collective-permute-start(f32[64,256]{1,0:T(8,128)S(1)} %bitcast.49), channel_id=1, source_target_pairs={{0,4},{4,0},{8,12},{12,8},{16,20},{20,16},{24,28},{28,24},{1,5},{5... | collective-permute-start | bytes 196616 | tf_op jit(solution)/shard_map/ppermute | solution.py:87
  53.0 4.4 %collective-permute-start.7 = (f32[64,256]{1,0:T(8,128)S(1)}, f32[64,256]{1,0:T(8,128)S(1)}, u32[]{:S(2)}, u32[]{:S(2)}) collective-permute-start(f32[64,256]{1,0:T(8,128)S(1)} %fusion.37), channel_id=1, source_target_pairs={{0,4},{4,0},{8,12},{12,8},{16,20},{20,16},{24,28},{28,24},{1,5},{5... | collective-permute-start | bytes 196616 | tf_op jit(solution)/shard_map/ppermute | solution.py:24
  57.4 4.3 %collective-permute-start.8 = (f32[64,256]{1,0:T(8,128)S(1)}, f32[64,256]{1,0:T(8,128)S(1)}, u32[]{:S(2)}, u32[]{:S(2)}) collective-permute-start(f32[64,256]{1,0:T(8,128)S(1)} %add.111), channel_id=1, source_target_pairs={{0,8},{4,12},{8,0},{12,4},{16,24},{20,28},{24,16},{28,20},{1,9},{5... | collective-permute-start | bytes 196616 | tf_op jit(solution)/shard_map/ppermute | solution.py:24
  61.7 5.9 %collective-permute-start.9 = (f32[64,256]{1,0:T(8,128)S(1)}, f32[64,256]{1,0:T(8,128)S(1)}, u32[]{:S(2)}, u32[]{:S(2)}) collective-permute-start(f32[64,256]{1,0:T(8,128)S(1)} %add.112), channel_id=1, source_target_pairs={{0,16},{4,20},{8,24},{12,28},{16,0},{20,4},{24,8},{28,12},{1,17},{... | collective-permute-start | bytes 196616 | tf_op jit(solution)/shard_map/ppermute | solution.py:24

commit v7 on v5

--- a/solution.py
+++ b/solution.py
@@ -22,6 +22,24 @@
     mask = 1 << bit
     pairs = [(source, source ^ mask) for source in range(lax.axis_size(axis))]
     return lax.ppermute(value, axis, pairs)
+
+
+def group_sum(value, bits):
+    groups = lax.axis_size("ev")
+    my_index = lax.axis_index("ev")
+    masks = [0]
+    for bit in bits:
+        masks = masks + [mask | (1 << bit) for mask in masks]
+    values = [value]
+    for mask in masks[1:]:
+        pairs = [(source, source ^ mask) for source in range(groups)]
+        values.append(lax.ppermute(value, "ev", pairs))
+    mine = sum(((my_index >> bit) & 1) << place for place, bit in enumerate(bits))
+    order = jnp.arange(len(masks), dtype=jnp.int32) ^ mine
+    ordered = jnp.take(jnp.stack(values), order, axis=0)
+    while ordered.shape[0] > 1:
+        ordered = ordered[0::2] + ordered[1::2]
+    return ordered[0]
 
 
 def split3(value):
@@ -91,8 +109,8 @@
         precision=high,
         preferred_element_type=jnp.float32,
     )
-    for level in range(levels):
-        partial_gram = partial_gram + exchange(partial_gram, "ev", level)
+    for start in range(0, levels, 2):
+        partial_gram = group_sum(partial_gram, list(range(start, min(start + 2, levels))))
     return partial_gram
 
 

time: 54.1 us -> 53.7 us (level)
  waiting for transfers between devices: 14.4 us -> 11.2 us
  starting transfers between devices: 17.8 us -> 19.2 us
  local copies, waits for them, and re-layouts: 2.91 us -> 4.04 us
    ppermute x3 -> x4, waiting for transfers between devices: 9.73 us -> 6.47 us  [group_sum(): values.append(lax.ppermute(value, 'ev', pairs))]
    ppermute x3 -> x4, starting transfers between devices: 4.94 us -> 6.3 us  [group_sum(): values.append(lax.ppermute(value, 'ev', pairs))]
    gather x0 -> x2, local copies, waits for them, and re-layouts: none -> 1.12 us  [group_sum(): ordered = jnp.take(jnp.stack(values), order, axis=0)]
    squeeze x0 -> x2, other arithmetic: none -> 0.65 us  [group_sum(): return ordered[0]]
    add x3 -> x2, other arithmetic: 0.66 us -> 0.03 us  [group_sum(): ordered = ordered[0::2] + ordered[1::2]]
  transfers between devices with their start and end apart: 10 -> 11, of which waited for: 6 -> 7; matrix products, arithmetic and copies ran while one was open for 1% -> 1% of each run, Pallas kernels for 0% -> 0%
where the time goes in v7:
time: 53.7 us; the launch traced here: 53.6 us
  starting transfers between devices  19.2 us (36%)
  waiting for transfers between devices  11.2 us (21%)
  matrix products  9.4 us (18%)
  blocking collectives  5.79 us (11%)
  local copies, waits for them, and re-layouts  4.04 us (8%)
  other arithmetic  3.7 us (7%)
    ppermute x7, starting transfers between devices, per_device(): arrived.append(lax.ppermute(block, 'ev', pairs))  12.9 us
    ppermute x4, waiting for transfers between devices, group_sum(): values.append(lax.ppermute(value, 'ev', pairs))  6.47 us
    dot_general x1, matrix products, per_device(): jnp.einsum('xcb,xbj->xcj', first, pick.astype(jnp.float32), precision=lax...  6.35 us
    ppermute x4, starting transfers between devices, group_sum(): values.append(lax.ppermute(value, 'ev', pairs))  6.3 us
    all_gather x1, blocking collectives, per_device(): lax.all_gather(sketch, 'col', axis=0, tiled=True)  5.79 us
    ppermute x7, waiting for transfers between devices, per_device(): arrived.append(lax.ppermute(block, 'ev', pairs))  4.72 us
    dot_general x1, matrix products, per_device(): jnp.einsum('xa,cab->xcb', hadamard(OUTER).astype(jnp.bfloat16), blocks, p...  2.69 us
    unnamed x1, other arithmetic  1.85 us
  transfers between devices with their start and end apart: 11, of which 7 were waited for; matrix products, arithmetic and copies ran while one was open for 1% of the time, Pallas kernels for 0%

profile of v7, /device:TPU:0, one launch (start us, length us, event | category | flops | bytes accessed | tf_op | source)
XLA Modules:
  0.0 53.6 jit_solution(10775405389190800187)
XLA Ops:
  0.0 0.8 %convert_element_type.16 = bf16[16384]{0:T(1024)(128)(2,1)S(1)} convert(s32[16384]{0:T(1024)} %param.4) | non-fusion elementwise | flops 16384 | bytes 98304 | tf_op jit(solution)/shard_map/convert_element_type | solution.py:74
  0.9 1.9 %multiply_bitcast_fusion = bf16[8,8,128,128]{3,1,2,0:T(8,128)(2,1)S(1)} fusion(bf16[64,16384]{1,0:T(8,128)(2,1)} %param.3, bf16[16384]{0:T(1024)(128)(2,1)S(1)} %convert_element_type.16), kind=kLoop, calls=%fused_computation.4 | loop fusion | flops 1048576 | bytes 4227072
  2.7 0.6 %copy.23 = bf16[8,8,128,128]{3,2,1,0:T(8,128)(2,1)S(1)} copy(bf16[8,8,128,128]{3,1,2,0:T(8,128)(2,1)S(1)} %multiply_bitcast_fusion) | data formatting | bytes 4194304
  3.3 2.7 %fusion.20 = f32[128,64,128]{2,0,1:T(8,128)} fusion(bf16[64,128,128]{2,1,0:T(8,128)(2,1)S(1)} %bitcast.52), kind=kOutput, calls=%fused_computation.36 | convolution fusion | flops 269025280 | bytes 6291456 | tf_op jit(solution)/shard_map/xa,cab->xcb/dot_general | solution.py:76
  7.0 6.3 %fusion = f32[128,64,16]{1,2,0:T(8,128)S(1)} fusion(f32[128,64,128]{2,0,1:T(8,128)} %fusion.20, s32[16]{0:T(128)S(1)} %xor.77, s32[128,16]{1,0:T(8,128)S(1)} %copy.12), kind=kOutput, calls=%fused_computation.2 | convolution fusion | flops 102498304 | bytes 4726848 | tf_op jit(solution)/shard_map/xcb,xbj->xcj/dot_general | solution.py:83
  13.4 0.7 %constant_dynamic-slice_fusion.7 = (f32[1,64,256]{1,0,2:T(1,128)S(1)}, f32[1,64,256]{1,0,2:T(1,128)S(1)}, f32[1,64,256]{1,0,2:T(1,128)S(1)}, f32[1,64,256]{1,0,2...) fusion(f32[8,64,256]{1,0,2:T(8,128)S(1)} %bitcast.53, ...), kind=kLoop, calls=%fused_computation.57 | loop fusion | bytes 1048608 | tf_op jit(solution)/shard_map/jit(dynamic_index_in_dim)/dynamic_slice | solution.py:92
  14.3 6.1 %collective-permute-start.6 = (f32[64,256]{1,0:T(8,128)S(1)}, f32[64,256]{1,0:T(8,128)S(1)}, u32[]{:S(2)}, u32[]{:S(2)}) collective-permute-start(f32[64,256]{1,0:T(8,128)S(1)} %bitcast.60), channel_id=1, source_target_pairs={{0,28},{4,24},{8,20},{12,16},{16,12},{20,8},{24,4},{28,0},{1,29},{... | collective-permute-start | bytes 196616 | tf_op jit(solution)/shard_map/ppermute | solution.py:98
  20.8 0.8 %collective-permute-start.4 = (f32[64,256]{1,0:T(8,128)S(1)}, f32[64,256]{1,0:T(8,128)S(1)}, u32[]{:S(2)}, u32[]{:S(2)}) collective-permute-start(f32[64,256]{1,0:T(8,128)S(1)} %bitcast.56), channel_id=1, source_target_pairs={{0,20},{4,16},{8,28},{12,24},{16,4},{20,0},{24,12},{28,8},{1,21},{... | collective-permute-start | bytes 196616 | tf_op jit(solution)/shard_map/ppermute | solution.py:98
  21.7 2.0 %collective-permute-start.3 = (f32[64,256]{1,0:T(8,128)S(1)}, f32[64,256]{1,0:T(8,128)S(1)}, u32[]{:S(2)}, u32[]{:S(2)}) collective-permute-start(f32[64,256]{1,0:T(8,128)S(1)} %bitcast.57), channel_id=1, source_target_pairs={{0,16},{4,20},{8,24},{12,28},{16,0},{20,4},{24,8},{28,12},{1,17},{... | collective-permute-start | bytes 196616 | tf_op jit(solution)/shard_map/ppermute | solution.py:98
  23.9 2.4 %collective-permute-start.2 = (f32[64,256]{1,0:T(8,128)S(1)}, f32[64,256]{1,0:T(8,128)S(1)}, u32[]{:S(2)}, u32[]{:S(2)}) collective-permute-start(f32[64,256]{1,0:T(8,128)S(1)} %bitcast.59), channel_id=1, source_target_pairs={{0,12},{4,8},{8,4},{12,0},{16,28},{20,24},{24,20},{28,16},{1,13},{... | collective-permute-start | bytes 196616 | tf_op jit(solution)/shard_map/ppermute | solution.py:98
  26.6 0.8 %collective-permute-start.1 = (f32[64,256]{1,0:T(8,128)S(1)}, f32[64,256]{1,0:T(8,128)S(1)}, u32[]{:S(2)}, u32[]{:S(2)}) collective-permute-start(f32[64,256]{1,0:T(8,128)S(1)} %bitcast.62), channel_id=1, source_target_pairs={{0,8},{4,12},{8,0},{12,4},{16,24},{20,28},{24,16},{28,20},{1,9},{5... | collective-permute-start | bytes 196616 | tf_op jit(solution)/shard_map/ppermute | solution.py:98
  27.8 1.8 %collective-permute-done.4 = f32[64,256]{1,0:T(8,128)S(1)} collective-permute-done((f32[64,256]{1,0:T(8,128)S(1)}, f32[64,256]{1,0:T(8,128)S(1)}, u32[]{:S(2)}, u32[]{:S(2)}) %collective-permute-start.4) | collective-permute-done | bytes 65568 | tf_op jit(solution)/shard_map/ppermute | solution.py:98
  29.6 2.0 %collective-permute-done.3 = f32[64,256]{1,0:T(8,128)S(1)} collective-permute-done((f32[64,256]{1,0:T(8,128)S(1)}, f32[64,256]{1,0:T(8,128)S(1)}, u32[]{:S(2)}, u32[]{:S(2)}) %collective-permute-start.3) | collective-permute-done | bytes 65568 | tf_op jit(solution)/shard_map/ppermute | solution.py:98
  31.6 0.9 %collective-permute-done.1 = f32[64,256]{1,0:T(8,128)S(1)} collective-permute-done((f32[64,256]{1,0:T(8,128)S(1)}, f32[64,256]{1,0:T(8,128)S(1)}, u32[]{:S(2)}, u32[]{:S(2)}) %collective-permute-start.1) | collective-permute-done | bytes 65568 | tf_op jit(solution)/shard_map/ppermute | solution.py:98
  32.6 5.8 %all_gather.3 = f32[256,256]{1,0:T(8,128)S(1)} all-gather(f32[64,256]{1,0:T(8,128)S(1)} %fusion.18), channel_id=1, replica_groups=mesh['ev'=8,'col'=4] {'col'}, dimensions={0}, use_global_device_ids=true | all-gather | bytes 327680 | tf_op jit(solution)/shard_map/all_gather | solution.py:108
  39.2 1.8 %collective-permute-start.8 = (f32[64,256]{1,0:T(8,128)S(1)}, f32[64,256]{1,0:T(8,128)S(1)}, u32[]{:S(2)}, u32[]{:S(2)}) collective-permute-start(f32[64,256]{1,0:T(8,128)S(1)} %fusion.40), channel_id=1, source_target_pairs={{0,8},{4,12},{8,0},{12,4},{16,24},{20,28},{24,16},{28,20},{1,9},{5... | collective-permute-start | bytes 196616 | tf_op jit(solution)/shard_map/ppermute | solution.py:36
  41.0 1.3 %collective-permute-start.7 = (f32[64,256]{1,0:T(8,128)S(1)}, f32[64,256]{1,0:T(8,128)S(1)}, u32[]{:S(2)}, u32[]{:S(2)}) collective-permute-start(f32[64,256]{1,0:T(8,128)S(1)} %fusion.40), channel_id=1, source_target_pairs={{0,4},{4,0},{8,12},{12,8},{16,20},{20,16},{24,28},{28,24},{1,5},{5... | collective-permute-start | bytes 196616 | tf_op jit(solution)/shard_map/ppermute | solution.py:36
  42.3 2.3 %collective-permute-done.9 = f32[64,256]{1,0:T(8,128)S(1)} collective-permute-done((f32[64,256]{1,0:T(8,128)S(1)}, f32[64,256]{1,0:T(8,128)S(1)}, u32[]{:S(2)}, u32[]{:S(2)}) %collective-permute-start.9) | collective-permute-done | bytes 65568 | tf_op jit(solution)/shard_map/ppermute | solution.py:36
  44.7 0.7 %collective-permute-done.7 = f32[64,256]{1,0:T(8,128)S(1)} collective-permute-done((f32[64,256]{1,0:T(8,128)S(1)}, f32[64,256]{1,0:T(8,128)S(1)}, u32[]{:S(2)}, u32[]{:S(2)}) %collective-permute-start.7) | collective-permute-done | bytes 65568 | tf_op jit(solution)/shard_map/ppermute | solution.py:36
  45.5 0.6 %gather_fusion = f32[4,64,256]{2,1,0:T(8,128)S(1)} fusion(f32[4,64,256]{2,1,0:T(8,128)S(1)} %pad_maximum_fusion, s32[1024]{0:T(1024)S(1)} %pad_clamp_fusion.1), kind=kCustom, calls=%fused_computation | custom fusion | bytes 524304 | tf_op jit(solution)/shard_map/jit(_take)/gather | solution.py:39
  46.2 2.8 %collective-permute-start.10 = (f32[64,256]{1,0:T(8,128)S(1)}, f32[64,256]{1,0:T(8,128)S(1)}, u32[]{:S(2)}, u32[]{:S(2)}) collective-permute-start(f32[64,256]{1,0:T(8,128)S(1)} %fusion.44), channel_id=1, source_target_pairs={{0,16},{4,20},{8,24},{12,28},{16,0},{20,4},{24,8},{28,12},{1,17},{... | collective-permute-start | bytes 196616 | tf_op jit(solution)/shard_map/ppermute | solution.py:36
  48.9 3.3 %collective-permute-done.10 = f32[64,256]{1,0:T(8,128)S(1)} collective-permute-done((f32[64,256]{1,0:T(8,128)S(1)}, f32[64,256]{1,0:T(8,128)S(1)}, u32[]{:S(2)}, u32[]{:S(2)}) %collective-permute-start.10) | collective-permute-done | bytes 65568 | tf_op jit(solution)/shard_map/ppermute | solution.py:36
  52.3 0.6 %gather_fusion.1 = f32[2,64,256]{2,1,0:T(8,128)S(1)} fusion(f32[2,64,256]{2,1,0:T(8,128)S(1)} %pad_maximum_fusion.1, s32[1024]{0:T(1024)S(1)} %pad_clamp_fusion), kind=kCustom, calls=%fused_computation.1 | custom fusion | bytes 262152 | tf_op jit(solution)/shard_map/jit(_take)/gather | solution.py:39
  52.9 0.6 %fusion.11 = f32[64,256]{1,0:T(8,128)} fusion(f32[2,64,256]{2,1,0:T(8,128)S(1)} %broadcast_select_fusion.1), kind=kLoop, calls=%fused_computation.24 | loop fusion | flops 16384 | bytes 196608 | tf_op jit(solution)/shard_map/squeeze | solution.py:42
  (42 shorter events, 3.6 us)
Async XLA Ops:
  3.3 2.9 %copy-start = (s32[2048]{0:T(1024)S(1)}, s32[2048]{0:T(1024)}, u32[]{:S(2)}) copy-start(s32[2048]{0:T(1024)} %param.5) | copy-start | bytes 24580
  14.3 12.3 %collective-permute-start.6 = (f32[64,256]{1,0:T(8,128)S(1)}, f32[64,256]{1,0:T(8,128)S(1)}, u32[]{:S(2)}, u32[]{:S(2)}) collective-permute-start(f32[64,256]{1,0:T(8,128)S(1)} %bitcast.60), channel_id=1, source_target_pairs={{0,28},{4,24},{8,20},{12,16},{16,12},{20,8},{24,4},{28,0},{1,29},{... | collective-permute-start | bytes 196616 | tf_op jit(solution)/shard_map/ppermute | solution.py:98
  20.5 7.0 %collective-permute-start.5 = (f32[64,256]{1,0:T(8,128)S(1)}, f32[64,256]{1,0:T(8,128)S(1)}, u32[]{:S(2)}, u32[]{:S(2)}) collective-permute-start(f32[64,256]{1,0:T(8,128)S(1)} %bitcast.58), channel_id=1, source_target_pairs={{0,24},{4,28},{8,16},{12,20},{16,8},{20,12},{24,0},{28,4},{1,25},{... | collective-permute-start | bytes 196616 | tf_op jit(solution)/shard_map/ppermute | solution.py:98
  20.8 8.8 %collective-permute-start.4 = (f32[64,256]{1,0:T(8,128)S(1)}, f32[64,256]{1,0:T(8,128)S(1)}, u32[]{:S(2)}, u32[]{:S(2)}) collective-permute-start(f32[64,256]{1,0:T(8,128)S(1)} %bitcast.56), channel_id=1, source_target_pairs={{0,20},{4,16},{8,28},{12,24},{16,4},{20,0},{24,12},{28,8},{1,21},{... | collective-permute-start | bytes 196616 | tf_op jit(solution)/shard_map/ppermute | solution.py:98
  21.7 9.9 %collective-permute-start.3 = (f32[64,256]{1,0:T(8,128)S(1)}, f32[64,256]{1,0:T(8,128)S(1)}, u32[]{:S(2)}, u32[]{:S(2)}) collective-permute-start(f32[64,256]{1,0:T(8,128)S(1)} %bitcast.57), channel_id=1, source_target_pairs={{0,16},{4,20},{8,24},{12,28},{16,0},{20,4},{24,8},{28,12},{1,17},{... | collective-permute-start | bytes 196616 | tf_op jit(solution)/shard_map/ppermute | solution.py:98
  23.9 7.8 %collective-permute-start.2 = (f32[64,256]{1,0:T(8,128)S(1)}, f32[64,256]{1,0:T(8,128)S(1)}, u32[]{:S(2)}, u32[]{:S(2)}) collective-permute-start(f32[64,256]{1,0:T(8,128)S(1)} %bitcast.59), channel_id=1, source_target_pairs={{0,12},{4,8},{8,4},{12,0},{16,28},{20,24},{24,20},{28,16},{1,13},{... | collective-permute-start | bytes 196616 | tf_op jit(solution)/shard_map/ppermute | solution.py:98
  26.6 5.9 %collective-permute-start.1 = (f32[64,256]{1,0:T(8,128)S(1)}, f32[64,256]{1,0:T(8,128)S(1)}, u32[]{:S(2)}, u32[]{:S(2)}) collective-permute-start(f32[64,256]{1,0:T(8,128)S(1)} %bitcast.62), channel_id=1, source_target_pairs={{0,8},{4,12},{8,0},{12,4},{16,24},{20,28},{24,16},{28,20},{1,9},{5... | collective-permute-start | bytes 196616 | tf_op jit(solution)/shard_map/ppermute | solution.py:98
  27.4 5.1 %collective-permute-start = (f32[64,256]{1,0:T(8,128)S(1)}, f32[64,256]{1,0:T(8,128)S(1)}, u32[]{:S(2)}, u32[]{:S(2)}) collective-permute-start(f32[64,256]{1,0:T(8,128)S(1)} %bitcast.61), channel_id=1, source_target_pairs={{0,4},{4,0},{8,12},{12,8},{16,20},{20,16},{24,28},{28,24},{1,5},{5... | collective-permute-start | bytes 196616 | tf_op jit(solution)/shard_map/ppermute | solution.py:98
  38.7 5.9 %collective-permute-start.9 = (f32[64,256]{1,0:T(8,128)S(1)}, f32[64,256]{1,0:T(8,128)S(1)}, u32[]{:S(2)}, u32[]{:S(2)}) collective-permute-start(f32[64,256]{1,0:T(8,128)S(1)} %fusion.40), channel_id=1, source_target_pairs={{0,12},{4,8},{8,4},{12,0},{16,28},{20,24},{24,20},{28,16},{1,13},{... | collective-permute-start | bytes 196616 | tf_op jit(solution)/shard_map/ppermute | solution.py:36
  39.2 5.5 %collective-permute-start.8 = (f32[64,256]{1,0:T(8,128)S(1)}, f32[64,256]{1,0:T(8,128)S(1)}, u32[]{:S(2)}, u32[]{:S(2)}) collective-permute-start(f32[64,256]{1,0:T(8,128)S(1)} %fusion.40), channel_id=1, source_target_pairs={{0,8},{4,12},{8,0},{12,4},{16,24},{20,28},{24,16},{28,20},{1,9},{5... | collective-permute-start | bytes 196616 | tf_op jit(solution)/shard_map/ppermute | solution.py:36
  41.0 4.4 %collective-permute-start.7 = (f32[64,256]{1,0:T(8,128)S(1)}, f32[64,256]{1,0:T(8,128)S(1)}, u32[]{:S(2)}, u32[]{:S(2)}) collective-permute-start(f32[64,256]{1,0:T(8,128)S(1)} %fusion.40), channel_id=1, source_target_pairs={{0,4},{4,0},{8,12},{12,8},{16,20},{20,16},{24,28},{28,24},{1,5},{5... | collective-permute-start | bytes 196616 | tf_op jit(solution)/shard_map/ppermute | solution.py:36
  46.2 6.1 %collective-permute-start.10 = (f32[64,256]{1,0:T(8,128)S(1)}, f32[64,256]{1,0:T(8,128)S(1)}, u32[]{:S(2)}, u32[]{:S(2)}) collective-permute-start(f32[64,256]{1,0:T(8,128)S(1)} %fusion.44), channel_id=1, source_target_pairs={{0,16},{4,20},{8,24},{12,28},{16,0},{20,4},{24,8},{28,12},{1,17},{... | collective-permute-start | bytes 196616 | tf_op jit(solution)/shard_map/ppermute | solution.py:36

commit v8 on v7

--- a/solution.py
+++ b/solution.py
@@ -3,6 +3,7 @@
 import jax
 import jax.numpy as jnp
 from jax import lax
+from jax.experimental import pallas as pl
 from jax.sharding import PartitionSpec as P
 
 STRIDE = 64
@@ -42,24 +43,54 @@
     return ordered[0]
 
 
-def split3(value):
-    hi = lax.reduce_precision(value, exponent_bits=8, mantissa_bits=7)
-    rest = value - hi
-    mid = lax.reduce_precision(rest, exponent_bits=8, mantissa_bits=7)
-    low = rest - mid
-    return tuple(piece.astype(jnp.bfloat16) for piece in (hi, mid, low))
+def factors(offsets, my_index, groups, length):
+    inner = length // OUTER
+    rows = STRIDE * jnp.arange(offsets.shape[0], dtype=jnp.int32) + offsets
+    y = rows % inner
+    x = rows % length // inner
+    p = rows // length
+    lanes = jnp.arange(inner, dtype=jnp.int32)[:, None]
+    hy = 1 - 2 * (lax.population_count(y[None, :] & lanes) & 1)
+    outer = jnp.arange(OUTER, dtype=jnp.int32)[:, None]
+    parity = lax.population_count(x[None, :] & outer) + lax.population_count(p & my_index)[None, :]
+    hx = 1 - 2 * (parity & 1)
+    return hy.astype(jnp.bfloat16), hx.astype(jnp.float32)
 
 
-def selection(offsets, my_index, groups, inner):
-    per_row = inner // STRIDE
-    off = offsets.reshape(groups, OUTER, per_row)
-    rows = jnp.arange(per_row, dtype=jnp.int32)[None, None, :] * STRIDE + off
-    rows = rows.transpose(1, 0, 2)
-    lanes = jnp.arange(inner, dtype=jnp.int32)
-    parity = lax.population_count(rows[:, None, :, :] & lanes[None, :, None, None]) & 1
-    group_parity = lax.population_count(jnp.arange(groups, dtype=jnp.int32) & my_index) & 1
-    parity = parity ^ group_parity[None, None, :, None]
-    return (1 - 2 * parity).astype(jnp.bfloat16).reshape(OUTER, inner, groups * per_row)
+def sketch_kernel(panel_ref, sign_ref, hy_ref, hx_ref, out_ref):
+    block, samples = out_ref.shape
+    inner = sign_ref.shape[1]
+    rows = panel_ref[...].astype(jnp.float32).reshape(block, OUTER, inner) * sign_ref[...][None]
+    rows = rows.reshape(block * OUTER, inner).astype(jnp.bfloat16)
+    width = min(samples, 1024)
+    for part in range(samples // width):
+        lanes = pl.ds(part * width, width)
+        mixed = jnp.dot(rows, hy_ref[:, lanes], preferred_element_type=jnp.float32)
+        mixed = mixed.reshape(block, OUTER, width) * hx_ref[:, lanes][None]
+        out_ref[:, lanes] = jnp.sum(mixed, axis=1)
+
+
+def local_sketch(panel, sign, hy, hx):
+    columns, length = panel.shape
+    inner = length // OUTER
+    samples = hy.shape[1]
+    block = 8
+    flops = 2 * columns * length * samples + 2 * columns * OUTER * samples
+    return pl.pallas_call(
+        sketch_kernel,
+        out_shape=jax.ShapeDtypeStruct((columns, samples), jnp.float32),
+        grid=(columns // block,),
+        in_specs=[
+            pl.BlockSpec((block * OUTER, inner), lambda i: (i, 0)),
+            pl.BlockSpec((OUTER, inner), lambda i: (0, 0)),
+            pl.BlockSpec((inner, samples), lambda i: (0, 0)),
+            pl.BlockSpec((OUTER, samples), lambda i: (0, 0)),
+        ],
+        out_specs=pl.BlockSpec((block, samples), lambda i: (i, 0)),
+        cost_estimate=pl.CostEstimate(
+            flops=flops, transcendentals=0, bytes_accessed=columns * length * 2 + columns * samples * 4
+        ),
+    )(panel.reshape(columns * OUTER, inner), sign, hy, hx)
 
 
 def per_device(panel, signs, offsets):
@@ -71,24 +102,11 @@
     per_row = inner // STRIDE
     high = lax.Precision.HIGHEST
 
-    signed = panel * signs.astype(jnp.bfloat16)[None, :]
-    blocks = signed.reshape(columns, OUTER, inner)
-    first = jnp.einsum(
-        "xa,cab->xcb",
-        hadamard(OUTER).astype(jnp.bfloat16),
-        blocks,
-        preferred_element_type=jnp.float32,
-    )
-    pick = selection(offsets, my_index, groups, inner)
-    sampled = jnp.einsum(
-        "xcb,xbj->xcj",
-        first,
-        pick.astype(jnp.float32),
-        precision=lax.Precision.HIGH,
-        preferred_element_type=jnp.float32,
-    )
-    chunks = sampled.reshape(OUTER, columns, groups, per_row).transpose(2, 1, 0, 3)
-    chunks = chunks.reshape(groups, columns, OUTER * per_row)
+    sign = signs.reshape(OUTER, inner).astype(jnp.float32)
+    hy, hx = factors(offsets, my_index, groups, length)
+    sampled = local_sketch(panel, sign, hy, hx)
+
+    chunks = sampled.reshape(columns, groups, OUTER * per_row).transpose(1, 0, 2)
     own = lax.dynamic_index_in_dim(chunks, my_index, axis=0, keepdims=False)
     arrived = []
     for distance in range(1, groups):

time: 53.7 us -> 62.9 us (1.17)
  Pallas kernels: 0 us -> 12.3 us
  matrix products: 9.4 us -> 0.37 us
  waiting for transfers between devices: 11.2 us -> 14.7 us
  local copies, waits for them, and re-layouts: 4.04 us -> 6.97 us
  starting transfers between devices: 19.2 us -> 18.3 us
    pallas_call x0 -> x1, Pallas kernels: none -> 12.3 us  [local_sketch(): pl.pallas_call(sketch_kernel, out_shape=jax.ShapeDtypeStruct((columns, sa...]
    dot_general x2 -> x0, matrix products: 9.04 us -> none  [the longest x1 6.35 us: per_device(): jnp.einsum('xcb,xbj->xcj', first, pick.astype(jnp.float32), precision=lax...]
    reshape x2 -> x1, local copies, waits for them, and re-layouts: 0.54 us -> 4.23 us  [local_sketch(): panel.reshape(columns * OUTER, inner)]
    ppermute x7, waiting for transfers between devices: 4.72 us -> 7.02 us  [per_device(): arrived.append(lax.ppermute(block, 'ev', pairs))]
    unnamed x1 -> x0, other arithmetic: 1.85 us -> none
    convert_element_type x1 -> x2, other arithmetic: 0.84 us -> 2.26 us  [the longest x1 1.63 us: factors(): return (hy.astype(jnp.bfloat16), hx.astype(jnp.float32))]
    dynamic_slice x9 -> x0, local copies, waits for them, and re-layouts: 1.36 us -> none  [the longest x2 0.82 us: per_device(): own = lax.dynamic_index_in_dim(chunks, my_index, axis=0, keepdims=False)]
    ppermute x4, waiting for transfers between devices: 6.47 us -> 7.71 us  [group_sum(): values.append(lax.ppermute(value, 'ev', pairs))]
  transfers between devices with their start and end apart: 11 -> 11, of which waited for: 7 -> 6; matrix products, arithmetic and copies ran while one was open for 1% -> 0% of each run, Pallas kernels for 0% -> 0%
where the time goes in v8:
time: 62.9 us; the launch traced here: 62.6 us
  starting transfers between devices  18.3 us (29%)
  waiting for transfers between devices  14.7 us (23%)
  Pallas kernels  12.3 us (20%)
  local copies, waits for them, and re-layouts  6.97 us (11%)
  blocking collectives  5.79 us (9%)
  other arithmetic  3.93 us (6%)
    ppermute x7, starting transfers between devices, per_device(): arrived.append(lax.ppermute(block, 'ev', pairs))  12.6 us
    pallas_call x1, Pallas kernels, local_sketch(): pl.pallas_call(sketch_kernel, out_shape=jax.ShapeDtypeStruct((columns, sa...  12.3 us
    ppermute x4, waiting for transfers between devices, group_sum(): values.append(lax.ppermute(value, 'ev', pairs))  7.71 us
    ppermute x7, waiting for transfers between devices, per_device(): arrived.append(lax.ppermute(block, 'ev', pairs))  7.02 us
    all_gather x1, blocking collectives, per_device(): lax.all_gather(sketch, 'col', axis=0, tiled=True)  5.79 us
    ppermute x4, starting transfers between devices, group_sum(): values.append(lax.ppermute(value, 'ev', pairs))  5.7 us
    reshape x1, local copies, waits for them, and re-layouts, local_sketch(): panel.reshape(columns * OUTER, inner)  4.23 us
    convert_element_type x1, other arithmetic, factors(): return (hy.astype(jnp.bfloat16), hx.astype(jnp.float32))  1.63 us
  transfers between devices with their start and end apart: 11, of which 6 were waited for; matrix products, arithmetic and copies ran while one was open for 0% of the time, Pallas kernels for 0%

profile of v8, /device:TPU:0, one launch (start us, length us, event | category | flops | bytes accessed | tf_op | source)
XLA Modules:
  0.0 62.6 jit_solution(540185038276528693)
XLA Ops:
  0.0 0.7 %add_select_fusion.1 = (s32[2048]{0:T(1024)S(1)}, s32[2048]{0:T(1024)S(1)}, s32[2048]{0:T(1024)S(1)}) fusion(s32[2048]{0:T(1024)} %param.5, s32[]{:T(128)S(6)} %axis_index.11), kind=kLoop, calls=%fused_computation.30 | loop fusion | flops 94208 | bytes 32772 | tf_op jit(solution)/shard_map/jit(floor_divide)/jit(_where)/select_n | solution.py:50
  0.7 4.2 %reshape.69.panel_ref = bf16[8192,128]{1,0:T(8,128)(2,1)} reshape(bf16[64,16384]{1,0:T(8,128)(2,1)} %param.3) | data formatting | bytes 4194304 | tf_op jit(solution)/shard_map/reshape | solution.py:93
  5.0 0.6 %convert_bitcast_fusion.sign_ref = f32[128,128]{1,0:T(8,128)} fusion(s32[16384]{0:T(1024)S(1)} %copy-done), kind=kLoop, calls=%fused_computation.27 | loop fusion | flops 16384 | bytes 131072 | tf_op jit(solution)/shard_map/convert_element_type | solution.py:105
  5.6 1.6 %subtract_convert_fusion = (f32[128,2048]{1,0:T(8,128)}, bf16[128,2048]{1,0:T(8,128)(2,1)}) fusion(s32[2048]{0:T(1024)S(1)} %get-tuple-element.14, s32[2048]{0:T(1024)S(1)} %get-tuple-element.13, s32[2048]{0:T(1024)S(1)} %get-tuple-element.15), kind=kLoop, calls=%fused_computation.2 | loop fusion | flops 3407872 | bytes 1597440 | tf_op jit(solution)/shard_map/convert_element_type | solution.py:57
  7.2 12.3 %shard_map.37 = f32[64,2048]{1,0:T(8,128)} custom-call(bf16[8192,128]{1,0:T(8,128)(2,1)} %reshape.69.panel_ref, f32[128,128]{1,0:T(8,128)} %convert_bitcast_fusion.sign_ref, bf16[128,2048]{1,0:T(8,128)(2,1)} %get-tuple-element.17.hy_ref, f32[128,2048]{1,0:T(8,128)} %get-tuple-element.16.hx_ref), custom_call_target="tpu_custom_call" | custom-call | flops 4328521728 | bytes 2621440 | tf_op jit(solution)/shard_map/pallas_call | solution.py:79
  19.6 1.2 %copy.12 = f32[8,8,8,256]{3,2,1,0:T(8,128)S(1)} copy(f32[8,8,8,256]{3,1,2,0:T(8,128)} %bitcast.57) | data formatting | bytes 1048576
  21.2 3.0 %collective-permute-start = (f32[64,256]{1,0:T(8,128)S(1)}, f32[64,256]{1,0:T(8,128)S(1)}, u32[]{:S(2)}, u32[]{:S(2)}) collective-permute-start(f32[64,256]{1,0:T(8,128)S(1)} %bitcast.63), channel_id=1, source_target_pairs={{0,4},{4,0},{8,12},{12,8},{16,20},{20,16},{24,28},{28,24},{1,5},{5... | collective-permute-start | bytes 196616 | tf_op jit(solution)/shard_map/ppermute | solution.py:116
  24.2 1.6 %collective-permute-start.1 = (f32[64,256]{1,0:T(8,128)S(1)}, f32[64,256]{1,0:T(8,128)S(1)}, u32[]{:S(2)}, u32[]{:S(2)}) collective-permute-start(f32[64,256]{1,0:T(8,128)S(1)} %bitcast.61), channel_id=1, source_target_pairs={{0,8},{4,12},{8,0},{12,4},{16,24},{20,28},{24,16},{28,20},{1,9},{5... | collective-permute-start | bytes 196616 | tf_op jit(solution)/shard_map/ppermute | solution.py:116
  25.9 3.0 %collective-permute-start.3 = (f32[64,256]{1,0:T(8,128)S(1)}, f32[64,256]{1,0:T(8,128)S(1)}, u32[]{:S(2)}, u32[]{:S(2)}) collective-permute-start(f32[64,256]{1,0:T(8,128)S(1)} %bitcast.60), channel_id=1, source_target_pairs={{0,16},{4,20},{8,24},{12,28},{16,0},{20,4},{24,8},{28,12},{1,17},{... | collective-permute-start | bytes 196616 | tf_op jit(solution)/shard_map/ppermute | solution.py:116
  28.8 1.3 %collective-permute-start.4 = (f32[64,256]{1,0:T(8,128)S(1)}, f32[64,256]{1,0:T(8,128)S(1)}, u32[]{:S(2)}, u32[]{:S(2)}) collective-permute-start(f32[64,256]{1,0:T(8,128)S(1)} %bitcast.62), channel_id=1, source_target_pairs={{0,20},{4,16},{8,28},{12,24},{16,4},{20,0},{24,12},{28,8},{1,21},{... | collective-permute-start | bytes 196616 | tf_op jit(solution)/shard_map/ppermute | solution.py:116
  30.2 3.7 %collective-permute-start.5 = (f32[64,256]{1,0:T(8,128)S(1)}, f32[64,256]{1,0:T(8,128)S(1)}, u32[]{:S(2)}, u32[]{:S(2)}) collective-permute-start(f32[64,256]{1,0:T(8,128)S(1)} %bitcast.65), channel_id=1, source_target_pairs={{0,24},{4,28},{8,16},{12,20},{16,8},{20,12},{24,0},{28,4},{1,25},{... | collective-permute-start | bytes 196616 | tf_op jit(solution)/shard_map/ppermute | solution.py:116
  33.9 5.1 %collective-permute-done.4 = f32[64,256]{1,0:T(8,128)S(1)} collective-permute-done((f32[64,256]{1,0:T(8,128)S(1)}, f32[64,256]{1,0:T(8,128)S(1)}, u32[]{:S(2)}, u32[]{:S(2)}) %collective-permute-start.4) | collective-permute-done | bytes 65568 | tf_op jit(solution)/shard_map/ppermute | solution.py:116
  39.0 1.9 %collective-permute-done.6 = f32[64,256]{1,0:T(8,128)S(1)} collective-permute-done((f32[64,256]{1,0:T(8,128)S(1)}, f32[64,256]{1,0:T(8,128)S(1)}, u32[]{:S(2)}, u32[]{:S(2)}) %collective-permute-start.6) | collective-permute-done | bytes 65568 | tf_op jit(solution)/shard_map/ppermute | solution.py:116
  41.0 5.8 %all_gather.3 = f32[256,256]{1,0:T(8,128)S(1)} all-gather(f32[64,256]{1,0:T(8,128)S(1)} %fusion.7), channel_id=1, replica_groups=mesh['ev'=8,'col'=4] {'col'}, dimensions={0}, use_global_device_ids=true | all-gather | bytes 327680 | tf_op jit(solution)/shard_map/all_gather | solution.py:126
  47.1 0.6 collective-permute-start.7
  47.7 1.8 %collective-permute-start.8 = (f32[64,256]{1,0:T(8,128)S(1)}, f32[64,256]{1,0:T(8,128)S(1)}, u32[]{:S(2)}, u32[]{:S(2)}) collective-permute-start(f32[64,256]{1,0:T(8,128)S(1)} %fusion.16), channel_id=1, source_target_pairs={{0,8},{4,12},{8,0},{12,4},{16,24},{20,28},{24,16},{28,20},{1,9},{5... | collective-permute-start | bytes 196616 | tf_op jit(solution)/shard_map/ppermute | solution.py:37
  49.5 1.2 %collective-permute-start.9 = (f32[64,256]{1,0:T(8,128)S(1)}, f32[64,256]{1,0:T(8,128)S(1)}, u32[]{:S(2)}, u32[]{:S(2)}) collective-permute-start(f32[64,256]{1,0:T(8,128)S(1)} %fusion.16), channel_id=1, source_target_pairs={{0,12},{4,8},{8,4},{12,0},{16,28},{20,24},{24,20},{28,16},{1,13},{... | collective-permute-start | bytes 196616 | tf_op jit(solution)/shard_map/ppermute | solution.py:37
  50.7 0.8 %collective-permute-done.7 = f32[64,256]{1,0:T(8,128)S(1)} collective-permute-done((f32[64,256]{1,0:T(8,128)S(1)}, f32[64,256]{1,0:T(8,128)S(1)}, u32[]{:S(2)}, u32[]{:S(2)}) %collective-permute-start.7) | collective-permute-done | bytes 65568 | tf_op jit(solution)/shard_map/ppermute | solution.py:37
  52.0 2.7 %collective-permute-done.9 = f32[64,256]{1,0:T(8,128)S(1)} collective-permute-done((f32[64,256]{1,0:T(8,128)S(1)}, f32[64,256]{1,0:T(8,128)S(1)}, u32[]{:S(2)}, u32[]{:S(2)}) %collective-permute-start.9) | collective-permute-done | bytes 65568 | tf_op jit(solution)/shard_map/ppermute | solution.py:37
  54.7 0.6 gather_fusion
  55.4 2.1 %collective-permute-start.10 = (f32[64,256]{1,0:T(8,128)S(1)}, f32[64,256]{1,0:T(8,128)S(1)}, u32[]{:S(2)}, u32[]{:S(2)}) collective-permute-start(f32[64,256]{1,0:T(8,128)S(1)} %fusion.19), channel_id=1, source_target_pairs={{0,16},{4,20},{8,24},{12,28},{16,0},{20,4},{24,8},{28,12},{1,17},{... | collective-permute-start | bytes 196616 | tf_op jit(solution)/shard_map/ppermute | solution.py:37
  57.5 3.8 %collective-permute-done.10 = f32[64,256]{1,0:T(8,128)S(1)} collective-permute-done((f32[64,256]{1,0:T(8,128)S(1)}, f32[64,256]{1,0:T(8,128)S(1)}, u32[]{:S(2)}, u32[]{:S(2)}) %collective-permute-start.10) | collective-permute-done | bytes 65568 | tf_op jit(solution)/shard_map/ppermute | solution.py:37
  61.3 0.6 gather_fusion.1
  62.0 0.6 %fusion = f32[64,256]{1,0:T(8,128)} fusion(f32[2,64,256]{2,1,0:T(8,128)S(1)} %broadcast_select_fusion.1), kind=kLoop, calls=%fused_computation.9 | loop fusion | flops 16384 | bytes 196608 | tf_op jit(solution)/shard_map/squeeze | solution.py:43
  (33 shorter events, 1.6 us)
Async XLA Ops:
  0.7 4.2 %copy-start = (s32[16384]{0:T(1024)S(1)}, s32[16384]{0:T(1024)}, u32[]{:S(2)}) copy-start(s32[16384]{0:T(1024)} %param.4) | copy-start | bytes 196612
  21.2 9.0 %collective-permute-start = (f32[64,256]{1,0:T(8,128)S(1)}, f32[64,256]{1,0:T(8,128)S(1)}, u32[]{:S(2)}, u32[]{:S(2)}) collective-permute-start(f32[64,256]{1,0:T(8,128)S(1)} %bitcast.63), channel_id=1, source_target_pairs={{0,4},{4,0},{8,12},{12,8},{16,20},{20,16},{24,28},{28,24},{1,5},{5... | collective-permute-start | bytes 196616 | tf_op jit(solution)/shard_map/ppermute | solution.py:116
  24.2 9.6 %collective-permute-start.1 = (f32[64,256]{1,0:T(8,128)S(1)}, f32[64,256]{1,0:T(8,128)S(1)}, u32[]{:S(2)}, u32[]{:S(2)}) collective-permute-start(f32[64,256]{1,0:T(8,128)S(1)} %bitcast.61), channel_id=1, source_target_pairs={{0,8},{4,12},{8,0},{12,4},{16,24},{20,28},{24,16},{28,20},{1,9},{5... | collective-permute-start | bytes 196616 | tf_op jit(solution)/shard_map/ppermute | solution.py:116
  25.8 8.1 %collective-permute-start.2 = (f32[64,256]{1,0:T(8,128)S(1)}, f32[64,256]{1,0:T(8,128)S(1)}, u32[]{:S(2)}, u32[]{:S(2)}) collective-permute-start(f32[64,256]{1,0:T(8,128)S(1)} %bitcast.59), channel_id=1, source_target_pairs={{0,12},{4,8},{8,4},{12,0},{16,28},{20,24},{24,20},{28,16},{1,13},{... | collective-permute-start | bytes 196616 | tf_op jit(solution)/shard_map/ppermute | solution.py:116
  25.9 8.1 %collective-permute-start.3 = (f32[64,256]{1,0:T(8,128)S(1)}, f32[64,256]{1,0:T(8,128)S(1)}, u32[]{:S(2)}, u32[]{:S(2)}) collective-permute-start(f32[64,256]{1,0:T(8,128)S(1)} %bitcast.60), channel_id=1, source_target_pairs={{0,16},{4,20},{8,24},{12,28},{16,0},{20,4},{24,8},{28,12},{1,17},{... | collective-permute-start | bytes 196616 | tf_op jit(solution)/shard_map/ppermute | solution.py:116
  28.8 10.2 %collective-permute-start.4 = (f32[64,256]{1,0:T(8,128)S(1)}, f32[64,256]{1,0:T(8,128)S(1)}, u32[]{:S(2)}, u32[]{:S(2)}) collective-permute-start(f32[64,256]{1,0:T(8,128)S(1)} %bitcast.62), channel_id=1, source_target_pairs={{0,20},{4,16},{8,28},{12,24},{16,4},{20,0},{24,12},{28,8},{1,21},{... | collective-permute-start | bytes 196616 | tf_op jit(solution)/shard_map/ppermute | solution.py:116
  30.2 8.8 %collective-permute-start.5 = (f32[64,256]{1,0:T(8,128)S(1)}, f32[64,256]{1,0:T(8,128)S(1)}, u32[]{:S(2)}, u32[]{:S(2)}) collective-permute-start(f32[64,256]{1,0:T(8,128)S(1)} %bitcast.65), channel_id=1, source_target_pairs={{0,24},{4,28},{8,16},{12,20},{16,8},{20,12},{24,0},{28,4},{1,25},{... | collective-permute-start | bytes 196616 | tf_op jit(solution)/shard_map/ppermute | solution.py:116
  33.9 7.1 %collective-permute-start.6 = (f32[64,256]{1,0:T(8,128)S(1)}, f32[64,256]{1,0:T(8,128)S(1)}, u32[]{:S(2)}, u32[]{:S(2)}) collective-permute-start(f32[64,256]{1,0:T(8,128)S(1)} %bitcast.64), channel_id=1, source_target_pairs={{0,28},{4,24},{8,20},{12,16},{16,12},{20,8},{24,4},{28,0},{1,29},{... | collective-permute-start | bytes 196616 | tf_op jit(solution)/shard_map/ppermute | solution.py:116
  47.1 4.4 %collective-permute-start.7 = (f32[64,256]{1,0:T(8,128)S(1)}, f32[64,256]{1,0:T(8,128)S(1)}, u32[]{:S(2)}, u32[]{:S(2)}) collective-permute-start(f32[64,256]{1,0:T(8,128)S(1)} %fusion.16), channel_id=1, source_target_pairs={{0,4},{4,0},{8,12},{12,8},{16,20},{20,16},{24,28},{28,24},{1,5},{5... | collective-permute-start | bytes 196616 | tf_op jit(solution)/shard_map/ppermute | solution.py:37
  47.7 4.3 %collective-permute-start.8 = (f32[64,256]{1,0:T(8,128)S(1)}, f32[64,256]{1,0:T(8,128)S(1)}, u32[]{:S(2)}, u32[]{:S(2)}) collective-permute-start(f32[64,256]{1,0:T(8,128)S(1)} %fusion.16), channel_id=1, source_target_pairs={{0,8},{4,12},{8,0},{12,4},{16,24},{20,28},{24,16},{28,20},{1,9},{5... | collective-permute-start | bytes 196616 | tf_op jit(solution)/shard_map/ppermute | solution.py:37
  49.5 5.2 %collective-permute-start.9 = (f32[64,256]{1,0:T(8,128)S(1)}, f32[64,256]{1,0:T(8,128)S(1)}, u32[]{:S(2)}, u32[]{:S(2)}) collective-permute-start(f32[64,256]{1,0:T(8,128)S(1)} %fusion.16), channel_id=1, source_target_pairs={{0,12},{4,8},{8,4},{12,0},{16,28},{20,24},{24,20},{28,16},{1,13},{... | collective-permute-start | bytes 196616 | tf_op jit(solution)/shard_map/ppermute | solution.py:37
  55.4 5.9 %collective-permute-start.10 = (f32[64,256]{1,0:T(8,128)S(1)}, f32[64,256]{1,0:T(8,128)S(1)}, u32[]{:S(2)}, u32[]{:S(2)}) collective-permute-start(f32[64,256]{1,0:T(8,128)S(1)} %fusion.19), channel_id=1, source_target_pairs={{0,16},{4,20},{8,24},{12,28},{16,0},{20,4},{24,8},{28,12},{1,17},{... | collective-permute-start | bytes 196616 | tf_op jit(solution)/shard_map/ppermute | solution.py:37

commit v9 on v8

--- a/solution.py
+++ b/solution.py
@@ -59,20 +59,21 @@
 
 def sketch_kernel(panel_ref, sign_ref, hy_ref, hx_ref, out_ref):
     block, samples = out_ref.shape
-    inner = sign_ref.shape[1]
-    rows = panel_ref[...].astype(jnp.float32).reshape(block, OUTER, inner) * sign_ref[...][None]
-    rows = rows.reshape(block * OUTER, inner).astype(jnp.bfloat16)
+    inner = hy_ref.shape[0]
+    signed = panel_ref[...].astype(jnp.float32) * sign_ref[...]
+    rows = jnp.concatenate(
+        [signed[:, a * inner : (a + 1) * inner] for a in range(OUTER)], axis=0
+    ).astype(jnp.bfloat16)
     width = min(samples, 1024)
     for part in range(samples // width):
         lanes = pl.ds(part * width, width)
         mixed = jnp.dot(rows, hy_ref[:, lanes], preferred_element_type=jnp.float32)
-        mixed = mixed.reshape(block, OUTER, width) * hx_ref[:, lanes][None]
-        out_ref[:, lanes] = jnp.sum(mixed, axis=1)
+        mixed = mixed.reshape(OUTER, block, width) * hx_ref[:, lanes][:, None, :]
+        out_ref[:, lanes] = jnp.sum(mixed, axis=0)
 
 
 def local_sketch(panel, sign, hy, hx):
     columns, length = panel.shape
-    inner = length // OUTER
     samples = hy.shape[1]
     block = 8
     flops = 2 * columns * length * samples + 2 * columns * OUTER * samples
@@ -81,16 +82,16 @@
         out_shape=jax.ShapeDtypeStruct((columns, samples), jnp.float32),
         grid=(columns // block,),
         in_specs=[
-            pl.BlockSpec((block * OUTER, inner), lambda i: (i, 0)),
-            pl.BlockSpec((OUTER, inner), lambda i: (0, 0)),
-            pl.BlockSpec((inner, samples), lambda i: (0, 0)),
-            pl.BlockSpec((OUTER, samples), lambda i: (0, 0)),
+            pl.BlockSpec((block, length), lambda i: (i, 0)),
+            pl.BlockSpec((1, length), lambda i: (0, 0)),
+            pl.BlockSpec(hy.shape, lambda i: (0, 0)),
+            pl.BlockSpec(hx.shape, lambda i: (0, 0)),
         ],
         out_specs=pl.BlockSpec((block, samples), lambda i: (i, 0)),
         cost_estimate=pl.CostEstimate(
             flops=flops, transcendentals=0, bytes_accessed=columns * length * 2 + columns * samples * 4
         ),
-    )(panel.reshape(columns * OUTER, inner), sign, hy, hx)
+    )(panel, sign, hy, hx)
 
 
 def per_device(panel, signs, offsets):
@@ -102,7 +103,7 @@
     per_row = inner // STRIDE
     high = lax.Precision.HIGHEST
 
-    sign = signs.reshape(OUTER, inner).astype(jnp.float32)
+    sign = signs.reshape(1, length).astype(jnp.float32)
     hy, hx = factors(offsets, my_index, groups, length)
     sampled = local_sketch(panel, sign, hy, hx)
 

time: 62.9 us -> 59.4 us (0.944)
  local copies, waits for them, and re-layouts: 6.97 us -> 2.74 us
  other arithmetic: 3.93 us -> 4.77 us
    reshape x1 -> x0, local copies, waits for them, and re-layouts: 4.23 us -> none  [local_sketch(): panel.reshape(columns * OUTER, inner)]
    convert_element_type x1, other arithmetic: 0.64 us -> 1.48 us  [per_device(): sign = signs.reshape(1, length).astype(jnp.float32)]
where the time goes in v9:
time: 59.4 us; the launch traced here: 59.1 us
  starting transfers between devices  18.3 us (31%)
  waiting for transfers between devices  14.7 us (25%)
  Pallas kernels  12.3 us (21%)
  blocking collectives  5.79 us (10%)
  other arithmetic  4.77 us (8%)
  local copies, waits for them, and re-layouts  2.74 us (5%)
    ppermute x7, starting transfers between devices, per_device(): arrived.append(lax.ppermute(block, 'ev', pairs))  12.6 us
    pallas_call x1, Pallas kernels, local_sketch(): pl.pallas_call(sketch_kernel, out_shape=jax.ShapeDtypeStruct((columns, sa...  12.3 us
    ppermute x4, waiting for transfers between devices, group_sum(): values.append(lax.ppermute(value, 'ev', pairs))  7.72 us
    ppermute x7, waiting for transfers between devices, per_device(): arrived.append(lax.ppermute(block, 'ev', pairs))  7.02 us
    all_gather x1, blocking collectives, per_device(): lax.all_gather(sketch, 'col', axis=0, tiled=True)  5.79 us
    ppermute x4, starting transfers between devices, group_sum(): values.append(lax.ppermute(value, 'ev', pairs))  5.69 us
    convert_element_type x1, other arithmetic, factors(): return (hy.astype(jnp.bfloat16), hx.astype(jnp.float32))  1.62 us
    convert_element_type x1, other arithmetic, per_device(): sign = signs.reshape(1, length).astype(jnp.float32)  1.48 us
  transfers between devices with their start and end apart: 11, of which 6 were waited for; matrix products, arithmetic and copies ran while one was open for 0% of the time, Pallas kernels for 0%

profile of v9, /device:TPU:0, one launch (start us, length us, event | category | flops | bytes accessed | tf_op | source)
XLA Modules:
  0.0 59.1 jit_solution(129321209200715324)
XLA Ops:
  0.0 0.7 %add_select_fusion.1 = (s32[2048]{0:T(1024)S(1)}, s32[2048]{0:T(1024)S(1)}, s32[2048]{0:T(1024)S(1)}) fusion(s32[2048]{0:T(1024)} %param.5, s32[]{:T(128)S(6)} %axis_index.11), kind=kLoop, calls=%fused_computation.29 | loop fusion | flops 94208 | bytes 32772 | tf_op jit(solution)/shard_map/jit(floor_divide)/jit(_where)/select_n | solution.py:50
  0.7 1.5 %convert_element_type.11 = f32[16384]{0:T(1024)} convert(s32[16384]{0:T(1024)} %param.4) | non-fusion elementwise | flops 16384 | bytes 131072 | tf_op jit(solution)/shard_map/convert_element_type | solution.py:106
  2.2 1.6 %subtract_convert_fusion = (f32[128,2048]{1,0:T(8,128)}, bf16[128,2048]{1,0:T(8,128)(2,1)}) fusion(s32[2048]{0:T(1024)S(1)} %get-tuple-element.14, s32[2048]{0:T(1024)S(1)} %get-tuple-element.13, s32[2048]{0:T(1024)S(1)} %get-tuple-element.15), kind=kLoop, calls=%fused_computation.2 | loop fusion | flops 3407872 | bytes 1597440 | tf_op jit(solution)/shard_map/convert_element_type | solution.py:57
  3.8 12.3 %shard_map.37 = f32[64,2048]{1,0:T(8,128)} custom-call(bf16[64,16384]{1,0:T(8,128)(2,1)} %panel_ref.1, f32[1,16384]{1,0:T(1,128)} %bitcast.65, bf16[128,2048]{1,0:T(8,128)(2,1)} %get-tuple-element.17.hy_ref, f32[128,2048]{1,0:T(8,128)} %get-tuple-element.16.hx_ref), custom_call_target="tpu_custom_call" | custom-call | flops 4328521728 | bytes 2621440 | tf_op jit(solution)/shard_map/pallas_call | solution.py:80
  16.1 1.2 %copy.12 = f32[8,8,8,256]{3,2,1,0:T(8,128)S(1)} copy(f32[8,8,8,256]{3,1,2,0:T(8,128)} %bitcast.56) | data formatting | bytes 1048576
  17.8 3.0 %collective-permute-start = (f32[64,256]{1,0:T(8,128)S(1)}, f32[64,256]{1,0:T(8,128)S(1)}, u32[]{:S(2)}, u32[]{:S(2)}) collective-permute-start(f32[64,256]{1,0:T(8,128)S(1)} %bitcast.62), channel_id=1, source_target_pairs={{0,4},{4,0},{8,12},{12,8},{16,20},{20,16},{24,28},{28,24},{1,5},{5... | collective-permute-start | bytes 196616 | tf_op jit(solution)/shard_map/ppermute | solution.py:117
  20.8 1.6 %collective-permute-start.1 = (f32[64,256]{1,0:T(8,128)S(1)}, f32[64,256]{1,0:T(8,128)S(1)}, u32[]{:S(2)}, u32[]{:S(2)}) collective-permute-start(f32[64,256]{1,0:T(8,128)S(1)} %bitcast.60), channel_id=1, source_target_pairs={{0,8},{4,12},{8,0},{12,4},{16,24},{20,28},{24,16},{28,20},{1,9},{5... | collective-permute-start | bytes 196616 | tf_op jit(solution)/shard_map/ppermute | solution.py:117
  22.4 3.0 %collective-permute-start.3 = (f32[64,256]{1,0:T(8,128)S(1)}, f32[64,256]{1,0:T(8,128)S(1)}, u32[]{:S(2)}, u32[]{:S(2)}) collective-permute-start(f32[64,256]{1,0:T(8,128)S(1)} %bitcast.59), channel_id=1, source_target_pairs={{0,16},{4,20},{8,24},{12,28},{16,0},{20,4},{24,8},{28,12},{1,17},{... | collective-permute-start | bytes 196616 | tf_op jit(solution)/shard_map/ppermute | solution.py:117
  25.4 1.3 %collective-permute-start.4 = (f32[64,256]{1,0:T(8,128)S(1)}, f32[64,256]{1,0:T(8,128)S(1)}, u32[]{:S(2)}, u32[]{:S(2)}) collective-permute-start(f32[64,256]{1,0:T(8,128)S(1)} %bitcast.61), channel_id=1, source_target_pairs={{0,20},{4,16},{8,28},{12,24},{16,4},{20,0},{24,12},{28,8},{1,21},{... | collective-permute-start | bytes 196616 | tf_op jit(solution)/shard_map/ppermute | solution.py:117
  26.8 3.7 %collective-permute-start.5 = (f32[64,256]{1,0:T(8,128)S(1)}, f32[64,256]{1,0:T(8,128)S(1)}, u32[]{:S(2)}, u32[]{:S(2)}) collective-permute-start(f32[64,256]{1,0:T(8,128)S(1)} %bitcast.64), channel_id=1, source_target_pairs={{0,24},{4,28},{8,16},{12,20},{16,8},{20,12},{24,0},{28,4},{1,25},{... | collective-permute-start | bytes 196616 | tf_op jit(solution)/shard_map/ppermute | solution.py:117
  30.5 5.1 %collective-permute-done.4 = f32[64,256]{1,0:T(8,128)S(1)} collective-permute-done((f32[64,256]{1,0:T(8,128)S(1)}, f32[64,256]{1,0:T(8,128)S(1)}, u32[]{:S(2)}, u32[]{:S(2)}) %collective-permute-start.4) | collective-permute-done | bytes 65568 | tf_op jit(solution)/shard_map/ppermute | solution.py:117
  35.6 1.9 %collective-permute-done.6 = f32[64,256]{1,0:T(8,128)S(1)} collective-permute-done((f32[64,256]{1,0:T(8,128)S(1)}, f32[64,256]{1,0:T(8,128)S(1)}, u32[]{:S(2)}, u32[]{:S(2)}) %collective-permute-start.6) | collective-permute-done | bytes 65568 | tf_op jit(solution)/shard_map/ppermute | solution.py:117
  37.5 5.8 %all_gather.3 = f32[256,256]{1,0:T(8,128)S(1)} all-gather(f32[64,256]{1,0:T(8,128)S(1)} %fusion.7), channel_id=1, replica_groups=mesh['ev'=8,'col'=4] {'col'}, dimensions={0}, use_global_device_ids=true | all-gather | bytes 327680 | tf_op jit(solution)/shard_map/all_gather | solution.py:127
  43.7 0.6 collective-permute-start.7
  44.2 1.8 %collective-permute-start.8 = (f32[64,256]{1,0:T(8,128)S(1)}, f32[64,256]{1,0:T(8,128)S(1)}, u32[]{:S(2)}, u32[]{:S(2)}) collective-permute-start(f32[64,256]{1,0:T(8,128)S(1)} %fusion.16), channel_id=1, source_target_pairs={{0,8},{4,12},{8,0},{12,4},{16,24},{20,28},{24,16},{28,20},{1,9},{5... | collective-permute-start | bytes 196616 | tf_op jit(solution)/shard_map/ppermute | solution.py:37
  46.0 1.2 %collective-permute-start.9 = (f32[64,256]{1,0:T(8,128)S(1)}, f32[64,256]{1,0:T(8,128)S(1)}, u32[]{:S(2)}, u32[]{:S(2)}) collective-permute-start(f32[64,256]{1,0:T(8,128)S(1)} %fusion.16), channel_id=1, source_target_pairs={{0,12},{4,8},{8,4},{12,0},{16,28},{20,24},{24,20},{28,16},{1,13},{... | collective-permute-start | bytes 196616 | tf_op jit(solution)/shard_map/ppermute | solution.py:37
  47.2 0.8 %collective-permute-done.7 = f32[64,256]{1,0:T(8,128)S(1)} collective-permute-done((f32[64,256]{1,0:T(8,128)S(1)}, f32[64,256]{1,0:T(8,128)S(1)}, u32[]{:S(2)}, u32[]{:S(2)}) %collective-permute-start.7) | collective-permute-done | bytes 65568 | tf_op jit(solution)/shard_map/ppermute | solution.py:37
  48.1 0.4 collective-permute-done.8
  48.5 2.7 %collective-permute-done.9 = f32[64,256]{1,0:T(8,128)S(1)} collective-permute-done((f32[64,256]{1,0:T(8,128)S(1)}, f32[64,256]{1,0:T(8,128)S(1)}, u32[]{:S(2)}, u32[]{:S(2)}) %collective-permute-start.9) | collective-permute-done | bytes 65568 | tf_op jit(solution)/shard_map/ppermute | solution.py:37
  51.2 0.6 gather_fusion
  51.9 2.1 %collective-permute-start.10 = (f32[64,256]{1,0:T(8,128)S(1)}, f32[64,256]{1,0:T(8,128)S(1)}, u32[]{:S(2)}, u32[]{:S(2)}) collective-permute-start(f32[64,256]{1,0:T(8,128)S(1)} %fusion.19), channel_id=1, source_target_pairs={{0,16},{4,20},{8,24},{12,28},{16,0},{20,4},{24,8},{28,12},{1,17},{... | collective-permute-start | bytes 196616 | tf_op jit(solution)/shard_map/ppermute | solution.py:37
  54.1 3.8 %collective-permute-done.10 = f32[64,256]{1,0:T(8,128)S(1)} collective-permute-done((f32[64,256]{1,0:T(8,128)S(1)}, f32[64,256]{1,0:T(8,128)S(1)}, u32[]{:S(2)}, u32[]{:S(2)}) %collective-permute-start.10) | collective-permute-done | bytes 65568 | tf_op jit(solution)/shard_map/ppermute | solution.py:37
  57.9 0.6 gather_fusion.1
  58.5 0.6 %fusion = f32[64,256]{1,0:T(8,128)} fusion(f32[2,64,256]{2,1,0:T(8,128)S(1)} %broadcast_select_fusion.1), kind=kLoop, calls=%fused_computation.9 | loop fusion | flops 16384 | bytes 196608 | tf_op jit(solution)/shard_map/squeeze | solution.py:43
  (30 shorter events, 1.1 us)
Async XLA Ops:
  17.8 9.0 %collective-permute-start = (f32[64,256]{1,0:T(8,128)S(1)}, f32[64,256]{1,0:T(8,128)S(1)}, u32[]{:S(2)}, u32[]{:S(2)}) collective-permute-start(f32[64,256]{1,0:T(8,128)S(1)} %bitcast.62), channel_id=1, source_target_pairs={{0,4},{4,0},{8,12},{12,8},{16,20},{20,16},{24,28},{28,24},{1,5},{5... | collective-permute-start | bytes 196616 | tf_op jit(solution)/shard_map/ppermute | solution.py:117
  20.8 9.6 %collective-permute-start.1 = (f32[64,256]{1,0:T(8,128)S(1)}, f32[64,256]{1,0:T(8,128)S(1)}, u32[]{:S(2)}, u32[]{:S(2)}) collective-permute-start(f32[64,256]{1,0:T(8,128)S(1)} %bitcast.60), channel_id=1, source_target_pairs={{0,8},{4,12},{8,0},{12,4},{16,24},{20,28},{24,16},{28,20},{1,9},{5... | collective-permute-start | bytes 196616 | tf_op jit(solution)/shard_map/ppermute | solution.py:117
  22.4 8.1 %collective-permute-start.2 = (f32[64,256]{1,0:T(8,128)S(1)}, f32[64,256]{1,0:T(8,128)S(1)}, u32[]{:S(2)}, u32[]{:S(2)}) collective-permute-start(f32[64,256]{1,0:T(8,128)S(1)} %bitcast.58), channel_id=1, source_target_pairs={{0,12},{4,8},{8,4},{12,0},{16,28},{20,24},{24,20},{28,16},{1,13},{... | collective-permute-start | bytes 196616 | tf_op jit(solution)/shard_map/ppermute | solution.py:117
  22.4 8.1 %collective-permute-start.3 = (f32[64,256]{1,0:T(8,128)S(1)}, f32[64,256]{1,0:T(8,128)S(1)}, u32[]{:S(2)}, u32[]{:S(2)}) collective-permute-start(f32[64,256]{1,0:T(8,128)S(1)} %bitcast.59), channel_id=1, source_target_pairs={{0,16},{4,20},{8,24},{12,28},{16,0},{20,4},{24,8},{28,12},{1,17},{... | collective-permute-start | bytes 196616 | tf_op jit(solution)/shard_map/ppermute | solution.py:117
  25.4 10.2 %collective-permute-start.4 = (f32[64,256]{1,0:T(8,128)S(1)}, f32[64,256]{1,0:T(8,128)S(1)}, u32[]{:S(2)}, u32[]{:S(2)}) collective-permute-start(f32[64,256]{1,0:T(8,128)S(1)} %bitcast.61), channel_id=1, source_target_pairs={{0,20},{4,16},{8,28},{12,24},{16,4},{20,0},{24,12},{28,8},{1,21},{... | collective-permute-start | bytes 196616 | tf_op jit(solution)/shard_map/ppermute | solution.py:117
  26.8 8.8 %collective-permute-start.5 = (f32[64,256]{1,0:T(8,128)S(1)}, f32[64,256]{1,0:T(8,128)S(1)}, u32[]{:S(2)}, u32[]{:S(2)}) collective-permute-start(f32[64,256]{1,0:T(8,128)S(1)} %bitcast.64), channel_id=1, source_target_pairs={{0,24},{4,28},{8,16},{12,20},{16,8},{20,12},{24,0},{28,4},{1,25},{... | collective-permute-start | bytes 196616 | tf_op jit(solution)/shard_map/ppermute | solution.py:117
  30.4 7.1 %collective-permute-start.6 = (f32[64,256]{1,0:T(8,128)S(1)}, f32[64,256]{1,0:T(8,128)S(1)}, u32[]{:S(2)}, u32[]{:S(2)}) collective-permute-start(f32[64,256]{1,0:T(8,128)S(1)} %bitcast.63), channel_id=1, source_target_pairs={{0,28},{4,24},{8,20},{12,16},{16,12},{20,8},{24,4},{28,0},{1,29},{... | collective-permute-start | bytes 196616 | tf_op jit(solution)/shard_map/ppermute | solution.py:117
  43.7 4.4 %collective-permute-start.7 = (f32[64,256]{1,0:T(8,128)S(1)}, f32[64,256]{1,0:T(8,128)S(1)}, u32[]{:S(2)}, u32[]{:S(2)}) collective-permute-start(f32[64,256]{1,0:T(8,128)S(1)} %fusion.16), channel_id=1, source_target_pairs={{0,4},{4,0},{8,12},{12,8},{16,20},{20,16},{24,28},{28,24},{1,5},{5... | collective-permute-start | bytes 196616 | tf_op jit(solution)/shard_map/ppermute | solution.py:37
  44.2 4.3 %collective-permute-start.8 = (f32[64,256]{1,0:T(8,128)S(1)}, f32[64,256]{1,0:T(8,128)S(1)}, u32[]{:S(2)}, u32[]{:S(2)}) collective-permute-start(f32[64,256]{1,0:T(8,128)S(1)} %fusion.16), channel_id=1, source_target_pairs={{0,8},{4,12},{8,0},{12,4},{16,24},{20,28},{24,16},{28,20},{1,9},{5... | collective-permute-start | bytes 196616 | tf_op jit(solution)/shard_map/ppermute | solution.py:37
  46.0 5.2 %collective-permute-start.9 = (f32[64,256]{1,0:T(8,128)S(1)}, f32[64,256]{1,0:T(8,128)S(1)}, u32[]{:S(2)}, u32[]{:S(2)}) collective-permute-start(f32[64,256]{1,0:T(8,128)S(1)} %fusion.16), channel_id=1, source_target_pairs={{0,12},{4,8},{8,4},{12,0},{16,28},{20,24},{24,20},{28,16},{1,13},{... | collective-permute-start | bytes 196616 | tf_op jit(solution)/shard_map/ppermute | solution.py:37
  51.9 5.9 %collective-permute-start.10 = (f32[64,256]{1,0:T(8,128)S(1)}, f32[64,256]{1,0:T(8,128)S(1)}, u32[]{:S(2)}, u32[]{:S(2)}) collective-permute-start(f32[64,256]{1,0:T(8,128)S(1)} %fusion.19), channel_id=1, source_target_pairs={{0,16},{4,20},{8,24},{12,28},{16,0},{20,4},{24,8},{28,12},{1,17},{... | collective-permute-start | bytes 196616 | tf_op jit(solution)/shard_map/ppermute | solution.py:37

commit v10 on v7

--- a/solution.py
+++ b/solution.py
@@ -42,26 +42,6 @@
     return ordered[0]
 
 
-def split3(value):
-    hi = lax.reduce_precision(value, exponent_bits=8, mantissa_bits=7)
-    rest = value - hi
-    mid = lax.reduce_precision(rest, exponent_bits=8, mantissa_bits=7)
-    low = rest - mid
-    return tuple(piece.astype(jnp.bfloat16) for piece in (hi, mid, low))
-
-
-def selection(offsets, my_index, groups, inner):
-    per_row = inner // STRIDE
-    off = offsets.reshape(groups, OUTER, per_row)
-    rows = jnp.arange(per_row, dtype=jnp.int32)[None, None, :] * STRIDE + off
-    rows = rows.transpose(1, 0, 2)
-    lanes = jnp.arange(inner, dtype=jnp.int32)
-    parity = lax.population_count(rows[:, None, :, :] & lanes[None, :, None, None]) & 1
-    group_parity = lax.population_count(jnp.arange(groups, dtype=jnp.int32) & my_index) & 1
-    parity = parity ^ group_parity[None, None, :, None]
-    return (1 - 2 * parity).astype(jnp.bfloat16).reshape(OUTER, inner, groups * per_row)
-
-
 def per_device(panel, signs, offsets):
     columns, length = panel.shape
     groups = lax.axis_size("ev")
@@ -71,24 +51,21 @@
     per_row = inner // STRIDE
     high = lax.Precision.HIGHEST
 
-    signed = panel * signs.astype(jnp.bfloat16)[None, :]
-    blocks = signed.reshape(columns, OUTER, inner)
-    first = jnp.einsum(
-        "xa,cab->xcb",
-        hadamard(OUTER).astype(jnp.bfloat16),
-        blocks,
+    signed = jnp.where(signs[None, :] > 0, panel, -panel)
+    events = signed.reshape(columns, OUTER, inner).transpose(2, 1, 0).reshape(inner, OUTER * columns)
+    mixed = jnp.dot(
+        hadamard(inner).astype(jnp.bfloat16), events, preferred_element_type=jnp.float32
+    ).reshape(inner, OUTER, columns)
+    full = jnp.einsum(
+        "xa,yac->yxc", hadamard(OUTER), mixed, precision=lax.Precision.HIGH,
         preferred_element_type=jnp.float32,
-    )
-    pick = selection(offsets, my_index, groups, inner)
-    sampled = jnp.einsum(
-        "xcb,xbj->xcj",
-        first,
-        pick.astype(jnp.float32),
-        precision=lax.Precision.HIGH,
-        preferred_element_type=jnp.float32,
-    )
-    chunks = sampled.reshape(OUTER, columns, groups, per_row).transpose(2, 1, 0, 3)
-    chunks = chunks.reshape(groups, columns, OUTER * per_row)
+    ).reshape(inner * OUTER, columns)
+    rows = STRIDE * jnp.arange(offsets.shape[0], dtype=jnp.int32) + offsets
+    spot = rows % inner * OUTER + rows % length // inner
+    flip = (1 - 2 * (lax.population_count(rows // length & my_index) & 1)).astype(jnp.float32)
+    sampled = (jnp.take(full, spot, axis=0) * flip[:, None]).T
+
+    chunks = sampled.reshape(columns, groups, OUTER * per_row).transpose(1, 0, 2)
     own = lax.dynamic_index_in_dim(chunks, my_index, axis=0, keepdims=False)
     arrived = []
     for distance in range(1, groups):

time: 53.7 us -> 65.5 us (1.22)
  local copies, waits for them, and re-layouts: 4.04 us -> 18.2 us
  matrix products: 9.4 us -> 4.66 us
  other arithmetic: 3.7 us -> 5.87 us
    gather x0 -> x1, local copies, waits for them, and re-layouts: none -> 8.84 us  [per_device(): sampled = (jnp.take(full, spot, axis=0) * flip[:, None]).T]
    reshape x2 -> x1, local copies, waits for them, and re-layouts: 0.54 us -> 6.96 us  [per_device(): full = jnp.einsum('xa,yac->yxc', hadamard(OUTER), mixed, precision=lax.Pr...]
    dot_general x2, matrix products: 9.04 us -> 4.3 us  [the longest x1 3.54 us: per_device(): jnp.einsum('xa,yac->yxc', hadamard(OUTER), mixed, precision=lax.Precision...]
    dynamic_slice x9 -> x0, local copies, waits for them, and re-layouts: 1.36 us -> none  [the longest x2 0.82 us: per_device(): own = lax.dynamic_index_in_dim(chunks, my_index, axis=0, keepdims=False)]
    gt x0 -> x1, other arithmetic: none -> 0.85 us  [per_device(): signed = jnp.where(signs[None, :] > 0, panel, -panel)]
    and x1, other arithmetic: 0.01 us -> 0.72 us  [per_device(): sampled = (jnp.take(full, spot, axis=0) * flip[:, None]).T]
    another operation x0 -> x9, local copies, waits for them, and re-layouts: none -> 0.71 us
    mul x1, other arithmetic: 0.01 us -> 0.71 us  [per_device(): sampled = (jnp.take(full, spot, axis=0) * flip[:, None]).T]
where the time goes in v10:
time: 65.5 us; the launch traced here: 65.1 us
  starting transfers between devices  19.1 us (29%)
  local copies, waits for them, and re-layouts  18.2 us (28%)
  waiting for transfers between devices  11.2 us (17%)
  other arithmetic  5.87 us (9%)
  blocking collectives  5.79 us (9%)
  matrix products  4.66 us (7%)
    ppermute x7, starting transfers between devices, per_device(): arrived.append(lax.ppermute(block, 'ev', pairs))  12.8 us
    gather x1, local copies, waits for them, and re-layouts, per_device(): sampled = (jnp.take(full, spot, axis=0) * flip[:, None]).T  8.84 us
    reshape x1, local copies, waits for them, and re-layouts, per_device(): full = jnp.einsum('xa,yac->yxc', hadamard(OUTER), mixed, precision=lax.Pr...  6.96 us
    ppermute x4, waiting for transfers between devices, group_sum(): values.append(lax.ppermute(value, 'ev', pairs))  6.47 us
    ppermute x4, starting transfers between devices, group_sum(): values.append(lax.ppermute(value, 'ev', pairs))  6.29 us
    all_gather x1, blocking collectives, per_device(): lax.all_gather(sketch, 'col', axis=0, tiled=True)  5.79 us
    ppermute x7, waiting for transfers between devices, per_device(): arrived.append(lax.ppermute(block, 'ev', pairs))  4.72 us
    dot_general x1, matrix products, per_device(): jnp.einsum('xa,yac->yxc', hadamard(OUTER), mixed, precision=lax.Precision...  3.54 us
  transfers between devices with their start and end apart: 11, of which 7 were waited for; matrix products, arithmetic and copies ran while one was open for 1% of the time, Pallas kernels for 0%

profile of v10, /device:TPU:0, one launch (start us, length us, event | category | flops | bytes accessed | tf_op | source)
XLA Modules:
  0.0 65.1 jit_solution(18148439418171948133)
XLA Ops:
  0.0 0.7 %compare_and_fusion = (pred[2048]{0:T(1024)(128)(4,1)S(1)}, s32[2048]{0:T(1024)S(1)}) fusion(s32[2048]{0:T(1024)} %param.5), kind=kLoop, calls=%fused_computation.62 | loop fusion | flops 90112 | bytes 18432 | tf_op jit(solution)/shard_map/jit(_take)/and | solution.py:66
  0.7 0.7 %fusion.28 = f32[2048]{0:T(1024)S(1)} fusion(s32[2048]{0:T(1024)} %param.5, s32[]{:T(128)S(6)} %axis_index.11), kind=kLoop, calls=%fused_computation.56 | loop fusion | flops 47104 | bytes 16388 | tf_op jit(solution)/shard_map/convert_element_type | solution.py:65
  1.5 0.9 %broadcast_compare_fusion = pred[16384]{0:T(1024)(128)(4,1)S(1)} fusion(s32[16384]{0:T(1024)} %param.4), kind=kLoop, calls=%fused_computation.34 | loop fusion | flops 16384 | bytes 81920 | tf_op jit(solution)/shard_map/gt | solution.py:54
  2.3 1.9 %fusion = bf16[8,8,128,128]{3,1,2,0:T(8,128)(2,1)S(1)} fusion(bf16[64,16384]{1,0:T(8,128)(2,1)} %param.3, pred[16384]{0:T(1024)(128)(4,1)S(1)} %broadcast_compare_fusion), kind=kLoop, calls=%fused_computation.5 | loop fusion | flops 2097152 | bytes 4210688
  4.8 0.8 %fusion.1 = f32[128,128,64]{1,0,2:T(8,128)S(1)} fusion(bf16[64,128,128]{2,1,0:T(8,128)(2,1)S(1)} %bitcast.63), kind=kOutput, calls=%fused_computation.6 | convolution fusion | flops 269025280 | bytes 6291456 | tf_op jit(solution)/shard_map/dot_general | solution.py:56
  5.6 3.5 %convolution_bitcast_fusion = f32[128,128,64]{1,0,2:T(8,128)} fusion(f32[128,128,64]{1,0,2:T(8,128)S(1)} %fusion.1), kind=kOutput, calls=%fused_computation.4 | convolution fusion | flops 805879808 | bytes 8388608 | tf_op jit(solution)/shard_map/xa,yac->yxc/dot_general | solution.py:59
  9.1 7.0 %copy.21 = f32[128,128,64]{2,1,0:T(8,128)} copy(f32[128,128,64]{1,0,2:T(8,128)} %convolution_bitcast_fusion) | data formatting | bytes 8388608 | tf_op jit(solution)/shard_map/reshape | solution.py:62
  16.1 8.8 %gather_fusion = f32[2048,64]{1,0:T(8,128)S(1)} fusion(f32[16384,64]{1,0:T(8,128)} %bitcast.62, s32[2048]{0:T(1024)S(1)} %broadcast_clamp_fusion), kind=kCustom, calls=%fused_computation | custom fusion | bytes 1056768 | tf_op jit(solution)/shard_map/jit(_take)/gather | solution.py:66
  25.0 0.7 %select_multiply_fusion = f32[2048,64]{1,0:T(8,128)S(1)} fusion(f32[2048,64]{1,0:T(8,128)S(1)} %gather_fusion, f32[2048]{0:T(1024)S(1)} %fusion.28, pred[2048]{0:T(1024)(128)(4,1)S(1)} %get-tuple-element.5), kind=kLoop, calls=%fused_computation.8 | loop fusion | flops 262144 | bytes 1058816 | tf_op jit(solution)/shard_map/mul | solution.py:66
  25.9 6.1 %collective-permute-start.6 = (f32[64,256]{1,0:T(8,128)S(1)}, f32[64,256]{1,0:T(8,128)S(1)}, u32[]{:S(2)}, u32[]{:S(2)}) collective-permute-start(f32[64,256]{1,0:T(8,128)S(1)} %bitcast.70), channel_id=1, source_target_pairs={{0,28},{4,24},{8,20},{12,16},{16,12},{20,8},{24,4},{28,0},{1,29},{... | collective-permute-start | bytes 196616 | tf_op jit(solution)/shard_map/ppermute | solution.py:75
  32.4 0.8 %collective-permute-start.4 = (f32[64,256]{1,0:T(8,128)S(1)}, f32[64,256]{1,0:T(8,128)S(1)}, u32[]{:S(2)}, u32[]{:S(2)}) collective-permute-start(f32[64,256]{1,0:T(8,128)S(1)} %bitcast.66), channel_id=1, source_target_pairs={{0,20},{4,16},{8,28},{12,24},{16,4},{20,0},{24,12},{28,8},{1,21},{... | collective-permute-start | bytes 196616 | tf_op jit(solution)/shard_map/ppermute | solution.py:75
  33.3 2.0 %collective-permute-start.3 = (f32[64,256]{1,0:T(8,128)S(1)}, f32[64,256]{1,0:T(8,128)S(1)}, u32[]{:S(2)}, u32[]{:S(2)}) collective-permute-start(f32[64,256]{1,0:T(8,128)S(1)} %bitcast.67), channel_id=1, source_target_pairs={{0,16},{4,20},{8,24},{12,28},{16,0},{20,4},{24,8},{28,12},{1,17},{... | collective-permute-start | bytes 196616 | tf_op jit(solution)/shard_map/ppermute | solution.py:75
  35.4 2.4 %collective-permute-start.2 = (f32[64,256]{1,0:T(8,128)S(1)}, f32[64,256]{1,0:T(8,128)S(1)}, u32[]{:S(2)}, u32[]{:S(2)}) collective-permute-start(f32[64,256]{1,0:T(8,128)S(1)} %bitcast.69), channel_id=1, source_target_pairs={{0,12},{4,8},{8,4},{12,0},{16,28},{20,24},{24,20},{28,16},{1,13},{... | collective-permute-start | bytes 196616 | tf_op jit(solution)/shard_map/ppermute | solution.py:75
  38.2 0.8 %collective-permute-start.1 = (f32[64,256]{1,0:T(8,128)S(1)}, f32[64,256]{1,0:T(8,128)S(1)}, u32[]{:S(2)}, u32[]{:S(2)}) collective-permute-start(f32[64,256]{1,0:T(8,128)S(1)} %bitcast.72), channel_id=1, source_target_pairs={{0,8},{4,12},{8,0},{12,4},{16,24},{20,28},{24,16},{28,20},{1,9},{5... | collective-permute-start | bytes 196616 | tf_op jit(solution)/shard_map/ppermute | solution.py:75
  39.4 1.8 %collective-permute-done.4 = f32[64,256]{1,0:T(8,128)S(1)} collective-permute-done((f32[64,256]{1,0:T(8,128)S(1)}, f32[64,256]{1,0:T(8,128)S(1)}, u32[]{:S(2)}, u32[]{:S(2)}) %collective-permute-start.4) | collective-permute-done | bytes 65568 | tf_op jit(solution)/shard_map/ppermute | solution.py:75
  41.2 2.0 %collective-permute-done.3 = f32[64,256]{1,0:T(8,128)S(1)} collective-permute-done((f32[64,256]{1,0:T(8,128)S(1)}, f32[64,256]{1,0:T(8,128)S(1)}, u32[]{:S(2)}, u32[]{:S(2)}) %collective-permute-start.3) | collective-permute-done | bytes 65568 | tf_op jit(solution)/shard_map/ppermute | solution.py:75
  43.2 0.9 %collective-permute-done.1 = f32[64,256]{1,0:T(8,128)S(1)} collective-permute-done((f32[64,256]{1,0:T(8,128)S(1)}, f32[64,256]{1,0:T(8,128)S(1)}, u32[]{:S(2)}, u32[]{:S(2)}) %collective-permute-start.1) | collective-permute-done | bytes 65568 | tf_op jit(solution)/shard_map/ppermute | solution.py:75
  44.1 5.8 %all_gather.3 = f32[256,256]{1,0:T(8,128)S(1)} all-gather(f32[64,256]{1,0:T(8,128)S(1)} %fusion.14), channel_id=1, replica_groups=mesh['ev'=8,'col'=4] {'col'}, dimensions={0}, use_global_device_ids=true | all-gather | bytes 327680 | tf_op jit(solution)/shard_map/all_gather | solution.py:85
  50.8 1.8 %collective-permute-start.8 = (f32[64,256]{1,0:T(8,128)S(1)}, f32[64,256]{1,0:T(8,128)S(1)}, u32[]{:S(2)}, u32[]{:S(2)}) collective-permute-start(f32[64,256]{1,0:T(8,128)S(1)} %fusion.49), channel_id=1, source_target_pairs={{0,8},{4,12},{8,0},{12,4},{16,24},{20,28},{24,16},{28,20},{1,9},{5... | collective-permute-start | bytes 196616 | tf_op jit(solution)/shard_map/ppermute | solution.py:36
  52.6 1.3 %collective-permute-start.7 = (f32[64,256]{1,0:T(8,128)S(1)}, f32[64,256]{1,0:T(8,128)S(1)}, u32[]{:S(2)}, u32[]{:S(2)}) collective-permute-start(f32[64,256]{1,0:T(8,128)S(1)} %fusion.49), channel_id=1, source_target_pairs={{0,4},{4,0},{8,12},{12,8},{16,20},{20,16},{24,28},{28,24},{1,5},{5... | collective-permute-start | bytes 196616 | tf_op jit(solution)/shard_map/ppermute | solution.py:36
  53.9 2.3 %collective-permute-done.9 = f32[64,256]{1,0:T(8,128)S(1)} collective-permute-done((f32[64,256]{1,0:T(8,128)S(1)}, f32[64,256]{1,0:T(8,128)S(1)}, u32[]{:S(2)}, u32[]{:S(2)}) %collective-permute-start.9) | collective-permute-done | bytes 65568 | tf_op jit(solution)/shard_map/ppermute | solution.py:36
  56.3 0.7 %collective-permute-done.7 = f32[64,256]{1,0:T(8,128)S(1)} collective-permute-done((f32[64,256]{1,0:T(8,128)S(1)}, f32[64,256]{1,0:T(8,128)S(1)}, u32[]{:S(2)}, u32[]{:S(2)}) %collective-permute-start.7) | collective-permute-done | bytes 65568 | tf_op jit(solution)/shard_map/ppermute | solution.py:36
  57.7 2.7 %collective-permute-start.10 = (f32[64,256]{1,0:T(8,128)S(1)}, f32[64,256]{1,0:T(8,128)S(1)}, u32[]{:S(2)}, u32[]{:S(2)}) collective-permute-start(f32[64,256]{1,0:T(8,128)S(1)} %fusion.53), channel_id=1, source_target_pairs={{0,16},{4,20},{8,24},{12,28},{16,0},{20,4},{24,8},{28,12},{1,17},{... | collective-permute-start | bytes 196616 | tf_op jit(solution)/shard_map/ppermute | solution.py:36
  60.5 3.3 %collective-permute-done.10 = f32[64,256]{1,0:T(8,128)S(1)} collective-permute-done((f32[64,256]{1,0:T(8,128)S(1)}, f32[64,256]{1,0:T(8,128)S(1)}, u32[]{:S(2)}, u32[]{:S(2)}) %collective-permute-start.10) | collective-permute-done | bytes 65568 | tf_op jit(solution)/shard_map/ppermute | solution.py:36
  (37 shorter events, 5.0 us)
Async XLA Ops:
  25.9 12.3 %collective-permute-start.6 = (f32[64,256]{1,0:T(8,128)S(1)}, f32[64,256]{1,0:T(8,128)S(1)}, u32[]{:S(2)}, u32[]{:S(2)}) collective-permute-start(f32[64,256]{1,0:T(8,128)S(1)} %bitcast.70), channel_id=1, source_target_pairs={{0,28},{4,24},{8,20},{12,16},{16,12},{20,8},{24,4},{28,0},{1,29},{... | collective-permute-start | bytes 196616 | tf_op jit(solution)/shard_map/ppermute | solution.py:75
  32.0 7.0 %collective-permute-start.5 = (f32[64,256]{1,0:T(8,128)S(1)}, f32[64,256]{1,0:T(8,128)S(1)}, u32[]{:S(2)}, u32[]{:S(2)}) collective-permute-start(f32[64,256]{1,0:T(8,128)S(1)} %bitcast.68), channel_id=1, source_target_pairs={{0,24},{4,28},{8,16},{12,20},{16,8},{20,12},{24,0},{28,4},{1,25},{... | collective-permute-start | bytes 196616 | tf_op jit(solution)/shard_map/ppermute | solution.py:75
  32.4 8.8 %collective-permute-start.4 = (f32[64,256]{1,0:T(8,128)S(1)}, f32[64,256]{1,0:T(8,128)S(1)}, u32[]{:S(2)}, u32[]{:S(2)}) collective-permute-start(f32[64,256]{1,0:T(8,128)S(1)} %bitcast.66), channel_id=1, source_target_pairs={{0,20},{4,16},{8,28},{12,24},{16,4},{20,0},{24,12},{28,8},{1,21},{... | collective-permute-start | bytes 196616 | tf_op jit(solution)/shard_map/ppermute | solution.py:75
  33.3 9.9 %collective-permute-start.3 = (f32[64,256]{1,0:T(8,128)S(1)}, f32[64,256]{1,0:T(8,128)S(1)}, u32[]{:S(2)}, u32[]{:S(2)}) collective-permute-start(f32[64,256]{1,0:T(8,128)S(1)} %bitcast.67), channel_id=1, source_target_pairs={{0,16},{4,20},{8,24},{12,28},{16,0},{20,4},{24,8},{28,12},{1,17},{... | collective-permute-start | bytes 196616 | tf_op jit(solution)/shard_map/ppermute | solution.py:75
  35.4 7.8 %collective-permute-start.2 = (f32[64,256]{1,0:T(8,128)S(1)}, f32[64,256]{1,0:T(8,128)S(1)}, u32[]{:S(2)}, u32[]{:S(2)}) collective-permute-start(f32[64,256]{1,0:T(8,128)S(1)} %bitcast.69), channel_id=1, source_target_pairs={{0,12},{4,8},{8,4},{12,0},{16,28},{20,24},{24,20},{28,16},{1,13},{... | collective-permute-start | bytes 196616 | tf_op jit(solution)/shard_map/ppermute | solution.py:75
  38.2 5.9 %collective-permute-start.1 = (f32[64,256]{1,0:T(8,128)S(1)}, f32[64,256]{1,0:T(8,128)S(1)}, u32[]{:S(2)}, u32[]{:S(2)}) collective-permute-start(f32[64,256]{1,0:T(8,128)S(1)} %bitcast.72), channel_id=1, source_target_pairs={{0,8},{4,12},{8,0},{12,4},{16,24},{20,28},{24,16},{28,20},{1,9},{5... | collective-permute-start | bytes 196616 | tf_op jit(solution)/shard_map/ppermute | solution.py:75
  39.0 5.1 %collective-permute-start = (f32[64,256]{1,0:T(8,128)S(1)}, f32[64,256]{1,0:T(8,128)S(1)}, u32[]{:S(2)}, u32[]{:S(2)}) collective-permute-start(f32[64,256]{1,0:T(8,128)S(1)} %bitcast.71), channel_id=1, source_target_pairs={{0,4},{4,0},{8,12},{12,8},{16,20},{20,16},{24,28},{28,24},{1,5},{5... | collective-permute-start | bytes 196616 | tf_op jit(solution)/shard_map/ppermute | solution.py:75
  50.3 5.9 %collective-permute-start.9 = (f32[64,256]{1,0:T(8,128)S(1)}, f32[64,256]{1,0:T(8,128)S(1)}, u32[]{:S(2)}, u32[]{:S(2)}) collective-permute-start(f32[64,256]{1,0:T(8,128)S(1)} %fusion.49), channel_id=1, source_target_pairs={{0,12},{4,8},{8,4},{12,0},{16,28},{20,24},{24,20},{28,16},{1,13},{... | collective-permute-start | bytes 196616 | tf_op jit(solution)/shard_map/ppermute | solution.py:36
  50.8 5.5 %collective-permute-start.8 = (f32[64,256]{1,0:T(8,128)S(1)}, f32[64,256]{1,0:T(8,128)S(1)}, u32[]{:S(2)}, u32[]{:S(2)}) collective-permute-start(f32[64,256]{1,0:T(8,128)S(1)} %fusion.49), channel_id=1, source_target_pairs={{0,8},{4,12},{8,0},{12,4},{16,24},{20,28},{24,16},{28,20},{1,9},{5... | collective-permute-start | bytes 196616 | tf_op jit(solution)/shard_map/ppermute | solution.py:36
  52.6 4.4 %collective-permute-start.7 = (f32[64,256]{1,0:T(8,128)S(1)}, f32[64,256]{1,0:T(8,128)S(1)}, u32[]{:S(2)}, u32[]{:S(2)}) collective-permute-start(f32[64,256]{1,0:T(8,128)S(1)} %fusion.49), channel_id=1, source_target_pairs={{0,4},{4,0},{8,12},{12,8},{16,20},{20,16},{24,28},{28,24},{1,5},{5... | collective-permute-start | bytes 196616 | tf_op jit(solution)/shard_map/ppermute | solution.py:36
  57.7 6.1 %collective-permute-start.10 = (f32[64,256]{1,0:T(8,128)S(1)}, f32[64,256]{1,0:T(8,128)S(1)}, u32[]{:S(2)}, u32[]{:S(2)}) collective-permute-start(f32[64,256]{1,0:T(8,128)S(1)} %fusion.53), channel_id=1, source_target_pairs={{0,16},{4,20},{8,24},{12,28},{16,0},{20,4},{24,8},{28,12},{1,17},{... | collective-permute-start | bytes 196616 | tf_op jit(solution)/shard_map/ppermute | solution.py:36

commit v11 on v7

--- a/solution.py
+++ b/solution.py
@@ -26,7 +26,6 @@
 
 def group_sum(value, bits):
     groups = lax.axis_size("ev")
-    my_index = lax.axis_index("ev")
     masks = [0]
     for bit in bits:
         masks = masks + [mask | (1 << bit) for mask in masks]
@@ -34,12 +33,9 @@
     for mask in masks[1:]:
         pairs = [(source, source ^ mask) for source in range(groups)]
         values.append(lax.ppermute(value, "ev", pairs))
-    mine = sum(((my_index >> bit) & 1) << place for place, bit in enumerate(bits))
-    order = jnp.arange(len(masks), dtype=jnp.int32) ^ mine
-    ordered = jnp.take(jnp.stack(values), order, axis=0)
-    while ordered.shape[0] > 1:
-        ordered = ordered[0::2] + ordered[1::2]
-    return ordered[0]
+    while len(values) > 1:
+        values = [values[i] + values[i + 1] for i in range(0, len(values), 2)]
+    return values[0]
 
 
 def split3(value):

time: 53.7 us -> 53.3 us (level)
  local copies, waits for them, and re-layouts: 4.04 us -> 2.91 us
  waiting for transfers between devices: 11.2 us -> 12.2 us
    gather x2 -> x0, local copies, waits for them, and re-layouts: 1.12 us -> none  [group_sum(): ordered = jnp.take(jnp.stack(values), order, axis=0)]
    ppermute x4, waiting for transfers between devices: 6.47 us -> 7.52 us  [group_sum(): values.append(lax.ppermute(value, 'ev', pairs))]
    squeeze x2 -> x0, other arithmetic: 0.65 us -> none  [group_sum(): return ordered[0]]
    add x2, other arithmetic: 0.03 us -> 0.66 us  [group_sum(): values = [values[i] + values[i + 1] for i in range(0, len(values), 2)]]
where the time goes in v11:
time: 53.3 us; the launch traced here: 53.1 us
  starting transfers between devices  19.2 us (36%)
  waiting for transfers between devices  12.2 us (23%)
  matrix products  9.4 us (18%)
  blocking collectives  5.79 us (11%)
  other arithmetic  3.44 us (6%)
  local copies, waits for them, and re-layouts  2.91 us (5%)
    ppermute x7, starting transfers between devices, per_device(): arrived.append(lax.ppermute(block, 'ev', pairs))  12.9 us
    ppermute x4, waiting for transfers between devices, group_sum(): values.append(lax.ppermute(value, 'ev', pairs))  7.52 us
    dot_general x1, matrix products, per_device(): jnp.einsum('xcb,xbj->xcj', first, pick.astype(jnp.float32), precision=lax...  6.35 us
    ppermute x4, starting transfers between devices, group_sum(): values.append(lax.ppermute(value, 'ev', pairs))  6.31 us
    all_gather x1, blocking collectives, per_device(): lax.all_gather(sketch, 'col', axis=0, tiled=True)  5.79 us
    ppermute x7, waiting for transfers between devices, per_device(): arrived.append(lax.ppermute(block, 'ev', pairs))  4.64 us
    dot_general x1, matrix products, per_device(): jnp.einsum('xa,cab->xcb', hadamard(OUTER).astype(jnp.bfloat16), blocks, p...  2.69 us
    unnamed x1, other arithmetic  1.85 us
  transfers between devices with their start and end apart: 11, of which 7 were waited for; matrix products, arithmetic and copies ran while one was open for 1% of the time, Pallas kernels for 0%

profile of v11, /device:TPU:0, one launch (start us, length us, event | category | flops | bytes accessed | tf_op | source)
XLA Modules:
  0.0 53.1 jit_solution(5330982853184423284)
XLA Ops:
  0.0 0.8 %convert_element_type.16 = bf16[16384]{0:T(1024)(128)(2,1)S(1)} convert(s32[16384]{0:T(1024)} %param.4) | non-fusion elementwise | flops 16384 | bytes 98304 | tf_op jit(solution)/shard_map/convert_element_type | solution.py:70
  0.9 1.9 %multiply_bitcast_fusion = bf16[8,8,128,128]{3,1,2,0:T(8,128)(2,1)S(1)} fusion(bf16[64,16384]{1,0:T(8,128)(2,1)} %param.3, bf16[16384]{0:T(1024)(128)(2,1)S(1)} %convert_element_type.16), kind=kLoop, calls=%fused_computation.2 | loop fusion | flops 1048576 | bytes 4227072
  2.7 0.6 %copy.23 = bf16[8,8,128,128]{3,2,1,0:T(8,128)(2,1)S(1)} copy(bf16[8,8,128,128]{3,1,2,0:T(8,128)(2,1)S(1)} %multiply_bitcast_fusion) | data formatting | bytes 4194304
  3.3 2.7 %fusion.19 = f32[128,64,128]{2,0,1:T(8,128)} fusion(bf16[64,128,128]{2,1,0:T(8,128)(2,1)S(1)} %bitcast.39), kind=kOutput, calls=%fused_computation.27 | convolution fusion | flops 269025280 | bytes 6291456 | tf_op jit(solution)/shard_map/xa,cab->xcb/dot_general | solution.py:72
  7.0 6.3 %fusion = f32[128,64,16]{1,2,0:T(8,128)S(1)} fusion(f32[128,64,128]{2,0,1:T(8,128)} %fusion.19, s32[16]{0:T(128)S(1)} %xor.35, s32[128,16]{1,0:T(8,128)S(1)} %copy.12), kind=kOutput, calls=%fused_computation | convolution fusion | flops 102498304 | bytes 4726848 | tf_op jit(solution)/shard_map/xcb,xbj->xcj/dot_general | solution.py:79
  13.4 0.7 %constant_dynamic-slice_fusion.7 = (f32[1,64,256]{1,0,2:T(1,128)S(1)}, f32[1,64,256]{1,0,2:T(1,128)S(1)}, f32[1,64,256]{1,0,2:T(1,128)S(1)}, f32[1,64,256]{1,0,2...) fusion(f32[8,64,256]{1,0,2:T(8,128)S(1)} %bitcast.40, ...), kind=kLoop, calls=%fused_computation.42 | loop fusion | bytes 1048608 | tf_op jit(solution)/shard_map/jit(dynamic_index_in_dim)/dynamic_slice | solution.py:88
  14.3 6.1 %collective-permute-start.6 = (f32[64,256]{1,0:T(8,128)S(1)}, f32[64,256]{1,0:T(8,128)S(1)}, u32[]{:S(2)}, u32[]{:S(2)}) collective-permute-start(f32[64,256]{1,0:T(8,128)S(1)} %bitcast.48), channel_id=1, source_target_pairs={{0,28},{4,24},{8,20},{12,16},{16,12},{20,8},{24,4},{28,0},{1,29},{... | collective-permute-start | bytes 196616 | tf_op jit(solution)/shard_map/ppermute | solution.py:94
  20.8 0.8 %collective-permute-start.4 = (f32[64,256]{1,0:T(8,128)S(1)}, f32[64,256]{1,0:T(8,128)S(1)}, u32[]{:S(2)}, u32[]{:S(2)}) collective-permute-start(f32[64,256]{1,0:T(8,128)S(1)} %bitcast.42), channel_id=1, source_target_pairs={{0,20},{4,16},{8,28},{12,24},{16,4},{20,0},{24,12},{28,8},{1,21},{... | collective-permute-start | bytes 196616 | tf_op jit(solution)/shard_map/ppermute | solution.py:94
  21.7 2.0 %collective-permute-start.3 = (f32[64,256]{1,0:T(8,128)S(1)}, f32[64,256]{1,0:T(8,128)S(1)}, u32[]{:S(2)}, u32[]{:S(2)}) collective-permute-start(f32[64,256]{1,0:T(8,128)S(1)} %bitcast.43), channel_id=1, source_target_pairs={{0,16},{4,20},{8,24},{12,28},{16,0},{20,4},{24,8},{28,12},{1,17},{... | collective-permute-start | bytes 196616 | tf_op jit(solution)/shard_map/ppermute | solution.py:94
  23.9 2.4 %collective-permute-start.2 = (f32[64,256]{1,0:T(8,128)S(1)}, f32[64,256]{1,0:T(8,128)S(1)}, u32[]{:S(2)}, u32[]{:S(2)}) collective-permute-start(f32[64,256]{1,0:T(8,128)S(1)} %bitcast.44), channel_id=1, source_target_pairs={{0,12},{4,8},{8,4},{12,0},{16,28},{20,24},{24,20},{28,16},{1,13},{... | collective-permute-start | bytes 196616 | tf_op jit(solution)/shard_map/ppermute | solution.py:94
  26.5 0.8 %collective-permute-start.1 = (f32[64,256]{1,0:T(8,128)S(1)}, f32[64,256]{1,0:T(8,128)S(1)}, u32[]{:S(2)}, u32[]{:S(2)}) collective-permute-start(f32[64,256]{1,0:T(8,128)S(1)} %bitcast.47), channel_id=1, source_target_pairs={{0,8},{4,12},{8,0},{12,4},{16,24},{20,28},{24,16},{28,20},{1,9},{5... | collective-permute-start | bytes 196616 | tf_op jit(solution)/shard_map/ppermute | solution.py:94
  27.7 1.9 %collective-permute-done.4 = f32[64,256]{1,0:T(8,128)S(1)} collective-permute-done((f32[64,256]{1,0:T(8,128)S(1)}, f32[64,256]{1,0:T(8,128)S(1)}, u32[]{:S(2)}, u32[]{:S(2)}) %collective-permute-start.4) | collective-permute-done | bytes 65568 | tf_op jit(solution)/shard_map/ppermute | solution.py:94
  29.6 2.0 %collective-permute-done.3 = f32[64,256]{1,0:T(8,128)S(1)} collective-permute-done((f32[64,256]{1,0:T(8,128)S(1)}, f32[64,256]{1,0:T(8,128)S(1)}, u32[]{:S(2)}, u32[]{:S(2)}) %collective-permute-start.3) | collective-permute-done | bytes 65568 | tf_op jit(solution)/shard_map/ppermute | solution.py:94
  31.6 0.7 %collective-permute-done.1 = f32[64,256]{1,0:T(8,128)S(1)} collective-permute-done((f32[64,256]{1,0:T(8,128)S(1)}, f32[64,256]{1,0:T(8,128)S(1)}, u32[]{:S(2)}, u32[]{:S(2)}) %collective-permute-start.1) | collective-permute-done | bytes 65568 | tf_op jit(solution)/shard_map/ppermute | solution.py:94
  32.4 5.8 %all_gather.3 = f32[256,256]{1,0:T(8,128)S(1)} all-gather(f32[64,256]{1,0:T(8,128)S(1)} %fusion.17), channel_id=1, replica_groups=mesh['ev'=8,'col'=4] {'col'}, dimensions={0}, use_global_device_ids=true | all-gather | bytes 327680 | tf_op jit(solution)/shard_map/all_gather | solution.py:104
  38.6 1.2 %collective-permute-start.8 = (f32[64,256]{1,0:T(8,128)S(1)}, f32[64,256]{1,0:T(8,128)S(1)}, u32[]{:S(2)}, u32[]{:S(2)}) collective-permute-start(f32[64,256]{1,0:T(8,128)S(1)} %fusion.37), channel_id=1, source_target_pairs={{0,8},{4,12},{8,0},{12,4},{16,24},{20,28},{24,16},{28,20},{1,9},{5... | collective-permute-start | bytes 196616 | tf_op jit(solution)/shard_map/ppermute | solution.py:35
  39.8 1.1 %collective-permute-start.9 = (f32[64,256]{1,0:T(8,128)S(1)}, f32[64,256]{1,0:T(8,128)S(1)}, u32[]{:S(2)}, u32[]{:S(2)}) collective-permute-start(f32[64,256]{1,0:T(8,128)S(1)} %fusion.37), channel_id=1, source_target_pairs={{0,12},{4,8},{8,4},{12,0},{16,28},{20,24},{24,20},{28,16},{1,13},{... | collective-permute-start | bytes 196616 | tf_op jit(solution)/shard_map/ppermute | solution.py:35
  40.9 1.3 %collective-permute-start.7 = (f32[64,256]{1,0:T(8,128)S(1)}, f32[64,256]{1,0:T(8,128)S(1)}, u32[]{:S(2)}, u32[]{:S(2)}) collective-permute-start(f32[64,256]{1,0:T(8,128)S(1)} %fusion.37), channel_id=1, source_target_pairs={{0,4},{4,0},{8,12},{12,8},{16,20},{20,16},{24,28},{28,24},{1,5},{5... | collective-permute-start | bytes 196616 | tf_op jit(solution)/shard_map/ppermute | solution.py:35
  42.1 1.4 %collective-permute-done.8 = f32[64,256]{1,0:T(8,128)S(1)} collective-permute-done((f32[64,256]{1,0:T(8,128)S(1)}, f32[64,256]{1,0:T(8,128)S(1)}, u32[]{:S(2)}, u32[]{:S(2)}) %collective-permute-start.8) | collective-permute-done | bytes 65568 | tf_op jit(solution)/shard_map/ppermute | solution.py:35
  43.5 1.5 %collective-permute-done.9 = f32[64,256]{1,0:T(8,128)S(1)} collective-permute-done((f32[64,256]{1,0:T(8,128)S(1)}, f32[64,256]{1,0:T(8,128)S(1)}, u32[]{:S(2)}, u32[]{:S(2)}) %collective-permute-start.9) | collective-permute-done | bytes 65568 | tf_op jit(solution)/shard_map/ppermute | solution.py:35
  45.0 1.0 %collective-permute-done.7 = f32[64,256]{1,0:T(8,128)S(1)} collective-permute-done((f32[64,256]{1,0:T(8,128)S(1)}, f32[64,256]{1,0:T(8,128)S(1)}, u32[]{:S(2)}, u32[]{:S(2)}) %collective-permute-start.7) | collective-permute-done | bytes 65568 | tf_op jit(solution)/shard_map/ppermute | solution.py:35
  46.1 2.8 %collective-permute-start.10 = (f32[64,256]{1,0:T(8,128)S(1)}, f32[64,256]{1,0:T(8,128)S(1)}, u32[]{:S(2)}, u32[]{:S(2)}) collective-permute-start(f32[64,256]{1,0:T(8,128)S(1)} %add_add_fusion), channel_id=1, source_target_pairs={{0,16},{4,20},{8,24},{12,28},{16,0},{20,4},{24,8},{28,12},{1,17},{... | collective-permute-start | bytes 196616 | tf_op jit(solution)/shard_map/ppermute | solution.py:35
  48.8 3.6 %collective-permute-done.10 = f32[64,256]{1,0:T(8,128)S(1)} collective-permute-done((f32[64,256]{1,0:T(8,128)S(1)}, f32[64,256]{1,0:T(8,128)S(1)}, u32[]{:S(2)}, u32[]{:S(2)}) %collective-permute-start.10) | collective-permute-done | bytes 65568 | tf_op jit(solution)/shard_map/ppermute | solution.py:35
  52.4 0.6 %add.117 = f32[64,256]{1,0:T(8,128)} add(f32[64,256]{1,0:T(8,128)S(1)} %add_add_fusion, f32[64,256]{1,0:T(8,128)S(1)} %collective-permute-done.10) | non-fusion elementwise | flops 16384 | bytes 196608 | tf_op jit(solution)/shard_map/add | solution.py:37
  (28 shorter events, 2.7 us)
Async XLA Ops:
  3.3 2.9 %copy-start = (s32[2048]{0:T(1024)S(1)}, s32[2048]{0:T(1024)}, u32[]{:S(2)}) copy-start(s32[2048]{0:T(1024)} %param.5) | copy-start | bytes 24580
  14.3 12.2 %collective-permute-start.6 = (f32[64,256]{1,0:T(8,128)S(1)}, f32[64,256]{1,0:T(8,128)S(1)}, u32[]{:S(2)}, u32[]{:S(2)}) collective-permute-start(f32[64,256]{1,0:T(8,128)S(1)} %bitcast.48), channel_id=1, source_target_pairs={{0,28},{4,24},{8,20},{12,16},{16,12},{20,8},{24,4},{28,0},{1,29},{... | collective-permute-start | bytes 196616 | tf_op jit(solution)/shard_map/ppermute | solution.py:94
  20.5 6.8 %collective-permute-start.5 = (f32[64,256]{1,0:T(8,128)S(1)}, f32[64,256]{1,0:T(8,128)S(1)}, u32[]{:S(2)}, u32[]{:S(2)}) collective-permute-start(f32[64,256]{1,0:T(8,128)S(1)} %bitcast.46), channel_id=1, source_target_pairs={{0,24},{4,28},{8,16},{12,20},{16,8},{20,12},{24,0},{28,4},{1,25},{... | collective-permute-start | bytes 196616 | tf_op jit(solution)/shard_map/ppermute | solution.py:94
  20.8 8.8 %collective-permute-start.4 = (f32[64,256]{1,0:T(8,128)S(1)}, f32[64,256]{1,0:T(8,128)S(1)}, u32[]{:S(2)}, u32[]{:S(2)}) collective-permute-start(f32[64,256]{1,0:T(8,128)S(1)} %bitcast.42), channel_id=1, source_target_pairs={{0,20},{4,16},{8,28},{12,24},{16,4},{20,0},{24,12},{28,8},{1,21},{... | collective-permute-start | bytes 196616 | tf_op jit(solution)/shard_map/ppermute | solution.py:94
  21.7 9.9 %collective-permute-start.3 = (f32[64,256]{1,0:T(8,128)S(1)}, f32[64,256]{1,0:T(8,128)S(1)}, u32[]{:S(2)}, u32[]{:S(2)}) collective-permute-start(f32[64,256]{1,0:T(8,128)S(1)} %bitcast.43), channel_id=1, source_target_pairs={{0,16},{4,20},{8,24},{12,28},{16,0},{20,4},{24,8},{28,12},{1,17},{... | collective-permute-start | bytes 196616 | tf_op jit(solution)/shard_map/ppermute | solution.py:94
  23.9 7.8 %collective-permute-start.2 = (f32[64,256]{1,0:T(8,128)S(1)}, f32[64,256]{1,0:T(8,128)S(1)}, u32[]{:S(2)}, u32[]{:S(2)}) collective-permute-start(f32[64,256]{1,0:T(8,128)S(1)} %bitcast.44), channel_id=1, source_target_pairs={{0,12},{4,8},{8,4},{12,0},{16,28},{20,24},{24,20},{28,16},{1,13},{... | collective-permute-start | bytes 196616 | tf_op jit(solution)/shard_map/ppermute | solution.py:94
  26.5 5.9 %collective-permute-start.1 = (f32[64,256]{1,0:T(8,128)S(1)}, f32[64,256]{1,0:T(8,128)S(1)}, u32[]{:S(2)}, u32[]{:S(2)}) collective-permute-start(f32[64,256]{1,0:T(8,128)S(1)} %bitcast.47), channel_id=1, source_target_pairs={{0,8},{4,12},{8,0},{12,4},{16,24},{20,28},{24,16},{28,20},{1,9},{5... | collective-permute-start | bytes 196616 | tf_op jit(solution)/shard_map/ppermute | solution.py:94
  27.3 5.1 %collective-permute-start = (f32[64,256]{1,0:T(8,128)S(1)}, f32[64,256]{1,0:T(8,128)S(1)}, u32[]{:S(2)}, u32[]{:S(2)}) collective-permute-start(f32[64,256]{1,0:T(8,128)S(1)} %bitcast.45), channel_id=1, source_target_pairs={{0,4},{4,0},{8,12},{12,8},{16,20},{20,16},{24,28},{28,24},{1,5},{5... | collective-permute-start | bytes 196616 | tf_op jit(solution)/shard_map/ppermute | solution.py:94
  38.6 5.0 %collective-permute-start.8 = (f32[64,256]{1,0:T(8,128)S(1)}, f32[64,256]{1,0:T(8,128)S(1)}, u32[]{:S(2)}, u32[]{:S(2)}) collective-permute-start(f32[64,256]{1,0:T(8,128)S(1)} %fusion.37), channel_id=1, source_target_pairs={{0,8},{4,12},{8,0},{12,4},{16,24},{20,28},{24,16},{28,20},{1,9},{5... | collective-permute-start | bytes 196616 | tf_op jit(solution)/shard_map/ppermute | solution.py:35
  39.8 5.2 %collective-permute-start.9 = (f32[64,256]{1,0:T(8,128)S(1)}, f32[64,256]{1,0:T(8,128)S(1)}, u32[]{:S(2)}, u32[]{:S(2)}) collective-permute-start(f32[64,256]{1,0:T(8,128)S(1)} %fusion.37), channel_id=1, source_target_pairs={{0,12},{4,8},{8,4},{12,0},{16,28},{20,24},{24,20},{28,16},{1,13},{... | collective-permute-start | bytes 196616 | tf_op jit(solution)/shard_map/ppermute | solution.py:35
  40.9 5.2 %collective-permute-start.7 = (f32[64,256]{1,0:T(8,128)S(1)}, f32[64,256]{1,0:T(8,128)S(1)}, u32[]{:S(2)}, u32[]{:S(2)}) collective-permute-start(f32[64,256]{1,0:T(8,128)S(1)} %fusion.37), channel_id=1, source_target_pairs={{0,4},{4,0},{8,12},{12,8},{16,20},{20,16},{24,28},{28,24},{1,5},{5... | collective-permute-start | bytes 196616 | tf_op jit(solution)/shard_map/ppermute | solution.py:35
  46.1 6.4 %collective-permute-start.10 = (f32[64,256]{1,0:T(8,128)S(1)}, f32[64,256]{1,0:T(8,128)S(1)}, u32[]{:S(2)}, u32[]{:S(2)}) collective-permute-start(f32[64,256]{1,0:T(8,128)S(1)} %add_add_fusion), channel_id=1, source_target_pairs={{0,16},{4,20},{8,24},{12,28},{16,0},{20,4},{24,8},{28,12},{1,17},{... | collective-permute-start | bytes 196616 | tf_op jit(solution)/shard_map/ppermute | solution.py:35

commit v12 on v11

--- a/solution.py
+++ b/solution.py
@@ -105,8 +105,9 @@
         precision=high,
         preferred_element_type=jnp.float32,
     )
-    for start in range(0, levels, 2):
+    for start in range(1, levels, 2):
         partial_gram = group_sum(partial_gram, list(range(start, min(start + 2, levels))))
+    partial_gram = group_sum(partial_gram, [0])
     return partial_gram
 
 

time: 53.3 us -> 53.5 us (level)
  waiting for transfers between devices: 12.2 us -> 14.2 us
  starting transfers between devices: 19.2 us -> 17.3 us
    ppermute x4, waiting for transfers between devices: 7.52 us -> 9.58 us  [group_sum(): values.append(lax.ppermute(value, 'ev', pairs))]
    ppermute x4, starting transfers between devices: 6.31 us -> 4.45 us  [group_sum(): values.append(lax.ppermute(value, 'ev', pairs))]
where the time goes in v12:
time: 53.5 us; the launch traced here: 53.3 us
  starting transfers between devices  17.3 us (32%)
  waiting for transfers between devices  14.2 us (27%)
  matrix products  9.4 us (18%)
  blocking collectives  5.79 us (11%)
  other arithmetic  3.44 us (6%)
  local copies, waits for them, and re-layouts  2.91 us (5%)
    ppermute x7, starting transfers between devices, per_device(): arrived.append(lax.ppermute(block, 'ev', pairs))  12.9 us
    ppermute x4, waiting for transfers between devices, group_sum(): values.append(lax.ppermute(value, 'ev', pairs))  9.58 us
    dot_general x1, matrix products, per_device(): jnp.einsum('xcb,xbj->xcj', first, pick.astype(jnp.float32), precision=lax...  6.35 us
    all_gather x1, blocking collectives, per_device(): lax.all_gather(sketch, 'col', axis=0, tiled=True)  5.79 us
    ppermute x7, waiting for transfers between devices, per_device(): arrived.append(lax.ppermute(block, 'ev', pairs))  4.64 us
    ppermute x4, starting transfers between devices, group_sum(): values.append(lax.ppermute(value, 'ev', pairs))  4.45 us
    dot_general x1, matrix products, per_device(): jnp.einsum('xa,cab->xcb', hadamard(OUTER).astype(jnp.bfloat16), blocks, p...  2.69 us
    unnamed x1, other arithmetic  1.85 us
  transfers between devices with their start and end apart: 11, of which 7 were waited for; matrix products, arithmetic and copies ran while one was open for 1% of the time, Pallas kernels for 0%

profile of v12, /device:TPU:0, one launch (start us, length us, event | category | flops | bytes accessed | tf_op | source)
XLA Modules:
  0.0 53.3 jit_solution(5228322466640458141)
XLA Ops:
  0.0 0.8 %convert_element_type.16 = bf16[16384]{0:T(1024)(128)(2,1)S(1)} convert(s32[16384]{0:T(1024)} %param.4) | non-fusion elementwise | flops 16384 | bytes 98304 | tf_op jit(solution)/shard_map/convert_element_type | solution.py:70
  0.9 1.9 %multiply_bitcast_fusion = bf16[8,8,128,128]{3,1,2,0:T(8,128)(2,1)S(1)} fusion(bf16[64,16384]{1,0:T(8,128)(2,1)} %param.3, bf16[16384]{0:T(1024)(128)(2,1)S(1)} %convert_element_type.16), kind=kLoop, calls=%fused_computation.2 | loop fusion | flops 1048576 | bytes 4227072
  2.7 0.6 %copy.23 = bf16[8,8,128,128]{3,2,1,0:T(8,128)(2,1)S(1)} copy(bf16[8,8,128,128]{3,1,2,0:T(8,128)(2,1)S(1)} %multiply_bitcast_fusion) | data formatting | bytes 4194304
  3.3 2.7 %fusion.19 = f32[128,64,128]{2,0,1:T(8,128)} fusion(bf16[64,128,128]{2,1,0:T(8,128)(2,1)S(1)} %bitcast.39), kind=kOutput, calls=%fused_computation.27 | convolution fusion | flops 269025280 | bytes 6291456 | tf_op jit(solution)/shard_map/xa,cab->xcb/dot_general | solution.py:72
  6.1 0.5 reshape.30
  7.0 6.3 %fusion = f32[128,64,16]{1,2,0:T(8,128)S(1)} fusion(f32[128,64,128]{2,0,1:T(8,128)} %fusion.19, s32[16]{0:T(128)S(1)} %xor.35, s32[128,16]{1,0:T(8,128)S(1)} %copy.12), kind=kOutput, calls=%fused_computation | convolution fusion | flops 102498304 | bytes 4726848 | tf_op jit(solution)/shard_map/xcb,xbj->xcj/dot_general | solution.py:79
  13.4 0.7 %constant_dynamic-slice_fusion.7 = (f32[1,64,256]{1,0,2:T(1,128)S(1)}, f32[1,64,256]{1,0,2:T(1,128)S(1)}, f32[1,64,256]{1,0,2:T(1,128)S(1)}, f32[1,64,256]{1,0,2...) fusion(f32[8,64,256]{1,0,2:T(8,128)S(1)} %bitcast.40, ...), kind=kLoop, calls=%fused_computation.42 | loop fusion | bytes 1048608 | tf_op jit(solution)/shard_map/jit(dynamic_index_in_dim)/dynamic_slice | solution.py:88
  14.3 6.1 %collective-permute-start.6 = (f32[64,256]{1,0:T(8,128)S(1)}, f32[64,256]{1,0:T(8,128)S(1)}, u32[]{:S(2)}, u32[]{:S(2)}) collective-permute-start(f32[64,256]{1,0:T(8,128)S(1)} %bitcast.48), channel_id=1, source_target_pairs={{0,28},{4,24},{8,20},{12,16},{16,12},{20,8},{24,4},{28,0},{1,29},{... | collective-permute-start | bytes 196616 | tf_op jit(solution)/shard_map/ppermute | solution.py:94
  20.8 0.8 %collective-permute-start.4 = (f32[64,256]{1,0:T(8,128)S(1)}, f32[64,256]{1,0:T(8,128)S(1)}, u32[]{:S(2)}, u32[]{:S(2)}) collective-permute-start(f32[64,256]{1,0:T(8,128)S(1)} %bitcast.42), channel_id=1, source_target_pairs={{0,20},{4,16},{8,28},{12,24},{16,4},{20,0},{24,12},{28,8},{1,21},{... | collective-permute-start | bytes 196616 | tf_op jit(solution)/shard_map/ppermute | solution.py:94
  21.7 2.0 %collective-permute-start.3 = (f32[64,256]{1,0:T(8,128)S(1)}, f32[64,256]{1,0:T(8,128)S(1)}, u32[]{:S(2)}, u32[]{:S(2)}) collective-permute-start(f32[64,256]{1,0:T(8,128)S(1)} %bitcast.43), channel_id=1, source_target_pairs={{0,16},{4,20},{8,24},{12,28},{16,0},{20,4},{24,8},{28,12},{1,17},{... | collective-permute-start | bytes 196616 | tf_op jit(solution)/shard_map/ppermute | solution.py:94
  23.9 2.4 %collective-permute-start.2 = (f32[64,256]{1,0:T(8,128)S(1)}, f32[64,256]{1,0:T(8,128)S(1)}, u32[]{:S(2)}, u32[]{:S(2)}) collective-permute-start(f32[64,256]{1,0:T(8,128)S(1)} %bitcast.44), channel_id=1, source_target_pairs={{0,12},{4,8},{8,4},{12,0},{16,28},{20,24},{24,20},{28,16},{1,13},{... | collective-permute-start | bytes 196616 | tf_op jit(solution)/shard_map/ppermute | solution.py:94
  26.5 0.8 %collective-permute-start.1 = (f32[64,256]{1,0:T(8,128)S(1)}, f32[64,256]{1,0:T(8,128)S(1)}, u32[]{:S(2)}, u32[]{:S(2)}) collective-permute-start(f32[64,256]{1,0:T(8,128)S(1)} %bitcast.47), channel_id=1, source_target_pairs={{0,8},{4,12},{8,0},{12,4},{16,24},{20,28},{24,16},{28,20},{1,9},{5... | collective-permute-start | bytes 196616 | tf_op jit(solution)/shard_map/ppermute | solution.py:94
  27.7 1.9 %collective-permute-done.4 = f32[64,256]{1,0:T(8,128)S(1)} collective-permute-done((f32[64,256]{1,0:T(8,128)S(1)}, f32[64,256]{1,0:T(8,128)S(1)}, u32[]{:S(2)}, u32[]{:S(2)}) %collective-permute-start.4) | collective-permute-done | bytes 65568 | tf_op jit(solution)/shard_map/ppermute | solution.py:94
  29.6 2.0 %collective-permute-done.3 = f32[64,256]{1,0:T(8,128)S(1)} collective-permute-done((f32[64,256]{1,0:T(8,128)S(1)}, f32[64,256]{1,0:T(8,128)S(1)}, u32[]{:S(2)}, u32[]{:S(2)}) %collective-permute-start.3) | collective-permute-done | bytes 65568 | tf_op jit(solution)/shard_map/ppermute | solution.py:94
  31.6 0.7 %collective-permute-done.1 = f32[64,256]{1,0:T(8,128)S(1)} collective-permute-done((f32[64,256]{1,0:T(8,128)S(1)}, f32[64,256]{1,0:T(8,128)S(1)}, u32[]{:S(2)}, u32[]{:S(2)}) %collective-permute-start.1) | collective-permute-done | bytes 65568 | tf_op jit(solution)/shard_map/ppermute | solution.py:94
  32.4 5.8 %all_gather.3 = f32[256,256]{1,0:T(8,128)S(1)} all-gather(f32[64,256]{1,0:T(8,128)S(1)} %fusion.17), channel_id=1, replica_groups=mesh['ev'=8,'col'=4] {'col'}, dimensions={0}, use_global_device_ids=true | all-gather | bytes 327680 | tf_op jit(solution)/shard_map/all_gather | solution.py:104
  38.2 0.4 fusion.37
  38.6 2.9 %collective-permute-start.8 = (f32[64,256]{1,0:T(8,128)S(1)}, f32[64,256]{1,0:T(8,128)S(1)}, u32[]{:S(2)}, u32[]{:S(2)}) collective-permute-start(f32[64,256]{1,0:T(8,128)S(1)} %fusion.37), channel_id=1, source_target_pairs={{0,16},{4,20},{8,24},{12,28},{16,0},{20,4},{24,8},{28,12},{1,17},{... | collective-permute-start | bytes 196616 | tf_op jit(solution)/shard_map/ppermute | solution.py:35
  41.5 0.7 %collective-permute-start.9 = (f32[64,256]{1,0:T(8,128)S(1)}, f32[64,256]{1,0:T(8,128)S(1)}, u32[]{:S(2)}, u32[]{:S(2)}) collective-permute-start(f32[64,256]{1,0:T(8,128)S(1)} %fusion.37), channel_id=1, source_target_pairs={{0,24},{4,28},{8,16},{12,20},{16,8},{20,12},{24,0},{28,4},{1,25},{... | collective-permute-start | bytes 196616 | tf_op jit(solution)/shard_map/ppermute | solution.py:35
  42.4 3.4 %collective-permute-done.8 = f32[64,256]{1,0:T(8,128)S(1)} collective-permute-done((f32[64,256]{1,0:T(8,128)S(1)}, f32[64,256]{1,0:T(8,128)S(1)}, u32[]{:S(2)}, u32[]{:S(2)}) %collective-permute-start.8) | collective-permute-done | bytes 65568 | tf_op jit(solution)/shard_map/ppermute | solution.py:35
  45.8 2.2 %collective-permute-done.9 = f32[64,256]{1,0:T(8,128)S(1)} collective-permute-done((f32[64,256]{1,0:T(8,128)S(1)}, f32[64,256]{1,0:T(8,128)S(1)}, u32[]{:S(2)}, u32[]{:S(2)}) %collective-permute-start.9) | collective-permute-done | bytes 65568 | tf_op jit(solution)/shard_map/ppermute | solution.py:35
  48.3 0.6 %collective-permute-start.10 = (f32[64,256]{1,0:T(8,128)S(1)}, f32[64,256]{1,0:T(8,128)S(1)}, u32[]{:S(2)}, u32[]{:S(2)}) collective-permute-start(f32[64,256]{1,0:T(8,128)S(1)} %add_add_fusion), channel_id=1, source_target_pairs={{0,4},{4,0},{8,12},{12,8},{16,20},{20,16},{24,28},{28,24},{1,5},{5... | collective-permute-start | bytes 196616 | tf_op jit(solution)/shard_map/ppermute | solution.py:35
  48.9 3.7 %collective-permute-done.10 = f32[64,256]{1,0:T(8,128)S(1)} collective-permute-done((f32[64,256]{1,0:T(8,128)S(1)}, f32[64,256]{1,0:T(8,128)S(1)}, u32[]{:S(2)}, u32[]{:S(2)}) %collective-permute-start.10) | collective-permute-done | bytes 65568 | tf_op jit(solution)/shard_map/ppermute | solution.py:35
  52.6 0.6 %add.117 = f32[64,256]{1,0:T(8,128)} add(f32[64,256]{1,0:T(8,128)S(1)} %add_add_fusion, f32[64,256]{1,0:T(8,128)S(1)} %collective-permute-done.10) | non-fusion elementwise | flops 16384 | bytes 196608 | tf_op jit(solution)/shard_map/add | solution.py:37
  (28 shorter events, 2.3 us)
Async XLA Ops:
  3.3 2.9 %copy-start = (s32[2048]{0:T(1024)S(1)}, s32[2048]{0:T(1024)}, u32[]{:S(2)}) copy-start(s32[2048]{0:T(1024)} %param.5) | copy-start | bytes 24580
  14.3 12.2 %collective-permute-start.6 = (f32[64,256]{1,0:T(8,128)S(1)}, f32[64,256]{1,0:T(8,128)S(1)}, u32[]{:S(2)}, u32[]{:S(2)}) collective-permute-start(f32[64,256]{1,0:T(8,128)S(1)} %bitcast.48), channel_id=1, source_target_pairs={{0,28},{4,24},{8,20},{12,16},{16,12},{20,8},{24,4},{28,0},{1,29},{... | collective-permute-start | bytes 196616 | tf_op jit(solution)/shard_map/ppermute | solution.py:94
  20.5 6.8 %collective-permute-start.5 = (f32[64,256]{1,0:T(8,128)S(1)}, f32[64,256]{1,0:T(8,128)S(1)}, u32[]{:S(2)}, u32[]{:S(2)}) collective-permute-start(f32[64,256]{1,0:T(8,128)S(1)} %bitcast.46), channel_id=1, source_target_pairs={{0,24},{4,28},{8,16},{12,20},{16,8},{20,12},{24,0},{28,4},{1,25},{... | collective-permute-start | bytes 196616 | tf_op jit(solution)/shard_map/ppermute | solution.py:94
  20.8 8.8 %collective-permute-start.4 = (f32[64,256]{1,0:T(8,128)S(1)}, f32[64,256]{1,0:T(8,128)S(1)}, u32[]{:S(2)}, u32[]{:S(2)}) collective-permute-start(f32[64,256]{1,0:T(8,128)S(1)} %bitcast.42), channel_id=1, source_target_pairs={{0,20},{4,16},{8,28},{12,24},{16,4},{20,0},{24,12},{28,8},{1,21},{... | collective-permute-start | bytes 196616 | tf_op jit(solution)/shard_map/ppermute | solution.py:94
  21.7 9.9 %collective-permute-start.3 = (f32[64,256]{1,0:T(8,128)S(1)}, f32[64,256]{1,0:T(8,128)S(1)}, u32[]{:S(2)}, u32[]{:S(2)}) collective-permute-start(f32[64,256]{1,0:T(8,128)S(1)} %bitcast.43), channel_id=1, source_target_pairs={{0,16},{4,20},{8,24},{12,28},{16,0},{20,4},{24,8},{28,12},{1,17},{... | collective-permute-start | bytes 196616 | tf_op jit(solution)/shard_map/ppermute | solution.py:94
  23.9 7.8 %collective-permute-start.2 = (f32[64,256]{1,0:T(8,128)S(1)}, f32[64,256]{1,0:T(8,128)S(1)}, u32[]{:S(2)}, u32[]{:S(2)}) collective-permute-start(f32[64,256]{1,0:T(8,128)S(1)} %bitcast.44), channel_id=1, source_target_pairs={{0,12},{4,8},{8,4},{12,0},{16,28},{20,24},{24,20},{28,16},{1,13},{... | collective-permute-start | bytes 196616 | tf_op jit(solution)/shard_map/ppermute | solution.py:94
  26.5 5.9 %collective-permute-start.1 = (f32[64,256]{1,0:T(8,128)S(1)}, f32[64,256]{1,0:T(8,128)S(1)}, u32[]{:S(2)}, u32[]{:S(2)}) collective-permute-start(f32[64,256]{1,0:T(8,128)S(1)} %bitcast.47), channel_id=1, source_target_pairs={{0,8},{4,12},{8,0},{12,4},{16,24},{20,28},{24,16},{28,20},{1,9},{5... | collective-permute-start | bytes 196616 | tf_op jit(solution)/shard_map/ppermute | solution.py:94
  27.3 5.1 %collective-permute-start = (f32[64,256]{1,0:T(8,128)S(1)}, f32[64,256]{1,0:T(8,128)S(1)}, u32[]{:S(2)}, u32[]{:S(2)}) collective-permute-start(f32[64,256]{1,0:T(8,128)S(1)} %bitcast.45), channel_id=1, source_target_pairs={{0,4},{4,0},{8,12},{12,8},{16,20},{20,16},{24,28},{28,24},{1,5},{5... | collective-permute-start | bytes 196616 | tf_op jit(solution)/shard_map/ppermute | solution.py:94
  38.6 7.2 %collective-permute-start.8 = (f32[64,256]{1,0:T(8,128)S(1)}, f32[64,256]{1,0:T(8,128)S(1)}, u32[]{:S(2)}, u32[]{:S(2)}) collective-permute-start(f32[64,256]{1,0:T(8,128)S(1)} %fusion.37), channel_id=1, source_target_pairs={{0,16},{4,20},{8,24},{12,28},{16,0},{20,4},{24,8},{28,12},{1,17},{... | collective-permute-start | bytes 196616 | tf_op jit(solution)/shard_map/ppermute | solution.py:35
  41.5 6.6 %collective-permute-start.9 = (f32[64,256]{1,0:T(8,128)S(1)}, f32[64,256]{1,0:T(8,128)S(1)}, u32[]{:S(2)}, u32[]{:S(2)}) collective-permute-start(f32[64,256]{1,0:T(8,128)S(1)} %fusion.37), channel_id=1, source_target_pairs={{0,24},{4,28},{8,16},{12,20},{16,8},{20,12},{24,0},{28,4},{1,25},{... | collective-permute-start | bytes 196616 | tf_op jit(solution)/shard_map/ppermute | solution.py:35
  42.1 6.1 %collective-permute-start.7 = (f32[64,256]{1,0:T(8,128)S(1)}, f32[64,256]{1,0:T(8,128)S(1)}, u32[]{:S(2)}, u32[]{:S(2)}) collective-permute-start(f32[64,256]{1,0:T(8,128)S(1)} %fusion.37), channel_id=1, source_target_pairs={{0,8},{4,12},{8,0},{12,4},{16,24},{20,28},{24,16},{28,20},{1,9},{5... | collective-permute-start | bytes 196616 | tf_op jit(solution)/shard_map/ppermute | solution.py:35
  48.3 4.3 %collective-permute-start.10 = (f32[64,256]{1,0:T(8,128)S(1)}, f32[64,256]{1,0:T(8,128)S(1)}, u32[]{:S(2)}, u32[]{:S(2)}) collective-permute-start(f32[64,256]{1,0:T(8,128)S(1)} %add_add_fusion), channel_id=1, source_target_pairs={{0,4},{4,0},{8,12},{12,8},{16,20},{20,16},{24,28},{28,24},{1,5},{5... | collective-permute-start | bytes 196616 | tf_op jit(solution)/shard_map/ppermute | solution.py:35

commit v13 on v9

--- a/solution.py
+++ b/solution.py
@@ -27,7 +27,6 @@
 
 def group_sum(value, bits):
     groups = lax.axis_size("ev")
-    my_index = lax.axis_index("ev")
     masks = [0]
     for bit in bits:
         masks = masks + [mask | (1 << bit) for mask in masks]
@@ -35,12 +34,9 @@
     for mask in masks[1:]:
         pairs = [(source, source ^ mask) for source in range(groups)]
         values.append(lax.ppermute(value, "ev", pairs))
-    mine = sum(((my_index >> bit) & 1) << place for place, bit in enumerate(bits))
-    order = jnp.arange(len(masks), dtype=jnp.int32) ^ mine
-    ordered = jnp.take(jnp.stack(values), order, axis=0)
-    while ordered.shape[0] > 1:
-        ordered = ordered[0::2] + ordered[1::2]
-    return ordered[0]
+    while len(values) > 1:
+        values = [values[i] + values[i + 1] for i in range(0, len(values), 2)]
+    return values[0]
 
 
 def factors(offsets, my_index, groups, length):
@@ -58,28 +54,32 @@
 
 
 def sketch_kernel(panel_ref, sign_ref, hy_ref, hx_ref, out_ref):
-    block, samples = out_ref.shape
+    groups, block, chunk = out_ref.shape
     inner = hy_ref.shape[0]
-    signed = panel_ref[...].astype(jnp.float32) * sign_ref[...]
+    samples = hy_ref.shape[1]
+    signed = panel_ref[...].astype(jnp.float32) * sign_ref[...].astype(jnp.float32)
     rows = jnp.concatenate(
         [signed[:, a * inner : (a + 1) * inner] for a in range(OUTER)], axis=0
     ).astype(jnp.bfloat16)
-    width = min(samples, 1024)
+    width = min(samples, 512)
     for part in range(samples // width):
         lanes = pl.ds(part * width, width)
         mixed = jnp.dot(rows, hy_ref[:, lanes], preferred_element_type=jnp.float32)
         mixed = mixed.reshape(OUTER, block, width) * hx_ref[:, lanes][:, None, :]
-        out_ref[:, lanes] = jnp.sum(mixed, axis=0)
+        total = jnp.sum(mixed, axis=0)
+        for piece in range(width // chunk):
+            out_ref[(part * width) // chunk + piece] = total[:, piece * chunk : (piece + 1) * chunk]
 
 
-def local_sketch(panel, sign, hy, hx):
+def local_sketch(panel, sign, hy, hx, groups):
     columns, length = panel.shape
     samples = hy.shape[1]
-    block = 8
+    chunk = samples // groups
+    block = 16
     flops = 2 * columns * length * samples + 2 * columns * OUTER * samples
     return pl.pallas_call(
         sketch_kernel,
-        out_shape=jax.ShapeDtypeStruct((columns, samples), jnp.float32),
+        out_shape=jax.ShapeDtypeStruct((groups, columns, chunk), jnp.float32),
         grid=(columns // block,),
         in_specs=[
             pl.BlockSpec((block, length), lambda i: (i, 0)),
@@ -87,7 +87,7 @@
             pl.BlockSpec(hy.shape, lambda i: (0, 0)),
             pl.BlockSpec(hx.shape, lambda i: (0, 0)),
         ],
-        out_specs=pl.BlockSpec((block, samples), lambda i: (i, 0)),
+        out_specs=pl.BlockSpec((groups, block, chunk), lambda i: (0, i, 0)),
         cost_estimate=pl.CostEstimate(
             flops=flops, transcendentals=0, bytes_accessed=columns * length * 2 + columns * samples * 4
         ),
@@ -103,11 +103,9 @@
     per_row = inner // STRIDE
     high = lax.Precision.HIGHEST
 
-    sign = signs.reshape(1, length).astype(jnp.float32)
+    sign = signs.reshape(1, length)
     hy, hx = factors(offsets, my_index, groups, length)
-    sampled = local_sketch(panel, sign, hy, hx)
-
-    chunks = sampled.reshape(columns, groups, OUTER * per_row).transpose(1, 0, 2)
+    chunks = local_sketch(panel, sign, hy, hx, groups)
     own = lax.dynamic_index_in_dim(chunks, my_index, axis=0, keepdims=False)
     arrived = []
     for distance in range(1, groups):

time: 59.4 us -> 56.2 us (0.946)
  local copies, waits for them, and re-layouts: 2.74 us -> 1.06 us
  other arithmetic: 4.77 us -> 3.87 us
  Pallas kernels: 12.3 us -> 11.6 us
    convert_element_type x1 -> x0, other arithmetic: 1.48 us -> none  [per_device(): sign = signs.reshape(1, length).astype(jnp.float32)]
    unnamed x8 -> x0, local copies, waits for them, and re-layouts: 1.24 us -> none
    gather x2 -> x0, local copies, waits for them, and re-layouts: 1.12 us -> none  [group_sum(): ordered = jnp.take(jnp.stack(values), order, axis=0)]
    squeeze x0 -> x1, local copies, waits for them, and re-layouts: none -> 1.06 us  [per_device(): block = lax.dynamic_index_in_dim(chunks, target, axis=0, keepdims=False)]
    mul x1, other arithmetic: 0.04 us -> 0.87 us  [per_device(): sketch = chunks * scale]
    pallas_call x1, Pallas kernels: 12.3 us -> 11.6 us  [local_sketch(): pl.pallas_call(sketch_kernel, out_shape=jax.ShapeDtypeStruct((groups, col...]
    squeeze x2 -> x0, other arithmetic: 0.65 us -> none  [group_sum(): return ordered[0]]
    add x2, other arithmetic: 0.03 us -> 0.66 us  [group_sum(): values = [values[i] + values[i + 1] for i in range(0, len(values), 2)]]
where the time goes in v13:
time: 56.2 us; the launch traced here: 55.9 us
  starting transfers between devices  18.2 us (32%)
  waiting for transfers between devices  14.9 us (27%)
  Pallas kernels  11.6 us (21%)
  blocking collectives  5.79 us (10%)
  other arithmetic  3.87 us (7%)
  local copies, waits for them, and re-layouts  1.06 us (2%)
    ppermute x7, starting transfers between devices, per_device(): arrived.append(lax.ppermute(block, 'ev', pairs))  12.5 us
    pallas_call x1, Pallas kernels, local_sketch(): pl.pallas_call(sketch_kernel, out_shape=jax.ShapeDtypeStruct((groups, col...  11.6 us
    ppermute x4, waiting for transfers between devices, group_sum(): values.append(lax.ppermute(value, 'ev', pairs))  7.89 us
    ppermute x7, waiting for transfers between devices, per_device(): arrived.append(lax.ppermute(block, 'ev', pairs))  7.05 us
    all_gather x1, blocking collectives, per_device(): lax.all_gather(sketch, 'col', axis=0, tiled=True)  5.79 us
    ppermute x4, starting transfers between devices, group_sum(): values.append(lax.ppermute(value, 'ev', pairs))  5.69 us
    convert_element_type x1, other arithmetic, factors(): return (hy.astype(jnp.bfloat16), hx.astype(jnp.float32))  1.62 us
  transfers between devices with their start and end apart: 11, of which 6 were waited for; matrix products, arithmetic and copies ran while one was open for 0% of the time, Pallas kernels for 0%

profile of v13, /device:TPU:0, one launch (start us, length us, event | category | flops | bytes accessed | tf_op | source)
XLA Modules:
  0.0 55.9 jit_solution(17056218600900199252)
XLA Ops:
  0.0 0.7 %add_select_fusion.1 = (s32[2048]{0:T(1024)S(1)}, s32[2048]{0:T(1024)S(1)}, s32[2048]{0:T(1024)S(1)}) fusion(s32[2048]{0:T(1024)} %param.5, s32[]{:T(128)S(6)} %axis_index.15), kind=kLoop, calls=%fused_computation.20 | loop fusion | flops 94208 | bytes 32772 | tf_op jit(solution)/shard_map/jit(floor_divide)/jit(_where)/select_n | solution.py:46
  0.8 1.6 %subtract_convert_fusion = (f32[128,2048]{1,0:T(8,128)}, bf16[128,2048]{1,0:T(8,128)(2,1)}) fusion(s32[2048]{0:T(1024)S(1)} %get-tuple-element.13, s32[2048]{0:T(1024)S(1)} %get-tuple-element.12, s32[2048]{0:T(1024)S(1)} %get-tuple-element.14), kind=kLoop, calls=%fused_computation | loop fusion | flops 3407872 | bytes 1597440 | tf_op jit(solution)/shard_map/convert_element_type | solution.py:53
  2.4 11.6 %shard_map.37 = f32[8,64,256]{2,1,0:T(8,128)} custom-call(bf16[64,16384]{1,0:T(8,128)(2,1)} %panel_ref.1, s32[1,16384]{1,0:T(1,128)} %bitcast.33, bf16[128,2048]{1,0:T(8,128)(2,1)} %get-tuple-element.16.hy_ref, f32[128,2048]{1,0:T(8,128)} %get-tuple-element.15.hx_ref), custom_call_target="tpu_custom_call" | custom-call | flops 4328521728 | bytes 2621440 | tf_op jit(solution)/shard_map/pallas_call | solution.py:80
  14.0 1.1 %dynamic-slice_bitcast_fusion.6 = (f32[64,256]{1,0:T(8,128)S(1)}, f32[64,256]{1,0:T(8,128)S(1)}, f32[64,256]{1,0:T(8,128)S(1)}, f32[64,256]{1,0:T(8,128)S(1)}, f...) fusion(f32[8,64,256]{2,1,0:T(8,128)} %shard_map.37, s32[]{:T(128)S(6)} %select_n.49, ...), kind=kLoop, calls=%fused_computation.17 | loop fusion | bytes 917532 | tf_op jit(solution)/shard_map/jit(dynamic_index_in_dim)/squeeze | solution.py:113
  15.1 3.0 %collective-permute-start = (f32[64,256]{1,0:T(8,128)S(1)}, f32[64,256]{1,0:T(8,128)S(1)}, u32[]{:S(2)}, u32[]{:S(2)}) collective-permute-start(f32[64,256]{1,0:T(8,128)S(1)} %get-tuple-element.5), channel_id=1, source_target_pairs={{0,4},{4,0},{8,12},{12,8},{16,20},{20,16},{24,28},{28,24},{1,5},{5... | collective-permute-start | bytes 196616 | tf_op jit(solution)/shard_map/ppermute | solution.py:115
  18.1 1.6 %collective-permute-start.1 = (f32[64,256]{1,0:T(8,128)S(1)}, f32[64,256]{1,0:T(8,128)S(1)}, u32[]{:S(2)}, u32[]{:S(2)}) collective-permute-start(f32[64,256]{1,0:T(8,128)S(1)} %get-tuple-element.11), channel_id=1, source_target_pairs={{0,8},{4,12},{8,0},{12,4},{16,24},{20,28},{24,16},{28,20},{1,9},{5... | collective-permute-start | bytes 196616 | tf_op jit(solution)/shard_map/ppermute | solution.py:115
  19.7 3.0 %collective-permute-start.3 = (f32[64,256]{1,0:T(8,128)S(1)}, f32[64,256]{1,0:T(8,128)S(1)}, u32[]{:S(2)}, u32[]{:S(2)}) collective-permute-start(f32[64,256]{1,0:T(8,128)S(1)} %get-tuple-element.9), channel_id=1, source_target_pairs={{0,16},{4,20},{8,24},{12,28},{16,0},{20,4},{24,8},{28,12},{1,17},{... | collective-permute-start | bytes 196616 | tf_op jit(solution)/shard_map/ppermute | solution.py:115
  22.7 1.3 %collective-permute-start.4 = (f32[64,256]{1,0:T(8,128)S(1)}, f32[64,256]{1,0:T(8,128)S(1)}, u32[]{:S(2)}, u32[]{:S(2)}) collective-permute-start(f32[64,256]{1,0:T(8,128)S(1)} %get-tuple-element.8), channel_id=1, source_target_pairs={{0,20},{4,16},{8,28},{12,24},{16,4},{20,0},{24,12},{28,8},{1,21},{... | collective-permute-start | bytes 196616 | tf_op jit(solution)/shard_map/ppermute | solution.py:115
  24.0 3.6 %collective-permute-start.5 = (f32[64,256]{1,0:T(8,128)S(1)}, f32[64,256]{1,0:T(8,128)S(1)}, u32[]{:S(2)}, u32[]{:S(2)}) collective-permute-start(f32[64,256]{1,0:T(8,128)S(1)} %get-tuple-element.7), channel_id=1, source_target_pairs={{0,24},{4,28},{8,16},{12,20},{16,8},{20,12},{24,0},{28,4},{1,25},{... | collective-permute-start | bytes 196616 | tf_op jit(solution)/shard_map/ppermute | solution.py:115
  27.6 0.0 collective-permute-start.6
  27.6 5.3 %collective-permute-done.4 = f32[64,256]{1,0:T(8,128)S(1)} collective-permute-done((f32[64,256]{1,0:T(8,128)S(1)}, f32[64,256]{1,0:T(8,128)S(1)}, u32[]{:S(2)}, u32[]{:S(2)}) %collective-permute-start.4) | collective-permute-done | bytes 65568 | tf_op jit(solution)/shard_map/ppermute | solution.py:115
  32.9 1.8 %collective-permute-done.6 = f32[64,256]{1,0:T(8,128)S(1)} collective-permute-done((f32[64,256]{1,0:T(8,128)S(1)}, f32[64,256]{1,0:T(8,128)S(1)}, u32[]{:S(2)}, u32[]{:S(2)}) %collective-permute-start.6) | collective-permute-done | bytes 65568 | tf_op jit(solution)/shard_map/ppermute | solution.py:115
  34.7 0.9 %fusion.6 = f32[64,256]{1,0:T(8,128)S(1)} fusion(f32[64,256]{1,0:T(8,128)S(1)} %collective-permute-done.6, f32[64,256]{1,0:T(8,128)S(1)} %collective-permute-done.5, f32[64,256]{1,0:T(8,128)S(1)} %collective-permute-done.4, f32[64,256]{1,0:T(8,128)S(1)} %collective-permute-done.3, f32[64,256]{1,0:T(8,128)S(1)} %collective-permute-done.2, ...), kind=kLoop, calls=%fused_computation.9 | loop fusion | flops 131072 | bytes 589828 | tf_op jit(solution)/shard_map/mul | solution.py:122
  35.5 5.8 %all_gather.3 = f32[256,256]{1,0:T(8,128)S(1)} all-gather(f32[64,256]{1,0:T(8,128)S(1)} %fusion.6), channel_id=1, replica_groups=mesh['ev'=8,'col'=4] {'col'}, dimensions={0}, use_global_device_ids=true | all-gather | bytes 327680 | tf_op jit(solution)/shard_map/all_gather | solution.py:125
  41.3 0.4 fusion.13
  41.7 0.6 %collective-permute-start.7 = (f32[64,256]{1,0:T(8,128)S(1)}, f32[64,256]{1,0:T(8,128)S(1)}, u32[]{:S(2)}, u32[]{:S(2)}) collective-permute-start(f32[64,256]{1,0:T(8,128)S(1)} %fusion.13), channel_id=1, source_target_pairs={{0,4},{4,0},{8,12},{12,8},{16,20},{20,16},{24,28},{28,24},{1,5},{5... | collective-permute-start | bytes 196616 | tf_op jit(solution)/shard_map/ppermute | solution.py:36
  42.3 1.9 %collective-permute-start.8 = (f32[64,256]{1,0:T(8,128)S(1)}, f32[64,256]{1,0:T(8,128)S(1)}, u32[]{:S(2)}, u32[]{:S(2)}) collective-permute-start(f32[64,256]{1,0:T(8,128)S(1)} %fusion.13), channel_id=1, source_target_pairs={{0,8},{4,12},{8,0},{12,4},{16,24},{20,28},{24,16},{28,20},{1,9},{5... | collective-permute-start | bytes 196616 | tf_op jit(solution)/shard_map/ppermute | solution.py:36
  44.2 1.1 %collective-permute-start.9 = (f32[64,256]{1,0:T(8,128)S(1)}, f32[64,256]{1,0:T(8,128)S(1)}, u32[]{:S(2)}, u32[]{:S(2)}) collective-permute-start(f32[64,256]{1,0:T(8,128)S(1)} %fusion.13), channel_id=1, source_target_pairs={{0,12},{4,8},{8,4},{12,0},{16,28},{20,24},{24,20},{28,16},{1,13},{... | collective-permute-start | bytes 196616 | tf_op jit(solution)/shard_map/ppermute | solution.py:36
  45.2 0.9 %collective-permute-done.7 = f32[64,256]{1,0:T(8,128)S(1)} collective-permute-done((f32[64,256]{1,0:T(8,128)S(1)}, f32[64,256]{1,0:T(8,128)S(1)}, u32[]{:S(2)}, u32[]{:S(2)}) %collective-permute-start.7) | collective-permute-done | bytes 65568 | tf_op jit(solution)/shard_map/ppermute | solution.py:36
  46.1 0.4 collective-permute-done.8
  46.5 2.8 %collective-permute-done.9 = f32[64,256]{1,0:T(8,128)S(1)} collective-permute-done((f32[64,256]{1,0:T(8,128)S(1)}, f32[64,256]{1,0:T(8,128)S(1)}, u32[]{:S(2)}, u32[]{:S(2)}) %collective-permute-start.9) | collective-permute-done | bytes 65568 | tf_op jit(solution)/shard_map/ppermute | solution.py:36
  49.4 2.1 %collective-permute-start.10 = (f32[64,256]{1,0:T(8,128)S(1)}, f32[64,256]{1,0:T(8,128)S(1)}, u32[]{:S(2)}, u32[]{:S(2)}) collective-permute-start(f32[64,256]{1,0:T(8,128)S(1)} %add_add_fusion), channel_id=1, source_target_pairs={{0,16},{4,20},{8,24},{12,28},{16,0},{20,4},{24,8},{28,12},{1,17},{... | collective-permute-start | bytes 196616 | tf_op jit(solution)/shard_map/ppermute | solution.py:36
  51.5 3.8 %collective-permute-done.10 = f32[64,256]{1,0:T(8,128)S(1)} collective-permute-done((f32[64,256]{1,0:T(8,128)S(1)}, f32[64,256]{1,0:T(8,128)S(1)}, u32[]{:S(2)}, u32[]{:S(2)}) %collective-permute-start.10) | collective-permute-done | bytes 65568 | tf_op jit(solution)/shard_map/ppermute | solution.py:36
  55.3 0.6 %add.104 = f32[64,256]{1,0:T(8,128)} add(f32[64,256]{1,0:T(8,128)S(1)} %add_add_fusion, f32[64,256]{1,0:T(8,128)S(1)} %collective-permute-done.10) | non-fusion elementwise | flops 16384 | bytes 196608 | tf_op jit(solution)/shard_map/add | solution.py:38
  (7 shorter events, 0.0 us)
Async XLA Ops:
  15.1 8.9 %collective-permute-start = (f32[64,256]{1,0:T(8,128)S(1)}, f32[64,256]{1,0:T(8,128)S(1)}, u32[]{:S(2)}, u32[]{:S(2)}) collective-permute-start(f32[64,256]{1,0:T(8,128)S(1)} %get-tuple-element.5), channel_id=1, source_target_pairs={{0,4},{4,0},{8,12},{12,8},{16,20},{20,16},{24,28},{28,24},{1,5},{5... | collective-permute-start | bytes 196616 | tf_op jit(solution)/shard_map/ppermute | solution.py:115
  18.1 9.5 %collective-permute-start.1 = (f32[64,256]{1,0:T(8,128)S(1)}, f32[64,256]{1,0:T(8,128)S(1)}, u32[]{:S(2)}, u32[]{:S(2)}) collective-permute-start(f32[64,256]{1,0:T(8,128)S(1)} %get-tuple-element.11), channel_id=1, source_target_pairs={{0,8},{4,12},{8,0},{12,4},{16,24},{20,28},{24,16},{28,20},{1,9},{5... | collective-permute-start | bytes 196616 | tf_op jit(solution)/shard_map/ppermute | solution.py:115
  19.7 7.9 %collective-permute-start.2 = (f32[64,256]{1,0:T(8,128)S(1)}, f32[64,256]{1,0:T(8,128)S(1)}, u32[]{:S(2)}, u32[]{:S(2)}) collective-permute-start(f32[64,256]{1,0:T(8,128)S(1)} %get-tuple-element.10), channel_id=1, source_target_pairs={{0,12},{4,8},{8,4},{12,0},{16,28},{20,24},{24,20},{28,16},{1,13},{... | collective-permute-start | bytes 196616 | tf_op jit(solution)/shard_map/ppermute | solution.py:115
  19.7 7.9 %collective-permute-start.3 = (f32[64,256]{1,0:T(8,128)S(1)}, f32[64,256]{1,0:T(8,128)S(1)}, u32[]{:S(2)}, u32[]{:S(2)}) collective-permute-start(f32[64,256]{1,0:T(8,128)S(1)} %get-tuple-element.9), channel_id=1, source_target_pairs={{0,16},{4,20},{8,24},{12,28},{16,0},{20,4},{24,8},{28,12},{1,17},{... | collective-permute-start | bytes 196616 | tf_op jit(solution)/shard_map/ppermute | solution.py:115
  22.7 10.2 %collective-permute-start.4 = (f32[64,256]{1,0:T(8,128)S(1)}, f32[64,256]{1,0:T(8,128)S(1)}, u32[]{:S(2)}, u32[]{:S(2)}) collective-permute-start(f32[64,256]{1,0:T(8,128)S(1)} %get-tuple-element.8), channel_id=1, source_target_pairs={{0,20},{4,16},{8,28},{12,24},{16,4},{20,0},{24,12},{28,8},{1,21},{... | collective-permute-start | bytes 196616 | tf_op jit(solution)/shard_map/ppermute | solution.py:115
  24.0 8.9 %collective-permute-start.5 = (f32[64,256]{1,0:T(8,128)S(1)}, f32[64,256]{1,0:T(8,128)S(1)}, u32[]{:S(2)}, u32[]{:S(2)}) collective-permute-start(f32[64,256]{1,0:T(8,128)S(1)} %get-tuple-element.7), channel_id=1, source_target_pairs={{0,24},{4,28},{8,16},{12,20},{16,8},{20,12},{24,0},{28,4},{1,25},{... | collective-permute-start | bytes 196616 | tf_op jit(solution)/shard_map/ppermute | solution.py:115
  27.6 7.1 %collective-permute-start.6 = (f32[64,256]{1,0:T(8,128)S(1)}, f32[64,256]{1,0:T(8,128)S(1)}, u32[]{:S(2)}, u32[]{:S(2)}) collective-permute-start(f32[64,256]{1,0:T(8,128)S(1)} %get-tuple-element.6), channel_id=1, source_target_pairs={{0,28},{4,24},{8,20},{12,16},{16,12},{20,8},{24,4},{28,0},{1,29},{... | collective-permute-start | bytes 196616 | tf_op jit(solution)/shard_map/ppermute | solution.py:115
  41.7 4.4 %collective-permute-start.7 = (f32[64,256]{1,0:T(8,128)S(1)}, f32[64,256]{1,0:T(8,128)S(1)}, u32[]{:S(2)}, u32[]{:S(2)}) collective-permute-start(f32[64,256]{1,0:T(8,128)S(1)} %fusion.13), channel_id=1, source_target_pairs={{0,4},{4,0},{8,12},{12,8},{16,20},{20,16},{24,28},{28,24},{1,5},{5... | collective-permute-start | bytes 196616 | tf_op jit(solution)/shard_map/ppermute | solution.py:36
  42.3 4.3 %collective-permute-start.8 = (f32[64,256]{1,0:T(8,128)S(1)}, f32[64,256]{1,0:T(8,128)S(1)}, u32[]{:S(2)}, u32[]{:S(2)}) collective-permute-start(f32[64,256]{1,0:T(8,128)S(1)} %fusion.13), channel_id=1, source_target_pairs={{0,8},{4,12},{8,0},{12,4},{16,24},{20,28},{24,16},{28,20},{1,9},{5... | collective-permute-start | bytes 196616 | tf_op jit(solution)/shard_map/ppermute | solution.py:36
  44.2 5.2 %collective-permute-start.9 = (f32[64,256]{1,0:T(8,128)S(1)}, f32[64,256]{1,0:T(8,128)S(1)}, u32[]{:S(2)}, u32[]{:S(2)}) collective-permute-start(f32[64,256]{1,0:T(8,128)S(1)} %fusion.13), channel_id=1, source_target_pairs={{0,12},{4,8},{8,4},{12,0},{16,28},{20,24},{24,20},{28,16},{1,13},{... | collective-permute-start | bytes 196616 | tf_op jit(solution)/shard_map/ppermute | solution.py:36
  49.4 5.9 %collective-permute-start.10 = (f32[64,256]{1,0:T(8,128)S(1)}, f32[64,256]{1,0:T(8,128)S(1)}, u32[]{:S(2)}, u32[]{:S(2)}) collective-permute-start(f32[64,256]{1,0:T(8,128)S(1)} %add_add_fusion), channel_id=1, source_target_pairs={{0,16},{4,20},{8,24},{12,28},{16,0},{20,4},{24,8},{28,12},{1,17},{... | collective-permute-start | bytes 196616 | tf_op jit(solution)/shard_map/ppermute | solution.py:36

commit v14 on v11

--- a/solution.py
+++ b/solution.py
@@ -3,6 +3,7 @@
 import jax
 import jax.numpy as jnp
 from jax import lax
+from jax.experimental import pallas as pl
 from jax.sharding import PartitionSpec as P
 
 STRIDE = 64
@@ -38,24 +39,24 @@
     return values[0]
 
 
-def split3(value):
-    hi = lax.reduce_precision(value, exponent_bits=8, mantissa_bits=7)
-    rest = value - hi
-    mid = lax.reduce_precision(rest, exponent_bits=8, mantissa_bits=7)
-    low = rest - mid
-    return tuple(piece.astype(jnp.bfloat16) for piece in (hi, mid, low))
+def gather_kernel(full_ref, index_ref, out_ref):
+    out_ref[...] = jnp.take_along_axis(full_ref[...], index_ref[...], axis=1)
 
 
-def selection(offsets, my_index, groups, inner):
-    per_row = inner // STRIDE
-    off = offsets.reshape(groups, OUTER, per_row)
-    rows = jnp.arange(per_row, dtype=jnp.int32)[None, None, :] * STRIDE + off
-    rows = rows.transpose(1, 0, 2)
-    lanes = jnp.arange(inner, dtype=jnp.int32)
-    parity = lax.population_count(rows[:, None, :, :] & lanes[None, :, None, None]) & 1
-    group_parity = lax.population_count(jnp.arange(groups, dtype=jnp.int32) & my_index) & 1
-    parity = parity ^ group_parity[None, None, :, None]
-    return (1 - 2 * parity).astype(jnp.bfloat16).reshape(OUTER, inner, groups * per_row)
+def pick_lanes(full, index):
+    rows, lanes = full.shape
+    block = 1024
+    tiled = jnp.tile(index, (block // index.shape[0], 1))
+    return pl.pallas_call(
+        gather_kernel,
+        out_shape=jax.ShapeDtypeStruct((rows, lanes), full.dtype),
+        grid=(rows // block,),
+        in_specs=[
+            pl.BlockSpec((block, lanes), lambda i: (i, 0)),
+            pl.BlockSpec((block, lanes), lambda i: (0, 0)),
+        ],
+        out_specs=pl.BlockSpec((block, lanes), lambda i: (i, 0)),
+    )(full, tiled)
 
 
 def per_device(panel, signs, offsets):
@@ -70,21 +71,25 @@
     signed = panel * signs.astype(jnp.bfloat16)[None, :]
     blocks = signed.reshape(columns, OUTER, inner)
     first = jnp.einsum(
-        "xa,cab->xcb",
+        "xa,cab->cxb",
         hadamard(OUTER).astype(jnp.bfloat16),
         blocks,
         preferred_element_type=jnp.float32,
     )
-    pick = selection(offsets, my_index, groups, inner)
-    sampled = jnp.einsum(
-        "xcb,xbj->xcj",
-        first,
-        pick.astype(jnp.float32),
+    full = jnp.dot(
+        first.reshape(columns * OUTER, inner),
+        hadamard(inner),
         precision=lax.Precision.HIGH,
         preferred_element_type=jnp.float32,
     )
-    chunks = sampled.reshape(OUTER, columns, groups, per_row).transpose(2, 1, 0, 3)
-    chunks = chunks.reshape(groups, columns, OUTER * per_row)
+    width = groups * per_row
+    off = offsets.reshape(groups, OUTER, per_row).transpose(1, 0, 2)
+    wanted = (jnp.arange(per_row, dtype=jnp.int32)[None, None, :] * STRIDE + off).reshape(OUTER, width)
+    wanted = jnp.pad(wanted, ((0, 0), (0, inner - width)))
+    picked = pick_lanes(full, wanted).reshape(columns, OUTER, inner)[:, :, :width]
+    flip = (1 - 2 * (lax.population_count(jnp.arange(groups, dtype=jnp.int32) & my_index) & 1)).astype(jnp.float32)
+    picked = picked.reshape(columns, OUTER, groups, per_row) * flip[None, None, :, None]
+    chunks = picked.transpose(2, 0, 1, 3).reshape(groups, columns, OUTER * per_row)
     own = lax.dynamic_index_in_dim(chunks, my_index, axis=0, keepdims=False)
     arrived = []
     for distance in range(1, groups):

time: 53.3 us -> 60.9 us (1.14)
  Pallas kernels: 0 us -> 8.18 us
  matrix products: 9.4 us -> 4.55 us
  local copies, waits for them, and re-layouts: 2.91 us -> 6.9 us
    pallas_call x0 -> x1, Pallas kernels: none -> 8.18 us  [pick_lanes(): pl.pallas_call(gather_kernel, out_shape=jax.ShapeDtypeStruct((rows, lanes...]
    dot_general x2, matrix products: 9.04 us -> 4.19 us  [the longest x1 3.44 us: per_device(): jnp.dot(first.reshape(columns * OUTER, inner), hadamard(inner), precision...]
    unnamed x3 -> x5, local copies, waits for them, and re-layouts: 0.58 us -> 3.53 us
    another operation x0 -> x1, local copies, waits for them, and re-layouts: none -> 0.86 us  [pick_lanes(): tiled = jnp.tile(index, (block // index.shape[0], 1))]
where the time goes in v14:
time: 60.9 us; the launch traced here: 60.5 us
  starting transfers between devices  19.2 us (32%)
  waiting for transfers between devices  12.2 us (20%)
  Pallas kernels  8.18 us (13%)
  local copies, waits for them, and re-layouts  6.9 us (11%)
  blocking collectives  5.79 us (10%)
  matrix products  4.55 us (7%)
  other arithmetic  3.54 us (6%)
    ppermute x7, starting transfers between devices, per_device(): arrived.append(lax.ppermute(block, 'ev', pairs))  12.9 us
    pallas_call x1, Pallas kernels, pick_lanes(): pl.pallas_call(gather_kernel, out_shape=jax.ShapeDtypeStruct((rows, lanes...  8.18 us
    ppermute x4, waiting for transfers between devices, group_sum(): values.append(lax.ppermute(value, 'ev', pairs))  7.52 us
    ppermute x4, starting transfers between devices, group_sum(): values.append(lax.ppermute(value, 'ev', pairs))  6.3 us
    all_gather x1, blocking collectives, per_device(): lax.all_gather(sketch, 'col', axis=0, tiled=True)  5.79 us
    ppermute x7, waiting for transfers between devices, per_device(): arrived.append(lax.ppermute(block, 'ev', pairs))  4.64 us
    unnamed x5, local copies, waits for them, and re-layouts  3.53 us
    dot_general x1, matrix products, per_device(): jnp.dot(first.reshape(columns * OUTER, inner), hadamard(inner), precision...  3.44 us
  transfers between devices with their start and end apart: 11, of which 7 were waited for; matrix products, arithmetic and copies ran while one was open for 1% of the time, Pallas kernels for 0%

profile of v14, /device:TPU:0, one launch (start us, length us, event | category | flops | bytes accessed | tf_op | source)
XLA Modules:
  0.0 60.5 jit_solution(125285608148099450)
XLA Ops:
  0.0 0.8 %convert_element_type.19 = bf16[16384]{0:T(1024)(128)(2,1)S(1)} convert(s32[16384]{0:T(1024)} %param.4) | non-fusion elementwise | flops 16384 | bytes 98304 | tf_op jit(solution)/shard_map/convert_element_type | solution.py:71
  0.9 1.9 %multiply_bitcast_fusion = bf16[8,8,128,128]{3,1,2,0:T(8,128)(2,1)S(1)} fusion(bf16[64,16384]{1,0:T(8,128)(2,1)} %param.3, bf16[16384]{0:T(1024)(128)(2,1)S(1)} %convert_element_type.19), kind=kLoop, calls=%fused_computation | loop fusion | flops 1048576 | bytes 4227072
  3.3 0.7 %fusion.11 = f32[64,128,128]{1,2,0:T(8,128)S(1)} fusion(bf16[64,128,128]{2,1,0:T(8,128)(2,1)S(1)} %bitcast.48), kind=kOutput, calls=%fused_computation.19 | convolution fusion | flops 269025280 | bytes 6291456 | tf_op jit(solution)/shard_map/xa,cab->cxb/dot_general | solution.py:73
  4.1 3.4 %fusion.14.full_ref = f32[8192,128]{1,0:T(8,128)} fusion(f32[8192,128]{1,0:T(8,128)S(1)} %bitcast.47), kind=kOutput, calls=%fused_computation.22 | convolution fusion | flops 805879808 | bytes 8388608 | tf_op jit(solution)/shard_map/dot_general | solution.py:79
  8.3 0.9 %tile.4 = s32[8,128,128]{2,1,0:T(8,128)} broadcast(s32[128,128]{1,0:T(8,128)S(1)} %pad.4.clone), dimensions={1,2} | broadcast | bytes 589824 | tf_op jit(solution)/shard_map/tile | solution.py:49
  9.2 8.2 %shard_map.37 = f32[8192,128]{1,0:T(8,128)} custom-call(f32[8192,128]{1,0:T(8,128)} %fusion.14.full_ref, s32[1024,128]{1,0:T(8,128)} %bitcast.50), custom_call_target="tpu_custom_call" | custom-call | tf_op jit(solution)/shard_map/pallas_call | solution.py:50
  17.4 2.9 %copy.24 = f32[64,128,16]{1,0,2:T(8,128)S(1)} copy(f32[64,128,16]{2,1,0:T(8,128)} %bitcast.46) | data formatting | bytes 1048576
  20.9 0.7 %constant_dynamic-slice_fusion.7 = (f32[1,64,256]{1,0,2:T(1,128)S(1)}, f32[1,64,256]{1,0,2:T(1,128)S(1)}, f32[1,64,256]{1,0,2:T(1,128)S(1)}, f32[1,64,256]{1,0,2...) fusion(f32[8,64,256]{1,0,2:T(8,128)S(1)} %bitcast.49, ...), kind=kLoop, calls=%fused_computation.31 | loop fusion | bytes 1048608 | tf_op jit(solution)/shard_map/jit(dynamic_index_in_dim)/dynamic_slice | solution.py:93
  21.7 6.1 %collective-permute-start.6 = (f32[64,256]{1,0:T(8,128)S(1)}, f32[64,256]{1,0:T(8,128)S(1)}, u32[]{:S(2)}, u32[]{:S(2)}) collective-permute-start(f32[64,256]{1,0:T(8,128)S(1)} %bitcast.58), channel_id=1, source_target_pairs={{0,28},{4,24},{8,20},{12,16},{16,12},{20,8},{24,4},{28,0},{1,29},{... | collective-permute-start | bytes 196616 | tf_op jit(solution)/shard_map/ppermute | solution.py:99
  28.3 0.8 %collective-permute-start.4 = (f32[64,256]{1,0:T(8,128)S(1)}, f32[64,256]{1,0:T(8,128)S(1)}, u32[]{:S(2)}, u32[]{:S(2)}) collective-permute-start(f32[64,256]{1,0:T(8,128)S(1)} %bitcast.52), channel_id=1, source_target_pairs={{0,20},{4,16},{8,28},{12,24},{16,4},{20,0},{24,12},{28,8},{1,21},{... | collective-permute-start | bytes 196616 | tf_op jit(solution)/shard_map/ppermute | solution.py:99
  29.2 2.0 %collective-permute-start.3 = (f32[64,256]{1,0:T(8,128)S(1)}, f32[64,256]{1,0:T(8,128)S(1)}, u32[]{:S(2)}, u32[]{:S(2)}) collective-permute-start(f32[64,256]{1,0:T(8,128)S(1)} %bitcast.53), channel_id=1, source_target_pairs={{0,16},{4,20},{8,24},{12,28},{16,0},{20,4},{24,8},{28,12},{1,17},{... | collective-permute-start | bytes 196616 | tf_op jit(solution)/shard_map/ppermute | solution.py:99
  31.3 2.4 %collective-permute-start.2 = (f32[64,256]{1,0:T(8,128)S(1)}, f32[64,256]{1,0:T(8,128)S(1)}, u32[]{:S(2)}, u32[]{:S(2)}) collective-permute-start(f32[64,256]{1,0:T(8,128)S(1)} %bitcast.54), channel_id=1, source_target_pairs={{0,12},{4,8},{8,4},{12,0},{16,28},{20,24},{24,20},{28,16},{1,13},{... | collective-permute-start | bytes 196616 | tf_op jit(solution)/shard_map/ppermute | solution.py:99
  33.9 0.8 %collective-permute-start.1 = (f32[64,256]{1,0:T(8,128)S(1)}, f32[64,256]{1,0:T(8,128)S(1)}, u32[]{:S(2)}, u32[]{:S(2)}) collective-permute-start(f32[64,256]{1,0:T(8,128)S(1)} %bitcast.57), channel_id=1, source_target_pairs={{0,8},{4,12},{8,0},{12,4},{16,24},{20,28},{24,16},{28,20},{1,9},{5... | collective-permute-start | bytes 196616 | tf_op jit(solution)/shard_map/ppermute | solution.py:99
  35.2 1.9 %collective-permute-done.4 = f32[64,256]{1,0:T(8,128)S(1)} collective-permute-done((f32[64,256]{1,0:T(8,128)S(1)}, f32[64,256]{1,0:T(8,128)S(1)}, u32[]{:S(2)}, u32[]{:S(2)}) %collective-permute-start.4) | collective-permute-done | bytes 65568 | tf_op jit(solution)/shard_map/ppermute | solution.py:99
  37.1 2.0 %collective-permute-done.3 = f32[64,256]{1,0:T(8,128)S(1)} collective-permute-done((f32[64,256]{1,0:T(8,128)S(1)}, f32[64,256]{1,0:T(8,128)S(1)}, u32[]{:S(2)}, u32[]{:S(2)}) %collective-permute-start.3) | collective-permute-done | bytes 65568 | tf_op jit(solution)/shard_map/ppermute | solution.py:99
  39.9 5.8 %all_gather.3 = f32[256,256]{1,0:T(8,128)S(1)} all-gather(f32[64,256]{1,0:T(8,128)S(1)} %fusion.10), channel_id=1, replica_groups=mesh['ev'=8,'col'=4] {'col'}, dimensions={0}, use_global_device_ids=true | all-gather | bytes 327680 | tf_op jit(solution)/shard_map/all_gather | solution.py:109
  46.0 1.2 %collective-permute-start.8 = (f32[64,256]{1,0:T(8,128)S(1)}, f32[64,256]{1,0:T(8,128)S(1)}, u32[]{:S(2)}, u32[]{:S(2)}) collective-permute-start(f32[64,256]{1,0:T(8,128)S(1)} %fusion.31), channel_id=1, source_target_pairs={{0,8},{4,12},{8,0},{12,4},{16,24},{20,28},{24,16},{28,20},{1,9},{5... | collective-permute-start | bytes 196616 | tf_op jit(solution)/shard_map/ppermute | solution.py:36
  47.2 1.1 %collective-permute-start.9 = (f32[64,256]{1,0:T(8,128)S(1)}, f32[64,256]{1,0:T(8,128)S(1)}, u32[]{:S(2)}, u32[]{:S(2)}) collective-permute-start(f32[64,256]{1,0:T(8,128)S(1)} %fusion.31), channel_id=1, source_target_pairs={{0,12},{4,8},{8,4},{12,0},{16,28},{20,24},{24,20},{28,16},{1,13},{... | collective-permute-start | bytes 196616 | tf_op jit(solution)/shard_map/ppermute | solution.py:36
  48.3 1.3 %collective-permute-start.7 = (f32[64,256]{1,0:T(8,128)S(1)}, f32[64,256]{1,0:T(8,128)S(1)}, u32[]{:S(2)}, u32[]{:S(2)}) collective-permute-start(f32[64,256]{1,0:T(8,128)S(1)} %fusion.31), channel_id=1, source_target_pairs={{0,4},{4,0},{8,12},{12,8},{16,20},{20,16},{24,28},{28,24},{1,5},{5... | collective-permute-start | bytes 196616 | tf_op jit(solution)/shard_map/ppermute | solution.py:36
  49.6 1.4 %collective-permute-done.8 = f32[64,256]{1,0:T(8,128)S(1)} collective-permute-done((f32[64,256]{1,0:T(8,128)S(1)}, f32[64,256]{1,0:T(8,128)S(1)}, u32[]{:S(2)}, u32[]{:S(2)}) %collective-permute-start.8) | collective-permute-done | bytes 65568 | tf_op jit(solution)/shard_map/ppermute | solution.py:36
  51.0 1.5 %collective-permute-done.9 = f32[64,256]{1,0:T(8,128)S(1)} collective-permute-done((f32[64,256]{1,0:T(8,128)S(1)}, f32[64,256]{1,0:T(8,128)S(1)}, u32[]{:S(2)}, u32[]{:S(2)}) %collective-permute-start.9) | collective-permute-done | bytes 65568 | tf_op jit(solution)/shard_map/ppermute | solution.py:36
  52.4 1.0 %collective-permute-done.7 = f32[64,256]{1,0:T(8,128)S(1)} collective-permute-done((f32[64,256]{1,0:T(8,128)S(1)}, f32[64,256]{1,0:T(8,128)S(1)}, u32[]{:S(2)}, u32[]{:S(2)}) %collective-permute-start.7) | collective-permute-done | bytes 65568 | tf_op jit(solution)/shard_map/ppermute | solution.py:36
  53.5 2.8 %collective-permute-start.10 = (f32[64,256]{1,0:T(8,128)S(1)}, f32[64,256]{1,0:T(8,128)S(1)}, u32[]{:S(2)}, u32[]{:S(2)}) collective-permute-start(f32[64,256]{1,0:T(8,128)S(1)} %add_add_fusion), channel_id=1, source_target_pairs={{0,16},{4,20},{8,24},{12,28},{16,0},{20,4},{24,8},{28,12},{1,17},{... | collective-permute-start | bytes 196616 | tf_op jit(solution)/shard_map/ppermute | solution.py:36
  56.3 3.6 %collective-permute-done.10 = f32[64,256]{1,0:T(8,128)S(1)} collective-permute-done((f32[64,256]{1,0:T(8,128)S(1)}, f32[64,256]{1,0:T(8,128)S(1)}, u32[]{:S(2)}, u32[]{:S(2)}) %collective-permute-start.10) | collective-permute-done | bytes 65568 | tf_op jit(solution)/shard_map/ppermute | solution.py:36
  (31 shorter events, 5.1 us)
Async XLA Ops:
  4.0 3.5 %copy-start = (s32[2048]{0:T(1024)S(1)}, s32[2048]{0:T(1024)}, u32[]{:S(2)}) copy-start(s32[2048]{0:T(1024)} %param.5) | copy-start | bytes 24580
  21.7 12.2 %collective-permute-start.6 = (f32[64,256]{1,0:T(8,128)S(1)}, f32[64,256]{1,0:T(8,128)S(1)}, u32[]{:S(2)}, u32[]{:S(2)}) collective-permute-start(f32[64,256]{1,0:T(8,128)S(1)} %bitcast.58), channel_id=1, source_target_pairs={{0,28},{4,24},{8,20},{12,16},{16,12},{20,8},{24,4},{28,0},{1,29},{... | collective-permute-start | bytes 196616 | tf_op jit(solution)/shard_map/ppermute | solution.py:99
  27.9 6.8 %collective-permute-start.5 = (f32[64,256]{1,0:T(8,128)S(1)}, f32[64,256]{1,0:T(8,128)S(1)}, u32[]{:S(2)}, u32[]{:S(2)}) collective-permute-start(f32[64,256]{1,0:T(8,128)S(1)} %bitcast.56), channel_id=1, source_target_pairs={{0,24},{4,28},{8,16},{12,20},{16,8},{20,12},{24,0},{28,4},{1,25},{... | collective-permute-start | bytes 196616 | tf_op jit(solution)/shard_map/ppermute | solution.py:99
  28.3 8.8 %collective-permute-start.4 = (f32[64,256]{1,0:T(8,128)S(1)}, f32[64,256]{1,0:T(8,128)S(1)}, u32[]{:S(2)}, u32[]{:S(2)}) collective-permute-start(f32[64,256]{1,0:T(8,128)S(1)} %bitcast.52), channel_id=1, source_target_pairs={{0,20},{4,16},{8,28},{12,24},{16,4},{20,0},{24,12},{28,8},{1,21},{... | collective-permute-start | bytes 196616 | tf_op jit(solution)/shard_map/ppermute | solution.py:99
  29.2 9.9 %collective-permute-start.3 = (f32[64,256]{1,0:T(8,128)S(1)}, f32[64,256]{1,0:T(8,128)S(1)}, u32[]{:S(2)}, u32[]{:S(2)}) collective-permute-start(f32[64,256]{1,0:T(8,128)S(1)} %bitcast.53), channel_id=1, source_target_pairs={{0,16},{4,20},{8,24},{12,28},{16,0},{20,4},{24,8},{28,12},{1,17},{... | collective-permute-start | bytes 196616 | tf_op jit(solution)/shard_map/ppermute | solution.py:99
  31.3 7.8 %collective-permute-start.2 = (f32[64,256]{1,0:T(8,128)S(1)}, f32[64,256]{1,0:T(8,128)S(1)}, u32[]{:S(2)}, u32[]{:S(2)}) collective-permute-start(f32[64,256]{1,0:T(8,128)S(1)} %bitcast.54), channel_id=1, source_target_pairs={{0,12},{4,8},{8,4},{12,0},{16,28},{20,24},{24,20},{28,16},{1,13},{... | collective-permute-start | bytes 196616 | tf_op jit(solution)/shard_map/ppermute | solution.py:99
  33.9 5.9 %collective-permute-start.1 = (f32[64,256]{1,0:T(8,128)S(1)}, f32[64,256]{1,0:T(8,128)S(1)}, u32[]{:S(2)}, u32[]{:S(2)}) collective-permute-start(f32[64,256]{1,0:T(8,128)S(1)} %bitcast.57), channel_id=1, source_target_pairs={{0,8},{4,12},{8,0},{12,4},{16,24},{20,28},{24,16},{28,20},{1,9},{5... | collective-permute-start | bytes 196616 | tf_op jit(solution)/shard_map/ppermute | solution.py:99
  34.7 5.1 %collective-permute-start = (f32[64,256]{1,0:T(8,128)S(1)}, f32[64,256]{1,0:T(8,128)S(1)}, u32[]{:S(2)}, u32[]{:S(2)}) collective-permute-start(f32[64,256]{1,0:T(8,128)S(1)} %bitcast.55), channel_id=1, source_target_pairs={{0,4},{4,0},{8,12},{12,8},{16,20},{20,16},{24,28},{28,24},{1,5},{5... | collective-permute-start | bytes 196616 | tf_op jit(solution)/shard_map/ppermute | solution.py:99
  46.0 5.0 %collective-permute-start.8 = (f32[64,256]{1,0:T(8,128)S(1)}, f32[64,256]{1,0:T(8,128)S(1)}, u32[]{:S(2)}, u32[]{:S(2)}) collective-permute-start(f32[64,256]{1,0:T(8,128)S(1)} %fusion.31), channel_id=1, source_target_pairs={{0,8},{4,12},{8,0},{12,4},{16,24},{20,28},{24,16},{28,20},{1,9},{5... | collective-permute-start | bytes 196616 | tf_op jit(solution)/shard_map/ppermute | solution.py:36
  47.2 5.2 %collective-permute-start.9 = (f32[64,256]{1,0:T(8,128)S(1)}, f32[64,256]{1,0:T(8,128)S(1)}, u32[]{:S(2)}, u32[]{:S(2)}) collective-permute-start(f32[64,256]{1,0:T(8,128)S(1)} %fusion.31), channel_id=1, source_target_pairs={{0,12},{4,8},{8,4},{12,0},{16,28},{20,24},{24,20},{28,16},{1,13},{... | collective-permute-start | bytes 196616 | tf_op jit(solution)/shard_map/ppermute | solution.py:36
  48.3 5.2 %collective-permute-start.7 = (f32[64,256]{1,0:T(8,128)S(1)}, f32[64,256]{1,0:T(8,128)S(1)}, u32[]{:S(2)}, u32[]{:S(2)}) collective-permute-start(f32[64,256]{1,0:T(8,128)S(1)} %fusion.31), channel_id=1, source_target_pairs={{0,4},{4,0},{8,12},{12,8},{16,20},{20,16},{24,28},{28,24},{1,5},{5... | collective-permute-start | bytes 196616 | tf_op jit(solution)/shard_map/ppermute | solution.py:36
  53.5 6.3 %collective-permute-start.10 = (f32[64,256]{1,0:T(8,128)S(1)}, f32[64,256]{1,0:T(8,128)S(1)}, u32[]{:S(2)}, u32[]{:S(2)}) collective-permute-start(f32[64,256]{1,0:T(8,128)S(1)} %add_add_fusion), channel_id=1, source_target_pairs={{0,16},{4,20},{8,24},{12,28},{16,0},{20,4},{24,8},{28,12},{1,17},{... | collective-permute-start | bytes 196616 | tf_op jit(solution)/shard_map/ppermute | solution.py:36

commit v15 on v11

--- a/solution.py
+++ b/solution.py
@@ -70,14 +70,14 @@
     signed = panel * signs.astype(jnp.bfloat16)[None, :]
     blocks = signed.reshape(columns, OUTER, inner)
     first = jnp.einsum(
-        "xa,cab->xcb",
+        "xa,cab->cxb",
         hadamard(OUTER).astype(jnp.bfloat16),
         blocks,
         preferred_element_type=jnp.float32,
     )
     pick = selection(offsets, my_index, groups, inner)
     sampled = jnp.einsum(
-        "xcb,xbj->xcj",
+        "cxb,xbj->xcj",
         first,
         pick.astype(jnp.float32),
         precision=lax.Precision.HIGH,

time: 53.3 us -> 57 us (1.069)
  local copies, waits for them, and re-layouts: 2.91 us -> 8.31 us
  matrix products: 9.4 us -> 7.69 us
    transpose x0 -> x1, local copies, waits for them, and re-layouts: none -> 5.4 us  [per_device(): jnp.einsum('xa,cab->cxb', hadamard(OUTER).astype(jnp.bfloat16), blocks, p...]
    dot_general x2, matrix products: 9.04 us -> 7.33 us  [the longest x1 4.59 us: per_device(): jnp.einsum('cxb,xbj->xcj', first, pick.astype(jnp.float32), precision=lax...]
where the time goes in v15:
time: 57 us; the launch traced here: 56.7 us
  starting transfers between devices  19.2 us (34%)
  waiting for transfers between devices  12.2 us (21%)
  local copies, waits for them, and re-layouts  8.31 us (15%)
  matrix products  7.69 us (13%)
  blocking collectives  5.79 us (10%)
  other arithmetic  3.44 us (6%)
    ppermute x7, starting transfers between devices, per_device(): arrived.append(lax.ppermute(block, 'ev', pairs))  12.9 us
    ppermute x4, waiting for transfers between devices, group_sum(): values.append(lax.ppermute(value, 'ev', pairs))  7.52 us
    ppermute x4, starting transfers between devices, group_sum(): values.append(lax.ppermute(value, 'ev', pairs))  6.31 us
    all_gather x1, blocking collectives, per_device(): lax.all_gather(sketch, 'col', axis=0, tiled=True)  5.79 us
    transpose x1, local copies, waits for them, and re-layouts, per_device(): jnp.einsum('xa,cab->cxb', hadamard(OUTER).astype(jnp.bfloat16), blocks, p...  5.4 us
    ppermute x7, waiting for transfers between devices, per_device(): arrived.append(lax.ppermute(block, 'ev', pairs))  4.64 us
    dot_general x1, matrix products, per_device(): jnp.einsum('cxb,xbj->xcj', first, pick.astype(jnp.float32), precision=lax...  4.59 us
    dot_general x1, matrix products, per_device(): jnp.einsum('xa,cab->cxb', hadamard(OUTER).astype(jnp.bfloat16), blocks, p...  2.74 us
  transfers between devices with their start and end apart: 11, of which 7 were waited for; matrix products, arithmetic and copies ran while one was open for 1% of the time, Pallas kernels for 0%

profile of v15, /device:TPU:0, one launch (start us, length us, event | category | flops | bytes accessed | tf_op | source)
XLA Modules:
  0.0 56.7 jit_solution(17529206195576796089)
XLA Ops:
  0.0 0.8 %convert_element_type.14 = bf16[16384]{0:T(1024)(128)(2,1)S(1)} convert(s32[16384]{0:T(1024)} %param.4) | non-fusion elementwise | flops 16384 | bytes 98304 | tf_op jit(solution)/shard_map/convert_element_type | solution.py:70
  0.9 1.9 %multiply_bitcast_fusion = bf16[8,8,128,128]{3,1,2,0:T(8,128)(2,1)S(1)} fusion(bf16[64,16384]{1,0:T(8,128)(2,1)} %param.3, bf16[16384]{0:T(1024)(128)(2,1)S(1)} %convert_element_type.14), kind=kLoop, calls=%fused_computation.1 | loop fusion | flops 1048576 | bytes 4227072
  3.3 2.7 %convolution_bitcast_fusion = f32[64,128,128]{1,2,0:T(8,128)} fusion(bf16[64,128,128]{2,1,0:T(8,128)(2,1)S(1)} %bitcast.42), kind=kOutput, calls=%fused_computation | convolution fusion | flops 269025280 | bytes 6291456 | tf_op jit(solution)/shard_map/xa,cab->cxb/dot_general | solution.py:72
  6.0 5.4 %copy.15 = f32[64,128,128]{2,0,1:T(8,128)} copy(f32[64,128,128]{1,2,0:T(8,128)} %convolution_bitcast_fusion) | data formatting | bytes 8388608 | tf_op jit(solution)/shard_map/xa,cab->cxb/transpose | solution.py:72
  12.4 4.6 %fusion = f32[128,64,16]{1,2,0:T(8,128)S(1)} fusion(f32[64,128,128]{2,0,1:T(8,128)} %copy.15, s32[16]{0:T(128)S(1)} %xor.35, s32[128,16]{1,0:T(8,128)S(1)} %copy.14), kind=kOutput, calls=%fused_computation.3 | convolution fusion | flops 102498304 | bytes 4726848 | tf_op jit(solution)/shard_map/cxb,xbj->xcj/dot_general | solution.py:79
  17.1 0.7 %constant_dynamic-slice_fusion.7 = (f32[1,64,256]{1,0,2:T(1,128)S(1)}, f32[1,64,256]{1,0,2:T(1,128)S(1)}, f32[1,64,256]{1,0,2:T(1,128)S(1)}, f32[1,64,256]{1,0,2...) fusion(f32[8,64,256]{1,0,2:T(8,128)S(1)} %bitcast.43, ...), kind=kLoop, calls=%fused_computation.41 | loop fusion | bytes 1048608 | tf_op jit(solution)/shard_map/jit(dynamic_index_in_dim)/dynamic_slice | solution.py:88
  18.0 6.1 %collective-permute-start.6 = (f32[64,256]{1,0:T(8,128)S(1)}, f32[64,256]{1,0:T(8,128)S(1)}, u32[]{:S(2)}, u32[]{:S(2)}) collective-permute-start(f32[64,256]{1,0:T(8,128)S(1)} %bitcast.51), channel_id=1, source_target_pairs={{0,28},{4,24},{8,20},{12,16},{16,12},{20,8},{24,4},{28,0},{1,29},{... | collective-permute-start | bytes 196616 | tf_op jit(solution)/shard_map/ppermute | solution.py:94
  24.5 0.8 %collective-permute-start.4 = (f32[64,256]{1,0:T(8,128)S(1)}, f32[64,256]{1,0:T(8,128)S(1)}, u32[]{:S(2)}, u32[]{:S(2)}) collective-permute-start(f32[64,256]{1,0:T(8,128)S(1)} %bitcast.45), channel_id=1, source_target_pairs={{0,20},{4,16},{8,28},{12,24},{16,4},{20,0},{24,12},{28,8},{1,21},{... | collective-permute-start | bytes 196616 | tf_op jit(solution)/shard_map/ppermute | solution.py:94
  25.4 2.0 %collective-permute-start.3 = (f32[64,256]{1,0:T(8,128)S(1)}, f32[64,256]{1,0:T(8,128)S(1)}, u32[]{:S(2)}, u32[]{:S(2)}) collective-permute-start(f32[64,256]{1,0:T(8,128)S(1)} %bitcast.46), channel_id=1, source_target_pairs={{0,16},{4,20},{8,24},{12,28},{16,0},{20,4},{24,8},{28,12},{1,17},{... | collective-permute-start | bytes 196616 | tf_op jit(solution)/shard_map/ppermute | solution.py:94
  27.5 2.4 %collective-permute-start.2 = (f32[64,256]{1,0:T(8,128)S(1)}, f32[64,256]{1,0:T(8,128)S(1)}, u32[]{:S(2)}, u32[]{:S(2)}) collective-permute-start(f32[64,256]{1,0:T(8,128)S(1)} %bitcast.47), channel_id=1, source_target_pairs={{0,12},{4,8},{8,4},{12,0},{16,28},{20,24},{24,20},{28,16},{1,13},{... | collective-permute-start | bytes 196616 | tf_op jit(solution)/shard_map/ppermute | solution.py:94
  30.1 0.8 %collective-permute-start.1 = (f32[64,256]{1,0:T(8,128)S(1)}, f32[64,256]{1,0:T(8,128)S(1)}, u32[]{:S(2)}, u32[]{:S(2)}) collective-permute-start(f32[64,256]{1,0:T(8,128)S(1)} %bitcast.50), channel_id=1, source_target_pairs={{0,8},{4,12},{8,0},{12,4},{16,24},{20,28},{24,16},{28,20},{1,9},{5... | collective-permute-start | bytes 196616 | tf_op jit(solution)/shard_map/ppermute | solution.py:94
  31.4 1.9 %collective-permute-done.4 = f32[64,256]{1,0:T(8,128)S(1)} collective-permute-done((f32[64,256]{1,0:T(8,128)S(1)}, f32[64,256]{1,0:T(8,128)S(1)}, u32[]{:S(2)}, u32[]{:S(2)}) %collective-permute-start.4) | collective-permute-done | bytes 65568 | tf_op jit(solution)/shard_map/ppermute | solution.py:94
  33.3 2.0 %collective-permute-done.3 = f32[64,256]{1,0:T(8,128)S(1)} collective-permute-done((f32[64,256]{1,0:T(8,128)S(1)}, f32[64,256]{1,0:T(8,128)S(1)}, u32[]{:S(2)}, u32[]{:S(2)}) %collective-permute-start.3) | collective-permute-done | bytes 65568 | tf_op jit(solution)/shard_map/ppermute | solution.py:94
  35.3 0.7 %collective-permute-done.1 = f32[64,256]{1,0:T(8,128)S(1)} collective-permute-done((f32[64,256]{1,0:T(8,128)S(1)}, f32[64,256]{1,0:T(8,128)S(1)}, u32[]{:S(2)}, u32[]{:S(2)}) %collective-permute-start.1) | collective-permute-done | bytes 65568 | tf_op jit(solution)/shard_map/ppermute | solution.py:94
  36.1 5.8 %all_gather.3 = f32[256,256]{1,0:T(8,128)S(1)} all-gather(f32[64,256]{1,0:T(8,128)S(1)} %fusion.16), channel_id=1, replica_groups=mesh['ev'=8,'col'=4] {'col'}, dimensions={0}, use_global_device_ids=true | all-gather | bytes 327680 | tf_op jit(solution)/shard_map/all_gather | solution.py:104
  42.3 1.2 %collective-permute-start.8 = (f32[64,256]{1,0:T(8,128)S(1)}, f32[64,256]{1,0:T(8,128)S(1)}, u32[]{:S(2)}, u32[]{:S(2)}) collective-permute-start(f32[64,256]{1,0:T(8,128)S(1)} %fusion.35), channel_id=1, source_target_pairs={{0,8},{4,12},{8,0},{12,4},{16,24},{20,28},{24,16},{28,20},{1,9},{5... | collective-permute-start | bytes 196616 | tf_op jit(solution)/shard_map/ppermute | solution.py:35
  43.5 1.1 %collective-permute-start.9 = (f32[64,256]{1,0:T(8,128)S(1)}, f32[64,256]{1,0:T(8,128)S(1)}, u32[]{:S(2)}, u32[]{:S(2)}) collective-permute-start(f32[64,256]{1,0:T(8,128)S(1)} %fusion.35), channel_id=1, source_target_pairs={{0,12},{4,8},{8,4},{12,0},{16,28},{20,24},{24,20},{28,16},{1,13},{... | collective-permute-start | bytes 196616 | tf_op jit(solution)/shard_map/ppermute | solution.py:35
  44.5 1.3 %collective-permute-start.7 = (f32[64,256]{1,0:T(8,128)S(1)}, f32[64,256]{1,0:T(8,128)S(1)}, u32[]{:S(2)}, u32[]{:S(2)}) collective-permute-start(f32[64,256]{1,0:T(8,128)S(1)} %fusion.35), channel_id=1, source_target_pairs={{0,4},{4,0},{8,12},{12,8},{16,20},{20,16},{24,28},{28,24},{1,5},{5... | collective-permute-start | bytes 196616 | tf_op jit(solution)/shard_map/ppermute | solution.py:35
  45.8 1.4 %collective-permute-done.8 = f32[64,256]{1,0:T(8,128)S(1)} collective-permute-done((f32[64,256]{1,0:T(8,128)S(1)}, f32[64,256]{1,0:T(8,128)S(1)}, u32[]{:S(2)}, u32[]{:S(2)}) %collective-permute-start.8) | collective-permute-done | bytes 65568 | tf_op jit(solution)/shard_map/ppermute | solution.py:35
  47.2 1.5 %collective-permute-done.9 = f32[64,256]{1,0:T(8,128)S(1)} collective-permute-done((f32[64,256]{1,0:T(8,128)S(1)}, f32[64,256]{1,0:T(8,128)S(1)}, u32[]{:S(2)}, u32[]{:S(2)}) %collective-permute-start.9) | collective-permute-done | bytes 65568 | tf_op jit(solution)/shard_map/ppermute | solution.py:35
  48.7 1.0 %collective-permute-done.7 = f32[64,256]{1,0:T(8,128)S(1)} collective-permute-done((f32[64,256]{1,0:T(8,128)S(1)}, f32[64,256]{1,0:T(8,128)S(1)}, u32[]{:S(2)}, u32[]{:S(2)}) %collective-permute-start.7) | collective-permute-done | bytes 65568 | tf_op jit(solution)/shard_map/ppermute | solution.py:35
  49.7 2.8 %collective-permute-start.10 = (f32[64,256]{1,0:T(8,128)S(1)}, f32[64,256]{1,0:T(8,128)S(1)}, u32[]{:S(2)}, u32[]{:S(2)}) collective-permute-start(f32[64,256]{1,0:T(8,128)S(1)} %add_add_fusion), channel_id=1, source_target_pairs={{0,16},{4,20},{8,24},{12,28},{16,0},{20,4},{24,8},{28,12},{1,17},{... | collective-permute-start | bytes 196616 | tf_op jit(solution)/shard_map/ppermute | solution.py:35
  52.5 3.6 %collective-permute-done.10 = f32[64,256]{1,0:T(8,128)S(1)} collective-permute-done((f32[64,256]{1,0:T(8,128)S(1)}, f32[64,256]{1,0:T(8,128)S(1)}, u32[]{:S(2)}, u32[]{:S(2)}) %collective-permute-start.10) | collective-permute-done | bytes 65568 | tf_op jit(solution)/shard_map/ppermute | solution.py:35
  56.1 0.6 %add.117 = f32[64,256]{1,0:T(8,128)} add(f32[64,256]{1,0:T(8,128)S(1)} %add_add_fusion, f32[64,256]{1,0:T(8,128)S(1)} %collective-permute-done.10) | non-fusion elementwise | flops 16384 | bytes 196608 | tf_op jit(solution)/shard_map/add | solution.py:37
  (29 shorter events, 3.3 us)
Async XLA Ops:
  6.0 5.6 %copy-start = (s32[2048]{0:T(1024)S(1)}, s32[2048]{0:T(1024)}, u32[]{:S(2)}) copy-start(s32[2048]{0:T(1024)} %param.5) | copy-start | bytes 24580
  18.0 12.2 %collective-permute-start.6 = (f32[64,256]{1,0:T(8,128)S(1)}, f32[64,256]{1,0:T(8,128)S(1)}, u32[]{:S(2)}, u32[]{:S(2)}) collective-permute-start(f32[64,256]{1,0:T(8,128)S(1)} %bitcast.51), channel_id=1, source_target_pairs={{0,28},{4,24},{8,20},{12,16},{16,12},{20,8},{24,4},{28,0},{1,29},{... | collective-permute-start | bytes 196616 | tf_op jit(solution)/shard_map/ppermute | solution.py:94
  24.1 6.8 %collective-permute-start.5 = (f32[64,256]{1,0:T(8,128)S(1)}, f32[64,256]{1,0:T(8,128)S(1)}, u32[]{:S(2)}, u32[]{:S(2)}) collective-permute-start(f32[64,256]{1,0:T(8,128)S(1)} %bitcast.49), channel_id=1, source_target_pairs={{0,24},{4,28},{8,16},{12,20},{16,8},{20,12},{24,0},{28,4},{1,25},{... | collective-permute-start | bytes 196616 | tf_op jit(solution)/shard_map/ppermute | solution.py:94
  24.5 8.8 %collective-permute-start.4 = (f32[64,256]{1,0:T(8,128)S(1)}, f32[64,256]{1,0:T(8,128)S(1)}, u32[]{:S(2)}, u32[]{:S(2)}) collective-permute-start(f32[64,256]{1,0:T(8,128)S(1)} %bitcast.45), channel_id=1, source_target_pairs={{0,20},{4,16},{8,28},{12,24},{16,4},{20,0},{24,12},{28,8},{1,21},{... | collective-permute-start | bytes 196616 | tf_op jit(solution)/shard_map/ppermute | solution.py:94
  25.4 9.9 %collective-permute-start.3 = (f32[64,256]{1,0:T(8,128)S(1)}, f32[64,256]{1,0:T(8,128)S(1)}, u32[]{:S(2)}, u32[]{:S(2)}) collective-permute-start(f32[64,256]{1,0:T(8,128)S(1)} %bitcast.46), channel_id=1, source_target_pairs={{0,16},{4,20},{8,24},{12,28},{16,0},{20,4},{24,8},{28,12},{1,17},{... | collective-permute-start | bytes 196616 | tf_op jit(solution)/shard_map/ppermute | solution.py:94
  27.5 7.8 %collective-permute-start.2 = (f32[64,256]{1,0:T(8,128)S(1)}, f32[64,256]{1,0:T(8,128)S(1)}, u32[]{:S(2)}, u32[]{:S(2)}) collective-permute-start(f32[64,256]{1,0:T(8,128)S(1)} %bitcast.47), channel_id=1, source_target_pairs={{0,12},{4,8},{8,4},{12,0},{16,28},{20,24},{24,20},{28,16},{1,13},{... | collective-permute-start | bytes 196616 | tf_op jit(solution)/shard_map/ppermute | solution.py:94
  30.1 5.9 %collective-permute-start.1 = (f32[64,256]{1,0:T(8,128)S(1)}, f32[64,256]{1,0:T(8,128)S(1)}, u32[]{:S(2)}, u32[]{:S(2)}) collective-permute-start(f32[64,256]{1,0:T(8,128)S(1)} %bitcast.50), channel_id=1, source_target_pairs={{0,8},{4,12},{8,0},{12,4},{16,24},{20,28},{24,16},{28,20},{1,9},{5... | collective-permute-start | bytes 196616 | tf_op jit(solution)/shard_map/ppermute | solution.py:94
  31.0 5.1 %collective-permute-start = (f32[64,256]{1,0:T(8,128)S(1)}, f32[64,256]{1,0:T(8,128)S(1)}, u32[]{:S(2)}, u32[]{:S(2)}) collective-permute-start(f32[64,256]{1,0:T(8,128)S(1)} %bitcast.48), channel_id=1, source_target_pairs={{0,4},{4,0},{8,12},{12,8},{16,20},{20,16},{24,28},{28,24},{1,5},{5... | collective-permute-start | bytes 196616 | tf_op jit(solution)/shard_map/ppermute | solution.py:94
  42.3 5.0 %collective-permute-start.8 = (f32[64,256]{1,0:T(8,128)S(1)}, f32[64,256]{1,0:T(8,128)S(1)}, u32[]{:S(2)}, u32[]{:S(2)}) collective-permute-start(f32[64,256]{1,0:T(8,128)S(1)} %fusion.35), channel_id=1, source_target_pairs={{0,8},{4,12},{8,0},{12,4},{16,24},{20,28},{24,16},{28,20},{1,9},{5... | collective-permute-start | bytes 196616 | tf_op jit(solution)/shard_map/ppermute | solution.py:35
  43.5 5.2 %collective-permute-start.9 = (f32[64,256]{1,0:T(8,128)S(1)}, f32[64,256]{1,0:T(8,128)S(1)}, u32[]{:S(2)}, u32[]{:S(2)}) collective-permute-start(f32[64,256]{1,0:T(8,128)S(1)} %fusion.35), channel_id=1, source_target_pairs={{0,12},{4,8},{8,4},{12,0},{16,28},{20,24},{24,20},{28,16},{1,13},{... | collective-permute-start | bytes 196616 | tf_op jit(solution)/shard_map/ppermute | solution.py:35
  44.5 5.2 %collective-permute-start.7 = (f32[64,256]{1,0:T(8,128)S(1)}, f32[64,256]{1,0:T(8,128)S(1)}, u32[]{:S(2)}, u32[]{:S(2)}) collective-permute-start(f32[64,256]{1,0:T(8,128)S(1)} %fusion.35), channel_id=1, source_target_pairs={{0,4},{4,0},{8,12},{12,8},{16,20},{20,16},{24,28},{28,24},{1,5},{5... | collective-permute-start | bytes 196616 | tf_op jit(solution)/shard_map/ppermute | solution.py:35
  49.7 6.4 %collective-permute-start.10 = (f32[64,256]{1,0:T(8,128)S(1)}, f32[64,256]{1,0:T(8,128)S(1)}, u32[]{:S(2)}, u32[]{:S(2)}) collective-permute-start(f32[64,256]{1,0:T(8,128)S(1)} %add_add_fusion), channel_id=1, source_target_pairs={{0,16},{4,20},{8,24},{12,28},{16,0},{20,4},{24,8},{28,12},{1,17},{... | collective-permute-start | bytes 196616 | tf_op jit(solution)/shard_map/ppermute | solution.py:35

commit v16 on v11

--- a/solution.py
+++ b/solution.py
@@ -6,7 +6,7 @@
 from jax.sharding import PartitionSpec as P
 
 STRIDE = 64
-OUTER = 128
+OUTER = 64
 
 
 def hadamard(order):

time: 53.3 us -> 52.6 us (0.987)
    mul x0 -> x1, other arithmetic: none -> 1.85 us  [per_device(): signed = panel * signs.astype(jnp.bfloat16)[None, :]]
    unnamed x1 -> x0, other arithmetic: 1.85 us -> none
where the time goes in v16:
time: 52.6 us; the launch traced here: 52.4 us
  starting transfers between devices  19.2 us (37%)
  waiting for transfers between devices  12.2 us (23%)
  matrix products  9.08 us (17%)
  blocking collectives  5.79 us (11%)
  other arithmetic  3.42 us (7%)
  local copies, waits for them, and re-layouts  2.6 us (5%)
    ppermute x7, starting transfers between devices, per_device(): arrived.append(lax.ppermute(block, 'ev', pairs))  12.8 us
    ppermute x4, waiting for transfers between devices, group_sum(): values.append(lax.ppermute(value, 'ev', pairs))  7.52 us
    ppermute x4, starting transfers between devices, group_sum(): values.append(lax.ppermute(value, 'ev', pairs))  6.31 us
    dot_general x1, matrix products, per_device(): jnp.einsum('xcb,xbj->xcj', first, pick.astype(jnp.float32), precision=lax...  6.03 us
    all_gather x1, blocking collectives, per_device(): lax.all_gather(sketch, 'col', axis=0, tiled=True)  5.79 us
    ppermute x7, waiting for transfers between devices, per_device(): arrived.append(lax.ppermute(block, 'ev', pairs))  4.64 us
    dot_general x1, matrix products, per_device(): jnp.einsum('xa,cab->xcb', hadamard(OUTER).astype(jnp.bfloat16), blocks, p...  2.68 us
    mul x1, other arithmetic, per_device(): signed = panel * signs.astype(jnp.bfloat16)[None, :]  1.85 us
  transfers between devices with their start and end apart: 11, of which 7 were waited for; matrix products, arithmetic and copies ran while one was open for 1% of the time, Pallas kernels for 0%

profile of v16, /device:TPU:0, one launch (start us, length us, event | category | flops | bytes accessed | tf_op | source)
XLA Modules:
  0.0 52.4 jit_solution(9901148634769864523)
XLA Ops:
  0.0 0.8 %convert_element_type.16 = bf16[16384]{0:T(1024)(128)(2,1)S(1)} convert(s32[16384]{0:T(1024)} %param.4) | non-fusion elementwise | flops 16384 | bytes 98304 | tf_op jit(solution)/shard_map/convert_element_type | solution.py:70
  0.9 1.9 %broadcast_multiply_fusion = bf16[64,16384]{1,0:T(8,128)(2,1)S(1)} fusion(bf16[64,16384]{1,0:T(8,128)(2,1)} %param.3, bf16[16384]{0:T(1024)(128)(2,1)S(1)} %convert_element_type.16), kind=kLoop, calls=%fused_computation.7 | loop fusion | flops 1048576 | bytes 4227072 | tf_op jit(solution)/shard_map/mul | solution.py:70
  2.7 0.5 %copy.23 = bf16[8,8,64,256]{3,2,1,0:T(8,128)(2,1)S(1)} copy(bf16[8,8,64,256]{3,1,2,0:T(8,128)(2,1)S(1)} %bitcast.39) | data formatting | bytes 4194304
  3.3 2.7 %fusion.19 = f32[64,64,256]{2,0,1:T(8,128)} fusion(bf16[64,64,256]{2,1,0:T(8,128)(2,1)S(1)} %bitcast.38), kind=kOutput, calls=%fused_computation.27 | convolution fusion | flops 134352896 | bytes 6291456 | tf_op jit(solution)/shard_map/xa,cab->xcb/dot_general | solution.py:72
  6.6 6.0 %fusion = f32[64,64,32]{1,2,0:T(8,128)S(1)} fusion(f32[64,64,256]{2,0,1:T(8,128)} %fusion.19, s32[32]{0:T(128)S(1)} %xor.35, s32[64,32]{1,0:T(8,128)S(1)} %copy.12), kind=kOutput, calls=%fused_computation | convolution fusion | flops 204996608 | bytes 4726912 | tf_op jit(solution)/shard_map/xcb,xbj->xcj/dot_general | solution.py:79
  12.8 0.7 %constant_dynamic-slice_fusion.7 = (f32[1,64,256]{1,0,2:T(1,128)S(1)}, f32[1,64,256]{1,0,2:T(1,128)S(1)}, f32[1,64,256]{1,0,2:T(1,128)S(1)}, f32[1,64,256]{1,0,2...) fusion(f32[8,64,256]{1,0,2:T(8,128)S(1)} %bitcast.40, ...), kind=kLoop, calls=%fused_computation.41 | loop fusion | bytes 1048608 | tf_op jit(solution)/shard_map/jit(dynamic_index_in_dim)/dynamic_slice | solution.py:88
  13.6 6.1 %collective-permute-start.6 = (f32[64,256]{1,0:T(8,128)S(1)}, f32[64,256]{1,0:T(8,128)S(1)}, u32[]{:S(2)}, u32[]{:S(2)}) collective-permute-start(f32[64,256]{1,0:T(8,128)S(1)} %bitcast.48), channel_id=1, source_target_pairs={{0,28},{4,24},{8,20},{12,16},{16,12},{20,8},{24,4},{28,0},{1,29},{... | collective-permute-start | bytes 196616 | tf_op jit(solution)/shard_map/ppermute | solution.py:94
  20.2 0.8 %collective-permute-start.4 = (f32[64,256]{1,0:T(8,128)S(1)}, f32[64,256]{1,0:T(8,128)S(1)}, u32[]{:S(2)}, u32[]{:S(2)}) collective-permute-start(f32[64,256]{1,0:T(8,128)S(1)} %bitcast.42), channel_id=1, source_target_pairs={{0,20},{4,16},{8,28},{12,24},{16,4},{20,0},{24,12},{28,8},{1,21},{... | collective-permute-start | bytes 196616 | tf_op jit(solution)/shard_map/ppermute | solution.py:94
  21.0 2.0 %collective-permute-start.3 = (f32[64,256]{1,0:T(8,128)S(1)}, f32[64,256]{1,0:T(8,128)S(1)}, u32[]{:S(2)}, u32[]{:S(2)}) collective-permute-start(f32[64,256]{1,0:T(8,128)S(1)} %bitcast.43), channel_id=1, source_target_pairs={{0,16},{4,20},{8,24},{12,28},{16,0},{20,4},{24,8},{28,12},{1,17},{... | collective-permute-start | bytes 196616 | tf_op jit(solution)/shard_map/ppermute | solution.py:94
  23.2 2.4 %collective-permute-start.2 = (f32[64,256]{1,0:T(8,128)S(1)}, f32[64,256]{1,0:T(8,128)S(1)}, u32[]{:S(2)}, u32[]{:S(2)}) collective-permute-start(f32[64,256]{1,0:T(8,128)S(1)} %bitcast.44), channel_id=1, source_target_pairs={{0,12},{4,8},{8,4},{12,0},{16,28},{20,24},{24,20},{28,16},{1,13},{... | collective-permute-start | bytes 196616 | tf_op jit(solution)/shard_map/ppermute | solution.py:94
  25.8 0.8 %collective-permute-start.1 = (f32[64,256]{1,0:T(8,128)S(1)}, f32[64,256]{1,0:T(8,128)S(1)}, u32[]{:S(2)}, u32[]{:S(2)}) collective-permute-start(f32[64,256]{1,0:T(8,128)S(1)} %bitcast.47), channel_id=1, source_target_pairs={{0,8},{4,12},{8,0},{12,4},{16,24},{20,28},{24,16},{28,20},{1,9},{5... | collective-permute-start | bytes 196616 | tf_op jit(solution)/shard_map/ppermute | solution.py:94
  27.1 1.9 %collective-permute-done.4 = f32[64,256]{1,0:T(8,128)S(1)} collective-permute-done((f32[64,256]{1,0:T(8,128)S(1)}, f32[64,256]{1,0:T(8,128)S(1)}, u32[]{:S(2)}, u32[]{:S(2)}) %collective-permute-start.4) | collective-permute-done | bytes 65568 | tf_op jit(solution)/shard_map/ppermute | solution.py:94
  29.0 2.0 %collective-permute-done.3 = f32[64,256]{1,0:T(8,128)S(1)} collective-permute-done((f32[64,256]{1,0:T(8,128)S(1)}, f32[64,256]{1,0:T(8,128)S(1)}, u32[]{:S(2)}, u32[]{:S(2)}) %collective-permute-start.3) | collective-permute-done | bytes 65568 | tf_op jit(solution)/shard_map/ppermute | solution.py:94
  31.0 0.7 %collective-permute-done.1 = f32[64,256]{1,0:T(8,128)S(1)} collective-permute-done((f32[64,256]{1,0:T(8,128)S(1)}, f32[64,256]{1,0:T(8,128)S(1)}, u32[]{:S(2)}, u32[]{:S(2)}) %collective-permute-start.1) | collective-permute-done | bytes 65568 | tf_op jit(solution)/shard_map/ppermute | solution.py:94
  31.7 5.8 %all_gather.3 = f32[256,256]{1,0:T(8,128)S(1)} all-gather(f32[64,256]{1,0:T(8,128)S(1)} %fusion.12), channel_id=1, replica_groups=mesh['ev'=8,'col'=4] {'col'}, dimensions={0}, use_global_device_ids=true | all-gather | bytes 327680 | tf_op jit(solution)/shard_map/all_gather | solution.py:104
  37.9 1.2 %collective-permute-start.8 = (f32[64,256]{1,0:T(8,128)S(1)}, f32[64,256]{1,0:T(8,128)S(1)}, u32[]{:S(2)}, u32[]{:S(2)}) collective-permute-start(f32[64,256]{1,0:T(8,128)S(1)} %fusion.35), channel_id=1, source_target_pairs={{0,8},{4,12},{8,0},{12,4},{16,24},{20,28},{24,16},{28,20},{1,9},{5... | collective-permute-start | bytes 196616 | tf_op jit(solution)/shard_map/ppermute | solution.py:35
  39.1 1.1 %collective-permute-start.9 = (f32[64,256]{1,0:T(8,128)S(1)}, f32[64,256]{1,0:T(8,128)S(1)}, u32[]{:S(2)}, u32[]{:S(2)}) collective-permute-start(f32[64,256]{1,0:T(8,128)S(1)} %fusion.35), channel_id=1, source_target_pairs={{0,12},{4,8},{8,4},{12,0},{16,28},{20,24},{24,20},{28,16},{1,13},{... | collective-permute-start | bytes 196616 | tf_op jit(solution)/shard_map/ppermute | solution.py:35
  40.2 1.3 %collective-permute-start.7 = (f32[64,256]{1,0:T(8,128)S(1)}, f32[64,256]{1,0:T(8,128)S(1)}, u32[]{:S(2)}, u32[]{:S(2)}) collective-permute-start(f32[64,256]{1,0:T(8,128)S(1)} %fusion.35), channel_id=1, source_target_pairs={{0,4},{4,0},{8,12},{12,8},{16,20},{20,16},{24,28},{28,24},{1,5},{5... | collective-permute-start | bytes 196616 | tf_op jit(solution)/shard_map/ppermute | solution.py:35
  41.5 1.4 %collective-permute-done.8 = f32[64,256]{1,0:T(8,128)S(1)} collective-permute-done((f32[64,256]{1,0:T(8,128)S(1)}, f32[64,256]{1,0:T(8,128)S(1)}, u32[]{:S(2)}, u32[]{:S(2)}) %collective-permute-start.8) | collective-permute-done | bytes 65568 | tf_op jit(solution)/shard_map/ppermute | solution.py:35
  42.9 1.5 %collective-permute-done.9 = f32[64,256]{1,0:T(8,128)S(1)} collective-permute-done((f32[64,256]{1,0:T(8,128)S(1)}, f32[64,256]{1,0:T(8,128)S(1)}, u32[]{:S(2)}, u32[]{:S(2)}) %collective-permute-start.9) | collective-permute-done | bytes 65568 | tf_op jit(solution)/shard_map/ppermute | solution.py:35
  44.3 1.0 %collective-permute-done.7 = f32[64,256]{1,0:T(8,128)S(1)} collective-permute-done((f32[64,256]{1,0:T(8,128)S(1)}, f32[64,256]{1,0:T(8,128)S(1)}, u32[]{:S(2)}, u32[]{:S(2)}) %collective-permute-start.7) | collective-permute-done | bytes 65568 | tf_op jit(solution)/shard_map/ppermute | solution.py:35
  45.4 2.8 %collective-permute-start.10 = (f32[64,256]{1,0:T(8,128)S(1)}, f32[64,256]{1,0:T(8,128)S(1)}, u32[]{:S(2)}, u32[]{:S(2)}) collective-permute-start(f32[64,256]{1,0:T(8,128)S(1)} %add_add_fusion), channel_id=1, source_target_pairs={{0,16},{4,20},{8,24},{12,28},{16,0},{20,4},{24,8},{28,12},{1,17},{... | collective-permute-start | bytes 196616 | tf_op jit(solution)/shard_map/ppermute | solution.py:35
  48.2 3.6 %collective-permute-done.10 = f32[64,256]{1,0:T(8,128)S(1)} collective-permute-done((f32[64,256]{1,0:T(8,128)S(1)}, f32[64,256]{1,0:T(8,128)S(1)}, u32[]{:S(2)}, u32[]{:S(2)}) %collective-permute-start.10) | collective-permute-done | bytes 65568 | tf_op jit(solution)/shard_map/ppermute | solution.py:35
  51.8 0.6 %add.113 = f32[64,256]{1,0:T(8,128)} add(f32[64,256]{1,0:T(8,128)S(1)} %add_add_fusion, f32[64,256]{1,0:T(8,128)S(1)} %collective-permute-done.10) | non-fusion elementwise | flops 16384 | bytes 196608 | tf_op jit(solution)/shard_map/add | solution.py:37
  (28 shorter events, 2.4 us)
Async XLA Ops:
  3.3 2.8 %copy-start = (s32[2048]{0:T(1024)S(1)}, s32[2048]{0:T(1024)}, u32[]{:S(2)}) copy-start(s32[2048]{0:T(1024)} %param.5) | copy-start | bytes 24580
  13.6 12.2 %collective-permute-start.6 = (f32[64,256]{1,0:T(8,128)S(1)}, f32[64,256]{1,0:T(8,128)S(1)}, u32[]{:S(2)}, u32[]{:S(2)}) collective-permute-start(f32[64,256]{1,0:T(8,128)S(1)} %bitcast.48), channel_id=1, source_target_pairs={{0,28},{4,24},{8,20},{12,16},{16,12},{20,8},{24,4},{28,0},{1,29},{... | collective-permute-start | bytes 196616 | tf_op jit(solution)/shard_map/ppermute | solution.py:94
  19.8 6.8 %collective-permute-start.5 = (f32[64,256]{1,0:T(8,128)S(1)}, f32[64,256]{1,0:T(8,128)S(1)}, u32[]{:S(2)}, u32[]{:S(2)}) collective-permute-start(f32[64,256]{1,0:T(8,128)S(1)} %bitcast.46), channel_id=1, source_target_pairs={{0,24},{4,28},{8,16},{12,20},{16,8},{20,12},{24,0},{28,4},{1,25},{... | collective-permute-start | bytes 196616 | tf_op jit(solution)/shard_map/ppermute | solution.py:94
  20.2 8.8 %collective-permute-start.4 = (f32[64,256]{1,0:T(8,128)S(1)}, f32[64,256]{1,0:T(8,128)S(1)}, u32[]{:S(2)}, u32[]{:S(2)}) collective-permute-start(f32[64,256]{1,0:T(8,128)S(1)} %bitcast.42), channel_id=1, source_target_pairs={{0,20},{4,16},{8,28},{12,24},{16,4},{20,0},{24,12},{28,8},{1,21},{... | collective-permute-start | bytes 196616 | tf_op jit(solution)/shard_map/ppermute | solution.py:94
  21.0 9.9 %collective-permute-start.3 = (f32[64,256]{1,0:T(8,128)S(1)}, f32[64,256]{1,0:T(8,128)S(1)}, u32[]{:S(2)}, u32[]{:S(2)}) collective-permute-start(f32[64,256]{1,0:T(8,128)S(1)} %bitcast.43), channel_id=1, source_target_pairs={{0,16},{4,20},{8,24},{12,28},{16,0},{20,4},{24,8},{28,12},{1,17},{... | collective-permute-start | bytes 196616 | tf_op jit(solution)/shard_map/ppermute | solution.py:94
  23.2 7.8 %collective-permute-start.2 = (f32[64,256]{1,0:T(8,128)S(1)}, f32[64,256]{1,0:T(8,128)S(1)}, u32[]{:S(2)}, u32[]{:S(2)}) collective-permute-start(f32[64,256]{1,0:T(8,128)S(1)} %bitcast.44), channel_id=1, source_target_pairs={{0,12},{4,8},{8,4},{12,0},{16,28},{20,24},{24,20},{28,16},{1,13},{... | collective-permute-start | bytes 196616 | tf_op jit(solution)/shard_map/ppermute | solution.py:94
  25.8 5.9 %collective-permute-start.1 = (f32[64,256]{1,0:T(8,128)S(1)}, f32[64,256]{1,0:T(8,128)S(1)}, u32[]{:S(2)}, u32[]{:S(2)}) collective-permute-start(f32[64,256]{1,0:T(8,128)S(1)} %bitcast.47), channel_id=1, source_target_pairs={{0,8},{4,12},{8,0},{12,4},{16,24},{20,28},{24,16},{28,20},{1,9},{5... | collective-permute-start | bytes 196616 | tf_op jit(solution)/shard_map/ppermute | solution.py:94
  26.6 5.1 %collective-permute-start = (f32[64,256]{1,0:T(8,128)S(1)}, f32[64,256]{1,0:T(8,128)S(1)}, u32[]{:S(2)}, u32[]{:S(2)}) collective-permute-start(f32[64,256]{1,0:T(8,128)S(1)} %bitcast.45), channel_id=1, source_target_pairs={{0,4},{4,0},{8,12},{12,8},{16,20},{20,16},{24,28},{28,24},{1,5},{5... | collective-permute-start | bytes 196616 | tf_op jit(solution)/shard_map/ppermute | solution.py:94
  37.9 5.0 %collective-permute-start.8 = (f32[64,256]{1,0:T(8,128)S(1)}, f32[64,256]{1,0:T(8,128)S(1)}, u32[]{:S(2)}, u32[]{:S(2)}) collective-permute-start(f32[64,256]{1,0:T(8,128)S(1)} %fusion.35), channel_id=1, source_target_pairs={{0,8},{4,12},{8,0},{12,4},{16,24},{20,28},{24,16},{28,20},{1,9},{5... | collective-permute-start | bytes 196616 | tf_op jit(solution)/shard_map/ppermute | solution.py:35
  39.1 5.2 %collective-permute-start.9 = (f32[64,256]{1,0:T(8,128)S(1)}, f32[64,256]{1,0:T(8,128)S(1)}, u32[]{:S(2)}, u32[]{:S(2)}) collective-permute-start(f32[64,256]{1,0:T(8,128)S(1)} %fusion.35), channel_id=1, source_target_pairs={{0,12},{4,8},{8,4},{12,0},{16,28},{20,24},{24,20},{28,16},{1,13},{... | collective-permute-start | bytes 196616 | tf_op jit(solution)/shard_map/ppermute | solution.py:35
  40.2 5.2 %collective-permute-start.7 = (f32[64,256]{1,0:T(8,128)S(1)}, f32[64,256]{1,0:T(8,128)S(1)}, u32[]{:S(2)}, u32[]{:S(2)}) collective-permute-start(f32[64,256]{1,0:T(8,128)S(1)} %fusion.35), channel_id=1, source_target_pairs={{0,4},{4,0},{8,12},{12,8},{16,20},{20,16},{24,28},{28,24},{1,5},{5... | collective-permute-start | bytes 196616 | tf_op jit(solution)/shard_map/ppermute | solution.py:35
  45.4 6.4 %collective-permute-start.10 = (f32[64,256]{1,0:T(8,128)S(1)}, f32[64,256]{1,0:T(8,128)S(1)}, u32[]{:S(2)}, u32[]{:S(2)}) collective-permute-start(f32[64,256]{1,0:T(8,128)S(1)} %add_add_fusion), channel_id=1, source_target_pairs={{0,16},{4,20},{8,24},{12,28},{16,0},{20,4},{24,8},{28,12},{1,17},{... | collective-permute-start | bytes 196616 | tf_op jit(solution)/shard_map/ppermute | solution.py:35

commit v17 on v16

--- a/solution.py
+++ b/solution.py
@@ -6,7 +6,7 @@
 from jax.sharding import PartitionSpec as P
 
 STRIDE = 64
-OUTER = 64
+OUTER = 32
 
 
 def hadamard(order):

time: 52.6 us -> 53.8 us (1.023)
  waiting for transfers between devices: 12.2 us -> 14.6 us
  starting transfers between devices: 19.2 us -> 18.4 us
  local copies, waits for them, and re-layouts: 2.6 us -> 1.95 us
    ppermute x7, waiting for transfers between devices: 4.64 us -> 6.96 us  [per_device(): arrived.append(lax.ppermute(block, 'ev', pairs))]
    ppermute x4, starting transfers between devices: 6.31 us -> 5.59 us  [group_sum(): values.append(lax.ppermute(value, 'ev', pairs))]
    dynamic_slice x2, local copies, waits for them, and re-layouts: 0.82 us -> 0.17 us  [per_device(): own = lax.dynamic_index_in_dim(chunks, my_index, axis=0, keepdims=False)]
  transfers between devices with their start and end apart: 11 -> 11, of which waited for: 7 -> 6; matrix products, arithmetic and copies ran while one was open for 1% -> 1% of each run, Pallas kernels for 0% -> 0%
where the time goes in v17:
time: 53.8 us; the launch traced here: 53.6 us
  starting transfers between devices  18.4 us (34%)
  waiting for transfers between devices  14.6 us (27%)
  matrix products  9.18 us (17%)
  blocking collectives  5.79 us (11%)
  other arithmetic  3.41 us (6%)
  local copies, waits for them, and re-layouts  1.95 us (4%)
    ppermute x7, starting transfers between devices, per_device(): arrived.append(lax.ppermute(block, 'ev', pairs))  12.8 us
    ppermute x4, waiting for transfers between devices, group_sum(): values.append(lax.ppermute(value, 'ev', pairs))  7.65 us
    ppermute x7, waiting for transfers between devices, per_device(): arrived.append(lax.ppermute(block, 'ev', pairs))  6.96 us
    dot_general x1, matrix products, per_device(): jnp.einsum('xcb,xbj->xcj', first, pick.astype(jnp.float32), precision=lax...  6.16 us
    all_gather x1, blocking collectives, per_device(): lax.all_gather(sketch, 'col', axis=0, tiled=True)  5.79 us
    ppermute x4, starting transfers between devices, group_sum(): values.append(lax.ppermute(value, 'ev', pairs))  5.59 us
    dot_general x1, matrix products, per_device(): jnp.einsum('xa,cab->xcb', hadamard(OUTER).astype(jnp.bfloat16), blocks, p...  2.65 us
    mul x1, other arithmetic, per_device(): signed = panel * signs.astype(jnp.bfloat16)[None, :]  1.85 us
  transfers between devices with their start and end apart: 11, of which 6 were waited for; matrix products, arithmetic and copies ran while one was open for 1% of the time, Pallas kernels for 0%

profile of v17, /device:TPU:0, one launch (start us, length us, event | category | flops | bytes accessed | tf_op | source)
XLA Modules:
  0.0 53.6 jit_solution(7945113184643868314)
XLA Ops:
  0.2 0.8 %convert_element_type.16 = bf16[16384]{0:T(1024)(128)(2,1)S(1)} convert(s32[16384]{0:T(1024)} %param.4) | non-fusion elementwise | flops 16384 | bytes 98304 | tf_op jit(solution)/shard_map/convert_element_type | solution.py:70
  1.0 1.9 %broadcast_multiply_fusion = bf16[64,16384]{1,0:T(8,128)(2,1)S(1)} fusion(bf16[64,16384]{1,0:T(8,128)(2,1)} %param.3, bf16[16384]{0:T(1024)(128)(2,1)S(1)} %convert_element_type.16), kind=kLoop, calls=%fused_computation.9 | loop fusion | flops 1048576 | bytes 4227072 | tf_op jit(solution)/shard_map/mul | solution.py:70
  2.9 0.8 %copy.27 = bf16[8,8,32,512]{3,2,1,0:T(8,128)(2,1)S(1)} copy(bf16[8,8,32,512]{3,1,2,0:T(8,128)(2,1)S(1)} %bitcast.42) | data formatting | bytes 4194304
  3.6 2.7 %fusion.22 = f32[32,64,512]{2,0,1:T(8,128)} fusion(bf16[64,32,512]{2,1,0:T(8,128)(2,1)S(1)} %bitcast.41), kind=kOutput, calls=%fused_computation.29 | convolution fusion | flops 67139584 | bytes 6291456 | tf_op jit(solution)/shard_map/xa,cab->xcb/dot_general | solution.py:72
  6.3 0.1 reshape.30
  6.6 6.2 %fusion.6 = f32[8,64,32,8]{1,3,0,2:T(8,128)S(1)} fusion(s32[64]{0:T(128)S(1)} %xor.35, s32[32,64]{1,0:T(8,128)S(1)} %copy.14, f32[32,64,512]{2,0,1:T(8,128)} %fusion.22), kind=kOutput, calls=%fused_computation.7 | convolution fusion | flops 409993216 | bytes 4727040 | tf_op jit(solution)/shard_map/xcb,xbj->xcj/dot_general | solution.py:79
  13.1 3.0 %collective-permute-start = (f32[64,256]{1,0:T(8,128)S(1)}, f32[64,256]{1,0:T(8,128)S(1)}, u32[]{:S(2)}, u32[]{:S(2)}) collective-permute-start(f32[64,256]{1,0:T(8,128)S(1)} %bitcast.51), channel_id=1, source_target_pairs={{0,4},{4,0},{8,12},{12,8},{16,20},{20,16},{24,28},{28,24},{1,5},{5... | collective-permute-start | bytes 196616 | tf_op jit(solution)/shard_map/ppermute | solution.py:94
  16.2 1.7 %collective-permute-start.1 = (f32[64,256]{1,0:T(8,128)S(1)}, f32[64,256]{1,0:T(8,128)S(1)}, u32[]{:S(2)}, u32[]{:S(2)}) collective-permute-start(f32[64,256]{1,0:T(8,128)S(1)} %bitcast.49), channel_id=1, source_target_pairs={{0,8},{4,12},{8,0},{12,4},{16,24},{20,28},{24,16},{28,20},{1,9},{5... | collective-permute-start | bytes 196616 | tf_op jit(solution)/shard_map/ppermute | solution.py:94
  18.1 3.1 %collective-permute-start.3 = (f32[64,256]{1,0:T(8,128)S(1)}, f32[64,256]{1,0:T(8,128)S(1)}, u32[]{:S(2)}, u32[]{:S(2)}) collective-permute-start(f32[64,256]{1,0:T(8,128)S(1)} %bitcast.46), channel_id=1, source_target_pairs={{0,16},{4,20},{8,24},{12,28},{16,0},{20,4},{24,8},{28,12},{1,17},{... | collective-permute-start | bytes 196616 | tf_op jit(solution)/shard_map/ppermute | solution.py:94
  21.2 1.3 %collective-permute-start.4 = (f32[64,256]{1,0:T(8,128)S(1)}, f32[64,256]{1,0:T(8,128)S(1)}, u32[]{:S(2)}, u32[]{:S(2)}) collective-permute-start(f32[64,256]{1,0:T(8,128)S(1)} %bitcast.47), channel_id=1, source_target_pairs={{0,20},{4,16},{8,28},{12,24},{16,4},{20,0},{24,12},{28,8},{1,21},{... | collective-permute-start | bytes 196616 | tf_op jit(solution)/shard_map/ppermute | solution.py:94
  22.7 3.7 %collective-permute-start.5 = (f32[64,256]{1,0:T(8,128)S(1)}, f32[64,256]{1,0:T(8,128)S(1)}, u32[]{:S(2)}, u32[]{:S(2)}) collective-permute-start(f32[64,256]{1,0:T(8,128)S(1)} %bitcast.50), channel_id=1, source_target_pairs={{0,24},{4,28},{8,16},{12,20},{16,8},{20,12},{24,0},{28,4},{1,25},{... | collective-permute-start | bytes 196616 | tf_op jit(solution)/shard_map/ppermute | solution.py:94
  26.5 4.5 %collective-permute-done.4 = f32[64,256]{1,0:T(8,128)S(1)} collective-permute-done((f32[64,256]{1,0:T(8,128)S(1)}, f32[64,256]{1,0:T(8,128)S(1)}, u32[]{:S(2)}, u32[]{:S(2)}) %collective-permute-start.4) | collective-permute-done | bytes 65568 | tf_op jit(solution)/shard_map/ppermute | solution.py:94
  31.0 2.5 %collective-permute-done.6 = f32[64,256]{1,0:T(8,128)S(1)} collective-permute-done((f32[64,256]{1,0:T(8,128)S(1)}, f32[64,256]{1,0:T(8,128)S(1)}, u32[]{:S(2)}, u32[]{:S(2)}) %collective-permute-start.6) | collective-permute-done | bytes 65568 | tf_op jit(solution)/shard_map/ppermute | solution.py:94
  33.5 5.8 %all_gather.3 = f32[256,256]{1,0:T(8,128)S(1)} all-gather(f32[64,256]{1,0:T(8,128)S(1)} %fusion.15), channel_id=1, replica_groups=mesh['ev'=8,'col'=4] {'col'}, dimensions={0}, use_global_device_ids=true | all-gather | bytes 327680 | tf_op jit(solution)/shard_map/all_gather | solution.py:104
  39.3 0.4 fusion.36
  39.7 0.5 collective-permute-start.7
  40.2 1.6 %collective-permute-start.8 = (f32[64,256]{1,0:T(8,128)S(1)}, f32[64,256]{1,0:T(8,128)S(1)}, u32[]{:S(2)}, u32[]{:S(2)}) collective-permute-start(f32[64,256]{1,0:T(8,128)S(1)} %fusion.36), channel_id=1, source_target_pairs={{0,8},{4,12},{8,0},{12,4},{16,24},{20,28},{24,16},{28,20},{1,9},{5... | collective-permute-start | bytes 196616 | tf_op jit(solution)/shard_map/ppermute | solution.py:35
  41.8 1.4 %collective-permute-start.9 = (f32[64,256]{1,0:T(8,128)S(1)}, f32[64,256]{1,0:T(8,128)S(1)}, u32[]{:S(2)}, u32[]{:S(2)}) collective-permute-start(f32[64,256]{1,0:T(8,128)S(1)} %fusion.36), channel_id=1, source_target_pairs={{0,12},{4,8},{8,4},{12,0},{16,28},{20,24},{24,20},{28,16},{1,13},{... | collective-permute-start | bytes 196616 | tf_op jit(solution)/shard_map/ppermute | solution.py:35
  43.2 0.9 %collective-permute-done.7 = f32[64,256]{1,0:T(8,128)S(1)} collective-permute-done((f32[64,256]{1,0:T(8,128)S(1)}, f32[64,256]{1,0:T(8,128)S(1)}, u32[]{:S(2)}, u32[]{:S(2)}) %collective-permute-start.7) | collective-permute-done | bytes 65568 | tf_op jit(solution)/shard_map/ppermute | solution.py:35
  44.1 0.4 collective-permute-done.8
  44.5 2.5 %collective-permute-done.9 = f32[64,256]{1,0:T(8,128)S(1)} collective-permute-done((f32[64,256]{1,0:T(8,128)S(1)}, f32[64,256]{1,0:T(8,128)S(1)}, u32[]{:S(2)}, u32[]{:S(2)}) %collective-permute-start.9) | collective-permute-done | bytes 65568 | tf_op jit(solution)/shard_map/ppermute | solution.py:35
  47.0 2.0 %collective-permute-start.10 = (f32[64,256]{1,0:T(8,128)S(1)}, f32[64,256]{1,0:T(8,128)S(1)}, u32[]{:S(2)}, u32[]{:S(2)}) collective-permute-start(f32[64,256]{1,0:T(8,128)S(1)} %add_add_fusion), channel_id=1, source_target_pairs={{0,16},{4,20},{8,24},{12,28},{16,0},{20,4},{24,8},{28,12},{1,17},{... | collective-permute-start | bytes 196616 | tf_op jit(solution)/shard_map/ppermute | solution.py:35
  49.0 3.9 %collective-permute-done.10 = f32[64,256]{1,0:T(8,128)S(1)} collective-permute-done((f32[64,256]{1,0:T(8,128)S(1)}, f32[64,256]{1,0:T(8,128)S(1)}, u32[]{:S(2)}, u32[]{:S(2)}) %collective-permute-start.10) | collective-permute-done | bytes 65568 | tf_op jit(solution)/shard_map/ppermute | solution.py:35
  52.9 0.6 %add.109 = f32[64,256]{1,0:T(8,128)} add(f32[64,256]{1,0:T(8,128)S(1)} %add_add_fusion, f32[64,256]{1,0:T(8,128)S(1)} %collective-permute-done.10) | non-fusion elementwise | flops 16384 | bytes 196608 | tf_op jit(solution)/shard_map/add | solution.py:37
  (28 shorter events, 1.2 us)
Async XLA Ops:
  3.6 2.7 %copy-start = (s32[2048]{0:T(1024)S(1)}, s32[2048]{0:T(1024)}, u32[]{:S(2)}) copy-start(s32[2048]{0:T(1024)} %param.5) | copy-start | bytes 24580
  13.1 9.6 %collective-permute-start = (f32[64,256]{1,0:T(8,128)S(1)}, f32[64,256]{1,0:T(8,128)S(1)}, u32[]{:S(2)}, u32[]{:S(2)}) collective-permute-start(f32[64,256]{1,0:T(8,128)S(1)} %bitcast.51), channel_id=1, source_target_pairs={{0,4},{4,0},{8,12},{12,8},{16,20},{20,16},{24,28},{28,24},{1,5},{5... | collective-permute-start | bytes 196616 | tf_op jit(solution)/shard_map/ppermute | solution.py:94
  16.2 10.3 %collective-permute-start.1 = (f32[64,256]{1,0:T(8,128)S(1)}, f32[64,256]{1,0:T(8,128)S(1)}, u32[]{:S(2)}, u32[]{:S(2)}) collective-permute-start(f32[64,256]{1,0:T(8,128)S(1)} %bitcast.49), channel_id=1, source_target_pairs={{0,8},{4,12},{8,0},{12,4},{16,24},{20,28},{24,16},{28,20},{1,9},{5... | collective-permute-start | bytes 196616 | tf_op jit(solution)/shard_map/ppermute | solution.py:94
  17.9 8.6 %collective-permute-start.2 = (f32[64,256]{1,0:T(8,128)S(1)}, f32[64,256]{1,0:T(8,128)S(1)}, u32[]{:S(2)}, u32[]{:S(2)}) collective-permute-start(f32[64,256]{1,0:T(8,128)S(1)} %bitcast.45), channel_id=1, source_target_pairs={{0,12},{4,8},{8,4},{12,0},{16,28},{20,24},{24,20},{28,16},{1,13},{... | collective-permute-start | bytes 196616 | tf_op jit(solution)/shard_map/ppermute | solution.py:94
  18.1 8.5 %collective-permute-start.3 = (f32[64,256]{1,0:T(8,128)S(1)}, f32[64,256]{1,0:T(8,128)S(1)}, u32[]{:S(2)}, u32[]{:S(2)}) collective-permute-start(f32[64,256]{1,0:T(8,128)S(1)} %bitcast.46), channel_id=1, source_target_pairs={{0,16},{4,20},{8,24},{12,28},{16,0},{20,4},{24,8},{28,12},{1,17},{... | collective-permute-start | bytes 196616 | tf_op jit(solution)/shard_map/ppermute | solution.py:94
  21.2 9.8 %collective-permute-start.4 = (f32[64,256]{1,0:T(8,128)S(1)}, f32[64,256]{1,0:T(8,128)S(1)}, u32[]{:S(2)}, u32[]{:S(2)}) collective-permute-start(f32[64,256]{1,0:T(8,128)S(1)} %bitcast.47), channel_id=1, source_target_pairs={{0,20},{4,16},{8,28},{12,24},{16,4},{20,0},{24,12},{28,8},{1,21},{... | collective-permute-start | bytes 196616 | tf_op jit(solution)/shard_map/ppermute | solution.py:94
  22.7 8.3 %collective-permute-start.5 = (f32[64,256]{1,0:T(8,128)S(1)}, f32[64,256]{1,0:T(8,128)S(1)}, u32[]{:S(2)}, u32[]{:S(2)}) collective-permute-start(f32[64,256]{1,0:T(8,128)S(1)} %bitcast.50), channel_id=1, source_target_pairs={{0,24},{4,28},{8,16},{12,20},{16,8},{20,12},{24,0},{28,4},{1,25},{... | collective-permute-start | bytes 196616 | tf_op jit(solution)/shard_map/ppermute | solution.py:94
  26.4 7.1 %collective-permute-start.6 = (f32[64,256]{1,0:T(8,128)S(1)}, f32[64,256]{1,0:T(8,128)S(1)}, u32[]{:S(2)}, u32[]{:S(2)}) collective-permute-start(f32[64,256]{1,0:T(8,128)S(1)} %bitcast.48), channel_id=1, source_target_pairs={{0,28},{4,24},{8,20},{12,16},{16,12},{20,8},{24,4},{28,0},{1,29},{... | collective-permute-start | bytes 196616 | tf_op jit(solution)/shard_map/ppermute | solution.py:94
  39.7 4.4 %collective-permute-start.7 = (f32[64,256]{1,0:T(8,128)S(1)}, f32[64,256]{1,0:T(8,128)S(1)}, u32[]{:S(2)}, u32[]{:S(2)}) collective-permute-start(f32[64,256]{1,0:T(8,128)S(1)} %fusion.36), channel_id=1, source_target_pairs={{0,4},{4,0},{8,12},{12,8},{16,20},{20,16},{24,28},{28,24},{1,5},{5... | collective-permute-start | bytes 196616 | tf_op jit(solution)/shard_map/ppermute | solution.py:35
  40.2 4.3 %collective-permute-start.8 = (f32[64,256]{1,0:T(8,128)S(1)}, f32[64,256]{1,0:T(8,128)S(1)}, u32[]{:S(2)}, u32[]{:S(2)}) collective-permute-start(f32[64,256]{1,0:T(8,128)S(1)} %fusion.36), channel_id=1, source_target_pairs={{0,8},{4,12},{8,0},{12,4},{16,24},{20,28},{24,16},{28,20},{1,9},{5... | collective-permute-start | bytes 196616 | tf_op jit(solution)/shard_map/ppermute | solution.py:35
  41.8 5.2 %collective-permute-start.9 = (f32[64,256]{1,0:T(8,128)S(1)}, f32[64,256]{1,0:T(8,128)S(1)}, u32[]{:S(2)}, u32[]{:S(2)}) collective-permute-start(f32[64,256]{1,0:T(8,128)S(1)} %fusion.36), channel_id=1, source_target_pairs={{0,12},{4,8},{8,4},{12,0},{16,28},{20,24},{24,20},{28,16},{1,13},{... | collective-permute-start | bytes 196616 | tf_op jit(solution)/shard_map/ppermute | solution.py:35
  47.0 5.9 %collective-permute-start.10 = (f32[64,256]{1,0:T(8,128)S(1)}, f32[64,256]{1,0:T(8,128)S(1)}, u32[]{:S(2)}, u32[]{:S(2)}) collective-permute-start(f32[64,256]{1,0:T(8,128)S(1)} %add_add_fusion), channel_id=1, source_target_pairs={{0,16},{4,20},{8,24},{12,28},{16,0},{20,4},{24,8},{28,12},{1,17},{... | collective-permute-start | bytes 196616 | tf_op jit(solution)/shard_map/ppermute | solution.py:35

commit v18 on v16

--- a/solution.py
+++ b/solution.py
@@ -105,8 +105,8 @@
         precision=high,
         preferred_element_type=jnp.float32,
     )
-    for start in range(0, levels, 2):
-        partial_gram = group_sum(partial_gram, list(range(start, min(start + 2, levels))))
+    for start in range(0, levels, 3):
+        partial_gram = group_sum(partial_gram, list(range(start, min(start + 3, levels))))
     return partial_gram
 
 

time: 52.6 us -> 55.2 us (1.049)
  starting transfers between devices: 19.2 us -> 24.3 us
  waiting for transfers between devices: 12.2 us -> 9.65 us
    ppermute x4 -> x7, starting transfers between devices: 6.31 us -> 11.4 us  [group_sum(): values.append(lax.ppermute(value, 'ev', pairs))]
    ppermute x4 -> x7, waiting for transfers between devices: 7.52 us -> 5 us  [group_sum(): values.append(lax.ppermute(value, 'ev', pairs))]
  transfers between devices with their start and end apart: 11 -> 14, of which waited for: 7 -> 8; matrix products, arithmetic and copies ran while one was open for 1% -> 1% of each run, Pallas kernels for 0% -> 0%
where the time goes in v18:
time: 55.2 us; the launch traced here: 55 us
  starting transfers between devices  24.3 us (44%)
  waiting for transfers between devices  9.65 us (17%)
  matrix products  9.08 us (16%)
  blocking collectives  5.79 us (10%)
  other arithmetic  3.43 us (6%)
  local copies, waits for them, and re-layouts  2.6 us (5%)
    ppermute x7, starting transfers between devices, per_device(): arrived.append(lax.ppermute(block, 'ev', pairs))  12.8 us
    ppermute x7, starting transfers between devices, group_sum(): values.append(lax.ppermute(value, 'ev', pairs))  11.4 us
    dot_general x1, matrix products, per_device(): jnp.einsum('xcb,xbj->xcj', first, pick.astype(jnp.float32), precision=lax...  6.03 us
    all_gather x1, blocking collectives, per_device(): lax.all_gather(sketch, 'col', axis=0, tiled=True)  5.79 us
    ppermute x7, waiting for transfers between devices, group_sum(): values.append(lax.ppermute(value, 'ev', pairs))  5 us
    ppermute x7, waiting for transfers between devices, per_device(): arrived.append(lax.ppermute(block, 'ev', pairs))  4.65 us
    dot_general x1, matrix products, per_device(): jnp.einsum('xa,cab->xcb', hadamard(OUTER).astype(jnp.bfloat16), blocks, p...  2.68 us
    mul x1, other arithmetic, per_device(): signed = panel * signs.astype(jnp.bfloat16)[None, :]  1.85 us
  transfers between devices with their start and end apart: 14, of which 8 were waited for; matrix products, arithmetic and copies ran while one was open for 1% of the time, Pallas kernels for 0%

profile of v18, /device:TPU:0, one launch (start us, length us, event | category | flops | bytes accessed | tf_op | source)
XLA Modules:
  0.0 55.0 jit_solution(10665405963597538169)
XLA Ops:
  0.0 0.8 %convert_element_type.16 = bf16[16384]{0:T(1024)(128)(2,1)S(1)} convert(s32[16384]{0:T(1024)} %param.4) | non-fusion elementwise | flops 16384 | bytes 98304 | tf_op jit(solution)/shard_map/convert_element_type | solution.py:70
  0.9 1.9 %broadcast_multiply_fusion = bf16[64,16384]{1,0:T(8,128)(2,1)S(1)} fusion(bf16[64,16384]{1,0:T(8,128)(2,1)} %param.3, bf16[16384]{0:T(1024)(128)(2,1)S(1)} %convert_element_type.16), kind=kLoop, calls=%fused_computation.7 | loop fusion | flops 1048576 | bytes 4227072 | tf_op jit(solution)/shard_map/mul | solution.py:70
  3.3 2.7 %fusion.19 = f32[64,64,256]{2,0,1:T(8,128)} fusion(bf16[64,64,256]{2,1,0:T(8,128)(2,1)S(1)} %bitcast.38), kind=kOutput, calls=%fused_computation.27 | convolution fusion | flops 134352896 | bytes 6291456 | tf_op jit(solution)/shard_map/xa,cab->xcb/dot_general | solution.py:72
  6.6 6.0 %fusion = f32[64,64,32]{1,2,0:T(8,128)S(1)} fusion(f32[64,64,256]{2,0,1:T(8,128)} %fusion.19, s32[32]{0:T(128)S(1)} %xor.35, s32[64,32]{1,0:T(8,128)S(1)} %copy.12), kind=kOutput, calls=%fused_computation | convolution fusion | flops 204996608 | bytes 4726912 | tf_op jit(solution)/shard_map/xcb,xbj->xcj/dot_general | solution.py:79
  12.8 0.7 %constant_dynamic-slice_fusion.7 = (f32[1,64,256]{1,0,2:T(1,128)S(1)}, f32[1,64,256]{1,0,2:T(1,128)S(1)}, f32[1,64,256]{1,0,2:T(1,128)S(1)}, f32[1,64,256]{1,0,2...) fusion(f32[8,64,256]{1,0,2:T(8,128)S(1)} %bitcast.40, ...), kind=kLoop, calls=%fused_computation.41 | loop fusion | bytes 1048608 | tf_op jit(solution)/shard_map/jit(dynamic_index_in_dim)/dynamic_slice | solution.py:88
  13.6 6.1 %collective-permute-start.6 = (f32[64,256]{1,0:T(8,128)S(1)}, f32[64,256]{1,0:T(8,128)S(1)}, u32[]{:S(2)}, u32[]{:S(2)}) collective-permute-start(f32[64,256]{1,0:T(8,128)S(1)} %bitcast.48), channel_id=1, source_target_pairs={{0,28},{4,24},{8,20},{12,16},{16,12},{20,8},{24,4},{28,0},{1,29},{... | collective-permute-start | bytes 196616 | tf_op jit(solution)/shard_map/ppermute | solution.py:94
  20.2 0.8 %collective-permute-start.4 = (f32[64,256]{1,0:T(8,128)S(1)}, f32[64,256]{1,0:T(8,128)S(1)}, u32[]{:S(2)}, u32[]{:S(2)}) collective-permute-start(f32[64,256]{1,0:T(8,128)S(1)} %bitcast.42), channel_id=1, source_target_pairs={{0,20},{4,16},{8,28},{12,24},{16,4},{20,0},{24,12},{28,8},{1,21},{... | collective-permute-start | bytes 196616 | tf_op jit(solution)/shard_map/ppermute | solution.py:94
  21.0 2.0 %collective-permute-start.3 = (f32[64,256]{1,0:T(8,128)S(1)}, f32[64,256]{1,0:T(8,128)S(1)}, u32[]{:S(2)}, u32[]{:S(2)}) collective-permute-start(f32[64,256]{1,0:T(8,128)S(1)} %bitcast.43), channel_id=1, source_target_pairs={{0,16},{4,20},{8,24},{12,28},{16,0},{20,4},{24,8},{28,12},{1,17},{... | collective-permute-start | bytes 196616 | tf_op jit(solution)/shard_map/ppermute | solution.py:94
  23.2 2.4 %collective-permute-start.2 = (f32[64,256]{1,0:T(8,128)S(1)}, f32[64,256]{1,0:T(8,128)S(1)}, u32[]{:S(2)}, u32[]{:S(2)}) collective-permute-start(f32[64,256]{1,0:T(8,128)S(1)} %bitcast.44), channel_id=1, source_target_pairs={{0,12},{4,8},{8,4},{12,0},{16,28},{20,24},{24,20},{28,16},{1,13},{... | collective-permute-start | bytes 196616 | tf_op jit(solution)/shard_map/ppermute | solution.py:94
  25.8 0.8 %collective-permute-start.1 = (f32[64,256]{1,0:T(8,128)S(1)}, f32[64,256]{1,0:T(8,128)S(1)}, u32[]{:S(2)}, u32[]{:S(2)}) collective-permute-start(f32[64,256]{1,0:T(8,128)S(1)} %bitcast.47), channel_id=1, source_target_pairs={{0,8},{4,12},{8,0},{12,4},{16,24},{20,28},{24,16},{28,20},{1,9},{5... | collective-permute-start | bytes 196616 | tf_op jit(solution)/shard_map/ppermute | solution.py:94
  27.1 1.9 %collective-permute-done.4 = f32[64,256]{1,0:T(8,128)S(1)} collective-permute-done((f32[64,256]{1,0:T(8,128)S(1)}, f32[64,256]{1,0:T(8,128)S(1)}, u32[]{:S(2)}, u32[]{:S(2)}) %collective-permute-start.4) | collective-permute-done | bytes 65568 | tf_op jit(solution)/shard_map/ppermute | solution.py:94
  29.0 2.0 %collective-permute-done.3 = f32[64,256]{1,0:T(8,128)S(1)} collective-permute-done((f32[64,256]{1,0:T(8,128)S(1)}, f32[64,256]{1,0:T(8,128)S(1)}, u32[]{:S(2)}, u32[]{:S(2)}) %collective-permute-start.3) | collective-permute-done | bytes 65568 | tf_op jit(solution)/shard_map/ppermute | solution.py:94
  31.0 0.7 %collective-permute-done.1 = f32[64,256]{1,0:T(8,128)S(1)} collective-permute-done((f32[64,256]{1,0:T(8,128)S(1)}, f32[64,256]{1,0:T(8,128)S(1)}, u32[]{:S(2)}, u32[]{:S(2)}) %collective-permute-start.1) | collective-permute-done | bytes 65568 | tf_op jit(solution)/shard_map/ppermute | solution.py:94
  31.8 5.8 %all_gather.3 = f32[256,256]{1,0:T(8,128)S(1)} all-gather(f32[64,256]{1,0:T(8,128)S(1)} %fusion.12), channel_id=1, replica_groups=mesh['ev'=8,'col'=4] {'col'}, dimensions={0}, use_global_device_ids=true | all-gather | bytes 327680 | tf_op jit(solution)/shard_map/all_gather | solution.py:104
  37.9 3.2 %collective-permute-start.12 = (f32[64,256]{1,0:T(8,128)S(1)}, f32[64,256]{1,0:T(8,128)S(1)}, u32[]{:S(2)}, u32[]{:S(2)}) collective-permute-start(f32[64,256]{1,0:T(8,128)S(1)} %fusion.35), channel_id=1, source_target_pairs={{0,24},{4,28},{8,16},{12,20},{16,8},{20,12},{24,0},{28,4},{1,25},{... | collective-permute-start | bytes 196616 | tf_op jit(solution)/shard_map/ppermute | solution.py:35
  41.1 1.0 %collective-permute-start.13 = (f32[64,256]{1,0:T(8,128)S(1)}, f32[64,256]{1,0:T(8,128)S(1)}, u32[]{:S(2)}, u32[]{:S(2)}) collective-permute-start(f32[64,256]{1,0:T(8,128)S(1)} %fusion.35), channel_id=1, source_target_pairs={{0,28},{4,24},{8,20},{12,16},{16,12},{20,8},{24,4},{28,0},{1,29},{... | collective-permute-start | bytes 196616 | tf_op jit(solution)/shard_map/ppermute | solution.py:35
  42.8 2.8 %collective-permute-start.11 = (f32[64,256]{1,0:T(8,128)S(1)}, f32[64,256]{1,0:T(8,128)S(1)}, u32[]{:S(2)}, u32[]{:S(2)}) collective-permute-start(f32[64,256]{1,0:T(8,128)S(1)} %fusion.35), channel_id=1, source_target_pairs={{0,20},{4,16},{8,28},{12,24},{16,4},{20,0},{24,12},{28,8},{1,21},{... | collective-permute-start | bytes 196616 | tf_op jit(solution)/shard_map/ppermute | solution.py:35
  45.6 0.8 %collective-permute-start.8 = (f32[64,256]{1,0:T(8,128)S(1)}, f32[64,256]{1,0:T(8,128)S(1)}, u32[]{:S(2)}, u32[]{:S(2)}) collective-permute-start(f32[64,256]{1,0:T(8,128)S(1)} %fusion.35), channel_id=1, source_target_pairs={{0,8},{4,12},{8,0},{12,4},{16,24},{20,28},{24,16},{28,20},{1,9},{5... | collective-permute-start | bytes 196616 | tf_op jit(solution)/shard_map/ppermute | solution.py:35
  46.4 1.5 %collective-permute-start.9 = (f32[64,256]{1,0:T(8,128)S(1)}, f32[64,256]{1,0:T(8,128)S(1)}, u32[]{:S(2)}, u32[]{:S(2)}) collective-permute-start(f32[64,256]{1,0:T(8,128)S(1)} %fusion.35), channel_id=1, source_target_pairs={{0,12},{4,8},{8,4},{12,0},{16,28},{20,24},{24,20},{28,16},{1,13},{... | collective-permute-start | bytes 196616 | tf_op jit(solution)/shard_map/ppermute | solution.py:35
  48.0 0.8 %collective-permute-done.13 = f32[64,256]{1,0:T(8,128)S(1)} collective-permute-done((f32[64,256]{1,0:T(8,128)S(1)}, f32[64,256]{1,0:T(8,128)S(1)}, u32[]{:S(2)}, u32[]{:S(2)}) %collective-permute-start.13) | collective-permute-done | bytes 65568 | tf_op jit(solution)/shard_map/ppermute | solution.py:35
  48.8 1.4 %collective-permute-start.7 = (f32[64,256]{1,0:T(8,128)S(1)}, f32[64,256]{1,0:T(8,128)S(1)}, u32[]{:S(2)}, u32[]{:S(2)}) collective-permute-start(f32[64,256]{1,0:T(8,128)S(1)} %fusion.35), channel_id=1, source_target_pairs={{0,4},{4,0},{8,12},{12,8},{16,20},{20,16},{24,28},{28,24},{1,5},{5... | collective-permute-start | bytes 196616 | tf_op jit(solution)/shard_map/ppermute | solution.py:35
  50.2 2.1 %collective-permute-done.10 = f32[64,256]{1,0:T(8,128)S(1)} collective-permute-done((f32[64,256]{1,0:T(8,128)S(1)}, f32[64,256]{1,0:T(8,128)S(1)}, u32[]{:S(2)}, u32[]{:S(2)}) %collective-permute-start.10) | collective-permute-done | bytes 65568 | tf_op jit(solution)/shard_map/ppermute | solution.py:35
  52.3 1.0 %collective-permute-done.11 = f32[64,256]{1,0:T(8,128)S(1)} collective-permute-done((f32[64,256]{1,0:T(8,128)S(1)}, f32[64,256]{1,0:T(8,128)S(1)}, u32[]{:S(2)}, u32[]{:S(2)}) %collective-permute-start.11) | collective-permute-done | bytes 65568 | tf_op jit(solution)/shard_map/ppermute | solution.py:35
  54.3 0.7 %add_add_fusion = f32[64,256]{1,0:T(8,128)} fusion(f32[64,256]{1,0:T(8,128)S(1)} %collective-permute-done.12, f32[64,256]{1,0:T(8,128)S(1)} %collective-permute-done.13, f32[64,256]{1,0:T(8,128)S(1)} %collective-permute-done.10, f32[64,256]{1,0:T(8,128)S(1)} %collective-permute-done.11, f32[64,256]{1,0:T(8,128)S(1)} %collective-permute-done.8, ...), kind=kLoop, calls=%fused_computation.17 | loop fusion | flops 114688 | bytes 589824 | tf_op jit(solution)/shard_map/add | solution.py:37
  (33 shorter events, 4.7 us)
Async XLA Ops:
  3.3 2.8 %copy-start = (s32[2048]{0:T(1024)S(1)}, s32[2048]{0:T(1024)}, u32[]{:S(2)}) copy-start(s32[2048]{0:T(1024)} %param.5) | copy-start | bytes 24580
  13.6 12.2 %collective-permute-start.6 = (f32[64,256]{1,0:T(8,128)S(1)}, f32[64,256]{1,0:T(8,128)S(1)}, u32[]{:S(2)}, u32[]{:S(2)}) collective-permute-start(f32[64,256]{1,0:T(8,128)S(1)} %bitcast.48), channel_id=1, source_target_pairs={{0,28},{4,24},{8,20},{12,16},{16,12},{20,8},{24,4},{28,0},{1,29},{... | collective-permute-start | bytes 196616 | tf_op jit(solution)/shard_map/ppermute | solution.py:94
  19.8 6.8 %collective-permute-start.5 = (f32[64,256]{1,0:T(8,128)S(1)}, f32[64,256]{1,0:T(8,128)S(1)}, u32[]{:S(2)}, u32[]{:S(2)}) collective-permute-start(f32[64,256]{1,0:T(8,128)S(1)} %bitcast.46), channel_id=1, source_target_pairs={{0,24},{4,28},{8,16},{12,20},{16,8},{20,12},{24,0},{28,4},{1,25},{... | collective-permute-start | bytes 196616 | tf_op jit(solution)/shard_map/ppermute | solution.py:94
  20.2 8.8 %collective-permute-start.4 = (f32[64,256]{1,0:T(8,128)S(1)}, f32[64,256]{1,0:T(8,128)S(1)}, u32[]{:S(2)}, u32[]{:S(2)}) collective-permute-start(f32[64,256]{1,0:T(8,128)S(1)} %bitcast.42), channel_id=1, source_target_pairs={{0,20},{4,16},{8,28},{12,24},{16,4},{20,0},{24,12},{28,8},{1,21},{... | collective-permute-start | bytes 196616 | tf_op jit(solution)/shard_map/ppermute | solution.py:94
  21.0 9.9 %collective-permute-start.3 = (f32[64,256]{1,0:T(8,128)S(1)}, f32[64,256]{1,0:T(8,128)S(1)}, u32[]{:S(2)}, u32[]{:S(2)}) collective-permute-start(f32[64,256]{1,0:T(8,128)S(1)} %bitcast.43), channel_id=1, source_target_pairs={{0,16},{4,20},{8,24},{12,28},{16,0},{20,4},{24,8},{28,12},{1,17},{... | collective-permute-start | bytes 196616 | tf_op jit(solution)/shard_map/ppermute | solution.py:94
  23.2 7.8 %collective-permute-start.2 = (f32[64,256]{1,0:T(8,128)S(1)}, f32[64,256]{1,0:T(8,128)S(1)}, u32[]{:S(2)}, u32[]{:S(2)}) collective-permute-start(f32[64,256]{1,0:T(8,128)S(1)} %bitcast.44), channel_id=1, source_target_pairs={{0,12},{4,8},{8,4},{12,0},{16,28},{20,24},{24,20},{28,16},{1,13},{... | collective-permute-start | bytes 196616 | tf_op jit(solution)/shard_map/ppermute | solution.py:94
  25.8 5.9 %collective-permute-start.1 = (f32[64,256]{1,0:T(8,128)S(1)}, f32[64,256]{1,0:T(8,128)S(1)}, u32[]{:S(2)}, u32[]{:S(2)}) collective-permute-start(f32[64,256]{1,0:T(8,128)S(1)} %bitcast.47), channel_id=1, source_target_pairs={{0,8},{4,12},{8,0},{12,4},{16,24},{20,28},{24,16},{28,20},{1,9},{5... | collective-permute-start | bytes 196616 | tf_op jit(solution)/shard_map/ppermute | solution.py:94
  26.6 5.1 %collective-permute-start = (f32[64,256]{1,0:T(8,128)S(1)}, f32[64,256]{1,0:T(8,128)S(1)}, u32[]{:S(2)}, u32[]{:S(2)}) collective-permute-start(f32[64,256]{1,0:T(8,128)S(1)} %bitcast.45), channel_id=1, source_target_pairs={{0,4},{4,0},{8,12},{12,8},{16,20},{20,16},{24,28},{28,24},{1,5},{5... | collective-permute-start | bytes 196616 | tf_op jit(solution)/shard_map/ppermute | solution.py:94
  37.9 8.5 %collective-permute-start.12 = (f32[64,256]{1,0:T(8,128)S(1)}, f32[64,256]{1,0:T(8,128)S(1)}, u32[]{:S(2)}, u32[]{:S(2)}) collective-permute-start(f32[64,256]{1,0:T(8,128)S(1)} %fusion.35), channel_id=1, source_target_pairs={{0,24},{4,28},{8,16},{12,20},{16,8},{20,12},{24,0},{28,4},{1,25},{... | collective-permute-start | bytes 196616 | tf_op jit(solution)/shard_map/ppermute | solution.py:35
  41.1 7.7 %collective-permute-start.13 = (f32[64,256]{1,0:T(8,128)S(1)}, f32[64,256]{1,0:T(8,128)S(1)}, u32[]{:S(2)}, u32[]{:S(2)}) collective-permute-start(f32[64,256]{1,0:T(8,128)S(1)} %fusion.35), channel_id=1, source_target_pairs={{0,28},{4,24},{8,20},{12,16},{16,12},{20,8},{24,4},{28,0},{1,29},{... | collective-permute-start | bytes 196616 | tf_op jit(solution)/shard_map/ppermute | solution.py:35
  42.1 10.1 %collective-permute-start.10 = (f32[64,256]{1,0:T(8,128)S(1)}, f32[64,256]{1,0:T(8,128)S(1)}, u32[]{:S(2)}, u32[]{:S(2)}) collective-permute-start(f32[64,256]{1,0:T(8,128)S(1)} %fusion.35), channel_id=1, source_target_pairs={{0,16},{4,20},{8,24},{12,28},{16,0},{20,4},{24,8},{28,12},{1,17},{... | collective-permute-start | bytes 196616 | tf_op jit(solution)/shard_map/ppermute | solution.py:35
  42.8 10.5 %collective-permute-start.11 = (f32[64,256]{1,0:T(8,128)S(1)}, f32[64,256]{1,0:T(8,128)S(1)}, u32[]{:S(2)}, u32[]{:S(2)}) collective-permute-start(f32[64,256]{1,0:T(8,128)S(1)} %fusion.35), channel_id=1, source_target_pairs={{0,20},{4,16},{8,28},{12,24},{16,4},{20,0},{24,12},{28,8},{1,21},{... | collective-permute-start | bytes 196616 | tf_op jit(solution)/shard_map/ppermute | solution.py:35
  45.6 7.6 %collective-permute-start.8 = (f32[64,256]{1,0:T(8,128)S(1)}, f32[64,256]{1,0:T(8,128)S(1)}, u32[]{:S(2)}, u32[]{:S(2)}) collective-permute-start(f32[64,256]{1,0:T(8,128)S(1)} %fusion.35), channel_id=1, source_target_pairs={{0,8},{4,12},{8,0},{12,4},{16,24},{20,28},{24,16},{28,20},{1,9},{5... | collective-permute-start | bytes 196616 | tf_op jit(solution)/shard_map/ppermute | solution.py:35
  46.4 7.3 %collective-permute-start.9 = (f32[64,256]{1,0:T(8,128)S(1)}, f32[64,256]{1,0:T(8,128)S(1)}, u32[]{:S(2)}, u32[]{:S(2)}) collective-permute-start(f32[64,256]{1,0:T(8,128)S(1)} %fusion.35), channel_id=1, source_target_pairs={{0,12},{4,8},{8,4},{12,0},{16,28},{20,24},{24,20},{28,16},{1,13},{... | collective-permute-start | bytes 196616 | tf_op jit(solution)/shard_map/ppermute | solution.py:35
  48.8 5.5 %collective-permute-start.7 = (f32[64,256]{1,0:T(8,128)S(1)}, f32[64,256]{1,0:T(8,128)S(1)}, u32[]{:S(2)}, u32[]{:S(2)}) collective-permute-start(f32[64,256]{1,0:T(8,128)S(1)} %fusion.35), channel_id=1, source_target_pairs={{0,4},{4,0},{8,12},{12,8},{16,20},{20,16},{24,28},{28,24},{1,5},{5... | collective-permute-start | bytes 196616 | tf_op jit(solution)/shard_map/ppermute | solution.py:35

commit v19 on v16

--- a/solution.py
+++ b/solution.py
@@ -75,11 +75,11 @@
         blocks,
         preferred_element_type=jnp.float32,
     )
-    pick = selection(offsets, my_index, groups, inner)
+    pick = lax.optimization_barrier(selection(offsets, my_index, groups, inner).astype(jnp.float32))
     sampled = jnp.einsum(
         "xcb,xbj->xcj",
         first,
-        pick.astype(jnp.float32),
+        pick,
         precision=lax.Precision.HIGH,
         preferred_element_type=jnp.float32,
     )

time: 52.6 us -> 47.6 us (0.905)
  matrix products: 9.08 us -> 5.09 us
  other arithmetic: 3.42 us -> 1.55 us
  local copies, waits for them, and re-layouts: 2.6 us -> 3.41 us
    dot_general x1, matrix products: 6.03 us -> 4 us  [per_device(): jnp.einsum('xcb,xbj->xcj', first, pick, precision=lax.Precision.HIGH, pre...]
    dot_general x1, matrix products: 2.68 us -> 0.72 us  [per_device(): jnp.einsum('xa,cab->xcb', hadamard(OUTER).astype(jnp.bfloat16), blocks, p...]
    mul x1, other arithmetic: 1.85 us -> 0.27 us  [per_device(): signed = panel * signs.astype(jnp.bfloat16)[None, :]]
    convert_element_type x1, other arithmetic: 0.84 us -> 0.01 us  [per_device(): signed = panel * signs.astype(jnp.bfloat16)[None, :]]
    reshape x1, local copies, waits for them, and re-layouts: 0.26 us -> 1.07 us  [selection(): off = offsets.reshape(groups, OUTER, per_row)]
    convert_element_type x0 -> x1, other arithmetic: none -> 0.56 us  [per_device(): selection(offsets, my_index, groups, inner).astype(jnp.float32)]
where the time goes in v19:
time: 47.6 us; the launch traced here: 47.4 us
  starting transfers between devices  19.1 us (40%)
  waiting for transfers between devices  12.2 us (26%)
  blocking collectives  5.79 us (12%)
  matrix products  5.09 us (11%)
  local copies, waits for them, and re-layouts  3.41 us (7%)
  other arithmetic  1.55 us (3%)
    ppermute x7, starting transfers between devices, per_device(): arrived.append(lax.ppermute(block, 'ev', pairs))  12.8 us
    ppermute x4, waiting for transfers between devices, group_sum(): values.append(lax.ppermute(value, 'ev', pairs))  7.52 us
    ppermute x4, starting transfers between devices, group_sum(): values.append(lax.ppermute(value, 'ev', pairs))  6.31 us
    all_gather x1, blocking collectives, per_device(): lax.all_gather(sketch, 'col', axis=0, tiled=True)  5.79 us
    ppermute x7, waiting for transfers between devices, per_device(): arrived.append(lax.ppermute(block, 'ev', pairs))  4.64 us
    dot_general x1, matrix products, per_device(): jnp.einsum('xcb,xbj->xcj', first, pick, precision=lax.Precision.HIGH, pre...  4 us
    reshape x1, local copies, waits for them, and re-layouts, selection(): off = offsets.reshape(groups, OUTER, per_row)  1.07 us
  transfers between devices with their start and end apart: 11, of which 7 were waited for; matrix products, arithmetic and copies ran while one was open for 1% of the time, Pallas kernels for 0%

profile of v19, /device:TPU:0, one launch (start us, length us, event | category | flops | bytes accessed | tf_op | source)
XLA Modules:
  0.0 47.4 jit_solution(15673399310167849981)
XLA Ops:
  0.2 1.1 %reshape.30 = s32[8,64,4]{2,1,0:T(8,128)S(1)} reshape(s32[2048]{0:T(1024)} %param.5) | data formatting | bytes 16384 | tf_op jit(solution)/shard_map/reshape | solution.py:51
  1.5 0.6 %fusion.2 = f32[64,256,32]{1,2,0:T(8,128)S(1)} fusion(s32[32]{0:T(128)S(1)} %xor.35, s32[64,32]{1,0:T(8,128)S(1)} %copy.12), kind=kLoop, calls=%fused_computation.3 | loop fusion | flops 4194304 | bytes 2105472 | tf_op jit(solution)/shard_map/convert_element_type | solution.py:78
  2.4 0.5 %copy.23 = bf16[8,8,64,256]{3,2,1,0:T(8,128)(2,1)S(1)} copy(bf16[8,8,64,256]{3,1,2,0:T(8,128)(2,1)S(1)} %bitcast.40) | data formatting | bytes 4194304
  2.9 0.7 %fusion.16 = f32[64,64,256]{2,0,1:T(8,128)S(1)} fusion(bf16[64,64,256]{2,1,0:T(8,128)(2,1)S(1)} %bitcast.39), kind=kOutput, calls=%fused_computation.24 | convolution fusion | flops 134352896 | bytes 6291456 | tf_op jit(solution)/shard_map/xa,cab->xcb/dot_general | solution.py:72
  3.7 4.0 %fusion = f32[64,64,32]{1,2,0:T(8,128)S(1)} fusion(f32[64,256,32]{1,2,0:T(8,128)S(1)} %fusion.2, f32[64,64,256]{2,0,1:T(8,128)S(1)} %fusion.16), kind=kOutput, calls=%fused_computation | convolution fusion | flops 201326592 | bytes 6815744 | tf_op jit(solution)/shard_map/xcb,xbj->xcj/dot_general | solution.py:79
  7.8 0.7 %constant_dynamic-slice_fusion.7 = (f32[1,64,256]{1,0,2:T(1,128)S(1)}, f32[1,64,256]{1,0,2:T(1,128)S(1)}, f32[1,64,256]{1,0,2:T(1,128)S(1)}, f32[1,64,256]{1,0,2...) fusion(f32[8,64,256]{1,0,2:T(8,128)S(1)} %bitcast.42, ...), kind=kLoop, calls=%fused_computation.38 | loop fusion | bytes 1048608 | tf_op jit(solution)/shard_map/jit(dynamic_index_in_dim)/dynamic_slice | solution.py:88
  8.6 6.1 %collective-permute-start.6 = (f32[64,256]{1,0:T(8,128)S(1)}, f32[64,256]{1,0:T(8,128)S(1)}, u32[]{:S(2)}, u32[]{:S(2)}) collective-permute-start(f32[64,256]{1,0:T(8,128)S(1)} %bitcast.49), channel_id=1, source_target_pairs={{0,28},{4,24},{8,20},{12,16},{16,12},{20,8},{24,4},{28,0},{1,29},{... | collective-permute-start | bytes 196616 | tf_op jit(solution)/shard_map/ppermute | solution.py:94
  15.2 0.8 %collective-permute-start.4 = (f32[64,256]{1,0:T(8,128)S(1)}, f32[64,256]{1,0:T(8,128)S(1)}, u32[]{:S(2)}, u32[]{:S(2)}) collective-permute-start(f32[64,256]{1,0:T(8,128)S(1)} %bitcast.43), channel_id=1, source_target_pairs={{0,20},{4,16},{8,28},{12,24},{16,4},{20,0},{24,12},{28,8},{1,21},{... | collective-permute-start | bytes 196616 | tf_op jit(solution)/shard_map/ppermute | solution.py:94
  16.0 2.0 %collective-permute-start.3 = (f32[64,256]{1,0:T(8,128)S(1)}, f32[64,256]{1,0:T(8,128)S(1)}, u32[]{:S(2)}, u32[]{:S(2)}) collective-permute-start(f32[64,256]{1,0:T(8,128)S(1)} %bitcast.44), channel_id=1, source_target_pairs={{0,16},{4,20},{8,24},{12,28},{16,0},{20,4},{24,8},{28,12},{1,17},{... | collective-permute-start | bytes 196616 | tf_op jit(solution)/shard_map/ppermute | solution.py:94
  18.2 2.4 %collective-permute-start.2 = (f32[64,256]{1,0:T(8,128)S(1)}, f32[64,256]{1,0:T(8,128)S(1)}, u32[]{:S(2)}, u32[]{:S(2)}) collective-permute-start(f32[64,256]{1,0:T(8,128)S(1)} %bitcast.45), channel_id=1, source_target_pairs={{0,12},{4,8},{8,4},{12,0},{16,28},{20,24},{24,20},{28,16},{1,13},{... | collective-permute-start | bytes 196616 | tf_op jit(solution)/shard_map/ppermute | solution.py:94
  20.8 0.8 %collective-permute-start.1 = (f32[64,256]{1,0:T(8,128)S(1)}, f32[64,256]{1,0:T(8,128)S(1)}, u32[]{:S(2)}, u32[]{:S(2)}) collective-permute-start(f32[64,256]{1,0:T(8,128)S(1)} %bitcast.48), channel_id=1, source_target_pairs={{0,8},{4,12},{8,0},{12,4},{16,24},{20,28},{24,16},{28,20},{1,9},{5... | collective-permute-start | bytes 196616 | tf_op jit(solution)/shard_map/ppermute | solution.py:94
  22.1 1.9 %collective-permute-done.4 = f32[64,256]{1,0:T(8,128)S(1)} collective-permute-done((f32[64,256]{1,0:T(8,128)S(1)}, f32[64,256]{1,0:T(8,128)S(1)}, u32[]{:S(2)}, u32[]{:S(2)}) %collective-permute-start.4) | collective-permute-done | bytes 65568 | tf_op jit(solution)/shard_map/ppermute | solution.py:94
  24.0 2.0 %collective-permute-done.3 = f32[64,256]{1,0:T(8,128)S(1)} collective-permute-done((f32[64,256]{1,0:T(8,128)S(1)}, f32[64,256]{1,0:T(8,128)S(1)}, u32[]{:S(2)}, u32[]{:S(2)}) %collective-permute-start.3) | collective-permute-done | bytes 65568 | tf_op jit(solution)/shard_map/ppermute | solution.py:94
  26.0 0.7 %collective-permute-done.1 = f32[64,256]{1,0:T(8,128)S(1)} collective-permute-done((f32[64,256]{1,0:T(8,128)S(1)}, f32[64,256]{1,0:T(8,128)S(1)}, u32[]{:S(2)}, u32[]{:S(2)}) %collective-permute-start.1) | collective-permute-done | bytes 65568 | tf_op jit(solution)/shard_map/ppermute | solution.py:94
  26.7 5.8 %all_gather.3 = f32[256,256]{1,0:T(8,128)S(1)} all-gather(f32[64,256]{1,0:T(8,128)S(1)} %fusion.9), channel_id=1, replica_groups=mesh['ev'=8,'col'=4] {'col'}, dimensions={0}, use_global_device_ids=true | all-gather | bytes 327680 | tf_op jit(solution)/shard_map/all_gather | solution.py:104
  32.9 1.2 %collective-permute-start.8 = (f32[64,256]{1,0:T(8,128)S(1)}, f32[64,256]{1,0:T(8,128)S(1)}, u32[]{:S(2)}, u32[]{:S(2)}) collective-permute-start(f32[64,256]{1,0:T(8,128)S(1)} %fusion.30), channel_id=1, source_target_pairs={{0,8},{4,12},{8,0},{12,4},{16,24},{20,28},{24,16},{28,20},{1,9},{5... | collective-permute-start | bytes 196616 | tf_op jit(solution)/shard_map/ppermute | solution.py:35
  34.1 1.1 %collective-permute-start.9 = (f32[64,256]{1,0:T(8,128)S(1)}, f32[64,256]{1,0:T(8,128)S(1)}, u32[]{:S(2)}, u32[]{:S(2)}) collective-permute-start(f32[64,256]{1,0:T(8,128)S(1)} %fusion.30), channel_id=1, source_target_pairs={{0,12},{4,8},{8,4},{12,0},{16,28},{20,24},{24,20},{28,16},{1,13},{... | collective-permute-start | bytes 196616 | tf_op jit(solution)/shard_map/ppermute | solution.py:35
  35.2 1.3 %collective-permute-start.7 = (f32[64,256]{1,0:T(8,128)S(1)}, f32[64,256]{1,0:T(8,128)S(1)}, u32[]{:S(2)}, u32[]{:S(2)}) collective-permute-start(f32[64,256]{1,0:T(8,128)S(1)} %fusion.30), channel_id=1, source_target_pairs={{0,4},{4,0},{8,12},{12,8},{16,20},{20,16},{24,28},{28,24},{1,5},{5... | collective-permute-start | bytes 196616 | tf_op jit(solution)/shard_map/ppermute | solution.py:35
  36.5 1.4 %collective-permute-done.8 = f32[64,256]{1,0:T(8,128)S(1)} collective-permute-done((f32[64,256]{1,0:T(8,128)S(1)}, f32[64,256]{1,0:T(8,128)S(1)}, u32[]{:S(2)}, u32[]{:S(2)}) %collective-permute-start.8) | collective-permute-done | bytes 65568 | tf_op jit(solution)/shard_map/ppermute | solution.py:35
  37.9 1.5 %collective-permute-done.9 = f32[64,256]{1,0:T(8,128)S(1)} collective-permute-done((f32[64,256]{1,0:T(8,128)S(1)}, f32[64,256]{1,0:T(8,128)S(1)}, u32[]{:S(2)}, u32[]{:S(2)}) %collective-permute-start.9) | collective-permute-done | bytes 65568 | tf_op jit(solution)/shard_map/ppermute | solution.py:35
  39.3 1.1 %collective-permute-done.7 = f32[64,256]{1,0:T(8,128)S(1)} collective-permute-done((f32[64,256]{1,0:T(8,128)S(1)}, f32[64,256]{1,0:T(8,128)S(1)}, u32[]{:S(2)}, u32[]{:S(2)}) %collective-permute-start.7) | collective-permute-done | bytes 65568 | tf_op jit(solution)/shard_map/ppermute | solution.py:35
  40.4 2.8 %collective-permute-start.10 = (f32[64,256]{1,0:T(8,128)S(1)}, f32[64,256]{1,0:T(8,128)S(1)}, u32[]{:S(2)}, u32[]{:S(2)}) collective-permute-start(f32[64,256]{1,0:T(8,128)S(1)} %add_add_fusion), channel_id=1, source_target_pairs={{0,16},{4,20},{8,24},{12,28},{16,0},{20,4},{24,8},{28,12},{1,17},{... | collective-permute-start | bytes 196616 | tf_op jit(solution)/shard_map/ppermute | solution.py:35
  43.2 3.6 %collective-permute-done.10 = f32[64,256]{1,0:T(8,128)S(1)} collective-permute-done((f32[64,256]{1,0:T(8,128)S(1)}, f32[64,256]{1,0:T(8,128)S(1)}, u32[]{:S(2)}, u32[]{:S(2)}) %collective-permute-start.10) | collective-permute-done | bytes 65568 | tf_op jit(solution)/shard_map/ppermute | solution.py:35
  46.8 0.6 %add.113 = f32[64,256]{1,0:T(8,128)} add(f32[64,256]{1,0:T(8,128)S(1)} %add_add_fusion, f32[64,256]{1,0:T(8,128)S(1)} %collective-permute-done.10) | non-fusion elementwise | flops 16384 | bytes 196608 | tf_op jit(solution)/shard_map/add | solution.py:37
  (31 shorter events, 2.4 us)
Async XLA Ops:
  0.0 2.1 %copy-start.1 = (s32[16384]{0:T(1024)S(1)}, s32[16384]{0:T(1024)}, u32[]{:S(2)}) copy-start(s32[16384]{0:T(1024)} %param.4) | copy-start | bytes 196612
  0.0 2.1 %copy-start = (bf16[64,16384]{1,0:T(8,128)(2,1)S(1)}, bf16[64,16384]{1,0:T(8,128)(2,1)}, u32[]{:S(2)}) copy-start(bf16[64,16384]{1,0:T(8,128)(2,1)} %param.3) | copy-start | bytes 6291460
  8.6 12.2 %collective-permute-start.6 = (f32[64,256]{1,0:T(8,128)S(1)}, f32[64,256]{1,0:T(8,128)S(1)}, u32[]{:S(2)}, u32[]{:S(2)}) collective-permute-start(f32[64,256]{1,0:T(8,128)S(1)} %bitcast.49), channel_id=1, source_target_pairs={{0,28},{4,24},{8,20},{12,16},{16,12},{20,8},{24,4},{28,0},{1,29},{... | collective-permute-start | bytes 196616 | tf_op jit(solution)/shard_map/ppermute | solution.py:94
  14.8 6.8 %collective-permute-start.5 = (f32[64,256]{1,0:T(8,128)S(1)}, f32[64,256]{1,0:T(8,128)S(1)}, u32[]{:S(2)}, u32[]{:S(2)}) collective-permute-start(f32[64,256]{1,0:T(8,128)S(1)} %bitcast.47), channel_id=1, source_target_pairs={{0,24},{4,28},{8,16},{12,20},{16,8},{20,12},{24,0},{28,4},{1,25},{... | collective-permute-start | bytes 196616 | tf_op jit(solution)/shard_map/ppermute | solution.py:94
  15.2 8.8 %collective-permute-start.4 = (f32[64,256]{1,0:T(8,128)S(1)}, f32[64,256]{1,0:T(8,128)S(1)}, u32[]{:S(2)}, u32[]{:S(2)}) collective-permute-start(f32[64,256]{1,0:T(8,128)S(1)} %bitcast.43), channel_id=1, source_target_pairs={{0,20},{4,16},{8,28},{12,24},{16,4},{20,0},{24,12},{28,8},{1,21},{... | collective-permute-start | bytes 196616 | tf_op jit(solution)/shard_map/ppermute | solution.py:94
  16.0 9.9 %collective-permute-start.3 = (f32[64,256]{1,0:T(8,128)S(1)}, f32[64,256]{1,0:T(8,128)S(1)}, u32[]{:S(2)}, u32[]{:S(2)}) collective-permute-start(f32[64,256]{1,0:T(8,128)S(1)} %bitcast.44), channel_id=1, source_target_pairs={{0,16},{4,20},{8,24},{12,28},{16,0},{20,4},{24,8},{28,12},{1,17},{... | collective-permute-start | bytes 196616 | tf_op jit(solution)/shard_map/ppermute | solution.py:94
  18.2 7.8 %collective-permute-start.2 = (f32[64,256]{1,0:T(8,128)S(1)}, f32[64,256]{1,0:T(8,128)S(1)}, u32[]{:S(2)}, u32[]{:S(2)}) collective-permute-start(f32[64,256]{1,0:T(8,128)S(1)} %bitcast.45), channel_id=1, source_target_pairs={{0,12},{4,8},{8,4},{12,0},{16,28},{20,24},{24,20},{28,16},{1,13},{... | collective-permute-start | bytes 196616 | tf_op jit(solution)/shard_map/ppermute | solution.py:94
  20.8 5.9 %collective-permute-start.1 = (f32[64,256]{1,0:T(8,128)S(1)}, f32[64,256]{1,0:T(8,128)S(1)}, u32[]{:S(2)}, u32[]{:S(2)}) collective-permute-start(f32[64,256]{1,0:T(8,128)S(1)} %bitcast.48), channel_id=1, source_target_pairs={{0,8},{4,12},{8,0},{12,4},{16,24},{20,28},{24,16},{28,20},{1,9},{5... | collective-permute-start | bytes 196616 | tf_op jit(solution)/shard_map/ppermute | solution.py:94
  21.6 5.1 %collective-permute-start = (f32[64,256]{1,0:T(8,128)S(1)}, f32[64,256]{1,0:T(8,128)S(1)}, u32[]{:S(2)}, u32[]{:S(2)}) collective-permute-start(f32[64,256]{1,0:T(8,128)S(1)} %bitcast.46), channel_id=1, source_target_pairs={{0,4},{4,0},{8,12},{12,8},{16,20},{20,16},{24,28},{28,24},{1,5},{5... | collective-permute-start | bytes 196616 | tf_op jit(solution)/shard_map/ppermute | solution.py:94
  32.9 5.0 %collective-permute-start.8 = (f32[64,256]{1,0:T(8,128)S(1)}, f32[64,256]{1,0:T(8,128)S(1)}, u32[]{:S(2)}, u32[]{:S(2)}) collective-permute-start(f32[64,256]{1,0:T(8,128)S(1)} %fusion.30), channel_id=1, source_target_pairs={{0,8},{4,12},{8,0},{12,4},{16,24},{20,28},{24,16},{28,20},{1,9},{5... | collective-permute-start | bytes 196616 | tf_op jit(solution)/shard_map/ppermute | solution.py:35
  34.1 5.2 %collective-permute-start.9 = (f32[64,256]{1,0:T(8,128)S(1)}, f32[64,256]{1,0:T(8,128)S(1)}, u32[]{:S(2)}, u32[]{:S(2)}) collective-permute-start(f32[64,256]{1,0:T(8,128)S(1)} %fusion.30), channel_id=1, source_target_pairs={{0,12},{4,8},{8,4},{12,0},{16,28},{20,24},{24,20},{28,16},{1,13},{... | collective-permute-start | bytes 196616 | tf_op jit(solution)/shard_map/ppermute | solution.py:35
  35.2 5.2 %collective-permute-start.7 = (f32[64,256]{1,0:T(8,128)S(1)}, f32[64,256]{1,0:T(8,128)S(1)}, u32[]{:S(2)}, u32[]{:S(2)}) collective-permute-start(f32[64,256]{1,0:T(8,128)S(1)} %fusion.30), channel_id=1, source_target_pairs={{0,4},{4,0},{8,12},{12,8},{16,20},{20,16},{24,28},{28,24},{1,5},{5... | collective-permute-start | bytes 196616 | tf_op jit(solution)/shard_map/ppermute | solution.py:35
  40.4 6.4 %collective-permute-start.10 = (f32[64,256]{1,0:T(8,128)S(1)}, f32[64,256]{1,0:T(8,128)S(1)}, u32[]{:S(2)}, u32[]{:S(2)}) collective-permute-start(f32[64,256]{1,0:T(8,128)S(1)} %add_add_fusion), channel_id=1, source_target_pairs={{0,16},{4,20},{8,24},{12,28},{16,0},{20,4},{24,8},{28,12},{1,17},{... | collective-permute-start | bytes 196616 | tf_op jit(solution)/shard_map/ppermute | solution.py:35

commit v20 on v19

--- a/solution.py
+++ b/solution.py
@@ -6,7 +6,7 @@
 from jax.sharding import PartitionSpec as P
 
 STRIDE = 64
-OUTER = 64
+OUTER = 32
 
 
 def hadamard(order):

time: 47.6 us -> 51.7 us (1.086)
  other arithmetic: 1.55 us -> 4.48 us
  waiting for transfers between devices: 12.2 us -> 13.8 us
  local copies, waits for them, and re-layouts: 3.41 us -> 2.63 us
  matrix products: 5.09 us -> 5.78 us
    ppermute x7, waiting for transfers between devices: 4.64 us -> 6.97 us  [per_device(): arrived.append(lax.ppermute(block, 'ev', pairs))]
    mul x1, other arithmetic: 0.27 us -> 1.87 us  [per_device(): signed = panel * signs.astype(jnp.bfloat16)[None, :]]
    convert_element_type x1, other arithmetic: 0.01 us -> 0.85 us  [per_device(): signed = panel * signs.astype(jnp.bfloat16)[None, :]]
    dot_general x1, matrix products: 4 us -> 4.72 us  [per_device(): jnp.einsum('xcb,xbj->xcj', first, pick, precision=lax.Precision.HIGH, pre...]
    ppermute x4, waiting for transfers between devices: 7.52 us -> 6.85 us  [group_sum(): values.append(lax.ppermute(value, 'ev', pairs))]
    dynamic_slice x2, local copies, waits for them, and re-layouts: 0.82 us -> 0.17 us  [per_device(): own = lax.dynamic_index_in_dim(chunks, my_index, axis=0, keepdims=False)]
  transfers between devices with their start and end apart: 11 -> 11, of which waited for: 7 -> 5; matrix products, arithmetic and copies ran while one was open for 1% -> 1% of each run, Pallas kernels for 0% -> 0%
where the time goes in v20:
time: 51.7 us; the launch traced here: 51.5 us
  starting transfers between devices  18.7 us (36%)
  waiting for transfers between devices  13.8 us (27%)
  blocking collectives  5.79 us (11%)
  matrix products  5.78 us (11%)
  other arithmetic  4.48 us (9%)
  local copies, waits for them, and re-layouts  2.63 us (5%)
    ppermute x7, starting transfers between devices, per_device(): arrived.append(lax.ppermute(block, 'ev', pairs))  12.8 us
    ppermute x7, waiting for transfers between devices, per_device(): arrived.append(lax.ppermute(block, 'ev', pairs))  6.97 us
    ppermute x4, waiting for transfers between devices, group_sum(): values.append(lax.ppermute(value, 'ev', pairs))  6.85 us
    ppermute x4, starting transfers between devices, group_sum(): values.append(lax.ppermute(value, 'ev', pairs))  5.9 us
    all_gather x1, blocking collectives, per_device(): lax.all_gather(sketch, 'col', axis=0, tiled=True)  5.79 us
    dot_general x1, matrix products, per_device(): jnp.einsum('xcb,xbj->xcj', first, pick, precision=lax.Precision.HIGH, pre...  4.72 us
    mul x1, other arithmetic, per_device(): signed = panel * signs.astype(jnp.bfloat16)[None, :]  1.87 us
    convert_element_type x1, other arithmetic, per_device(): selection(offsets, my_index, groups, inner).astype(jnp.float32)  1.05 us
  transfers between devices with their start and end apart: 11, of which 5 were waited for; matrix products, arithmetic and copies ran while one was open for 1% of the time, Pallas kernels for 0%

profile of v20, /device:TPU:0, one launch (start us, length us, event | category | flops | bytes accessed | tf_op | source)
XLA Modules:
  0.0 51.5 jit_solution(12834523681602536183)
XLA Ops:
  0.2 0.8 %convert_element_type.18 = bf16[16384]{0:T(1024)(128)(2,1)S(1)} convert(s32[16384]{0:T(1024)} %param.4) | non-fusion elementwise | flops 16384 | bytes 98304 | tf_op jit(solution)/shard_map/convert_element_type | solution.py:70
  1.0 0.8 %reshape.30 = s32[8,32,8]{2,1,0:T(8,128)S(1)} reshape(s32[2048]{0:T(1024)} %param.5) | data formatting | bytes 16384 | tf_op jit(solution)/shard_map/reshape | solution.py:51
  2.0 1.9 %broadcast_multiply_fusion = bf16[64,16384]{1,0:T(8,128)(2,1)S(1)} fusion(bf16[64,16384]{1,0:T(8,128)(2,1)} %param.3, bf16[16384]{0:T(1024)(128)(2,1)S(1)} %convert_element_type.18), kind=kLoop, calls=%fused_computation.6 | loop fusion | flops 1048576 | bytes 4227072 | tf_op jit(solution)/shard_map/mul | solution.py:70
  3.9 0.8 %copy.27 = bf16[8,8,32,512]{3,2,1,0:T(8,128)(2,1)S(1)} copy(bf16[8,8,32,512]{3,1,2,0:T(8,128)(2,1)S(1)} %bitcast.43) | data formatting | bytes 4194304
  4.6 0.7 %fusion.19 = f32[32,64,512]{2,0,1:T(8,128)S(1)} fusion(bf16[64,32,512]{2,1,0:T(8,128)(2,1)S(1)} %bitcast.42), kind=kOutput, calls=%fused_computation.26 | convolution fusion | flops 67139584 | bytes 6291456 | tf_op jit(solution)/shard_map/xa,cab->xcb/dot_general | solution.py:72
  5.3 1.1 %fusion.2 = f32[32,512,64]{1,2,0:T(8,128)S(1)} fusion(s32[64]{0:T(128)S(1)} %xor.35, s32[32,64]{1,0:T(8,128)S(1)} %copy.14), kind=kLoop, calls=%fused_computation.3 | loop fusion | flops 8388608 | bytes 4202752 | tf_op jit(solution)/shard_map/convert_element_type | solution.py:78
  6.4 4.7 %fusion.3 = f32[8,64,32,8]{1,3,0,2:T(8,128)S(1)} fusion(f32[32,512,64]{1,2,0:T(8,128)S(1)} %fusion.2, f32[32,64,512]{2,0,1:T(8,128)S(1)} %fusion.19), kind=kOutput, calls=%fused_computation.4 | convolution fusion | flops 402653184 | bytes 8912896 | tf_op jit(solution)/shard_map/xcb,xbj->xcj/dot_general | solution.py:79
  11.4 3.0 %collective-permute-start = (f32[64,256]{1,0:T(8,128)S(1)}, f32[64,256]{1,0:T(8,128)S(1)}, u32[]{:S(2)}, u32[]{:S(2)}) collective-permute-start(f32[64,256]{1,0:T(8,128)S(1)} %bitcast.51), channel_id=1, source_target_pairs={{0,4},{4,0},{8,12},{12,8},{16,20},{20,16},{24,28},{28,24},{1,5},{5... | collective-permute-start | bytes 196616 | tf_op jit(solution)/shard_map/ppermute | solution.py:94
  14.5 1.6 %collective-permute-start.1 = (f32[64,256]{1,0:T(8,128)S(1)}, f32[64,256]{1,0:T(8,128)S(1)}, u32[]{:S(2)}, u32[]{:S(2)}) collective-permute-start(f32[64,256]{1,0:T(8,128)S(1)} %bitcast.50), channel_id=1, source_target_pairs={{0,8},{4,12},{8,0},{12,4},{16,24},{20,28},{24,16},{28,20},{1,9},{5... | collective-permute-start | bytes 196616 | tf_op jit(solution)/shard_map/ppermute | solution.py:94
  16.4 3.1 %collective-permute-start.3 = (f32[64,256]{1,0:T(8,128)S(1)}, f32[64,256]{1,0:T(8,128)S(1)}, u32[]{:S(2)}, u32[]{:S(2)}) collective-permute-start(f32[64,256]{1,0:T(8,128)S(1)} %bitcast.47), channel_id=1, source_target_pairs={{0,16},{4,20},{8,24},{12,28},{16,0},{20,4},{24,8},{28,12},{1,17},{... | collective-permute-start | bytes 196616 | tf_op jit(solution)/shard_map/ppermute | solution.py:94
  19.6 1.3 %collective-permute-start.4 = (f32[64,256]{1,0:T(8,128)S(1)}, f32[64,256]{1,0:T(8,128)S(1)}, u32[]{:S(2)}, u32[]{:S(2)}) collective-permute-start(f32[64,256]{1,0:T(8,128)S(1)} %bitcast.49), channel_id=1, source_target_pairs={{0,20},{4,16},{8,28},{12,24},{16,4},{20,0},{24,12},{28,8},{1,21},{... | collective-permute-start | bytes 196616 | tf_op jit(solution)/shard_map/ppermute | solution.py:94
  21.1 3.7 %collective-permute-start.5 = (f32[64,256]{1,0:T(8,128)S(1)}, f32[64,256]{1,0:T(8,128)S(1)}, u32[]{:S(2)}, u32[]{:S(2)}) collective-permute-start(f32[64,256]{1,0:T(8,128)S(1)} %bitcast.52), channel_id=1, source_target_pairs={{0,24},{4,28},{8,16},{12,20},{16,8},{20,12},{24,0},{28,4},{1,25},{... | collective-permute-start | bytes 196616 | tf_op jit(solution)/shard_map/ppermute | solution.py:94
  24.9 4.5 %collective-permute-done.4 = f32[64,256]{1,0:T(8,128)S(1)} collective-permute-done((f32[64,256]{1,0:T(8,128)S(1)}, f32[64,256]{1,0:T(8,128)S(1)}, u32[]{:S(2)}, u32[]{:S(2)}) %collective-permute-start.4) | collective-permute-done | bytes 65568 | tf_op jit(solution)/shard_map/ppermute | solution.py:94
  29.4 2.5 %collective-permute-done.6 = f32[64,256]{1,0:T(8,128)S(1)} collective-permute-done((f32[64,256]{1,0:T(8,128)S(1)}, f32[64,256]{1,0:T(8,128)S(1)}, u32[]{:S(2)}, u32[]{:S(2)}) %collective-permute-start.6) | collective-permute-done | bytes 65568 | tf_op jit(solution)/shard_map/ppermute | solution.py:94
  31.9 5.8 %all_gather.3 = f32[256,256]{1,0:T(8,128)S(1)} all-gather(f32[64,256]{1,0:T(8,128)S(1)} %fusion.12), channel_id=1, replica_groups=mesh['ev'=8,'col'=4] {'col'}, dimensions={0}, use_global_device_ids=true | all-gather | bytes 327680 | tf_op jit(solution)/shard_map/all_gather | solution.py:104
  37.7 0.4 fusion.31
  38.0 1.6 %collective-permute-start.9 = (f32[64,256]{1,0:T(8,128)S(1)}, f32[64,256]{1,0:T(8,128)S(1)}, u32[]{:S(2)}, u32[]{:S(2)}) collective-permute-start(f32[64,256]{1,0:T(8,128)S(1)} %fusion.31), channel_id=1, source_target_pairs={{0,12},{4,8},{8,4},{12,0},{16,28},{20,24},{24,20},{28,16},{1,13},{... | collective-permute-start | bytes 196616 | tf_op jit(solution)/shard_map/ppermute | solution.py:35
  39.6 0.4 collective-permute-start.8
  40.0 1.6 %collective-permute-start.7 = (f32[64,256]{1,0:T(8,128)S(1)}, f32[64,256]{1,0:T(8,128)S(1)}, u32[]{:S(2)}, u32[]{:S(2)}) collective-permute-start(f32[64,256]{1,0:T(8,128)S(1)} %fusion.31), channel_id=1, source_target_pairs={{0,4},{4,0},{8,12},{12,8},{16,20},{20,16},{24,28},{28,24},{1,5},{5... | collective-permute-start | bytes 196616 | tf_op jit(solution)/shard_map/ppermute | solution.py:35
  41.6 2.3 %collective-permute-done.9 = f32[64,256]{1,0:T(8,128)S(1)} collective-permute-done((f32[64,256]{1,0:T(8,128)S(1)}, f32[64,256]{1,0:T(8,128)S(1)}, u32[]{:S(2)}, u32[]{:S(2)}) %collective-permute-start.9) | collective-permute-done | bytes 65568 | tf_op jit(solution)/shard_map/ppermute | solution.py:35
  43.9 0.8 %collective-permute-done.7 = f32[64,256]{1,0:T(8,128)S(1)} collective-permute-done((f32[64,256]{1,0:T(8,128)S(1)}, f32[64,256]{1,0:T(8,128)S(1)}, u32[]{:S(2)}, u32[]{:S(2)}) %collective-permute-start.7) | collective-permute-done | bytes 65568 | tf_op jit(solution)/shard_map/ppermute | solution.py:35
  44.8 2.4 %collective-permute-start.10 = (f32[64,256]{1,0:T(8,128)S(1)}, f32[64,256]{1,0:T(8,128)S(1)}, u32[]{:S(2)}, u32[]{:S(2)}) collective-permute-start(f32[64,256]{1,0:T(8,128)S(1)} %add_add_fusion), channel_id=1, source_target_pairs={{0,16},{4,20},{8,24},{12,28},{16,0},{20,4},{24,8},{28,12},{1,17},{... | collective-permute-start | bytes 196616 | tf_op jit(solution)/shard_map/ppermute | solution.py:35
  47.1 3.7 %collective-permute-done.10 = f32[64,256]{1,0:T(8,128)S(1)} collective-permute-done((f32[64,256]{1,0:T(8,128)S(1)}, f32[64,256]{1,0:T(8,128)S(1)}, u32[]{:S(2)}, u32[]{:S(2)}) %collective-permute-start.10) | collective-permute-done | bytes 65568 | tf_op jit(solution)/shard_map/ppermute | solution.py:35
  50.8 0.6 %add.109 = f32[64,256]{1,0:T(8,128)} add(f32[64,256]{1,0:T(8,128)S(1)} %add_add_fusion, f32[64,256]{1,0:T(8,128)S(1)} %collective-permute-done.10) | non-fusion elementwise | flops 16384 | bytes 196608 | tf_op jit(solution)/shard_map/add | solution.py:37
  (27 shorter events, 1.2 us)
Async XLA Ops:
  11.4 9.7 %collective-permute-start = (f32[64,256]{1,0:T(8,128)S(1)}, f32[64,256]{1,0:T(8,128)S(1)}, u32[]{:S(2)}, u32[]{:S(2)}) collective-permute-start(f32[64,256]{1,0:T(8,128)S(1)} %bitcast.51), channel_id=1, source_target_pairs={{0,4},{4,0},{8,12},{12,8},{16,20},{20,16},{24,28},{28,24},{1,5},{5... | collective-permute-start | bytes 196616 | tf_op jit(solution)/shard_map/ppermute | solution.py:94
  14.5 10.3 %collective-permute-start.1 = (f32[64,256]{1,0:T(8,128)S(1)}, f32[64,256]{1,0:T(8,128)S(1)}, u32[]{:S(2)}, u32[]{:S(2)}) collective-permute-start(f32[64,256]{1,0:T(8,128)S(1)} %bitcast.50), channel_id=1, source_target_pairs={{0,8},{4,12},{8,0},{12,4},{16,24},{20,28},{24,16},{28,20},{1,9},{5... | collective-permute-start | bytes 196616 | tf_op jit(solution)/shard_map/ppermute | solution.py:94
  16.3 8.6 %collective-permute-start.2 = (f32[64,256]{1,0:T(8,128)S(1)}, f32[64,256]{1,0:T(8,128)S(1)}, u32[]{:S(2)}, u32[]{:S(2)}) collective-permute-start(f32[64,256]{1,0:T(8,128)S(1)} %bitcast.46), channel_id=1, source_target_pairs={{0,12},{4,8},{8,4},{12,0},{16,28},{20,24},{24,20},{28,16},{1,13},{... | collective-permute-start | bytes 196616 | tf_op jit(solution)/shard_map/ppermute | solution.py:94
  16.4 8.5 %collective-permute-start.3 = (f32[64,256]{1,0:T(8,128)S(1)}, f32[64,256]{1,0:T(8,128)S(1)}, u32[]{:S(2)}, u32[]{:S(2)}) collective-permute-start(f32[64,256]{1,0:T(8,128)S(1)} %bitcast.47), channel_id=1, source_target_pairs={{0,16},{4,20},{8,24},{12,28},{16,0},{20,4},{24,8},{28,12},{1,17},{... | collective-permute-start | bytes 196616 | tf_op jit(solution)/shard_map/ppermute | solution.py:94
  19.6 9.8 %collective-permute-start.4 = (f32[64,256]{1,0:T(8,128)S(1)}, f32[64,256]{1,0:T(8,128)S(1)}, u32[]{:S(2)}, u32[]{:S(2)}) collective-permute-start(f32[64,256]{1,0:T(8,128)S(1)} %bitcast.49), channel_id=1, source_target_pairs={{0,20},{4,16},{8,28},{12,24},{16,4},{20,0},{24,12},{28,8},{1,21},{... | collective-permute-start | bytes 196616 | tf_op jit(solution)/shard_map/ppermute | solution.py:94
  21.1 8.3 %collective-permute-start.5 = (f32[64,256]{1,0:T(8,128)S(1)}, f32[64,256]{1,0:T(8,128)S(1)}, u32[]{:S(2)}, u32[]{:S(2)}) collective-permute-start(f32[64,256]{1,0:T(8,128)S(1)} %bitcast.52), channel_id=1, source_target_pairs={{0,24},{4,28},{8,16},{12,20},{16,8},{20,12},{24,0},{28,4},{1,25},{... | collective-permute-start | bytes 196616 | tf_op jit(solution)/shard_map/ppermute | solution.py:94
  24.8 7.1 %collective-permute-start.6 = (f32[64,256]{1,0:T(8,128)S(1)}, f32[64,256]{1,0:T(8,128)S(1)}, u32[]{:S(2)}, u32[]{:S(2)}) collective-permute-start(f32[64,256]{1,0:T(8,128)S(1)} %bitcast.48), channel_id=1, source_target_pairs={{0,28},{4,24},{8,20},{12,16},{16,12},{20,8},{24,4},{28,0},{1,29},{... | collective-permute-start | bytes 196616 | tf_op jit(solution)/shard_map/ppermute | solution.py:94
  38.0 5.9 %collective-permute-start.9 = (f32[64,256]{1,0:T(8,128)S(1)}, f32[64,256]{1,0:T(8,128)S(1)}, u32[]{:S(2)}, u32[]{:S(2)}) collective-permute-start(f32[64,256]{1,0:T(8,128)S(1)} %fusion.31), channel_id=1, source_target_pairs={{0,12},{4,8},{8,4},{12,0},{16,28},{20,24},{24,20},{28,16},{1,13},{... | collective-permute-start | bytes 196616 | tf_op jit(solution)/shard_map/ppermute | solution.py:35
  39.6 4.3 %collective-permute-start.8 = (f32[64,256]{1,0:T(8,128)S(1)}, f32[64,256]{1,0:T(8,128)S(1)}, u32[]{:S(2)}, u32[]{:S(2)}) collective-permute-start(f32[64,256]{1,0:T(8,128)S(1)} %fusion.31), channel_id=1, source_target_pairs={{0,8},{4,12},{8,0},{12,4},{16,24},{20,28},{24,16},{28,20},{1,9},{5... | collective-permute-start | bytes 196616 | tf_op jit(solution)/shard_map/ppermute | solution.py:35
  40.0 4.7 %collective-permute-start.7 = (f32[64,256]{1,0:T(8,128)S(1)}, f32[64,256]{1,0:T(8,128)S(1)}, u32[]{:S(2)}, u32[]{:S(2)}) collective-permute-start(f32[64,256]{1,0:T(8,128)S(1)} %fusion.31), channel_id=1, source_target_pairs={{0,4},{4,0},{8,12},{12,8},{16,20},{20,16},{24,28},{28,24},{1,5},{5... | collective-permute-start | bytes 196616 | tf_op jit(solution)/shard_map/ppermute | solution.py:35
  44.8 6.0 %collective-permute-start.10 = (f32[64,256]{1,0:T(8,128)S(1)}, f32[64,256]{1,0:T(8,128)S(1)}, u32[]{:S(2)}, u32[]{:S(2)}) collective-permute-start(f32[64,256]{1,0:T(8,128)S(1)} %add_add_fusion), channel_id=1, source_target_pairs={{0,16},{4,20},{8,24},{12,28},{16,0},{20,4},{24,8},{28,12},{1,17},{... | collective-permute-start | bytes 196616 | tf_op jit(solution)/shard_map/ppermute | solution.py:35

commit v21 on v20

--- a/solution.py
+++ b/solution.py
@@ -6,7 +6,7 @@
 from jax.sharding import PartitionSpec as P
 
 STRIDE = 64
-OUTER = 32
+OUTER = 128
 
 
 def hadamard(order):

time: 51.7 us -> 48.7 us (0.942)
  other arithmetic: 4.48 us -> 1.36 us
  waiting for transfers between devices: 13.8 us -> 12.2 us
  local copies, waits for them, and re-layouts: 2.63 us -> 3.73 us
    ppermute x7, waiting for transfers between devices: 6.97 us -> 4.65 us  [per_device(): arrived.append(lax.ppermute(block, 'ev', pairs))]
    mul x1 -> x0, other arithmetic: 1.87 us -> none  [per_device(): signed = panel * signs.astype(jnp.bfloat16)[None, :]]
    convert_element_type x1, other arithmetic: 0.85 us -> 0.01 us  [per_device(): signed = panel * signs.astype(jnp.bfloat16)[None, :]]
    convert_element_type x1, other arithmetic: 1.05 us -> 0.35 us  [per_device(): selection(offsets, my_index, groups, inner).astype(jnp.float32)]
    ppermute x4, waiting for transfers between devices: 6.85 us -> 7.52 us  [group_sum(): values.append(lax.ppermute(value, 'ev', pairs))]
    dynamic_slice x2, local copies, waits for them, and re-layouts: 0.17 us -> 0.82 us  [per_device(): own = lax.dynamic_index_in_dim(chunks, my_index, axis=0, keepdims=False)]
  transfers between devices with their start and end apart: 11 -> 11, of which waited for: 5 -> 7; matrix products, arithmetic and copies ran while one was open for 1% -> 1% of each run, Pallas kernels for 0% -> 0%
where the time goes in v21:
time: 48.7 us; the launch traced here: 48.5 us
  starting transfers between devices  19.1 us (39%)
  waiting for transfers between devices  12.2 us (25%)
  matrix products  6.08 us (12%)
  blocking collectives  5.79 us (12%)
  local copies, waits for them, and re-layouts  3.73 us (8%)
  other arithmetic  1.36 us (3%)
    ppermute x7, starting transfers between devices, per_device(): arrived.append(lax.ppermute(block, 'ev', pairs))  12.8 us
    ppermute x4, waiting for transfers between devices, group_sum(): values.append(lax.ppermute(value, 'ev', pairs))  7.52 us
    ppermute x4, starting transfers between devices, group_sum(): values.append(lax.ppermute(value, 'ev', pairs))  6.3 us
    all_gather x1, blocking collectives, per_device(): lax.all_gather(sketch, 'col', axis=0, tiled=True)  5.79 us
    dot_general x1, matrix products, per_device(): jnp.einsum('xcb,xbj->xcj', first, pick, precision=lax.Precision.HIGH, pre...  4.97 us
    ppermute x7, waiting for transfers between devices, per_device(): arrived.append(lax.ppermute(block, 'ev', pairs))  4.65 us
    reshape x1, local copies, waits for them, and re-layouts, selection(): off = offsets.reshape(groups, OUTER, per_row)  1.28 us
  transfers between devices with their start and end apart: 11, of which 7 were waited for; matrix products, arithmetic and copies ran while one was open for 1% of the time, Pallas kernels for 0%

profile of v21, /device:TPU:0, one launch (start us, length us, event | category | flops | bytes accessed | tf_op | source)
XLA Modules:
  0.0 48.5 jit_solution(17204104086555271865)
XLA Ops:
  0.2 1.3 %reshape.30 = s32[8,128,2]{2,1,0:T(8,128)S(1)} reshape(s32[2048]{0:T(1024)} %param.5) | data formatting | bytes 16384 | tf_op jit(solution)/shard_map/reshape | solution.py:51
  2.5 0.6 %copy.23 = bf16[8,8,128,128]{3,2,1,0:T(8,128)(2,1)S(1)} copy(bf16[8,8,128,128]{3,1,2,0:T(8,128)(2,1)S(1)} %multiply_bitcast_fusion) | data formatting | bytes 4194304
  3.1 0.7 %fusion.16 = f32[128,64,128]{2,0,1:T(8,128)S(1)} fusion(bf16[64,128,128]{2,1,0:T(8,128)(2,1)S(1)} %bitcast.40), kind=kOutput, calls=%fused_computation.24 | convolution fusion | flops 269025280 | bytes 6291456 | tf_op jit(solution)/shard_map/xa,cab->xcb/dot_general | solution.py:72
  3.8 5.0 %fusion = f32[128,64,16]{1,2,0:T(8,128)S(1)} fusion(f32[128,128,16]{1,2,0:T(8,128)S(1)} %fusion.2, f32[128,64,128]{2,0,1:T(8,128)S(1)} %fusion.16), kind=kOutput, calls=%fused_computation | convolution fusion | flops 100663296 | bytes 5767168 | tf_op jit(solution)/shard_map/xcb,xbj->xcj/dot_general | solution.py:79
  8.9 0.7 %constant_dynamic-slice_fusion.7 = (f32[1,64,256]{1,0,2:T(1,128)S(1)}, f32[1,64,256]{1,0,2:T(1,128)S(1)}, f32[1,64,256]{1,0,2:T(1,128)S(1)}, f32[1,64,256]{1,0,2...) fusion(f32[8,64,256]{1,0,2:T(8,128)S(1)} %bitcast.41, ...), kind=kLoop, calls=%fused_computation.39 | loop fusion | bytes 1048608 | tf_op jit(solution)/shard_map/jit(dynamic_index_in_dim)/dynamic_slice | solution.py:88
  9.7 6.1 %collective-permute-start.6 = (f32[64,256]{1,0:T(8,128)S(1)}, f32[64,256]{1,0:T(8,128)S(1)}, u32[]{:S(2)}, u32[]{:S(2)}) collective-permute-start(f32[64,256]{1,0:T(8,128)S(1)} %bitcast.49), channel_id=1, source_target_pairs={{0,28},{4,24},{8,20},{12,16},{16,12},{20,8},{24,4},{28,0},{1,29},{... | collective-permute-start | bytes 196616 | tf_op jit(solution)/shard_map/ppermute | solution.py:94
  16.3 0.8 %collective-permute-start.4 = (f32[64,256]{1,0:T(8,128)S(1)}, f32[64,256]{1,0:T(8,128)S(1)}, u32[]{:S(2)}, u32[]{:S(2)}) collective-permute-start(f32[64,256]{1,0:T(8,128)S(1)} %bitcast.43), channel_id=1, source_target_pairs={{0,20},{4,16},{8,28},{12,24},{16,4},{20,0},{24,12},{28,8},{1,21},{... | collective-permute-start | bytes 196616 | tf_op jit(solution)/shard_map/ppermute | solution.py:94
  17.2 2.0 %collective-permute-start.3 = (f32[64,256]{1,0:T(8,128)S(1)}, f32[64,256]{1,0:T(8,128)S(1)}, u32[]{:S(2)}, u32[]{:S(2)}) collective-permute-start(f32[64,256]{1,0:T(8,128)S(1)} %bitcast.44), channel_id=1, source_target_pairs={{0,16},{4,20},{8,24},{12,28},{16,0},{20,4},{24,8},{28,12},{1,17},{... | collective-permute-start | bytes 196616 | tf_op jit(solution)/shard_map/ppermute | solution.py:94
  19.3 2.4 %collective-permute-start.2 = (f32[64,256]{1,0:T(8,128)S(1)}, f32[64,256]{1,0:T(8,128)S(1)}, u32[]{:S(2)}, u32[]{:S(2)}) collective-permute-start(f32[64,256]{1,0:T(8,128)S(1)} %bitcast.45), channel_id=1, source_target_pairs={{0,12},{4,8},{8,4},{12,0},{16,28},{20,24},{24,20},{28,16},{1,13},{... | collective-permute-start | bytes 196616 | tf_op jit(solution)/shard_map/ppermute | solution.py:94
  21.9 0.8 %collective-permute-start.1 = (f32[64,256]{1,0:T(8,128)S(1)}, f32[64,256]{1,0:T(8,128)S(1)}, u32[]{:S(2)}, u32[]{:S(2)}) collective-permute-start(f32[64,256]{1,0:T(8,128)S(1)} %bitcast.48), channel_id=1, source_target_pairs={{0,8},{4,12},{8,0},{12,4},{16,24},{20,28},{24,16},{28,20},{1,9},{5... | collective-permute-start | bytes 196616 | tf_op jit(solution)/shard_map/ppermute | solution.py:94
  23.2 1.9 %collective-permute-done.4 = f32[64,256]{1,0:T(8,128)S(1)} collective-permute-done((f32[64,256]{1,0:T(8,128)S(1)}, f32[64,256]{1,0:T(8,128)S(1)}, u32[]{:S(2)}, u32[]{:S(2)}) %collective-permute-start.4) | collective-permute-done | bytes 65568 | tf_op jit(solution)/shard_map/ppermute | solution.py:94
  25.1 2.0 %collective-permute-done.3 = f32[64,256]{1,0:T(8,128)S(1)} collective-permute-done((f32[64,256]{1,0:T(8,128)S(1)}, f32[64,256]{1,0:T(8,128)S(1)}, u32[]{:S(2)}, u32[]{:S(2)}) %collective-permute-start.3) | collective-permute-done | bytes 65568 | tf_op jit(solution)/shard_map/ppermute | solution.py:94
  27.1 0.7 %collective-permute-done.1 = f32[64,256]{1,0:T(8,128)S(1)} collective-permute-done((f32[64,256]{1,0:T(8,128)S(1)}, f32[64,256]{1,0:T(8,128)S(1)}, u32[]{:S(2)}, u32[]{:S(2)}) %collective-permute-start.1) | collective-permute-done | bytes 65568 | tf_op jit(solution)/shard_map/ppermute | solution.py:94
  27.9 5.8 %all_gather.3 = f32[256,256]{1,0:T(8,128)S(1)} all-gather(f32[64,256]{1,0:T(8,128)S(1)} %fusion.14), channel_id=1, replica_groups=mesh['ev'=8,'col'=4] {'col'}, dimensions={0}, use_global_device_ids=true | all-gather | bytes 327680 | tf_op jit(solution)/shard_map/all_gather | solution.py:104
  33.6 0.4 fusion.32
  34.0 1.2 %collective-permute-start.8 = (f32[64,256]{1,0:T(8,128)S(1)}, f32[64,256]{1,0:T(8,128)S(1)}, u32[]{:S(2)}, u32[]{:S(2)}) collective-permute-start(f32[64,256]{1,0:T(8,128)S(1)} %fusion.32), channel_id=1, source_target_pairs={{0,8},{4,12},{8,0},{12,4},{16,24},{20,28},{24,16},{28,20},{1,9},{5... | collective-permute-start | bytes 196616 | tf_op jit(solution)/shard_map/ppermute | solution.py:35
  35.2 1.1 %collective-permute-start.9 = (f32[64,256]{1,0:T(8,128)S(1)}, f32[64,256]{1,0:T(8,128)S(1)}, u32[]{:S(2)}, u32[]{:S(2)}) collective-permute-start(f32[64,256]{1,0:T(8,128)S(1)} %fusion.32), channel_id=1, source_target_pairs={{0,12},{4,8},{8,4},{12,0},{16,28},{20,24},{24,20},{28,16},{1,13},{... | collective-permute-start | bytes 196616 | tf_op jit(solution)/shard_map/ppermute | solution.py:35
  36.3 1.3 %collective-permute-start.7 = (f32[64,256]{1,0:T(8,128)S(1)}, f32[64,256]{1,0:T(8,128)S(1)}, u32[]{:S(2)}, u32[]{:S(2)}) collective-permute-start(f32[64,256]{1,0:T(8,128)S(1)} %fusion.32), channel_id=1, source_target_pairs={{0,4},{4,0},{8,12},{12,8},{16,20},{20,16},{24,28},{28,24},{1,5},{5... | collective-permute-start | bytes 196616 | tf_op jit(solution)/shard_map/ppermute | solution.py:35
  37.6 1.4 %collective-permute-done.8 = f32[64,256]{1,0:T(8,128)S(1)} collective-permute-done((f32[64,256]{1,0:T(8,128)S(1)}, f32[64,256]{1,0:T(8,128)S(1)}, u32[]{:S(2)}, u32[]{:S(2)}) %collective-permute-start.8) | collective-permute-done | bytes 65568 | tf_op jit(solution)/shard_map/ppermute | solution.py:35
  39.0 1.5 %collective-permute-done.9 = f32[64,256]{1,0:T(8,128)S(1)} collective-permute-done((f32[64,256]{1,0:T(8,128)S(1)}, f32[64,256]{1,0:T(8,128)S(1)}, u32[]{:S(2)}, u32[]{:S(2)}) %collective-permute-start.9) | collective-permute-done | bytes 65568 | tf_op jit(solution)/shard_map/ppermute | solution.py:35
  40.4 1.0 %collective-permute-done.7 = f32[64,256]{1,0:T(8,128)S(1)} collective-permute-done((f32[64,256]{1,0:T(8,128)S(1)}, f32[64,256]{1,0:T(8,128)S(1)}, u32[]{:S(2)}, u32[]{:S(2)}) %collective-permute-start.7) | collective-permute-done | bytes 65568 | tf_op jit(solution)/shard_map/ppermute | solution.py:35
  41.5 2.8 %collective-permute-start.10 = (f32[64,256]{1,0:T(8,128)S(1)}, f32[64,256]{1,0:T(8,128)S(1)}, u32[]{:S(2)}, u32[]{:S(2)}) collective-permute-start(f32[64,256]{1,0:T(8,128)S(1)} %add_add_fusion), channel_id=1, source_target_pairs={{0,16},{4,20},{8,24},{12,28},{16,0},{20,4},{24,8},{28,12},{1,17},{... | collective-permute-start | bytes 196616 | tf_op jit(solution)/shard_map/ppermute | solution.py:35
  44.3 3.6 %collective-permute-done.10 = f32[64,256]{1,0:T(8,128)S(1)} collective-permute-done((f32[64,256]{1,0:T(8,128)S(1)}, f32[64,256]{1,0:T(8,128)S(1)}, u32[]{:S(2)}, u32[]{:S(2)}) %collective-permute-start.10) | collective-permute-done | bytes 65568 | tf_op jit(solution)/shard_map/ppermute | solution.py:35
  47.9 0.6 %add.117 = f32[64,256]{1,0:T(8,128)} add(f32[64,256]{1,0:T(8,128)S(1)} %add_add_fusion, f32[64,256]{1,0:T(8,128)S(1)} %collective-permute-done.10) | non-fusion elementwise | flops 16384 | bytes 196608 | tf_op jit(solution)/shard_map/add | solution.py:37
  (31 shorter events, 2.5 us)
Async XLA Ops:
  0.0 2.2 %copy-start.1 = (s32[16384]{0:T(1024)S(1)}, s32[16384]{0:T(1024)}, u32[]{:S(2)}) copy-start(s32[16384]{0:T(1024)} %param.4) | copy-start | bytes 196612
  0.0 2.2 %copy-start = (bf16[64,16384]{1,0:T(8,128)(2,1)S(1)}, bf16[64,16384]{1,0:T(8,128)(2,1)}, u32[]{:S(2)}) copy-start(bf16[64,16384]{1,0:T(8,128)(2,1)} %param.3) | copy-start | bytes 6291460
  9.7 12.2 %collective-permute-start.6 = (f32[64,256]{1,0:T(8,128)S(1)}, f32[64,256]{1,0:T(8,128)S(1)}, u32[]{:S(2)}, u32[]{:S(2)}) collective-permute-start(f32[64,256]{1,0:T(8,128)S(1)} %bitcast.49), channel_id=1, source_target_pairs={{0,28},{4,24},{8,20},{12,16},{16,12},{20,8},{24,4},{28,0},{1,29},{... | collective-permute-start | bytes 196616 | tf_op jit(solution)/shard_map/ppermute | solution.py:94
  15.9 6.8 %collective-permute-start.5 = (f32[64,256]{1,0:T(8,128)S(1)}, f32[64,256]{1,0:T(8,128)S(1)}, u32[]{:S(2)}, u32[]{:S(2)}) collective-permute-start(f32[64,256]{1,0:T(8,128)S(1)} %bitcast.47), channel_id=1, source_target_pairs={{0,24},{4,28},{8,16},{12,20},{16,8},{20,12},{24,0},{28,4},{1,25},{... | collective-permute-start | bytes 196616 | tf_op jit(solution)/shard_map/ppermute | solution.py:94
  16.3 8.8 %collective-permute-start.4 = (f32[64,256]{1,0:T(8,128)S(1)}, f32[64,256]{1,0:T(8,128)S(1)}, u32[]{:S(2)}, u32[]{:S(2)}) collective-permute-start(f32[64,256]{1,0:T(8,128)S(1)} %bitcast.43), channel_id=1, source_target_pairs={{0,20},{4,16},{8,28},{12,24},{16,4},{20,0},{24,12},{28,8},{1,21},{... | collective-permute-start | bytes 196616 | tf_op jit(solution)/shard_map/ppermute | solution.py:94
  17.2 9.9 %collective-permute-start.3 = (f32[64,256]{1,0:T(8,128)S(1)}, f32[64,256]{1,0:T(8,128)S(1)}, u32[]{:S(2)}, u32[]{:S(2)}) collective-permute-start(f32[64,256]{1,0:T(8,128)S(1)} %bitcast.44), channel_id=1, source_target_pairs={{0,16},{4,20},{8,24},{12,28},{16,0},{20,4},{24,8},{28,12},{1,17},{... | collective-permute-start | bytes 196616 | tf_op jit(solution)/shard_map/ppermute | solution.py:94
  19.3 7.8 %collective-permute-start.2 = (f32[64,256]{1,0:T(8,128)S(1)}, f32[64,256]{1,0:T(8,128)S(1)}, u32[]{:S(2)}, u32[]{:S(2)}) collective-permute-start(f32[64,256]{1,0:T(8,128)S(1)} %bitcast.45), channel_id=1, source_target_pairs={{0,12},{4,8},{8,4},{12,0},{16,28},{20,24},{24,20},{28,16},{1,13},{... | collective-permute-start | bytes 196616 | tf_op jit(solution)/shard_map/ppermute | solution.py:94
  21.9 5.9 %collective-permute-start.1 = (f32[64,256]{1,0:T(8,128)S(1)}, f32[64,256]{1,0:T(8,128)S(1)}, u32[]{:S(2)}, u32[]{:S(2)}) collective-permute-start(f32[64,256]{1,0:T(8,128)S(1)} %bitcast.48), channel_id=1, source_target_pairs={{0,8},{4,12},{8,0},{12,4},{16,24},{20,28},{24,16},{28,20},{1,9},{5... | collective-permute-start | bytes 196616 | tf_op jit(solution)/shard_map/ppermute | solution.py:94
  22.7 5.1 %collective-permute-start = (f32[64,256]{1,0:T(8,128)S(1)}, f32[64,256]{1,0:T(8,128)S(1)}, u32[]{:S(2)}, u32[]{:S(2)}) collective-permute-start(f32[64,256]{1,0:T(8,128)S(1)} %bitcast.46), channel_id=1, source_target_pairs={{0,4},{4,0},{8,12},{12,8},{16,20},{20,16},{24,28},{28,24},{1,5},{5... | collective-permute-start | bytes 196616 | tf_op jit(solution)/shard_map/ppermute | solution.py:94
  34.0 5.0 %collective-permute-start.8 = (f32[64,256]{1,0:T(8,128)S(1)}, f32[64,256]{1,0:T(8,128)S(1)}, u32[]{:S(2)}, u32[]{:S(2)}) collective-permute-start(f32[64,256]{1,0:T(8,128)S(1)} %fusion.32), channel_id=1, source_target_pairs={{0,8},{4,12},{8,0},{12,4},{16,24},{20,28},{24,16},{28,20},{1,9},{5... | collective-permute-start | bytes 196616 | tf_op jit(solution)/shard_map/ppermute | solution.py:35
  35.2 5.2 %collective-permute-start.9 = (f32[64,256]{1,0:T(8,128)S(1)}, f32[64,256]{1,0:T(8,128)S(1)}, u32[]{:S(2)}, u32[]{:S(2)}) collective-permute-start(f32[64,256]{1,0:T(8,128)S(1)} %fusion.32), channel_id=1, source_target_pairs={{0,12},{4,8},{8,4},{12,0},{16,28},{20,24},{24,20},{28,16},{1,13},{... | collective-permute-start | bytes 196616 | tf_op jit(solution)/shard_map/ppermute | solution.py:35
  36.3 5.2 %collective-permute-start.7 = (f32[64,256]{1,0:T(8,128)S(1)}, f32[64,256]{1,0:T(8,128)S(1)}, u32[]{:S(2)}, u32[]{:S(2)}) collective-permute-start(f32[64,256]{1,0:T(8,128)S(1)} %fusion.32), channel_id=1, source_target_pairs={{0,4},{4,0},{8,12},{12,8},{16,20},{20,16},{24,28},{28,24},{1,5},{5... | collective-permute-start | bytes 196616 | tf_op jit(solution)/shard_map/ppermute | solution.py:35
  41.5 6.4 %collective-permute-start.10 = (f32[64,256]{1,0:T(8,128)S(1)}, f32[64,256]{1,0:T(8,128)S(1)}, u32[]{:S(2)}, u32[]{:S(2)}) collective-permute-start(f32[64,256]{1,0:T(8,128)S(1)} %add_add_fusion), channel_id=1, source_target_pairs={{0,16},{4,20},{8,24},{12,28},{16,0},{20,4},{24,8},{28,12},{1,17},{... | collective-permute-start | bytes 196616 | tf_op jit(solution)/shard_map/ppermute | solution.py:35

commit v22 on v16

--- a/solution.py
+++ b/solution.py
@@ -75,7 +75,7 @@
         blocks,
         preferred_element_type=jnp.float32,
     )
-    pick = selection(offsets, my_index, groups, inner)
+    pick = lax.optimization_barrier(selection(offsets, my_index, groups, inner))
     sampled = jnp.einsum(
         "xcb,xbj->xcj",
         first,

time: 52.6 us -> 47.4 us (0.901)
  matrix products: 9.08 us -> 4.7 us
  other arithmetic: 3.42 us -> 1.69 us
  local copies, waits for them, and re-layouts: 2.6 us -> 3.41 us
    dot_general x1, matrix products: 6.03 us -> 3.61 us  [per_device(): jnp.einsum('xcb,xbj->xcj', first, pick.astype(jnp.float32), precision=lax...]
    dot_general x1, matrix products: 2.68 us -> 0.72 us  [per_device(): jnp.einsum('xa,cab->xcb', hadamard(OUTER).astype(jnp.bfloat16), blocks, p...]
    mul x1, other arithmetic: 1.85 us -> 0.27 us  [per_device(): signed = panel * signs.astype(jnp.bfloat16)[None, :]]
    convert_element_type x1, other arithmetic: 0.84 us -> 0.01 us  [per_device(): signed = panel * signs.astype(jnp.bfloat16)[None, :]]
    reshape x1, local copies, waits for them, and re-layouts: 0.26 us -> 1.07 us  [selection(): off = offsets.reshape(groups, OUTER, per_row)]
    convert_element_type x0 -> x1, other arithmetic: none -> 0.69 us  [selection(): (1 - 2 * parity).astype(jnp.bfloat16)]
where the time goes in v22:
time: 47.4 us; the launch traced here: 47.1 us
  starting transfers between devices  19.1 us (40%)
  waiting for transfers between devices  12.2 us (26%)
  blocking collectives  5.79 us (12%)
  matrix products  4.7 us (10%)
  local copies, waits for them, and re-layouts  3.41 us (7%)
  other arithmetic  1.69 us (4%)
    ppermute x7, starting transfers between devices, per_device(): arrived.append(lax.ppermute(block, 'ev', pairs))  12.8 us
    ppermute x4, waiting for transfers between devices, group_sum(): values.append(lax.ppermute(value, 'ev', pairs))  7.53 us
    ppermute x4, starting transfers between devices, group_sum(): values.append(lax.ppermute(value, 'ev', pairs))  6.3 us
    all_gather x1, blocking collectives, per_device(): lax.all_gather(sketch, 'col', axis=0, tiled=True)  5.79 us
    ppermute x7, waiting for transfers between devices, per_device(): arrived.append(lax.ppermute(block, 'ev', pairs))  4.64 us
    dot_general x1, matrix products, per_device(): jnp.einsum('xcb,xbj->xcj', first, pick.astype(jnp.float32), precision=lax...  3.61 us
    reshape x1, local copies, waits for them, and re-layouts, selection(): off = offsets.reshape(groups, OUTER, per_row)  1.07 us
  transfers between devices with their start and end apart: 11, of which 7 were waited for; matrix products, arithmetic and copies ran while one was open for 1% of the time, Pallas kernels for 0%

profile of v22, /device:TPU:0, one launch (start us, length us, event | category | flops | bytes accessed | tf_op | source)
XLA Modules:
  0.0 47.1 jit_solution(14145758645757978765)
XLA Ops:
  0.2 1.1 %reshape.30 = s32[8,64,4]{2,1,0:T(8,128)S(1)} reshape(s32[2048]{0:T(1024)} %param.5) | data formatting | bytes 16384 | tf_op jit(solution)/shard_map/reshape | solution.py:51
  1.5 0.7 %subtract_convert_fusion = bf16[64,256,32]{1,2,0:T(8,128)(2,1)S(1)} fusion(s32[32]{0:T(128)S(1)} %xor.35, s32[64,32]{1,0:T(8,128)S(1)} %copy.12), kind=kLoop, calls=%fused_computation.2 | loop fusion | flops 3670016 | bytes 1056896 | tf_op jit(solution)/shard_map/convert_element_type | solution.py:58
  2.5 0.5 %copy.23 = bf16[8,8,64,256]{3,2,1,0:T(8,128)(2,1)S(1)} copy(bf16[8,8,64,256]{3,1,2,0:T(8,128)(2,1)S(1)} %bitcast.40) | data formatting | bytes 4194304
  3.1 0.7 %fusion.15 = f32[64,64,256]{2,0,1:T(8,128)S(1)} fusion(bf16[64,64,256]{2,1,0:T(8,128)(2,1)S(1)} %bitcast.39), kind=kOutput, calls=%fused_computation.23 | convolution fusion | flops 134352896 | bytes 6291456 | tf_op jit(solution)/shard_map/xa,cab->xcb/dot_general | solution.py:72
  3.8 3.6 %fusion = f32[64,64,32]{1,2,0:T(8,128)S(1)} fusion(bf16[64,256,32]{1,2,0:T(8,128)(2,1)S(1)} %subtract_convert_fusion, f32[64,64,256]{2,0,1:T(8,128)S(1)} %fusion.15), kind=kOutput, calls=%fused_computation | convolution fusion | flops 201326592 | bytes 5767168 | tf_op jit(solution)/shard_map/xcb,xbj->xcj/dot_general | solution.py:79
  7.5 0.7 %constant_dynamic-slice_fusion.7 = (f32[1,64,256]{1,0,2:T(1,128)S(1)}, f32[1,64,256]{1,0,2:T(1,128)S(1)}, f32[1,64,256]{1,0,2:T(1,128)S(1)}, f32[1,64,256]{1,0,2...) fusion(f32[8,64,256]{1,0,2:T(8,128)S(1)} %bitcast.41, ...), kind=kLoop, calls=%fused_computation.37 | loop fusion | bytes 1048608 | tf_op jit(solution)/shard_map/jit(dynamic_index_in_dim)/dynamic_slice | solution.py:88
  8.4 6.1 %collective-permute-start.6 = (f32[64,256]{1,0:T(8,128)S(1)}, f32[64,256]{1,0:T(8,128)S(1)}, u32[]{:S(2)}, u32[]{:S(2)}) collective-permute-start(f32[64,256]{1,0:T(8,128)S(1)} %bitcast.49), channel_id=1, source_target_pairs={{0,28},{4,24},{8,20},{12,16},{16,12},{20,8},{24,4},{28,0},{1,29},{... | collective-permute-start | bytes 196616 | tf_op jit(solution)/shard_map/ppermute | solution.py:94
  14.9 0.8 %collective-permute-start.4 = (f32[64,256]{1,0:T(8,128)S(1)}, f32[64,256]{1,0:T(8,128)S(1)}, u32[]{:S(2)}, u32[]{:S(2)}) collective-permute-start(f32[64,256]{1,0:T(8,128)S(1)} %bitcast.43), channel_id=1, source_target_pairs={{0,20},{4,16},{8,28},{12,24},{16,4},{20,0},{24,12},{28,8},{1,21},{... | collective-permute-start | bytes 196616 | tf_op jit(solution)/shard_map/ppermute | solution.py:94
  15.8 2.0 %collective-permute-start.3 = (f32[64,256]{1,0:T(8,128)S(1)}, f32[64,256]{1,0:T(8,128)S(1)}, u32[]{:S(2)}, u32[]{:S(2)}) collective-permute-start(f32[64,256]{1,0:T(8,128)S(1)} %bitcast.44), channel_id=1, source_target_pairs={{0,16},{4,20},{8,24},{12,28},{16,0},{20,4},{24,8},{28,12},{1,17},{... | collective-permute-start | bytes 196616 | tf_op jit(solution)/shard_map/ppermute | solution.py:94
  17.9 2.4 %collective-permute-start.2 = (f32[64,256]{1,0:T(8,128)S(1)}, f32[64,256]{1,0:T(8,128)S(1)}, u32[]{:S(2)}, u32[]{:S(2)}) collective-permute-start(f32[64,256]{1,0:T(8,128)S(1)} %bitcast.45), channel_id=1, source_target_pairs={{0,12},{4,8},{8,4},{12,0},{16,28},{20,24},{24,20},{28,16},{1,13},{... | collective-permute-start | bytes 196616 | tf_op jit(solution)/shard_map/ppermute | solution.py:94
  20.5 0.8 %collective-permute-start.1 = (f32[64,256]{1,0:T(8,128)S(1)}, f32[64,256]{1,0:T(8,128)S(1)}, u32[]{:S(2)}, u32[]{:S(2)}) collective-permute-start(f32[64,256]{1,0:T(8,128)S(1)} %bitcast.48), channel_id=1, source_target_pairs={{0,8},{4,12},{8,0},{12,4},{16,24},{20,28},{24,16},{28,20},{1,9},{5... | collective-permute-start | bytes 196616 | tf_op jit(solution)/shard_map/ppermute | solution.py:94
  21.8 1.9 %collective-permute-done.4 = f32[64,256]{1,0:T(8,128)S(1)} collective-permute-done((f32[64,256]{1,0:T(8,128)S(1)}, f32[64,256]{1,0:T(8,128)S(1)}, u32[]{:S(2)}, u32[]{:S(2)}) %collective-permute-start.4) | collective-permute-done | bytes 65568 | tf_op jit(solution)/shard_map/ppermute | solution.py:94
  23.7 2.0 %collective-permute-done.3 = f32[64,256]{1,0:T(8,128)S(1)} collective-permute-done((f32[64,256]{1,0:T(8,128)S(1)}, f32[64,256]{1,0:T(8,128)S(1)}, u32[]{:S(2)}, u32[]{:S(2)}) %collective-permute-start.3) | collective-permute-done | bytes 65568 | tf_op jit(solution)/shard_map/ppermute | solution.py:94
  25.7 0.7 %collective-permute-done.1 = f32[64,256]{1,0:T(8,128)S(1)} collective-permute-done((f32[64,256]{1,0:T(8,128)S(1)}, f32[64,256]{1,0:T(8,128)S(1)}, u32[]{:S(2)}, u32[]{:S(2)}) %collective-permute-start.1) | collective-permute-done | bytes 65568 | tf_op jit(solution)/shard_map/ppermute | solution.py:94
  26.5 5.8 %all_gather.3 = f32[256,256]{1,0:T(8,128)S(1)} all-gather(f32[64,256]{1,0:T(8,128)S(1)} %fusion.8), channel_id=1, replica_groups=mesh['ev'=8,'col'=4] {'col'}, dimensions={0}, use_global_device_ids=true | all-gather | bytes 327680 | tf_op jit(solution)/shard_map/all_gather | solution.py:104
  32.6 1.2 %collective-permute-start.8 = (f32[64,256]{1,0:T(8,128)S(1)}, f32[64,256]{1,0:T(8,128)S(1)}, u32[]{:S(2)}, u32[]{:S(2)}) collective-permute-start(f32[64,256]{1,0:T(8,128)S(1)} %fusion.29), channel_id=1, source_target_pairs={{0,8},{4,12},{8,0},{12,4},{16,24},{20,28},{24,16},{28,20},{1,9},{5... | collective-permute-start | bytes 196616 | tf_op jit(solution)/shard_map/ppermute | solution.py:35
  33.8 1.1 %collective-permute-start.9 = (f32[64,256]{1,0:T(8,128)S(1)}, f32[64,256]{1,0:T(8,128)S(1)}, u32[]{:S(2)}, u32[]{:S(2)}) collective-permute-start(f32[64,256]{1,0:T(8,128)S(1)} %fusion.29), channel_id=1, source_target_pairs={{0,12},{4,8},{8,4},{12,0},{16,28},{20,24},{24,20},{28,16},{1,13},{... | collective-permute-start | bytes 196616 | tf_op jit(solution)/shard_map/ppermute | solution.py:35
  34.9 1.3 %collective-permute-start.7 = (f32[64,256]{1,0:T(8,128)S(1)}, f32[64,256]{1,0:T(8,128)S(1)}, u32[]{:S(2)}, u32[]{:S(2)}) collective-permute-start(f32[64,256]{1,0:T(8,128)S(1)} %fusion.29), channel_id=1, source_target_pairs={{0,4},{4,0},{8,12},{12,8},{16,20},{20,16},{24,28},{28,24},{1,5},{5... | collective-permute-start | bytes 196616 | tf_op jit(solution)/shard_map/ppermute | solution.py:35
  36.2 1.4 %collective-permute-done.8 = f32[64,256]{1,0:T(8,128)S(1)} collective-permute-done((f32[64,256]{1,0:T(8,128)S(1)}, f32[64,256]{1,0:T(8,128)S(1)}, u32[]{:S(2)}, u32[]{:S(2)}) %collective-permute-start.8) | collective-permute-done | bytes 65568 | tf_op jit(solution)/shard_map/ppermute | solution.py:35
  37.6 1.5 %collective-permute-done.9 = f32[64,256]{1,0:T(8,128)S(1)} collective-permute-done((f32[64,256]{1,0:T(8,128)S(1)}, f32[64,256]{1,0:T(8,128)S(1)}, u32[]{:S(2)}, u32[]{:S(2)}) %collective-permute-start.9) | collective-permute-done | bytes 65568 | tf_op jit(solution)/shard_map/ppermute | solution.py:35
  39.1 1.0 %collective-permute-done.7 = f32[64,256]{1,0:T(8,128)S(1)} collective-permute-done((f32[64,256]{1,0:T(8,128)S(1)}, f32[64,256]{1,0:T(8,128)S(1)}, u32[]{:S(2)}, u32[]{:S(2)}) %collective-permute-start.7) | collective-permute-done | bytes 65568 | tf_op jit(solution)/shard_map/ppermute | solution.py:35
  40.1 2.8 %collective-permute-start.10 = (f32[64,256]{1,0:T(8,128)S(1)}, f32[64,256]{1,0:T(8,128)S(1)}, u32[]{:S(2)}, u32[]{:S(2)}) collective-permute-start(f32[64,256]{1,0:T(8,128)S(1)} %add_add_fusion), channel_id=1, source_target_pairs={{0,16},{4,20},{8,24},{12,28},{16,0},{20,4},{24,8},{28,12},{1,17},{... | collective-permute-start | bytes 196616 | tf_op jit(solution)/shard_map/ppermute | solution.py:35
  42.9 3.6 %collective-permute-done.10 = f32[64,256]{1,0:T(8,128)S(1)} collective-permute-done((f32[64,256]{1,0:T(8,128)S(1)}, f32[64,256]{1,0:T(8,128)S(1)}, u32[]{:S(2)}, u32[]{:S(2)}) %collective-permute-start.10) | collective-permute-done | bytes 65568 | tf_op jit(solution)/shard_map/ppermute | solution.py:35
  46.5 0.6 %add.113 = f32[64,256]{1,0:T(8,128)} add(f32[64,256]{1,0:T(8,128)S(1)} %add_add_fusion, f32[64,256]{1,0:T(8,128)S(1)} %collective-permute-done.10) | non-fusion elementwise | flops 16384 | bytes 196608 | tf_op jit(solution)/shard_map/add | solution.py:37
  (31 shorter events, 2.4 us)
Async XLA Ops:
  0.0 2.2 %copy-start.1 = (s32[16384]{0:T(1024)S(1)}, s32[16384]{0:T(1024)}, u32[]{:S(2)}) copy-start(s32[16384]{0:T(1024)} %param.4) | copy-start | bytes 196612
  0.0 2.2 %copy-start = (bf16[64,16384]{1,0:T(8,128)(2,1)S(1)}, bf16[64,16384]{1,0:T(8,128)(2,1)}, u32[]{:S(2)}) copy-start(bf16[64,16384]{1,0:T(8,128)(2,1)} %param.3) | copy-start | bytes 6291460
  8.4 12.2 %collective-permute-start.6 = (f32[64,256]{1,0:T(8,128)S(1)}, f32[64,256]{1,0:T(8,128)S(1)}, u32[]{:S(2)}, u32[]{:S(2)}) collective-permute-start(f32[64,256]{1,0:T(8,128)S(1)} %bitcast.49), channel_id=1, source_target_pairs={{0,28},{4,24},{8,20},{12,16},{16,12},{20,8},{24,4},{28,0},{1,29},{... | collective-permute-start | bytes 196616 | tf_op jit(solution)/shard_map/ppermute | solution.py:94
  14.5 6.8 %collective-permute-start.5 = (f32[64,256]{1,0:T(8,128)S(1)}, f32[64,256]{1,0:T(8,128)S(1)}, u32[]{:S(2)}, u32[]{:S(2)}) collective-permute-start(f32[64,256]{1,0:T(8,128)S(1)} %bitcast.47), channel_id=1, source_target_pairs={{0,24},{4,28},{8,16},{12,20},{16,8},{20,12},{24,0},{28,4},{1,25},{... | collective-permute-start | bytes 196616 | tf_op jit(solution)/shard_map/ppermute | solution.py:94
  14.9 8.8 %collective-permute-start.4 = (f32[64,256]{1,0:T(8,128)S(1)}, f32[64,256]{1,0:T(8,128)S(1)}, u32[]{:S(2)}, u32[]{:S(2)}) collective-permute-start(f32[64,256]{1,0:T(8,128)S(1)} %bitcast.43), channel_id=1, source_target_pairs={{0,20},{4,16},{8,28},{12,24},{16,4},{20,0},{24,12},{28,8},{1,21},{... | collective-permute-start | bytes 196616 | tf_op jit(solution)/shard_map/ppermute | solution.py:94
  15.8 9.9 %collective-permute-start.3 = (f32[64,256]{1,0:T(8,128)S(1)}, f32[64,256]{1,0:T(8,128)S(1)}, u32[]{:S(2)}, u32[]{:S(2)}) collective-permute-start(f32[64,256]{1,0:T(8,128)S(1)} %bitcast.44), channel_id=1, source_target_pairs={{0,16},{4,20},{8,24},{12,28},{16,0},{20,4},{24,8},{28,12},{1,17},{... | collective-permute-start | bytes 196616 | tf_op jit(solution)/shard_map/ppermute | solution.py:94
  17.9 7.8 %collective-permute-start.2 = (f32[64,256]{1,0:T(8,128)S(1)}, f32[64,256]{1,0:T(8,128)S(1)}, u32[]{:S(2)}, u32[]{:S(2)}) collective-permute-start(f32[64,256]{1,0:T(8,128)S(1)} %bitcast.45), channel_id=1, source_target_pairs={{0,12},{4,8},{8,4},{12,0},{16,28},{20,24},{24,20},{28,16},{1,13},{... | collective-permute-start | bytes 196616 | tf_op jit(solution)/shard_map/ppermute | solution.py:94
  20.5 5.9 %collective-permute-start.1 = (f32[64,256]{1,0:T(8,128)S(1)}, f32[64,256]{1,0:T(8,128)S(1)}, u32[]{:S(2)}, u32[]{:S(2)}) collective-permute-start(f32[64,256]{1,0:T(8,128)S(1)} %bitcast.48), channel_id=1, source_target_pairs={{0,8},{4,12},{8,0},{12,4},{16,24},{20,28},{24,16},{28,20},{1,9},{5... | collective-permute-start | bytes 196616 | tf_op jit(solution)/shard_map/ppermute | solution.py:94
  21.4 5.1 %collective-permute-start = (f32[64,256]{1,0:T(8,128)S(1)}, f32[64,256]{1,0:T(8,128)S(1)}, u32[]{:S(2)}, u32[]{:S(2)}) collective-permute-start(f32[64,256]{1,0:T(8,128)S(1)} %bitcast.46), channel_id=1, source_target_pairs={{0,4},{4,0},{8,12},{12,8},{16,20},{20,16},{24,28},{28,24},{1,5},{5... | collective-permute-start | bytes 196616 | tf_op jit(solution)/shard_map/ppermute | solution.py:94
  32.6 5.0 %collective-permute-start.8 = (f32[64,256]{1,0:T(8,128)S(1)}, f32[64,256]{1,0:T(8,128)S(1)}, u32[]{:S(2)}, u32[]{:S(2)}) collective-permute-start(f32[64,256]{1,0:T(8,128)S(1)} %fusion.29), channel_id=1, source_target_pairs={{0,8},{4,12},{8,0},{12,4},{16,24},{20,28},{24,16},{28,20},{1,9},{5... | collective-permute-start | bytes 196616 | tf_op jit(solution)/shard_map/ppermute | solution.py:35
  33.8 5.2 %collective-permute-start.9 = (f32[64,256]{1,0:T(8,128)S(1)}, f32[64,256]{1,0:T(8,128)S(1)}, u32[]{:S(2)}, u32[]{:S(2)}) collective-permute-start(f32[64,256]{1,0:T(8,128)S(1)} %fusion.29), channel_id=1, source_target_pairs={{0,12},{4,8},{8,4},{12,0},{16,28},{20,24},{24,20},{28,16},{1,13},{... | collective-permute-start | bytes 196616 | tf_op jit(solution)/shard_map/ppermute | solution.py:35
  34.9 5.2 %collective-permute-start.7 = (f32[64,256]{1,0:T(8,128)S(1)}, f32[64,256]{1,0:T(8,128)S(1)}, u32[]{:S(2)}, u32[]{:S(2)}) collective-permute-start(f32[64,256]{1,0:T(8,128)S(1)} %fusion.29), channel_id=1, source_target_pairs={{0,4},{4,0},{8,12},{12,8},{16,20},{20,16},{24,28},{28,24},{1,5},{5... | collective-permute-start | bytes 196616 | tf_op jit(solution)/shard_map/ppermute | solution.py:35
  40.1 6.4 %collective-permute-start.10 = (f32[64,256]{1,0:T(8,128)S(1)}, f32[64,256]{1,0:T(8,128)S(1)}, u32[]{:S(2)}, u32[]{:S(2)}) collective-permute-start(f32[64,256]{1,0:T(8,128)S(1)} %add_add_fusion), channel_id=1, source_target_pairs={{0,16},{4,20},{8,24},{12,28},{16,0},{20,4},{24,8},{28,12},{1,17},{... | collective-permute-start | bytes 196616 | tf_op jit(solution)/shard_map/ppermute | solution.py:35

commit v23 on v22

--- a/solution.py
+++ b/solution.py
@@ -38,14 +38,6 @@
     return values[0]
 
 
-def split3(value):
-    hi = lax.reduce_precision(value, exponent_bits=8, mantissa_bits=7)
-    rest = value - hi
-    mid = lax.reduce_precision(rest, exponent_bits=8, mantissa_bits=7)
-    low = rest - mid
-    return tuple(piece.astype(jnp.bfloat16) for piece in (hi, mid, low))
-
-
 def selection(offsets, my_index, groups, inner):
     per_row = inner // STRIDE
     off = offsets.reshape(groups, OUTER, per_row)
@@ -76,12 +68,11 @@
         preferred_element_type=jnp.float32,
     )
     pick = lax.optimization_barrier(selection(offsets, my_index, groups, inner))
+    high_part = lax.reduce_precision(first, exponent_bits=8, mantissa_bits=7)
     sampled = jnp.einsum(
-        "xcb,xbj->xcj",
-        first,
-        pick.astype(jnp.float32),
-        precision=lax.Precision.HIGH,
-        preferred_element_type=jnp.float32,
+        "xcb,xbj->xcj", high_part.astype(jnp.bfloat16), pick, preferred_element_type=jnp.float32
+    ) + jnp.einsum(
+        "xcb,xbj->xcj", (first - high_part).astype(jnp.bfloat16), pick, preferred_element_type=jnp.float32
     )
     chunks = sampled.reshape(OUTER, columns, groups, per_row).transpose(2, 1, 0, 3)
     chunks = chunks.reshape(groups, columns, OUTER * per_row)

time: 47.4 us -> 46.4 us (0.979)
  matrix products: 4.7 us -> 3.74 us
    dot_general x1 -> x2, matrix products: 3.61 us -> 2.64 us  [the longest x1 1.34 us: per_device(): jnp.einsum('xcb,xbj->xcj', high_part.astype(jnp.bfloat16), pick, preferre...]
where the time goes in v23:
time: 46.4 us; the launch traced here: 46.2 us
  starting transfers between devices  19.1 us (41%)
  waiting for transfers between devices  12.2 us (26%)
  blocking collectives  5.79 us (12%)
  matrix products  3.74 us (8%)
  local copies, waits for them, and re-layouts  3.4 us (7%)
  other arithmetic  1.69 us (4%)
    ppermute x7, starting transfers between devices, per_device(): arrived.append(lax.ppermute(block, 'ev', pairs))  12.8 us
    ppermute x4, waiting for transfers between devices, group_sum(): values.append(lax.ppermute(value, 'ev', pairs))  7.52 us
    ppermute x4, starting transfers between devices, group_sum(): values.append(lax.ppermute(value, 'ev', pairs))  6.3 us
    all_gather x1, blocking collectives, per_device(): lax.all_gather(sketch, 'col', axis=0, tiled=True)  5.79 us
    ppermute x7, waiting for transfers between devices, per_device(): arrived.append(lax.ppermute(block, 'ev', pairs))  4.65 us
    dot_general x1, matrix products, per_device(): jnp.einsum('xcb,xbj->xcj', high_part.astype(jnp.bfloat16), pick, preferre...  1.34 us
    dot_general x1, matrix products, per_device(): jnp.einsum('xcb,xbj->xcj', (first - high_part).astype(jnp.bfloat16), pick...  1.3 us
    reshape x1, local copies, waits for them, and re-layouts, selection(): off = offsets.reshape(groups, OUTER, per_row)  1.07 us
  transfers between devices with their start and end apart: 11, of which 7 were waited for; matrix products, arithmetic and copies ran while one was open for 1% of the time, Pallas kernels for 0%

profile of v23, /device:TPU:0, one launch (start us, length us, event | category | flops | bytes accessed | tf_op | source)
XLA Modules:
  0.0 46.2 jit_solution(3015298661186954206)
XLA Ops:
  0.2 1.1 %reshape.30 = s32[8,64,4]{2,1,0:T(8,128)S(1)} reshape(s32[2048]{0:T(1024)} %param.5) | data formatting | bytes 16384 | tf_op jit(solution)/shard_map/reshape | solution.py:43
  1.5 0.7 %subtract_convert_fusion = bf16[64,256,32]{1,2,0:T(8,128)(2,1)S(1)} fusion(s32[32]{0:T(128)S(1)} %xor.35, s32[64,32]{1,0:T(8,128)S(1)} %copy.17), kind=kLoop, calls=%fused_computation.7 | loop fusion | flops 3670016 | bytes 1056896 | tf_op jit(solution)/shard_map/convert_element_type | solution.py:50
  3.1 0.7 %reduce-precision_convert_fusion = (bf16[64,64,256]{2,0,1:T(8,128)(2,1)S(1)}, bf16[64,64,256]{2,0,1:T(8,128)(2,1)S(1)}) fusion(bf16[64,64,256]{2,1,0:T(8,128)(2,1)S(1)} %bitcast.42), kind=kOutput, calls=%fused_computation.1 | convolution fusion | flops 138547200 | bytes 6291456 | tf_op jit(solution)/shard_map/xa,cab->xcb/dot_general | solution.py:64
  3.8 1.3 %fusion.1 = f32[64,64,32]{1,2,0:T(8,128)S(1)} fusion(bf16[64,256,32]{1,2,0:T(8,128)(2,1)S(1)} %subtract_convert_fusion, bf16[64,64,256]{2,0,1:T(8,128)(2,1)S(1)} %get-tuple-element.6), kind=kOutput, calls=%fused_computation.3 | convolution fusion | flops 67108864 | bytes 3670016 | tf_op jit(solution)/shard_map/xcb,xbj->xcj/dot_general | solution.py:74
  5.1 1.3 %fusion.5 = f32[64,64,32]{1,2,0:T(8,128)S(1)} fusion(f32[64,64,32]{1,2,0:T(8,128)S(1)} %fusion.1, bf16[64,256,32]{1,2,0:T(8,128)(2,1)S(1)} %subtract_convert_fusion, bf16[64,64,256]{2,0,1:T(8,128)(2,1)S(1)} %get-tuple-element.5), kind=kOutput, calls=%fused_computation.8 | convolution fusion | flops 67239936 | bytes 4194304 | tf_op jit(solution)/shard_map/xcb,xbj->xcj/dot_general | solution.py:72
  6.6 0.7 %constant_dynamic-slice_fusion.7 = (f32[1,64,256]{1,0,2:T(1,128)S(1)}, f32[1,64,256]{1,0,2:T(1,128)S(1)}, f32[1,64,256]{1,0,2:T(1,128)S(1)}, f32[1,64,256]{1,0,2...) fusion(f32[8,64,256]{1,0,2:T(8,128)S(1)} %bitcast.45, ...), kind=kLoop, calls=%fused_computation.43 | loop fusion | bytes 1048608 | tf_op jit(solution)/shard_map/jit(dynamic_index_in_dim)/dynamic_slice | solution.py:79
  7.4 6.1 %collective-permute-start.6 = (f32[64,256]{1,0:T(8,128)S(1)}, f32[64,256]{1,0:T(8,128)S(1)}, u32[]{:S(2)}, u32[]{:S(2)}) collective-permute-start(f32[64,256]{1,0:T(8,128)S(1)} %bitcast.52), channel_id=1, source_target_pairs={{0,28},{4,24},{8,20},{12,16},{16,12},{20,8},{24,4},{28,0},{1,29},{... | collective-permute-start | bytes 196616 | tf_op jit(solution)/shard_map/ppermute | solution.py:85
  13.9 0.8 %collective-permute-start.4 = (f32[64,256]{1,0:T(8,128)S(1)}, f32[64,256]{1,0:T(8,128)S(1)}, u32[]{:S(2)}, u32[]{:S(2)}) collective-permute-start(f32[64,256]{1,0:T(8,128)S(1)} %bitcast.46), channel_id=1, source_target_pairs={{0,20},{4,16},{8,28},{12,24},{16,4},{20,0},{24,12},{28,8},{1,21},{... | collective-permute-start | bytes 196616 | tf_op jit(solution)/shard_map/ppermute | solution.py:85
  14.8 2.0 %collective-permute-start.3 = (f32[64,256]{1,0:T(8,128)S(1)}, f32[64,256]{1,0:T(8,128)S(1)}, u32[]{:S(2)}, u32[]{:S(2)}) collective-permute-start(f32[64,256]{1,0:T(8,128)S(1)} %bitcast.47), channel_id=1, source_target_pairs={{0,16},{4,20},{8,24},{12,28},{16,0},{20,4},{24,8},{28,12},{1,17},{... | collective-permute-start | bytes 196616 | tf_op jit(solution)/shard_map/ppermute | solution.py:85
  16.9 2.4 %collective-permute-start.2 = (f32[64,256]{1,0:T(8,128)S(1)}, f32[64,256]{1,0:T(8,128)S(1)}, u32[]{:S(2)}, u32[]{:S(2)}) collective-permute-start(f32[64,256]{1,0:T(8,128)S(1)} %bitcast.48), channel_id=1, source_target_pairs={{0,12},{4,8},{8,4},{12,0},{16,28},{20,24},{24,20},{28,16},{1,13},{... | collective-permute-start | bytes 196616 | tf_op jit(solution)/shard_map/ppermute | solution.py:85
  19.6 0.8 %collective-permute-start.1 = (f32[64,256]{1,0:T(8,128)S(1)}, f32[64,256]{1,0:T(8,128)S(1)}, u32[]{:S(2)}, u32[]{:S(2)}) collective-permute-start(f32[64,256]{1,0:T(8,128)S(1)} %bitcast.51), channel_id=1, source_target_pairs={{0,8},{4,12},{8,0},{12,4},{16,24},{20,28},{24,16},{28,20},{1,9},{5... | collective-permute-start | bytes 196616 | tf_op jit(solution)/shard_map/ppermute | solution.py:85
  20.8 1.9 %collective-permute-done.4 = f32[64,256]{1,0:T(8,128)S(1)} collective-permute-done((f32[64,256]{1,0:T(8,128)S(1)}, f32[64,256]{1,0:T(8,128)S(1)}, u32[]{:S(2)}, u32[]{:S(2)}) %collective-permute-start.4) | collective-permute-done | bytes 65568 | tf_op jit(solution)/shard_map/ppermute | solution.py:85
  22.7 2.0 %collective-permute-done.3 = f32[64,256]{1,0:T(8,128)S(1)} collective-permute-done((f32[64,256]{1,0:T(8,128)S(1)}, f32[64,256]{1,0:T(8,128)S(1)}, u32[]{:S(2)}, u32[]{:S(2)}) %collective-permute-start.3) | collective-permute-done | bytes 65568 | tf_op jit(solution)/shard_map/ppermute | solution.py:85
  24.7 0.7 %collective-permute-done.1 = f32[64,256]{1,0:T(8,128)S(1)} collective-permute-done((f32[64,256]{1,0:T(8,128)S(1)}, f32[64,256]{1,0:T(8,128)S(1)}, u32[]{:S(2)}, u32[]{:S(2)}) %collective-permute-start.1) | collective-permute-done | bytes 65568 | tf_op jit(solution)/shard_map/ppermute | solution.py:85
  25.5 5.8 %all_gather.3 = f32[256,256]{1,0:T(8,128)S(1)} all-gather(f32[64,256]{1,0:T(8,128)S(1)} %fusion.14), channel_id=1, replica_groups=mesh['ev'=8,'col'=4] {'col'}, dimensions={0}, use_global_device_ids=true | all-gather | bytes 327680 | tf_op jit(solution)/shard_map/all_gather | solution.py:95
  31.7 1.2 %collective-permute-start.8 = (f32[64,256]{1,0:T(8,128)S(1)}, f32[64,256]{1,0:T(8,128)S(1)}, u32[]{:S(2)}, u32[]{:S(2)}) collective-permute-start(f32[64,256]{1,0:T(8,128)S(1)} %fusion.35), channel_id=1, source_target_pairs={{0,8},{4,12},{8,0},{12,4},{16,24},{20,28},{24,16},{28,20},{1,9},{5... | collective-permute-start | bytes 196616 | tf_op jit(solution)/shard_map/ppermute | solution.py:35
  32.9 1.1 %collective-permute-start.9 = (f32[64,256]{1,0:T(8,128)S(1)}, f32[64,256]{1,0:T(8,128)S(1)}, u32[]{:S(2)}, u32[]{:S(2)}) collective-permute-start(f32[64,256]{1,0:T(8,128)S(1)} %fusion.35), channel_id=1, source_target_pairs={{0,12},{4,8},{8,4},{12,0},{16,28},{20,24},{24,20},{28,16},{1,13},{... | collective-permute-start | bytes 196616 | tf_op jit(solution)/shard_map/ppermute | solution.py:35
  34.0 1.3 %collective-permute-start.7 = (f32[64,256]{1,0:T(8,128)S(1)}, f32[64,256]{1,0:T(8,128)S(1)}, u32[]{:S(2)}, u32[]{:S(2)}) collective-permute-start(f32[64,256]{1,0:T(8,128)S(1)} %fusion.35), channel_id=1, source_target_pairs={{0,4},{4,0},{8,12},{12,8},{16,20},{20,16},{24,28},{28,24},{1,5},{5... | collective-permute-start | bytes 196616 | tf_op jit(solution)/shard_map/ppermute | solution.py:35
  35.2 1.4 %collective-permute-done.8 = f32[64,256]{1,0:T(8,128)S(1)} collective-permute-done((f32[64,256]{1,0:T(8,128)S(1)}, f32[64,256]{1,0:T(8,128)S(1)}, u32[]{:S(2)}, u32[]{:S(2)}) %collective-permute-start.8) | collective-permute-done | bytes 65568 | tf_op jit(solution)/shard_map/ppermute | solution.py:35
  36.6 1.5 %collective-permute-done.9 = f32[64,256]{1,0:T(8,128)S(1)} collective-permute-done((f32[64,256]{1,0:T(8,128)S(1)}, f32[64,256]{1,0:T(8,128)S(1)}, u32[]{:S(2)}, u32[]{:S(2)}) %collective-permute-start.9) | collective-permute-done | bytes 65568 | tf_op jit(solution)/shard_map/ppermute | solution.py:35
  38.1 1.0 %collective-permute-done.7 = f32[64,256]{1,0:T(8,128)S(1)} collective-permute-done((f32[64,256]{1,0:T(8,128)S(1)}, f32[64,256]{1,0:T(8,128)S(1)}, u32[]{:S(2)}, u32[]{:S(2)}) %collective-permute-start.7) | collective-permute-done | bytes 65568 | tf_op jit(solution)/shard_map/ppermute | solution.py:35
  39.2 2.8 %collective-permute-start.10 = (f32[64,256]{1,0:T(8,128)S(1)}, f32[64,256]{1,0:T(8,128)S(1)}, u32[]{:S(2)}, u32[]{:S(2)}) collective-permute-start(f32[64,256]{1,0:T(8,128)S(1)} %add_add_fusion), channel_id=1, source_target_pairs={{0,16},{4,20},{8,24},{12,28},{16,0},{20,4},{24,8},{28,12},{1,17},{... | collective-permute-start | bytes 196616 | tf_op jit(solution)/shard_map/ppermute | solution.py:35
  41.9 3.6 %collective-permute-done.10 = f32[64,256]{1,0:T(8,128)S(1)} collective-permute-done((f32[64,256]{1,0:T(8,128)S(1)}, f32[64,256]{1,0:T(8,128)S(1)}, u32[]{:S(2)}, u32[]{:S(2)}) %collective-permute-start.10) | collective-permute-done | bytes 65568 | tf_op jit(solution)/shard_map/ppermute | solution.py:35
  45.5 0.6 %add.117 = f32[64,256]{1,0:T(8,128)} add(f32[64,256]{1,0:T(8,128)S(1)} %add_add_fusion, f32[64,256]{1,0:T(8,128)S(1)} %collective-permute-done.10) | non-fusion elementwise | flops 16384 | bytes 196608 | tf_op jit(solution)/shard_map/add | solution.py:37
  (32 shorter events, 3.0 us)
Async XLA Ops:
  0.0 2.2 %copy-start.1 = (s32[16384]{0:T(1024)S(1)}, s32[16384]{0:T(1024)}, u32[]{:S(2)}) copy-start(s32[16384]{0:T(1024)} %param.4) | copy-start | bytes 196612
  0.0 2.2 %copy-start = (bf16[64,16384]{1,0:T(8,128)(2,1)S(1)}, bf16[64,16384]{1,0:T(8,128)(2,1)}, u32[]{:S(2)}) copy-start(bf16[64,16384]{1,0:T(8,128)(2,1)} %param.3) | copy-start | bytes 6291460
  7.4 12.1 %collective-permute-start.6 = (f32[64,256]{1,0:T(8,128)S(1)}, f32[64,256]{1,0:T(8,128)S(1)}, u32[]{:S(2)}, u32[]{:S(2)}) collective-permute-start(f32[64,256]{1,0:T(8,128)S(1)} %bitcast.52), channel_id=1, source_target_pairs={{0,28},{4,24},{8,20},{12,16},{16,12},{20,8},{24,4},{28,0},{1,29},{... | collective-permute-start | bytes 196616 | tf_op jit(solution)/shard_map/ppermute | solution.py:85
  13.6 6.8 %collective-permute-start.5 = (f32[64,256]{1,0:T(8,128)S(1)}, f32[64,256]{1,0:T(8,128)S(1)}, u32[]{:S(2)}, u32[]{:S(2)}) collective-permute-start(f32[64,256]{1,0:T(8,128)S(1)} %bitcast.50), channel_id=1, source_target_pairs={{0,24},{4,28},{8,16},{12,20},{16,8},{20,12},{24,0},{28,4},{1,25},{... | collective-permute-start | bytes 196616 | tf_op jit(solution)/shard_map/ppermute | solution.py:85
  13.9 8.8 %collective-permute-start.4 = (f32[64,256]{1,0:T(8,128)S(1)}, f32[64,256]{1,0:T(8,128)S(1)}, u32[]{:S(2)}, u32[]{:S(2)}) collective-permute-start(f32[64,256]{1,0:T(8,128)S(1)} %bitcast.46), channel_id=1, source_target_pairs={{0,20},{4,16},{8,28},{12,24},{16,4},{20,0},{24,12},{28,8},{1,21},{... | collective-permute-start | bytes 196616 | tf_op jit(solution)/shard_map/ppermute | solution.py:85
  14.8 9.9 %collective-permute-start.3 = (f32[64,256]{1,0:T(8,128)S(1)}, f32[64,256]{1,0:T(8,128)S(1)}, u32[]{:S(2)}, u32[]{:S(2)}) collective-permute-start(f32[64,256]{1,0:T(8,128)S(1)} %bitcast.47), channel_id=1, source_target_pairs={{0,16},{4,20},{8,24},{12,28},{16,0},{20,4},{24,8},{28,12},{1,17},{... | collective-permute-start | bytes 196616 | tf_op jit(solution)/shard_map/ppermute | solution.py:85
  16.9 7.8 %collective-permute-start.2 = (f32[64,256]{1,0:T(8,128)S(1)}, f32[64,256]{1,0:T(8,128)S(1)}, u32[]{:S(2)}, u32[]{:S(2)}) collective-permute-start(f32[64,256]{1,0:T(8,128)S(1)} %bitcast.48), channel_id=1, source_target_pairs={{0,12},{4,8},{8,4},{12,0},{16,28},{20,24},{24,20},{28,16},{1,13},{... | collective-permute-start | bytes 196616 | tf_op jit(solution)/shard_map/ppermute | solution.py:85
  19.6 5.9 %collective-permute-start.1 = (f32[64,256]{1,0:T(8,128)S(1)}, f32[64,256]{1,0:T(8,128)S(1)}, u32[]{:S(2)}, u32[]{:S(2)}) collective-permute-start(f32[64,256]{1,0:T(8,128)S(1)} %bitcast.51), channel_id=1, source_target_pairs={{0,8},{4,12},{8,0},{12,4},{16,24},{20,28},{24,16},{28,20},{1,9},{5... | collective-permute-start | bytes 196616 | tf_op jit(solution)/shard_map/ppermute | solution.py:85
  20.4 5.1 %collective-permute-start = (f32[64,256]{1,0:T(8,128)S(1)}, f32[64,256]{1,0:T(8,128)S(1)}, u32[]{:S(2)}, u32[]{:S(2)}) collective-permute-start(f32[64,256]{1,0:T(8,128)S(1)} %bitcast.49), channel_id=1, source_target_pairs={{0,4},{4,0},{8,12},{12,8},{16,20},{20,16},{24,28},{28,24},{1,5},{5... | collective-permute-start | bytes 196616 | tf_op jit(solution)/shard_map/ppermute | solution.py:85
  31.7 5.0 %collective-permute-start.8 = (f32[64,256]{1,0:T(8,128)S(1)}, f32[64,256]{1,0:T(8,128)S(1)}, u32[]{:S(2)}, u32[]{:S(2)}) collective-permute-start(f32[64,256]{1,0:T(8,128)S(1)} %fusion.35), channel_id=1, source_target_pairs={{0,8},{4,12},{8,0},{12,4},{16,24},{20,28},{24,16},{28,20},{1,9},{5... | collective-permute-start | bytes 196616 | tf_op jit(solution)/shard_map/ppermute | solution.py:35
  32.9 5.2 %collective-permute-start.9 = (f32[64,256]{1,0:T(8,128)S(1)}, f32[64,256]{1,0:T(8,128)S(1)}, u32[]{:S(2)}, u32[]{:S(2)}) collective-permute-start(f32[64,256]{1,0:T(8,128)S(1)} %fusion.35), channel_id=1, source_target_pairs={{0,12},{4,8},{8,4},{12,0},{16,28},{20,24},{24,20},{28,16},{1,13},{... | collective-permute-start | bytes 196616 | tf_op jit(solution)/shard_map/ppermute | solution.py:35
  34.0 5.2 %collective-permute-start.7 = (f32[64,256]{1,0:T(8,128)S(1)}, f32[64,256]{1,0:T(8,128)S(1)}, u32[]{:S(2)}, u32[]{:S(2)}) collective-permute-start(f32[64,256]{1,0:T(8,128)S(1)} %fusion.35), channel_id=1, source_target_pairs={{0,4},{4,0},{8,12},{12,8},{16,20},{20,16},{24,28},{28,24},{1,5},{5... | collective-permute-start | bytes 196616 | tf_op jit(solution)/shard_map/ppermute | solution.py:35
  39.2 6.3 %collective-permute-start.10 = (f32[64,256]{1,0:T(8,128)S(1)}, f32[64,256]{1,0:T(8,128)S(1)}, u32[]{:S(2)}, u32[]{:S(2)}) collective-permute-start(f32[64,256]{1,0:T(8,128)S(1)} %add_add_fusion), channel_id=1, source_target_pairs={{0,16},{4,20},{8,24},{12,28},{16,0},{20,4},{24,8},{28,12},{1,17},{... | collective-permute-start | bytes 196616 | tf_op jit(solution)/shard_map/ppermute | solution.py:35
